TPU v7x, 32 devices: a whole 2x2x4 slice. The times are simulated.
32 devices in a mesh: ctx: 8 (over z, y), head: 4 (over x, core).
Axes of the slice: x: 2, y: 2, z: 4, core: 2. Of those that a mesh axis runs over, the one named last changes fastest.
Arguments:
- x_pool: bfloat16 [3072, 5120], P(('ctx', 'head')), may hold values from -6 to 6
- pool_dest: int32 [3072], replicated, may hold values from -1 to 2047, as said below
- seq_len: int32 [8, 8], P('ctx'), may hold values from 1 to 128, 256 in all within a row
- norm_gain: float32 [5120], replicated, may hold values from 0.1 to 1.9
- w_query: bfloat16 [5120, 2560], P(None, 'head'), may hold values from -0.078125 to 0.078125
- q_bias: float32 [2560], P('head'), may hold values from -102 to 102
- key_projection_weight: bfloat16 [5120, 512], P(None, 'head'), may hold values from -0.078125 to 0.078125
- key_bias_vector: float32 [512], P('head'), may hold values from -5 to 5
- value_projection_weight: bfloat16 [5120, 512], P(None, 'head'), may hold values from -0.078125 to 0.078125
- value_bias_vector: float32 [512], P('head'), may hold values from -3 to 3
- w_out: bfloat16 [2560, 5120], P('head'), may hold values from -0.125 to 0.125
Outputs:
- attn_out: bfloat16 [2048, 5120], P('ctx', 'head')
Inputs may be any that keep to these rules, and one draw needn't show every extreme that they name: `pool_dest`: each value is -1 for an empty pool row or o * 256 + j for slot j of context shard o; every slot of every shard is named by exactly one pool row; the pool rows of one device name at most 12 slots of any one shard. `seq_len`: each shard's lengths sum to 256.
All inputs are finite; a program needn't handle non-finite values.
Results may differ from a plain program's by a relative error of at most 0.005.
The roundings to bfloat16 on the way count: a program that leaves them out, or rounds other values in their place, can miss the bound.
Values may be sent and summed in bfloat16 or wider, within the bound.
No kernel may reach another device: no remote copies, remote signals or barrier semaphores. Data moves between devices by JAX's collectives and lax.ppermute only.
A program may use at most 128 MiB of HBM per device.

v0:
```python
import math

import jax
import jax.numpy as jnp
from jax import lax
from jax.sharding import PartitionSpec as P

HEAD_SIZE = 128
PACKED_SLOTS = 256


rope_base = 1000000.0
norm_eps = 1e-06


def send_places(targets, owner_count, capacity, pack_len):
    is_filled = targets >= 0
    owner_ids = jnp.where(is_filled, targets // pack_len, -1)
    membership = (owner_ids[:, None] == jnp.arange(owner_count, dtype=jnp.int32)[None, :]).astype(
        jnp.int32
    )
    earlier = jnp.cumsum(membership, axis=0) - membership
    rank_in = jnp.sum(earlier * membership, axis=1)
    return jnp.where(is_filled, owner_ids * capacity + rank_in, owner_count * capacity)


def slot_order(targets, owner_count, capacity, pack_len):
    places = send_places(targets, owner_count, capacity, pack_len)
    blank_slots = jnp.full((owner_count * capacity,), -1, jnp.int32)
    return blank_slots.at[places].set(jnp.where(targets >= 0, targets % pack_len, -1), mode="drop")


def place_rows(buffer, incoming, slot_ids):
    where_to = jnp.where(slot_ids >= 0, slot_ids, buffer.shape[0])
    return buffer.at[where_to].set(incoming, mode="drop")


def positions_of(lengths_row, pack_len):
    seq_ends = jnp.cumsum(lengths_row)
    index_col = jnp.arange(pack_len, dtype=jnp.int32)[:, None]
    finished = (seq_ends[None, :] <= index_col).astype(jnp.int32)
    segment = jnp.sum(finished, axis=1)
    sequence_starts = index_col[:, 0] - jnp.sum(finished * lengths_row[None, :], axis=1)
    return (segment, sequence_starts)


def apply_rotary(values, sequence_starts, head_dim):
    half_dim = head_dim // 2
    frequency = jnp.exp(
        jnp.arange(half_dim, dtype=jnp.float32) * (-2.0 * math.log(rope_base) / head_dim)
    )
    angles = sequence_starts.astype(jnp.float32)[:, None] * frequency[None, :]
    cosine = jnp.cos(angles)[:, None, :]
    sine_table = jnp.sin(angles)[:, None, :]
    first_half = values[..., :half_dim]
    second_half = values[..., half_dim:]
    return jnp.concatenate(
        [
            first_half * cosine - second_half * sine_table,
            second_half * cosine + first_half * sine_table,
        ],
        axis=-1,
    )


def local(
    x_pool,
    pool_dest,
    seq_len,
    norm_gain,
    w_query,
    q_bias,
    key_projection_weight,
    key_bias_vector,
    value_projection_weight,
    value_bias_vector,
    w_out,
):
    ctx_count = lax.axis_size("ctx")
    head_count = lax.axis_size("head")
    pool_rows = x_pool.shape[0]
    width = x_pool.shape[1]
    capacity = pool_rows // ctx_count
    pack_len = PACKED_SLOTS
    head_dim = HEAD_SIZE
    ctx_index = lax.axis_index("ctx")
    table_rows = pool_dest.reshape(ctx_count * head_count, pool_rows)
    my_row = lax.dynamic_index_in_dim(
        table_rows, lax.axis_index(("ctx", "head")), 0, keepdims=False
    )
    places = send_places(my_row, ctx_count, capacity, pack_len)
    source_rows = (
        jnp.full((ctx_count * capacity,), pool_rows, jnp.int32)
        .at[places]
        .set(jnp.arange(pool_rows, dtype=jnp.int32), mode="drop")
    )
    padded_pool = jnp.concatenate([x_pool, jnp.zeros((1, width), x_pool.dtype)], axis=0)
    outgoing = padded_pool[source_rows]
    all_slots = jax.vmap(lambda targets: slot_order(targets, ctx_count, capacity, pack_len))(
        table_rows
    )
    my_slots = lax.dynamic_index_in_dim(
        all_slots.reshape(ctx_count * head_count, ctx_count, capacity), ctx_index, 1, keepdims=False
    )
    empty_pack = jnp.zeros((pack_len, width), x_pool.dtype)
    fanned = jnp.broadcast_to(
        outgoing.reshape(ctx_count, 1, capacity, width), (ctx_count, head_count, capacity, width)
    )
    fanned = fanned.reshape(ctx_count * head_count * capacity, width)
    arrived = lax.all_to_all(fanned, ("ctx", "head"), split_axis=0, concat_axis=0, tiled=True)
    packed = place_rows(empty_pack, arrived, my_slots.reshape(-1))
    segment, sequence_starts = positions_of(seq_len[0], pack_len)
    values_wide = packed.astype(jnp.float32)
    normalized_input = (
        values_wide
        * lax.rsqrt(jnp.mean(values_wide * values_wide, axis=-1, keepdims=True) + norm_eps)
        * norm_gain
    ).astype(jnp.bfloat16)
    local_heads = w_query.shape[1] // head_dim
    local_kv = key_projection_weight.shape[1] // head_dim
    query_group_count = local_heads // local_kv
    query_matrix = jnp.dot(normalized_input, w_query, preferred_element_type=jnp.float32) + q_bias
    query_matrix = apply_rotary(
        query_matrix.reshape(pack_len, local_heads, head_dim), sequence_starts, head_dim
    ).astype(jnp.bfloat16)
    query_matrix = query_matrix.reshape(pack_len, local_kv, query_group_count, head_dim)
    projected_key_rows = (
        jnp.dot(normalized_input, key_projection_weight, preferred_element_type=jnp.float32)
        + key_bias_vector
    )
    projected_key_rows = apply_rotary(
        projected_key_rows.reshape(pack_len, local_kv, head_dim), sequence_starts, head_dim
    ).astype(jnp.bfloat16)
    projected_value_rows = (
        jnp.dot(normalized_input, value_projection_weight, preferred_element_type=jnp.float32)
        + value_bias_vector
    ).astype(jnp.bfloat16)
    projected_value_rows = projected_value_rows.reshape(pack_len, local_kv, head_dim)
    block_len = min(512, pack_len)
    block_count = pack_len // block_len
    score_scale = 1.0 / math.sqrt(head_dim)
    slot_ids = jnp.arange(pack_len, dtype=jnp.int32)

    def attend(block_index):
        row_start = block_index * block_len
        query_slots = row_start + jnp.arange(block_len, dtype=jnp.int32)
        scores = (
            jnp.einsum(
                "qkgd,tkd->kgqt",
                query_matrix,
                projected_key_rows,
                preferred_element_type=jnp.float32,
            )
            * score_scale
        )
        allowed = (segment[:, None] == segment[None, :]) & (
            slot_ids[None, :] <= query_slots[:, None]
        )
        scores = jnp.where(allowed[None, None], scores, -1e30)
        row_max = jnp.max(scores, axis=-1, keepdims=True)
        weights = jnp.exp(scores - row_max)
        row_total = jnp.sum(weights, axis=-1, keepdims=True)
        probability = (weights / row_total).astype(jnp.bfloat16)
        mixed_block = jnp.einsum(
            "kgqt,tkd->qkgd", probability, projected_value_rows, preferred_element_type=jnp.float32
        )
        return mixed_block.astype(jnp.bfloat16).reshape(block_len, local_heads * head_dim)

    mixed_heads = lax.map(attend, jnp.arange(block_count, dtype=jnp.int32)).reshape(
        pack_len, local_heads * head_dim
    )
    partial_out = jnp.dot(mixed_heads, w_out, preferred_element_type=jnp.float32)
    return lax.psum_scatter(partial_out, "head", scatter_dimension=1, tiled=True).astype(
        jnp.bfloat16
    )


def solution(mesh):
    in_specs = (
        P(("ctx", "head"), None),
        P(),
        P("ctx", None),
        P(),
        P(None, "head"),
        P("head"),
        P(None, "head"),
        P("head"),
        P(None, "head"),
        P("head"),
        P("head", None),
    )
    out_specs = P("ctx", "head")
    return jax.shard_map(local, mesh=mesh, in_specs=in_specs, out_specs=out_specs, check_vma=False)
```

profile of v0, /device:TPU:0, one launch (start us, length us, event | category | flops | bytes accessed | tf_op | source)
XLA Modules:
  0.0 239.8 jit_solution(2713453215714285160)
XLA Ops:
  6.5 0.0 copy-start
  6.5 0.9 reshape.521
  7.4 0.1 fusion.34
  7.5 0.1 reduce_window_sum.30
  7.7 0.2 select_reduce_fusion
  7.9 0.9 scatter_custom_fusion
  8.8 1.3 concatenate.20
  10.1 2.1 gather_fusion
  12.2 1.3 broadcast_in_dim.91
  13.5 3.1 %broadcast_in_dim.92 = bf16[8,4,12,5120]{3,2,1,0:T(8,128)(2,1)} broadcast(bf16[8,12,5120]{2,1,0:T(8,128)(2,1)S(1)} %broadcast_in_dim.91), dimensions={0,2,3} | broadcast | bytes 4915200 | tf_op jit(solution)/shard_map/broadcast_in_dim | solution.py:106
  16.5 0.0 copy-start.2
  16.5 0.0 copy-start.4
  16.5 0.0 copy-start.3
  16.6 0.0 copy-start.5
  16.6 7.4 %all-to-all-start = ((bf16[32,12,5120]{2,1,0:T(8,128)(2,1)}), bf16[32,12,5120]{2,1,0:T(8,128)(2,1)}, u32[]{:S(2)}, u32[]{:S(2)}) async-start(bf16[32,12,5120]{2,1,0:T(8,128)(2,1)} %bitcast.65), calls=%async_computation | async-start | bytes 10485760 | tf_op jit(solution)/shard_map/all_to_all | solution.py:110
  24.0 0.0 reduce-scatter.2.cloned.1.call-start
  24.0 0.0 copy-done.2
  24.0 0.1 reshape.520
  24.1 0.1 copy.31
  24.2 2.5 %fusion.61 = s32[32,96]{0,1:T(8,128)S(1)} fusion(s32[32,96]{0,1:T(8,128)S(1)} %copy.31), kind=kOutput, calls=%fused_computation.123 | output fusion | flops 2503680 | bytes 24576 | tf_op jit(solution)/shard_map/vmap(jit(cumsum))/reduce_window_sum | solution.py:22
  26.8 0.1 copy.32
  26.9 0.0 copy-done.4
  26.9 0.1 multiply_reduce_fusion
  27.0 0.0 copy-done.3
  27.0 0.1 and_reduce_fusion
  27.0 0.1 reshape.559
  27.1 0.1 reshape.561
  27.2 12.0 %scatter_custom_fusion.2 = s32[3072]{0:T(1024)S(1)} fusion(s32[3072]{0:T(1024)S(1)} %reshape.559, s32[3072]{0:T(1024)S(1)} %reshape.561, s32[]{:T(128)} %constant.100.clone.1), kind=kCustom, calls=%fused_computation.93 | custom fusion | bytes 12292
  39.2 0.1 reshape.522
  39.3 0.1 dynamic-slice_reduce_fusion
  39.4 0.1 reshape.523
  39.5 0.0 copy-done.5
  39.5 0.2 reduce-window.8
  39.7 0.1 select_reduce_fusion.1
  39.8 0.1 fusion.22
  39.9 0.5 multiply_cosine_fusion
  40.5 100.3 %all-to-all-done = bf16[32,12,5120]{2,1,0:T(8,128)(2,1)} async-done(((bf16[32,12,5120]{2,1,0:T(8,128)(2,1)}), bf16[32,12,5120]{2,1,0:T(8,128)(2,1)}, u32[]{:S(2)}, u32[]{:S(2)}) %all-to-all-start) | async-done | bytes 3932192 | tf_op jit(solution)/shard_map/all_to_all | solution.py:110
  140.7 7.1 %reshape.555 = bf16[384,5120]{1,0:T(8,128)(2,1)} reshape(bf16[32,12,5120]{2,1,0:T(8,128)(2,1)} %all-to-all-done) | data formatting | bytes 7864320 | tf_op jit(solution)/shard_map/all_to_all | solution.py:110
  147.8 0.0 copy-start.6
  147.8 0.0 copy-start.7
  147.8 9.0 %scatter_custom_fusion.1 = bf16[256,5120]{1,0:T(8,128)(2,1)} fusion(s32[384]{0:T(512)S(1)} %fusion.49, bf16[384,5120]{1,0:T(8,128)(2,1)} %reshape.555, bf16[]{:T(256)} %constant.99.clone.1), kind=kCustom, calls=%fused_computation.18 | custom fusion | bytes 2621952 | tf_op jit(solution)/shard_map/scatter | solution.py:35
  156.8 2.5 %fusion = f32[256]{0:T(256)S(1)} fusion(bf16[256,5120]{1,0:T(8,128)(2,1)} %scatter_custom_fusion.1), kind=kLoop, calls=%fused_computation.6 | loop fusion | flops 3931904 | bytes 2622464 | tf_op jit(solution)/shard_map/reduce_sum | solution.py:116
  159.3 0.0 copy-done.6
  159.3 0.0 copy-done.7
  159.3 0.0 copy-done.1
  159.3 5.2 %convolution_add_fusion = f32[256,640]{1,0:T(8,128)S(1)} fusion(bf16[5120,640]{1,0:T(8,128)(2,1)} %param.15, f32[640]{0:T(1024)S(1)} %copy-done.7, bf16[256,5120]{1,0:T(8,128)(2,1)S(1)} %copy-done.1, f32[5120]{0:T(1024)S(1)} %copy-done.6, f32[256]{0:T(256)S(1)} %add_rsqrt_fusion), kind=kOutput, calls=%fused_computation.21 | convolution fusion | flops 1683128320 | bytes 9854464 | tf_op jit(solution)/shard_map/dot_general | solution.py:122
  164.5 0.0 copy-start.8
  164.5 0.2 copy.33
  164.8 0.2 copy.45
  165.0 0.2 copy.44
  165.3 0.0 copy-done.8
  165.3 3.3 %fusion.13 = f32[256,1,128]{0,2,1:T(8,128)S(1)} fusion(bf16[5120,128]{1,0:T(8,128)(2,1)} %param.17, f32[128]{0:T(128)S(1)} %copy-done.8, bf16[256,5120]{1,0:T(8,128)(2,1)} %scatter_custom_fusion.1, f32[5120]{0:T(1024)S(1)} %copy-done.6, f32[256]{0:T(256)S(1)} %add_rsqrt_fusion), kind=kOutput, calls=%fused_computation.25 | convolution fusion | flops 340819968 | bytes 4085248 | tf_op jit(solution)/shard_map/dot_general | solution.py:128
  168.6 0.3 fusion.36
  168.9 0.0 copy-start.9
  168.9 0.2 subtract_convert_fusion
  169.1 0.5 fusion.62
  169.5 0.2 fusion.12
  169.7 0.0 copy-done
  169.7 0.0 copy-done.9
  169.8 3.0 %convolution_convert_fusion = bf16[128,5,256]{2,0,1:T(8,128)(2,1)S(1)} fusion(bf16[5120,128]{1,0:T(8,128)(2,1)S(1)} %copy-done, f32[1,5,256,256]{2,3,1,0:T(8,128)S(1)} %get-tuple-element.39, f32[5,256]{1,0:T(8,128)S(1)} %fusion.12, f32[5,256]{1,0:T(8,128)S(1)} %get-tuple-element.38, f32[128]{0:T(128)S(1)} %copy-done.9, ...), kind=kOutput, calls=%fused_computation.22 | convolution fusion | flops 425885696 | bytes 5602816 | tf_op jit(solution)/shard_map/while/body/eval_jaxpr/kgqt,tkd->qkgd/dot_general | solution.py:164
  172.8 7.4 %fusion.63 = f32[256,5120]{1,0:T(8,128)} fusion(bf16[256,640]{0,1:T(8,128)(2,1)S(1)} %bitcast.67, bf16[640,5120]{1,0:T(8,128)(2,1)} %param.21), kind=kOutput, calls=%fused_computation.125 | convolution fusion | flops 1677721600 | bytes 12124160 | tf_op jit(solution)/shard_map/dot_general | solution.py:172
  180.2 0.0 reduce-scatter.2.cloned.1.call-update
  180.2 50.5 %reduce-scatter.2.cloned.1.call-done = f32[256,1280]{1,0:T(8,128)} async-done(((f32[256,5120]{1,0:T(8,128)}), f32[256,1280]{1,0:T(8,128)}) %reduce-scatter.2.cloned.1.call-update) | async-done | bytes 1310736 | tf_op jit(solution)/shard_map/reduce_scatter | solution.py:173
  230.7 2.2 convert_element_type.61
  (15 shorter events, 0.2 us)
Async XLA Ops:
  6.5 163.2 %copy-start = (bf16[5120,128]{1,0:T(8,128)(2,1)S(1)}, bf16[5120,128]{1,0:T(8,128)(2,1)}, u32[]{:S(2)}) copy-start(bf16[5120,128]{1,0:T(8,128)(2,1)} %param.19) | copy-start | bytes 3932164
  16.5 7.5 %copy-start.2 = (s32[3072]{0:T(1024)S(1)}, s32[3072]{0:T(1024)}, u32[]{:S(2)}) copy-start(s32[3072]{0:T(1024)} %param.12) | copy-start | bytes 36868
  16.5 10.3 %copy-start.4 = (s32[2]{0:T(128)S(1)}, s32[2]{0:T(128)}, u32[]{:S(2)}) copy-start(s32[2]{0:T(128)} %constant.124) | copy-start | bytes 28
  16.5 10.4 %copy-start.3 = (s32[2]{0:T(128)S(1)}, s32[2]{0:T(128)}, u32[]{:S(2)}) copy-start(s32[2]{0:T(128)} %constant.127) | copy-start | bytes 28
  16.6 22.9 %copy-start.5 = (s32[1,8]{1,0:T(1,128)S(1)}, s32[1,8]{1,0:T(1,128)}, u32[]{:S(2)}) copy-start(s32[1,8]{1,0:T(1,128)} %param.13) | copy-start | bytes 100
  16.6 124.2 %all-to-all-start = ((bf16[32,12,5120]{2,1,0:T(8,128)(2,1)}), bf16[32,12,5120]{2,1,0:T(8,128)(2,1)}, u32[]{:S(2)}, u32[]{:S(2)}) async-start(bf16[32,12,5120]{2,1,0:T(8,128)(2,1)} %bitcast.65), calls=%async_computation | async-start | bytes 10485760 | tf_op jit(solution)/shard_map/all_to_all | solution.py:110
  24.0 206.7 %reduce-scatter.2.cloned.1.call-start = ((), (), s32[]{:S(2)}) async-start(), calls=%async_computation.2 | async-start | bytes 6553600 | tf_op jit(solution)/shard_map/reduce_scatter | solution.py:173
  147.8 11.5 %copy-start.6 = (f32[5120]{0:T(1024)S(1)}, f32[5120]{0:T(1024)}, u32[]{:S(2)}) copy-start(f32[5120]{0:T(1024)} %param.14) | copy-start | bytes 61444
  147.8 11.5 %copy-start.7 = (f32[640]{0:T(1024)S(1)}, f32[640]{0:T(1024)}, u32[]{:S(2)}) copy-start(f32[640]{0:T(1024)} %param.16) | copy-start | bytes 7684
  156.8 2.5 %copy-start.1 = (bf16[256,5120]{1,0:T(8,128)(2,1)S(1)}, bf16[256,5120]{1,0:T(8,128)(2,1)}, u32[]{:S(2)}) copy-start(bf16[256,5120]{1,0:T(8,128)(2,1)} %scatter_custom_fusion.1) | copy-start | bytes 7864324
  164.5 0.8 copy-start.8
  168.9 0.9 copy-start.9
Sparse Core Ops, SparseCore 0:
  180.3 50.3 reduce-scatter.1
where the time goes:
time: 240 us
  waiting for transfers between devices  151 us (63%)
  local copies, waits for them, and re-layouts  39 us (16%)
  matrix products  19.3 us (8%)
  between operations  13.7 us (6%)
  other arithmetic  9.51 us (4%)
  starting transfers between devices  7.46 us (3%)
    all_to_all x1, waiting for transfers between devices, local(): lax.all_to_all(fanned, ('ctx', 'head'), split_axis=0, concat_axis=0, tile...  100 us
    reduce_scatter x1, waiting for transfers between devices, local(): lax.psum_scatter(partial_out, 'head', scatter_dimension=1, tiled=True)  50.5 us
    unnamed x25, local copies, waits for them, and re-layouts  12.6 us
    scatter x1, local copies, waits for them, and re-layouts, place_rows(): return buffer.at[where_to].set(incoming, mode='drop')  8.97 us
    all_to_all x1, starting transfers between devices, local(): lax.all_to_all(fanned, ('ctx', 'head'), split_axis=0, concat_axis=0, tile...  7.42 us
    dot_general x1, matrix products, local(): jnp.dot(mixed_heads, w_out, preferred_element_type=jnp.float32)  7.41 us
    all_to_all x1, local copies, waits for them, and re-layouts, local(): lax.all_to_all(fanned, ('ctx', 'head'), split_axis=0, concat_axis=0, tile...  7.09 us
    dot_general x1, matrix products, local(): jnp.dot(normalized_input, w_query, preferred_element_type=jnp.float32)  5.15 us
  transfers between devices with their start and end apart: 2, of which 2 were waited for; matrix products, arithmetic and copies ran while one was open for 7% of the time, Pallas kernels for 0%

commit v1 on v0

v1 whole, which is shorter than its diff:
```python
import math

import jax
import jax.numpy as jnp
from jax import lax
from jax.sharding import PartitionSpec as P

HEAD_SIZE = 128
PACKED_SLOTS = 256


rope_base = 1000000.0
norm_eps = 1e-06


def send_places(targets, owner_count, capacity, pack_len):
    is_filled = targets >= 0
    owner_ids = jnp.where(is_filled, targets // pack_len, -1)
    membership = (owner_ids[:, None] == jnp.arange(owner_count, dtype=jnp.int32)[None, :]).astype(
        jnp.int32
    )
    earlier = jnp.cumsum(membership, axis=0) - membership
    rank_in = jnp.sum(earlier * membership, axis=1)
    return jnp.where(is_filled, owner_ids * capacity + rank_in, owner_count * capacity)


def one_hot_rows(index, count):
    return (index[:, None] == jnp.arange(count, dtype=jnp.int32)[None, :]).astype(jnp.bfloat16)


def select_rows(index, values):
    picked = jnp.dot(
        one_hot_rows(index, values.shape[0]), values, preferred_element_type=jnp.float32
    )
    return picked.astype(values.dtype)


def apply_rotary(values, sequence_starts, head_dim):
    half_dim = head_dim // 2
    frequency = jnp.exp(
        jnp.arange(half_dim, dtype=jnp.float32) * (-2.0 * math.log(rope_base) / head_dim)
    )
    angles = sequence_starts.astype(jnp.float32)[:, None] * frequency[None, :]
    cosine = jnp.cos(angles)[:, None, :]
    sine_table = jnp.sin(angles)[:, None, :]
    first_half = values[..., :half_dim]
    second_half = values[..., half_dim:]
    return jnp.concatenate(
        [
            first_half * cosine - second_half * sine_table,
            second_half * cosine + first_half * sine_table,
        ],
        axis=-1,
    )


def local(
    x_pool,
    pool_dest,
    seq_len,
    norm_gain,
    w_query,
    q_bias,
    key_projection_weight,
    key_bias_vector,
    value_projection_weight,
    value_bias_vector,
    w_out,
):
    ctx_count = lax.axis_size("ctx")
    head_count = lax.axis_size("head")
    pool_rows = x_pool.shape[0]
    capacity = pool_rows // ctx_count
    group_rows = pool_rows * head_count
    group_cap = capacity * head_count
    pack_len = PACKED_SLOTS
    head_dim = HEAD_SIZE
    ctx_index = lax.axis_index("ctx")

    all_lengths = lax.all_gather(seq_len, "ctx", tiled=True)
    group_x = lax.all_gather(x_pool, "head", tiled=True)

    dest_grid = pool_dest.reshape(ctx_count, group_rows)
    my_dest = lax.dynamic_index_in_dim(dest_grid, ctx_index, 0, keepdims=False)
    is_filled = my_dest >= 0
    owner = jnp.where(is_filled, my_dest // pack_len, 0)
    slot = jnp.where(is_filled, my_dest % pack_len, 0)
    seq_ends = jnp.cumsum(all_lengths, axis=1).astype(jnp.int32)
    row_ends = jnp.take(seq_ends, owner, axis=0)
    row_lengths = jnp.take(all_lengths, owner, axis=0)
    finished = (row_ends <= slot[:, None]).astype(jnp.int32)
    sequence_starts = slot - jnp.sum(finished * row_lengths, axis=1)

    values_wide = group_x.astype(jnp.float32)
    normalized_input = (
        values_wide
        * lax.rsqrt(jnp.mean(values_wide * values_wide, axis=-1, keepdims=True) + norm_eps)
        * norm_gain
    ).astype(jnp.bfloat16)
    local_heads = w_query.shape[1] // head_dim
    local_kv = key_projection_weight.shape[1] // head_dim
    query_group_count = local_heads // local_kv
    query_matrix = jnp.dot(normalized_input, w_query, preferred_element_type=jnp.float32) + q_bias
    query_matrix = apply_rotary(
        query_matrix.reshape(group_rows, local_heads, head_dim), sequence_starts, head_dim
    ).astype(jnp.bfloat16)
    projected_key_rows = (
        jnp.dot(normalized_input, key_projection_weight, preferred_element_type=jnp.float32)
        + key_bias_vector
    )
    projected_key_rows = apply_rotary(
        projected_key_rows.reshape(group_rows, local_kv, head_dim), sequence_starts, head_dim
    ).astype(jnp.bfloat16)
    projected_value_rows = (
        jnp.dot(normalized_input, value_projection_weight, preferred_element_type=jnp.float32)
        + value_bias_vector
    ).astype(jnp.bfloat16)
    qkv = jnp.concatenate(
        [
            query_matrix.reshape(group_rows, local_heads * head_dim),
            projected_key_rows.reshape(group_rows, local_kv * head_dim),
            projected_value_rows,
        ],
        axis=1,
    )

    places = send_places(my_dest, ctx_count, group_cap, pack_len)
    send_hot = (
        places[None, :] == jnp.arange(ctx_count * group_cap, dtype=jnp.int32)[:, None]
    ).astype(jnp.bfloat16)
    outgoing = jnp.dot(send_hot, qkv, preferred_element_type=jnp.float32).astype(jnp.bfloat16)
    arrived = lax.all_to_all(outgoing, "ctx", split_axis=0, concat_axis=0, tiled=True)

    mine = (pool_dest >= 0) & (pool_dest // pack_len == ctx_index)
    mine_grid = mine.reshape(ctx_count, group_rows).astype(jnp.int32)
    rank_in = jnp.cumsum(mine_grid, axis=1) - mine_grid
    arrived_index = (
        jnp.arange(ctx_count, dtype=jnp.int32)[:, None] * group_cap + rank_in
    ).reshape(-1)
    my_slot_of_row = jnp.where(mine, pool_dest - ctx_index * pack_len, -1)
    slot_ids = jnp.arange(pack_len, dtype=jnp.int32)
    names_slot = my_slot_of_row[None, :] == slot_ids[:, None]
    source_of_slot = jnp.sum(jnp.where(names_slot, arrived_index[None, :], 0), axis=1)
    packed_qkv = select_rows(source_of_slot, arrived)

    q_width = local_heads * head_dim
    kv_width = local_kv * head_dim
    query_matrix = packed_qkv[:, :q_width].reshape(pack_len, local_kv, query_group_count, head_dim)
    projected_key_rows = packed_qkv[:, q_width : q_width + kv_width].reshape(
        pack_len, local_kv, head_dim
    )
    projected_value_rows = packed_qkv[:, q_width + kv_width :].reshape(pack_len, local_kv, head_dim)

    own_lengths = seq_len[0]
    own_ends = jnp.cumsum(own_lengths).astype(jnp.int32)
    segment = jnp.sum((own_ends[None, :] <= slot_ids[:, None]).astype(jnp.int32), axis=1)

    score_scale = 1.0 / math.sqrt(head_dim)
    scores = (
        jnp.einsum(
            "qkgd,tkd->kgqt",
            query_matrix,
            projected_key_rows,
            preferred_element_type=jnp.float32,
        )
        * score_scale
    )
    allowed = (segment[:, None] == segment[None, :]) & (slot_ids[None, :] <= slot_ids[:, None])
    scores = jnp.where(allowed[None, None], scores, -1e30)
    row_max = jnp.max(scores, axis=-1, keepdims=True)
    weights = jnp.exp(scores - row_max)
    row_total = jnp.sum(weights, axis=-1, keepdims=True)
    probability = (weights / row_total).astype(jnp.bfloat16)
    mixed_heads = jnp.einsum(
        "kgqt,tkd->qkgd", probability, projected_value_rows, preferred_element_type=jnp.float32
    )
    mixed_heads = mixed_heads.astype(jnp.bfloat16).reshape(pack_len, local_heads * head_dim)
    partial_out = jnp.dot(mixed_heads, w_out, preferred_element_type=jnp.float32)
    return lax.psum_scatter(partial_out, "head", scatter_dimension=1, tiled=True).astype(
        jnp.bfloat16
    )


def solution(mesh):
    in_specs = (
        P(("ctx", "head"), None),
        P(),
        P("ctx", None),
        P(),
        P(None, "head"),
        P("head"),
        P(None, "head"),
        P("head"),
        P(None, "head"),
        P("head"),
        P("head", None),
    )
    out_specs = P("ctx", "head")
    return jax.shard_map(local, mesh=mesh, in_specs=in_specs, out_specs=out_specs, check_vma=False)
```

time: 240 us -> 154 us (0.64)
  waiting for transfers between devices: 151 us -> 75.2 us
  local copies, waits for them, and re-layouts: 39 us -> 4.49 us
  blocking collectives: 0 us -> 22.3 us
    all_to_all x1, waiting for transfers between devices: 100 us -> 16.3 us  [local(): lax.all_to_all(outgoing, 'ctx', split_axis=0, concat_axis=0, tiled=True)]
    all_gather x0 -> x1, blocking collectives: none -> 22.3 us  [local(): all_lengths = lax.all_gather(seq_len, 'ctx', tiled=True)]
    unnamed x25 -> x16, local copies, waits for them, and re-layouts: 12.6 us -> 0.29 us
    scatter x2 -> x0, local copies, waits for them, and re-layouts: 9.85 us -> none  [the longest x1 8.97 us: place_rows(): return buffer.at[where_to].set(incoming, mode='drop')]
    all_gather x0 -> x1, waiting for transfers between devices: none -> 8.57 us  [local(): group_x = lax.all_gather(x_pool, 'head', tiled=True)]
    all_to_all x1 -> x0, local copies, waits for them, and re-layouts: 7.09 us -> none  [local(): lax.all_to_all(fanned, ('ctx', 'head'), split_axis=0, concat_axis=0, tile...]
    broadcast_in_dim x2 -> x0, local copies, waits for them, and re-layouts: 4.39 us -> none  [local(): jnp.broadcast_to(outgoing.reshape(ctx_count, 1, capacity, width), (ctx_co...]
    dot_general x2 -> x5, matrix products: 3.49 us -> 6.63 us  [the longest x1 4.03 us: local(): jnp.dot(normalized_input, value_projection_weight, preferred_element_type...]
  transfers between devices with their start and end apart: 2 -> 3, of which waited for: 2 -> 3; matrix products, arithmetic and copies ran while one was open for 7% -> 5% of each run, Pallas kernels for 0% -> 0%
where the time goes in v1:
time: 154 us
  waiting for transfers between devices  75.2 us (49%)
  blocking collectives  22.3 us (14%)
  matrix products  21.1 us (14%)
  between operations  13.7 us (9%)
  other arithmetic  11.4 us (7%)
  starting transfers between devices  5.74 us (4%)
  local copies, waits for them, and re-layouts  4.49 us (3%)
    reduce_scatter x1, waiting for transfers between devices, local(): lax.psum_scatter(partial_out, 'head', scatter_dimension=1, tiled=True)  49.7 us
    all_gather x1, blocking collectives, local(): all_lengths = lax.all_gather(seq_len, 'ctx', tiled=True)  22.3 us
    all_to_all x1, waiting for transfers between devices, local(): lax.all_to_all(outgoing, 'ctx', split_axis=0, concat_axis=0, tiled=True)  16.3 us
    all_gather x1, waiting for transfers between devices, local(): group_x = lax.all_gather(x_pool, 'head', tiled=True)  8.57 us
    dot_general x1, matrix products, local(): jnp.dot(mixed_heads, w_out, preferred_element_type=jnp.float32)  7.41 us
    dot_general x1, matrix products, local(): jnp.dot(normalized_input, w_query, preferred_element_type=jnp.float32)  5.55 us
    all_to_all x1, starting transfers between devices, local(): lax.all_to_all(outgoing, 'ctx', split_axis=0, concat_axis=0, tiled=True)  5.52 us
    dot_general x1, matrix products, local(): jnp.dot(normalized_input, value_projection_weight, preferred_element_type...  4.03 us
  transfers between devices with their start and end apart: 3, of which 3 were waited for; matrix products, arithmetic and copies ran while one was open for 5% of the time, Pallas kernels for 0%

profile of v1, /device:TPU:0, one launch (start us, length us, event | category | flops | bytes accessed | tf_op | source)
XLA Modules:
  0.0 154.0 jit_solution(416668922146082135)
XLA Ops:
  6.5 0.0 copy-start
  6.5 0.0 all-gather.3.cloned.1.call-start
  6.5 0.7 all-gather.3.cloned.1.call-update
  7.3 0.8 reduce-window.32
  8.1 22.3 %all-gather = s32[8,1,8]{2,1,0:T(1,128)S(1)} all-gather(s32[1,1,8]{2,1,0:T(1,128)} %bitcast.83), channel_id=1, replica_groups=mesh['ctx'=8,'head'=4] {'ctx'}, dimensions={0}, use_global_device_ids=true | all-gather | bytes 288 | tf_op jit(solution)/shard_map/all_gather | solution.py:80
  30.4 0.2 reduce_window_sum.54
  30.6 0.1 add.90
  30.6 0.7 reshape.367
  31.4 0.9 reduce-window.30
  32.3 0.2 slice_reduce_fusion
  32.5 0.1 add_bitcast_fusion
  32.6 0.1 copy.35
  32.8 0.0 copy-start.4
  32.8 0.0 copy-start.6
  32.8 1.1 gather_fusion.1
  33.9 1.1 gather_fusion
  35.1 0.3 fusion.20
  35.4 0.2 fusion.19
  35.6 0.4 multiply_cosine_fusion.1
  36.1 8.6 %all-gather.3.cloned.1.call-done = bf16[384,5120]{1,0:T(8,128)(2,1)} async-done(((bf16[96,5120]{1,0:T(8,128)(2,1)}), bf16[384,5120]{1,0:T(8,128)(2,1)}) %all-gather.3.cloned.1.call-update) | async-done | bytes 3932176 | tf_op jit(solution)/shard_map/all_gather | solution.py:81
  44.6 0.0 copy-start.1
  44.6 3.1 %fusion = f32[384]{0:T(512)S(1)} fusion(bf16[384,5120]{1,0:T(8,128)(2,1)} %all-gather.3.cloned.1.call-done), kind=kLoop, calls=%fused_computation.4 | loop fusion | flops 5897856 | bytes 3933696 | tf_op jit(solution)/shard_map/reduce_sum | solution.py:97
  47.8 0.0 copy-done
  47.8 0.0 copy-done.4
  47.8 0.0 copy-done.6
  47.8 0.1 copy-done.1
  47.9 0.0 copy-start.5
  47.9 1.5 fusion.6
  49.5 1.1 fusion.31
  50.5 0.0 copy-done.5
  50.6 5.5 %convolution_add_fusion = f32[384,640]{1,0:T(8,128)S(1)} fusion(bf16[5120,640]{1,0:T(8,128)(2,1)} %param.17, f32[640]{0:T(1024)S(1)} %copy-done.5, bf16[384,5120]{1,0:T(8,128)(2,1)S(1)} %copy-done.1, f32[5120]{0:T(1024)S(1)} %copy-done.4, f32[384]{0:T(512)S(1)} %add_rsqrt_fusion), kind=kOutput, calls=%fused_computation.14 | convolution fusion | flops 2524692480 | bytes 11493376 | tf_op jit(solution)/shard_map/dot_general | solution.py:103
  56.1 0.0 copy-start.7
  56.1 0.3 copy.36
  56.4 0.1 subtract_convert_fusion
  56.6 0.1 pad_maximum_fusion
  56.7 0.1 copy-done.7
  56.8 0.0 copy-start.2
  56.8 4.0 %fusion.7 = bf16[384,128]{0,1:T(8,128)(2,1)S(1)} fusion(bf16[5120,128]{1,0:T(8,128)(2,1)} %param.21, f32[128]{0:T(128)S(1)} %copy-done.7, bf16[384,5120]{1,0:T(8,128)(2,1)} %all-gather.3.cloned.1.call-done, f32[5120]{0:T(1024)} %param.16, f32[384]{0:T(512)S(1)} %add_rsqrt_fusion), kind=kOutput, calls=%fused_computation.22 | convolution fusion | flops 511279104 | bytes 5363712 | tf_op jit(solution)/shard_map/dot_general | solution.py:115
  60.8 0.0 copy-start.3
  60.8 0.0 copy-done.2
  60.8 1.4 convolution_convert_fusion
  62.2 5.5 %all-to-all-start = ((bf16[8,48,896]{2,1,0:T(8,128)(2,1)}), bf16[8,48,896]{2,1,0:T(8,128)(2,1)S(1)}, u32[]{:S(2)}, u32[]{:S(2)}) async-start(bf16[8,48,896]{2,1,0:T(8,128)(2,1)} %bitcast.9), calls=%async_computation | async-start | bytes 1376256 | tf_op jit(solution)/shard_map/all_to_all | solution.py:132
  67.8 0.2 reduce-scatter.2.cloned.1.call-start
  68.0 0.0 copy-done.3
  68.1 0.9 reduce-window.21
  68.9 0.2 slice_reduce_fusion.1
  69.2 0.1 broadcast_add_fusion
  69.3 0.1 convert_reduce_fusion
  69.4 0.4 select_reduce_fusion
  69.8 0.1 fusion.17
  69.9 16.3 %all-to-all-done = bf16[8,48,896]{2,1,0:T(8,128)(2,1)S(1)} async-done(((bf16[8,48,896]{2,1,0:T(8,128)(2,1)}), bf16[8,48,896]{2,1,0:T(8,128)(2,1)S(1)}, u32[]{:S(2)}, u32[]{:S(2)}) %all-to-all-start) | async-done | bytes 688160 | tf_op jit(solution)/shard_map/all_to_all | solution.py:132
  86.2 0.5 convolution_convert_fusion.1
  86.7 0.2 copy.37
  86.9 0.4 fusion.49
  87.2 0.2 fusion.5
  87.4 0.4 convolution_convert_fusion.2
  87.8 7.4 %fusion.50 = f32[256,5120]{1,0:T(8,128)} fusion(bf16[256,640]{0,1:T(8,128)(2,1)S(1)} %bitcast.79, bf16[640,5120]{1,0:T(8,128)(2,1)} %param.23), kind=kOutput, calls=%fused_computation.123 | convolution fusion | flops 1677721600 | bytes 12124160 | tf_op jit(solution)/shard_map/dot_general | solution.py:178
  95.2 0.0 reduce-scatter.2.cloned.1.call-update
  95.2 49.7 %reduce-scatter.2.cloned.1.call-done = f32[256,1280]{1,0:T(8,128)} async-done(((f32[256,5120]{1,0:T(8,128)}), f32[256,1280]{1,0:T(8,128)}) %reduce-scatter.2.cloned.1.call-update) | async-done | bytes 1310736 | tf_op jit(solution)/shard_map/reduce_scatter | solution.py:179
  144.9 2.2 %convert_element_type.88 = bf16[256,1280]{1,0:T(8,128)(2,1)} convert(f32[256,1280]{1,0:T(8,128)} %reduce-scatter.2.cloned.1.call-done) | non-fusion elementwise | flops 327680 | bytes 1966080 | tf_op jit(solution)/shard_map/convert_element_type | solution.py:179
  (22 shorter events, 0.3 us)
Async XLA Ops:
  6.5 41.2 %copy-start = (bf16[5120,128]{1,0:T(8,128)(2,1)S(1)}, bf16[5120,128]{1,0:T(8,128)(2,1)}, u32[]{:S(2)}) copy-start(bf16[5120,128]{1,0:T(8,128)(2,1)} %param.19) | copy-start | bytes 3932164
  6.5 38.1 %all-gather.3.cloned.1.call-start = ((), (), s32[]{:S(2)}) async-start(), calls=%async_computation.2 | async-start | bytes 4915200 | tf_op jit(solution)/shard_map/all_gather | solution.py:81
  32.8 15.0 %copy-start.4 = (f32[5120]{0:T(1024)S(1)}, f32[5120]{0:T(1024)}, u32[]{:S(2)}) copy-start(f32[5120]{0:T(1024)} %param.16) | copy-start | bytes 61444
  32.8 15.0 %copy-start.6 = (f32[128]{0:T(128)S(1)}, f32[128]{0:T(128)}, u32[]{:S(2)}) copy-start(f32[128]{0:T(128)} %param.20) | copy-start | bytes 1540
  44.6 3.3 %copy-start.1 = (bf16[384,5120]{1,0:T(8,128)(2,1)S(1)}, bf16[384,5120]{1,0:T(8,128)(2,1)}, u32[]{:S(2)}) copy-start(bf16[384,5120]{1,0:T(8,128)(2,1)} %all-gather.3.cloned.1.call-done) | copy-start | bytes 11796484
  47.9 2.6 %copy-start.5 = (f32[640]{0:T(1024)S(1)}, f32[640]{0:T(1024)}, u32[]{:S(2)}) copy-start(f32[640]{0:T(1024)} %param.18) | copy-start | bytes 7684
  56.1 0.7 copy-start.7
  56.8 4.0 %copy-start.2 = (bf16[384,64]{0,1:T(8,128)(2,1)S(1)}, bf16[384,64]{0,1:T(8,128)(2,1)}, u32[]{:S(2)}) copy-start(bf16[384,64]{0,1:T(8,128)(2,1)} %get-tuple-element.13) | copy-start | bytes 147460
  60.8 7.2 %copy-start.3 = (s32[3072]{0:T(1024)S(1)}, s32[3072]{0:T(1024)}, u32[]{:S(2)}) copy-start(s32[3072]{0:T(1024)} %param.14) | copy-start | bytes 36868
  62.2 23.9 %all-to-all-start = ((bf16[8,48,896]{2,1,0:T(8,128)(2,1)}), bf16[8,48,896]{2,1,0:T(8,128)(2,1)S(1)}, u32[]{:S(2)}, u32[]{:S(2)}) async-start(bf16[8,48,896]{2,1,0:T(8,128)(2,1)} %bitcast.9), calls=%async_computation | async-start | bytes 1376256 | tf_op jit(solution)/shard_map/all_to_all | solution.py:132
  67.8 77.2 %reduce-scatter.2.cloned.1.call-start = ((), (), s32[]{:S(2)}) async-start(), calls=%async_computation.3 | async-start | bytes 6553600 | tf_op jit(solution)/shard_map/reduce_scatter | solution.py:179
Sparse Core Ops, SparseCore 0:
  8.9 35.6 all-gather.2
  95.3 49.5 reduce-scatter.1

commit v2 on v1

--- a/solution.py
+++ b/solution.py
@@ -77,7 +77,9 @@
     head_dim = HEAD_SIZE
     ctx_index = lax.axis_index("ctx")
 
-    all_lengths = lax.all_gather(seq_len, "ctx", tiled=True)
+    all_lengths = (
+        lax.all_gather(seq_len.astype(jnp.float32), "ctx", tiled=True).astype(jnp.int32)
+    )
     group_x = lax.all_gather(x_pool, "head", tiled=True)
 
     dest_grid = pool_dest.reshape(ctx_count, group_rows)
@@ -176,9 +178,25 @@
     )
     mixed_heads = mixed_heads.astype(jnp.bfloat16).reshape(pack_len, local_heads * head_dim)
     partial_out = jnp.dot(mixed_heads, w_out, preferred_element_type=jnp.float32)
-    return lax.psum_scatter(partial_out, "head", scatter_dimension=1, tiled=True).astype(
-        jnp.bfloat16
-    )
+    return halving_scatter(partial_out, "head", head_count).astype(jnp.bfloat16)
+
+
+def halving_scatter(partial, axis_name, count):
+    bits = count.bit_length() - 1
+    if count != 1 << bits or bits == 0:
+        return lax.psum_scatter(partial, axis_name, scatter_dimension=1, tiled=True)
+    rows, width = partial.shape
+    block = width // count
+    me = lax.axis_index(axis_name)
+    blocks = partial.reshape((rows,) + (2,) * bits + (block,))
+    for stage in range(bits):
+        axis = bits - stage
+        bit = (me >> stage) & 1
+        keep = lax.dynamic_index_in_dim(blocks, bit, axis, keepdims=False)
+        send = lax.dynamic_index_in_dim(blocks, 1 - bit, axis, keepdims=False)
+        pairs = [(i, i ^ (1 << stage)) for i in range(count)]
+        blocks = keep + lax.ppermute(send, axis_name, pairs)
+    return blocks.reshape(rows, block)
 
 
 def solution(mesh):

time: 154 us -> 146 us (0.948)
  waiting for transfers between devices: 75.2 us -> 52.1 us
  local copies, waits for them, and re-layouts: 4.49 us -> 22.5 us
  matrix products: 21.1 us -> 15.7 us
  other arithmetic: 11.4 us -> 13.7 us
    reduce_scatter x1 -> x0, waiting for transfers between devices: 49.7 us -> none  [local(): lax.psum_scatter(partial_out, 'head', scatter_dimension=1, tiled=True)]
    ppermute x0 -> x2, waiting for transfers between devices: none -> 35.7 us  [halving_scatter(): blocks = keep + lax.ppermute(send, axis_name, pairs)]
    all_to_all x1, waiting for transfers between devices: 16.3 us -> 6.72 us  [local(): lax.all_to_all(outgoing, 'ctx', split_axis=0, concat_axis=0, tiled=True)]
    dot_general x0 -> x1, local copies, waits for them, and re-layouts: none -> 9.49 us  [local(): jnp.dot(mixed_heads, w_out, preferred_element_type=jnp.float32)]
    unnamed x16 -> x26, local copies, waits for them, and re-layouts: 0.29 us -> 5.93 us
    dot_general x1, matrix products: 7.41 us -> 2.25 us  [local(): jnp.dot(mixed_heads, w_out, preferred_element_type=jnp.float32)]
    squeeze x0 -> x2, local copies, waits for them, and re-layouts: none -> 2.9 us  [halving_scatter(): send = lax.dynamic_index_in_dim(blocks, 1 - bit, axis, keepdims=False)]
    add x0 -> x1, other arithmetic: none -> 2.84 us  [halving_scatter(): blocks = keep + lax.ppermute(send, axis_name, pairs)]
  transfers between devices with their start and end apart: 3 -> 4, of which waited for: 3 -> 4; matrix products, arithmetic and copies ran while one was open for 5% -> 12% of each run, Pallas kernels for 0% -> 0%
where the time goes in v2:
time: 146 us
  waiting for transfers between devices  52.1 us (36%)
  local copies, waits for them, and re-layouts  22.5 us (15%)
  blocking collectives  22.1 us (15%)
  matrix products  15.7 us (11%)
  between operations  13.8 us (9%)
  other arithmetic  13.7 us (9%)
  starting transfers between devices  6.08 us (4%)
    ppermute x2, waiting for transfers between devices, halving_scatter(): blocks = keep + lax.ppermute(send, axis_name, pairs)  35.7 us
    all_gather x1, blocking collectives, local(): lax.all_gather(seq_len.astype(jnp.float32), 'ctx', tiled=True)  22.1 us
    dot_general x1, local copies, waits for them, and re-layouts, local(): jnp.dot(mixed_heads, w_out, preferred_element_type=jnp.float32)  9.49 us
    all_gather x1, waiting for transfers between devices, local(): group_x = lax.all_gather(x_pool, 'head', tiled=True)  8.98 us
    all_to_all x1, waiting for transfers between devices, local(): lax.all_to_all(outgoing, 'ctx', split_axis=0, concat_axis=0, tiled=True)  6.72 us
    unnamed x26, local copies, waits for them, and re-layouts  5.93 us
    dot_general x1, matrix products, local(): jnp.dot(normalized_input, w_query, preferred_element_type=jnp.float32)  5.52 us
    all_to_all x1, starting transfers between devices, local(): lax.all_to_all(outgoing, 'ctx', split_axis=0, concat_axis=0, tiled=True)  5.52 us
  transfers between devices with their start and end apart: 4, of which 4 were waited for; matrix products, arithmetic and copies ran while one was open for 12% of the time, Pallas kernels for 0%

profile of v2, /device:TPU:0, one launch (start us, length us, event | category | flops | bytes accessed | tf_op | source)
XLA Modules:
  0.0 146.0 jit_solution(279279936360170773)
XLA Ops:
  6.5 0.0 copy-start
  6.5 0.0 all-gather.3.cloned.1.call-start
  6.5 0.7 all-gather.3.cloned.1.call-update
  7.3 0.7 reshape.369
  8.0 0.7 convert_bitcast_fusion.1
  8.6 22.1 %all-gather = f32[8,1,8]{2,1,0:T(1,128)S(1)} all-gather(f32[1,1,8]{2,1,0:T(1,128)S(1)} %convert_bitcast_fusion.1), channel_id=1, replica_groups=mesh['ctx'=8,'head'=4] {'ctx'}, dimensions={0}, use_global_device_ids=true | all-gather | bytes 288 | tf_op jit(solution)/shard_map/all_gather | solution.py:81
  30.8 0.2 reduce_window_sum.54
  31.0 1.1 gather_fusion.1
  32.1 0.0 copy-start.8
  32.1 0.0 copy-start.9
  32.2 1.1 gather_fusion
  33.3 0.9 reduce-window.30
  34.2 0.2 slice_reduce_fusion
  34.4 0.1 add_bitcast_fusion
  34.5 0.1 copy.42
  34.7 0.2 fusion.20
  35.0 0.3 fusion.21
  35.2 0.4 multiply_cosine_fusion.1
  35.7 9.0 %all-gather.3.cloned.1.call-done = bf16[384,5120]{1,0:T(8,128)(2,1)} async-done(((bf16[96,5120]{1,0:T(8,128)(2,1)}), bf16[384,5120]{1,0:T(8,128)(2,1)}) %all-gather.3.cloned.1.call-update) | async-done | bytes 3932176 | tf_op jit(solution)/shard_map/all_gather | solution.py:83
  44.6 3.1 %fusion = f32[384]{0:T(512)S(1)} fusion(bf16[384,5120]{1,0:T(8,128)(2,1)} %all-gather.3.cloned.1.call-done), kind=kLoop, calls=%fused_computation.4 | loop fusion | flops 5897856 | bytes 3933696 | tf_op jit(solution)/shard_map/reduce_sum | solution.py:99
  47.8 0.0 copy-done.8
  47.8 0.0 copy-done.9
  47.8 0.2 copy-done.4
  47.9 5.5 %convolution_add_fusion = f32[384,640]{1,0:T(8,128)S(1)} fusion(bf16[5120,640]{1,0:T(8,128)(2,1)} %param.17, f32[640]{0:T(1024)S(1)} %copy-done.9, bf16[384,5120]{1,0:T(8,128)(2,1)S(1)} %copy-done.4, f32[5120]{0:T(1024)S(1)} %copy-done.8, f32[384]{0:T(512)S(1)} %add_rsqrt_fusion), kind=kOutput, calls=%fused_computation.19 | convolution fusion | flops 2524692480 | bytes 11493376 | tf_op jit(solution)/shard_map/dot_general | solution.py:105
  53.5 0.3 copy.43
  53.8 0.0 copy-start.7
  53.8 0.0 copy-start.11
  53.9 3.8 %fusion.7 = f32[384,1,128]{0,2,1:T(8,128)S(1)} fusion(bf16[5120,128]{1,0:T(8,128)(2,1)S(1)} %copy-done, f32[128]{0:T(128)S(1)} %copy-done.10, bf16[384,5120]{1,0:T(8,128)(2,1)} %all-gather.3.cloned.1.call-done, f32[5120]{0:T(1024)S(1)} %copy-done.8, f32[384]{0:T(512)S(1)} %add_rsqrt_fusion), kind=kOutput, calls=%fused_computation.26 | convolution fusion | flops 511229952 | bytes 5462016 | tf_op jit(solution)/shard_map/dot_general | solution.py:110
  57.6 0.4 fusion.32
  58.1 0.1 subtract_convert_fusion
  58.2 0.1 pad_maximum_fusion
  58.3 1.5 %fusion.8 = bf16[384,128]{0,1:T(8,128)(2,1)S(1)} fusion(bf16[5120,128]{1,0:T(8,128)(2,1)S(1)} %copy-done.7, f32[128]{0:T(128)S(1)} %copy-done.11, bf16[384,5120]{1,0:T(8,128)(2,1)S(1)} %copy-done.5, f32[5120]{0:T(1024)S(1)} %copy-done.8, f32[384]{0:T(512)S(1)} %add_rsqrt_fusion), kind=kOutput, calls=%fused_computation.27 | convolution fusion | flops 511279104 | bytes 5363712 | tf_op jit(solution)/shard_map/dot_general | solution.py:117
  59.8 0.0 copy-start.6
  59.8 0.0 copy-start.12
  59.9 1.4 convolution_convert_fusion
  61.3 5.5 %all-to-all-start = ((bf16[8,48,896]{2,1,0:T(8,128)(2,1)}), bf16[8,48,896]{2,1,0:T(8,128)(2,1)S(1)}, u32[]{:S(2)}, u32[]{:S(2)}) async-start(bf16[8,48,896]{2,1,0:T(8,128)(2,1)} %bitcast.10), calls=%async_computation | async-start | bytes 1376256 | tf_op jit(solution)/shard_map/all_to_all | solution.py:134
  66.8 0.0 copy-done.6
  66.9 0.9 reduce-window.21
  67.7 0.2 slice_reduce_fusion.1
  68.0 0.1 broadcast_add_fusion
  68.1 0.1 add.110
  68.2 0.2 reduce-window.32
  68.4 9.5 %copy.57 = bf16[5120,640]{1,0:T(8,128)(2,1)} copy(bf16[5120,640]{0,1:T(8,128)(2,1)} %bitcast.91) | data formatting | bytes 13107200 | tf_op jit(solution)/shard_map/dot_general | solution.py:180
  77.9 0.1 convert_reduce_fusion
  77.9 0.4 select_reduce_fusion
  78.4 0.1 fusion.18
  78.5 6.7 %all-to-all-done = bf16[8,48,896]{2,1,0:T(8,128)(2,1)S(1)} async-done(((bf16[8,48,896]{2,1,0:T(8,128)(2,1)}), bf16[8,48,896]{2,1,0:T(8,128)(2,1)S(1)}, u32[]{:S(2)}, u32[]{:S(2)}) %all-to-all-start) | async-done | bytes 688160 | tf_op jit(solution)/shard_map/all_to_all | solution.py:134
  85.2 0.5 convolution_convert_fusion.1
  85.7 0.2 copy.45
  85.9 0.4 fusion.51
  86.3 0.2 fusion.6
  86.5 0.4 convolution_convert_fusion.2
  86.8 1.9 %copy-done.1 = bf16[5120,640]{1,0:T(8,128)(2,1)S(1)} copy-done((bf16[5120,640]{1,0:T(8,128)(2,1)S(1)}, bf16[5120,640]{1,0:T(8,128)(2,1)}, u32[]{:S(2)}) %copy-start.1) | copy-done | bytes 6553624
  88.8 2.3 %fusion.52 = f32[256,2,2,1280]{3,0,2,1:T(8,128)S(1)} fusion(bf16[256,640,1,1]{0,1,3,2:T(8,128)(2,1)S(1)} %bitcast.96, bf16[2,2,1280,640]{3,2,1,0:T(8,128)(2,1)S(1)} %bitcast.90), kind=kOutput, calls=%fused_computation.131 | convolution fusion | flops 1677721600 | bytes 12124160 | tf_op jit(solution)/shard_map/dot_general | solution.py:180
  91.0 2.3 %copy-done.2 = f32[256,2,2,1280]{3,0,2,1:T(8,128)} copy-done((f32[256,2,2,1280]{3,0,2,1:T(8,128)}, f32[256,2,2,1280]{3,0,2,1:T(8,128)S(1)}, u32[]{:S(2)}) %copy-start.2) | copy-done | bytes 5242904
  93.3 1.7 %dynamic-slice_bitcast_fusion = f32[256,2,1280]{2,0,1:T(8,128)} fusion(f32[256,2,2,1280]{3,0,2,1:T(8,128)S(1)} %fusion.52, s32[]{:T(128)S(6)} %select_n.118), kind=kLoop, calls=%fused_computation.10 | loop fusion | bytes 5242884 | tf_op jit(solution)/shard_map/jit(dynamic_index_in_dim)/squeeze | solution.py:196
  95.1 0.0 collective-permute-start
  95.1 5.2 %collective-permute-done = f32[256,2,1280]{2,0,1:T(8,128)} collective-permute-done((f32[256,2,1280]{2,0,1:T(8,128)}, f32[256,2,1280]{2,0,1:T(8,128)}, u32[]{:S(2)}, u32[]{:S(2)}) %collective-permute-start) | collective-permute-done | bytes 2621472 | tf_op jit(solution)/shard_map/ppermute | solution.py:198
  100.3 2.8 %bitcast_add_fusion = f32[256,2,1280]{2,0,1:T(8,128)S(1)} fusion(f32[256,2,1280]{2,0,1:T(8,128)} %collective-permute-done, f32[256,2,2,1280]{3,0,2,1:T(8,128)} %copy-done.2, s32[]{:T(128)S(6)} %select_n.117), kind=kLoop, calls=%fused_computation.9 | loop fusion | flops 655360 | bytes 7864324 | tf_op jit(solution)/shard_map/add | solution.py:198
  103.2 1.5 %copy-done.3 = f32[256,2,1280]{2,0,1:T(8,128)} copy-done((f32[256,2,1280]{2,0,1:T(8,128)}, f32[256,2,1280]{2,0,1:T(8,128)S(1)}, u32[]{:S(2)}) %copy-start.3) | copy-done | bytes 2621464
  104.7 1.2 dynamic-slice_bitcast_fusion.1
  105.8 0.6 collective-permute-start.1
  106.4 30.5 %collective-permute-done.1 = f32[256,1280]{1,0:T(8,128)S(1)} collective-permute-done((f32[256,1280]{1,0:T(8,128)}, f32[256,1280]{1,0:T(8,128)S(1)}, u32[]{:S(2)}, u32[]{:S(2)}) %collective-permute-start.1) | collective-permute-done | bytes 1310752 | tf_op jit(solution)/shard_map/ppermute | solution.py:198
  136.9 2.3 %fusion.4 = bf16[256,1280]{1,0:T(8,128)(2,1)} fusion(f32[256,1280]{1,0:T(8,128)S(1)} %collective-permute-done.1, f32[256,2,1280]{2,0,1:T(8,128)} %copy-done.3, s32[]{:T(128)S(6)} %select_n.119), kind=kLoop, calls=%fused_computation.15 | loop fusion | flops 655360 | bytes 3276804 | tf_op jit(solution)/shard_map/convert_element_type | solution.py:181
  (36 shorter events, 0.4 us)
Async XLA Ops:
  6.5 47.3 %copy-start = (bf16[5120,128]{1,0:T(8,128)(2,1)S(1)}, bf16[5120,128]{1,0:T(8,128)(2,1)}, u32[]{:S(2)}) copy-start(bf16[5120,128]{1,0:T(8,128)(2,1)} %param.19) | copy-start | bytes 3932164
  6.5 38.1 %all-gather.3.cloned.1.call-start = ((), (), s32[]{:S(2)}) async-start(), calls=%async_computation.1 | async-start | bytes 4915200 | tf_op jit(solution)/shard_map/all_gather | solution.py:83
  32.1 15.6 %copy-start.8 = (f32[5120]{0:T(1024)S(1)}, f32[5120]{0:T(1024)}, u32[]{:S(2)}) copy-start(f32[5120]{0:T(1024)} %param.16) | copy-start | bytes 61444
  32.1 15.6 %copy-start.9 = (f32[640]{0:T(1024)S(1)}, f32[640]{0:T(1024)}, u32[]{:S(2)}) copy-start(f32[640]{0:T(1024)} %param.18) | copy-start | bytes 7684
  44.6 3.3 %copy-start.4 = (bf16[384,5120]{1,0:T(8,128)(2,1)S(1)}, bf16[384,5120]{1,0:T(8,128)(2,1)}, u32[]{:S(2)}) copy-start(bf16[384,5120]{1,0:T(8,128)(2,1)} %all-gather.3.cloned.1.call-done) | copy-start | bytes 11796484
  47.9 5.9 %copy-start.10 = (f32[128]{0:T(128)S(1)}, f32[128]{0:T(128)}, u32[]{:S(2)}) copy-start(f32[128]{0:T(128)} %param.20) | copy-start | bytes 1540
  53.8 4.5 %copy-start.5 = (bf16[384,5120]{1,0:T(8,128)(2,1)S(1)}, bf16[384,5120]{1,0:T(8,128)(2,1)}, u32[]{:S(2)}) copy-start(bf16[384,5120]{1,0:T(8,128)(2,1)} %all-gather.3.cloned.1.call-done) | copy-start | bytes 11796484
  53.8 4.5 %copy-start.7 = (bf16[5120,128]{1,0:T(8,128)(2,1)S(1)}, bf16[5120,128]{1,0:T(8,128)(2,1)}, u32[]{:S(2)}) copy-start(bf16[5120,128]{1,0:T(8,128)(2,1)} %param.21) | copy-start | bytes 3932164
  53.8 4.5 %copy-start.11 = (f32[128]{0:T(128)S(1)}, f32[128]{0:T(128)}, u32[]{:S(2)}) copy-start(f32[128]{0:T(128)} %param.22) | copy-start | bytes 1540
  59.8 7.0 %copy-start.6 = (s32[3072]{0:T(1024)S(1)}, s32[3072]{0:T(1024)}, u32[]{:S(2)}) copy-start(s32[3072]{0:T(1024)} %param.14) | copy-start | bytes 36868
  59.8 8.3 %copy-start.12 = (s32[1,8]{1,0:T(1,128)S(1)}, s32[1,8]{1,0:T(1,128)}, u32[]{:S(2)}) copy-start(s32[1,8]{1,0:T(1,128)} %param.15) | copy-start | bytes 100
  61.3 23.9 %all-to-all-start = ((bf16[8,48,896]{2,1,0:T(8,128)(2,1)}), bf16[8,48,896]{2,1,0:T(8,128)(2,1)S(1)}, u32[]{:S(2)}, u32[]{:S(2)}) async-start(bf16[8,48,896]{2,1,0:T(8,128)(2,1)} %bitcast.10), calls=%async_computation | async-start | bytes 1376256 | tf_op jit(solution)/shard_map/all_to_all | solution.py:134
  85.9 2.9 %copy-start.1 = (bf16[5120,640]{1,0:T(8,128)(2,1)S(1)}, bf16[5120,640]{1,0:T(8,128)(2,1)}, u32[]{:S(2)}) copy-start(bf16[5120,640]{1,0:T(8,128)(2,1)} %copy.57) | copy-start | bytes 19660804
  91.0 2.3 %copy-start.2 = (f32[256,2,2,1280]{3,0,2,1:T(8,128)}, f32[256,2,2,1280]{3,0,2,1:T(8,128)S(1)}, u32[]{:S(2)}) copy-start(f32[256,2,2,1280]{3,0,2,1:T(8,128)S(1)} %fusion.52) | copy-start | bytes 15728644
  95.1 5.3 %collective-permute-start = (f32[256,2,1280]{2,0,1:T(8,128)}, f32[256,2,1280]{2,0,1:T(8,128)}, u32[]{:S(2)}, u32[]{:S(2)}) collective-permute-start(f32[256,2,1280]{2,0,1:T(8,128)} %dynamic-slice_bitcast_fusion), channel_id=1, source_target_pairs={{0,1},{1,0},{2,3},{3,2},{4,5},{5,4},{6,7},{7,6},{8,9},{9,8},{10,11... | collective-permute-start | bytes 7864328 | tf_op jit(solution)/shard_map/ppermute | solution.py:198
  103.2 1.5 %copy-start.3 = (f32[256,2,1280]{2,0,1:T(8,128)}, f32[256,2,1280]{2,0,1:T(8,128)S(1)}, u32[]{:S(2)}) copy-start(f32[256,2,1280]{2,0,1:T(8,128)S(1)} %bitcast_add_fusion) | copy-start | bytes 7864324
  105.8 31.0 %collective-permute-start.1 = (f32[256,1280]{1,0:T(8,128)}, f32[256,1280]{1,0:T(8,128)S(1)}, u32[]{:S(2)}, u32[]{:S(2)}) collective-permute-start(f32[256,1280]{1,0:T(8,128)} %dynamic-slice_bitcast_fusion.1), channel_id=1, source_target_pairs={{0,2},{1,3},{2,0},{3,1},{4,6},{5,7},{6,4},{7,5},{8,10},{9,11},{10,... | collective-permute-start | bytes 3932168 | tf_op jit(solution)/shard_map/ppermute | solution.py:198
Sparse Core Ops, SparseCore 0:
  8.9 35.6 all-gather.2

commit v3 on v2

--- a/solution.py
+++ b/solution.py
@@ -77,10 +77,13 @@
     head_dim = HEAD_SIZE
     ctx_index = lax.axis_index("ctx")
 
-    all_lengths = (
-        lax.all_gather(seq_len.astype(jnp.float32), "ctx", tiled=True).astype(jnp.int32)
-    )
-    group_x = lax.all_gather(x_pool, "head", tiled=True)
+    length_rows = jnp.where(
+        jnp.arange(ctx_count, dtype=jnp.int32)[:, None] == ctx_index,
+        seq_len.astype(jnp.float32),
+        0.0,
+    )
+    all_lengths = lax.psum(length_rows, "ctx").astype(jnp.int32)
+    group_x = doubling_gather(x_pool, "head", head_count)
 
     dest_grid = pool_dest.reshape(ctx_count, group_rows)
     my_dest = lax.dynamic_index_in_dim(dest_grid, ctx_index, 0, keepdims=False)
@@ -185,18 +188,35 @@
     bits = count.bit_length() - 1
     if count != 1 << bits or bits == 0:
         return lax.psum_scatter(partial, axis_name, scatter_dimension=1, tiled=True)
-    rows, width = partial.shape
-    block = width // count
+    block = partial.shape[1] // count
     me = lax.axis_index(axis_name)
-    blocks = partial.reshape((rows,) + (2,) * bits + (block,))
+    pieces = [(b, partial[:, b * block : (b + 1) * block]) for b in range(count)]
     for stage in range(bits):
-        axis = bits - stage
         bit = (me >> stage) & 1
-        keep = lax.dynamic_index_in_dim(blocks, bit, axis, keepdims=False)
-        send = lax.dynamic_index_in_dim(blocks, 1 - bit, axis, keepdims=False)
+        lows = [(b, x) for b, x in pieces if not (b >> stage) & 1]
+        highs = [x for b, x in pieces if (b >> stage) & 1]
+        keep = [jnp.where(bit == 0, lo, hi) for (_, lo), hi in zip(lows, highs)]
+        send = jnp.stack([jnp.where(bit == 0, hi, lo) for (_, lo), hi in zip(lows, highs)])
         pairs = [(i, i ^ (1 << stage)) for i in range(count)]
-        blocks = keep + lax.ppermute(send, axis_name, pairs)
-    return blocks.reshape(rows, block)
+        got = lax.ppermute(send, axis_name, pairs)
+        pieces = [(b, k + got[i]) for i, ((b, _), k) in enumerate(zip(lows, keep))]
+    return pieces[0][1]
+
+
+def doubling_gather(part, axis_name, count):
+    bits = count.bit_length() - 1
+    if count != 1 << bits or bits == 0:
+        return lax.all_gather(part, axis_name, tiled=True)
+    me = lax.axis_index(axis_name)
+    have = part[None]
+    for stage in reversed(range(bits)):
+        bit = (me >> stage) & 1
+        pairs = [(i, i ^ (1 << stage)) for i in range(count)]
+        got = lax.ppermute(have, axis_name, pairs)
+        first = jnp.where(bit == 0, have, got)
+        second = jnp.where(bit == 0, got, have)
+        have = jnp.stack([first, second], axis=1).reshape((-1,) + part.shape)
+    return have.reshape((count * part.shape[0],) + part.shape[1:])
 
 
 def solution(mesh):

time: 146 us -> 146 us (level)
  local copies, waits for them, and re-layouts: 22.5 us -> 6.21 us
  waiting for transfers between devices: 52.1 us -> 67.6 us
  between operations: 13.8 us -> 0.33 us
  other arithmetic: 13.7 us -> 22.9 us
  matrix products: 15.7 us -> 18.3 us
  starting transfers between devices: 6.08 us -> 8.29 us
    all_gather x1 -> x0, blocking collectives: 22.1 us -> none  [local(): lax.all_gather(seq_len.astype(jnp.float32), 'ctx', tiled=True)]
    psum x0 -> x1, blocking collectives: none -> 21.9 us  [local(): all_lengths = lax.psum(length_rows, 'ctx').astype(jnp.int32)]
    ppermute x2 -> x4, waiting for transfers between devices: 35.7 us -> 54.8 us  [the longest x2 34.2 us: halving_scatter(): got = lax.ppermute(send, axis_name, pairs)]
    dot_general x1 -> x0, local copies, waits for them, and re-layouts: 9.49 us -> none  [local(): jnp.dot(mixed_heads, w_out, preferred_element_type=jnp.float32)]
    all_gather x1 -> x0, waiting for transfers between devices: 8.98 us -> none  [local(): group_x = lax.all_gather(x_pool, 'head', tiled=True)]
    convert_element_type x2 -> x3, other arithmetic: 0.01 us -> 8.05 us  [the longest x1 4.45 us: local(): normalized_input = (values_wide * lax.rsqrt(jnp.mean(values_wide * values...]
    all_to_all x1, waiting for transfers between devices: 6.72 us -> 12.8 us  [local(): lax.all_to_all(outgoing, 'ctx', split_axis=0, concat_axis=0, tiled=True)]
    unnamed x26 -> x18, local copies, waits for them, and re-layouts: 5.93 us -> 0.95 us
  transfers between devices with their start and end apart: 4 -> 5, of which waited for: 4 -> 4; matrix products, arithmetic and copies ran while one was open for 12% -> 7% of each run, Pallas kernels for 0% -> 0%
where the time goes in v3:
time: 146 us
  waiting for transfers between devices  67.6 us (46%)
  other arithmetic  22.9 us (16%)
  blocking collectives  21.9 us (15%)
  matrix products  18.3 us (13%)
  starting transfers between devices  8.29 us (6%)
  local copies, waits for them, and re-layouts  6.21 us (4%)
    ppermute x2, waiting for transfers between devices, halving_scatter(): got = lax.ppermute(send, axis_name, pairs)  34.2 us
    psum x1, blocking collectives, local(): all_lengths = lax.psum(length_rows, 'ctx').astype(jnp.int32)  21.9 us
    ppermute x2, waiting for transfers between devices, doubling_gather(): got = lax.ppermute(have, axis_name, pairs)  20.6 us
    all_to_all x1, waiting for transfers between devices, local(): lax.all_to_all(outgoing, 'ctx', split_axis=0, concat_axis=0, tiled=True)  12.8 us
    dot_general x1, matrix products, local(): jnp.dot(normalized_input, w_query, preferred_element_type=jnp.float32)  5.48 us
    dot_general x1, matrix products, local(): jnp.dot(mixed_heads, w_out, preferred_element_type=jnp.float32)  5.18 us
    convert_element_type x1, other arithmetic, local(): normalized_input = (values_wide * lax.rsqrt(jnp.mean(values_wide * values...  4.45 us
    dot_general x1, matrix products, local(): jnp.dot(normalized_input, value_projection_weight, preferred_element_type...  3.74 us
  transfers between devices with their start and end apart: 5, of which 4 were waited for; matrix products, arithmetic and copies ran while one was open for 7% of the time, Pallas kernels for 0%

profile of v3, /device:TPU:0, one launch (start us, length us, event | category | flops | bytes accessed | tf_op | source)
XLA Modules:
  0.0 145.6 jit_solution(3284785367039680409)
XLA Ops:
  0.0 2.9 %collective-permute-start = (bf16[1,96,5120]{2,1,0:T(8,128)(2,1)}, bf16[1,96,5120]{2,1,0:T(8,128)(2,1)}, u32[]{:S(2)}, u32[]{:S(2)}) collective-permute-start(bf16[1,96,5120]{2,1,0:T(8,128)(2,1)} %bitcast.124), channel_id=1, source_target_pairs={{0,2},{1,3},{2,0},{3,1},{4,6},{5,7},{6,4},{7,5},{8,10},{9,11},{10,... | collective-permute-start | bytes 2949128 | tf_op jit(solution)/shard_map/ppermute | solution.py:215
  2.9 0.7 reshape.386
  3.7 0.7 convert_bitcast_fusion
  4.4 0.1 broadcast_select_fusion
  4.4 20.6 %collective-permute-done = bf16[1,96,5120]{2,1,0:T(8,128)(2,1)} collective-permute-done((bf16[1,96,5120]{2,1,0:T(8,128)(2,1)}, bf16[1,96,5120]{2,1,0:T(8,128)(2,1)}, u32[]{:S(2)}, u32[]{:S(2)}) %collective-permute-start) | collective-permute-done | bytes 983072 | tf_op jit(solution)/shard_map/ppermute | solution.py:215
  25.0 1.6 %select_bitcast_fusion.6 = (bf16[1,1,96,5120]{3,2,1,0:T(8,128)(2,1)S(1)}, bf16[1,1,96,5120]{3,2,1,0:T(8,128)(2,1)S(1)}) fusion(bf16[1,96,5120]{2,1,0:T(8,128)(2,1)} %collective-permute-done, pred[]{:T(512)S(6)} %eq.112, bf16[96,5120]{1,0:T(8,128)(2,1)} %param.13), kind=kLoop, calls=%fused_computation.37 | loop fusion | flops 983040 | bytes 3932161 | tf_op jit(solution)/shard_map/stack | solution.py:218
  26.6 1.5 maximum_bitcast_fusion
  28.1 0.0 collective-permute-start.1
  28.1 21.9 %psum.7 = f32[8,8]{1,0:T(8,128)S(1)} all-reduce(f32[8,8]{1,0:T(8,128)S(1)} %broadcast_select_fusion), channel_id=1, replica_groups=mesh['ctx'=8,'head'=4] {'ctx'}, use_global_device_ids=true, to_apply=%region_7.8 | all-reduce | flops 64 | bytes 512 | tf_op jit(solution)/shard_map/psum | solution.py:85
  50.1 0.2 reduce_window_sum.54
  50.2 1.6 %gather_fusion.1 = s32[384,8]{1,0:T(8,128)} fusion(s32[8,8]{1,0:T(8,128)S(1)} %convert_element_type.93, s32[1024]{0:T(1024)S(1)} %pad_clamp_fusion), kind=kCustom, calls=%fused_computation.1.clone | custom fusion | bytes 26112 | tf_op jit(solution)/shard_map/jit(_take)/gather | solution.py:95
  51.8 1.6 %gather_fusion = s32[384,8]{1,0:T(8,128)} fusion(s32[8,8]{1,0:T(8,128)S(1)} %reduce_window_sum.54, s32[1024]{0:T(1024)S(1)} %pad_clamp_fusion), kind=kCustom, calls=%fused_computation.clone | custom fusion | bytes 26112 | tf_op jit(solution)/shard_map/jit(_take)/gather | solution.py:94
  53.5 0.9 reduce-window.30
  54.3 0.2 slice_reduce_fusion
  54.6 0.1 add_bitcast_fusion
  54.7 0.1 copy.28
  54.8 0.1 add.100
  54.9 1.3 fusion.22
  56.2 0.2 fusion.21
  56.5 0.4 multiply_cosine_fusion.1
  56.9 0.0 collective-permute-done.1
  56.9 1.8 %select_bitcast_fusion.1 = (bf16[2,1,96,5120]{3,2,1,0:T(8,128)(2,1)S(1)}, bf16[2,1,96,5120]{3,2,1,0:T(8,128)(2,1)S(1)}) fusion(bf16[2,96,5120]{2,1,0:T(8,128)(2,1)} %collective-permute-done.1, pred[]{:T(512)S(6)} %eq.113, bf16[1,1,96,5120]{3,2,1,0:T(8,128)(2,1)S(1)} %get-tuple-element.18, bf16[1,1,96,5120]{3,2,1,0:T(8,128)(2,1)S(1)} %get-tuple-element.17), kind=kLoop, calls=%fused_computation.12 | loop fusion | flops 2949120 | bytes 7864321 | tf_op jit(solution)/shard_map/stack | solution.py:218
  58.7 3.6 %maximum_convert_fusion = f32[2,2,96,5120]{3,2,1,0:T(8,128)} fusion(bf16[2,1,96,5120]{3,2,1,0:T(8,128)(2,1)S(1)} %get-tuple-element.16, bf16[2,1,96,5120]{3,2,1,0:T(8,128)(2,1)S(1)} %get-tuple-element.15), kind=kLoop, calls=%fused_computation.6 | loop fusion | flops 3932160 | bytes 11796480 | tf_op jit(solution)/shard_map/convert_element_type | solution.py:99
  62.3 0.9 multiply_reduce_fusion
  63.2 0.1 rsqrt.12
  63.3 4.5 %fusion.1 = bf16[384,5120]{1,0:T(8,128)(2,1)S(1)} fusion(f32[2,2,96,5120]{3,2,1,0:T(8,128)} %maximum_convert_fusion, f32[5120]{0:T(1024)S(1)} %copy-done.4, f32[384]{0:T(512)S(1)} %rsqrt.12), kind=kLoop, calls=%fused_computation.4 | loop fusion | flops 5898240 | bytes 11818496 | tf_op jit(solution)/shard_map/convert_element_type | solution.py:104
  67.7 0.0 copy-done
  67.8 0.0 copy-done.5
  67.8 0.0 copy-start.7
  67.8 1.3 fusion.8
  69.1 1.1 fusion.33
  70.2 5.5 %convolution_add_fusion = f32[384,640]{1,0:T(8,128)S(1)} fusion(bf16[384,5120]{1,0:T(8,128)(2,1)S(1)} %fusion.1, bf16[5120,640]{1,0:T(8,128)(2,1)} %param.17, f32[640]{0:T(1024)S(1)} %copy-done.7), kind=kOutput, calls=%fused_computation.27 | convolution fusion | flops 2516828160 | bytes 11471360 | tf_op jit(solution)/shard_map/dot_general | solution.py:108
  75.7 0.0 copy-start.6
  75.7 0.3 copy.30
  76.0 0.3 copy-done.6
  76.3 3.7 %fusion.9 = bf16[384,128]{0,1:T(8,128)(2,1)S(1)} fusion(bf16[384,5120]{1,0:T(8,128)(2,1)} %copy-done.1, bf16[5120,128]{1,0:T(8,128)(2,1)} %param.21, f32[128]{0:T(128)S(1)} %copy-done.6), kind=kOutput, calls=%fused_computation.35 | convolution fusion | flops 503414784 | bytes 5341696 | tf_op jit(solution)/shard_map/dot_general | solution.py:120
  80.1 0.0 copy-start.2
  80.1 0.1 subtract_convert_fusion
  80.2 0.1 pad_maximum_fusion.1
  80.3 0.6 copy-done.2
  80.9 1.4 convolution_convert_fusion
  82.3 3.7 %all-to-all-start = ((bf16[8,48,896]{2,1,0:T(8,128)(2,1)}), bf16[8,48,896]{2,1,0:T(8,128)(2,1)S(1)}, u32[]{:S(2)}, u32[]{:S(2)}) async-start(bf16[8,48,896]{2,1,0:T(8,128)(2,1)} %bitcast.16), calls=%async_computation | async-start | bytes 1376256 | tf_op jit(solution)/shard_map/all_to_all | solution.py:137
  86.1 0.9 reduce-window.21
  87.0 0.2 slice_reduce_fusion.1
  87.2 0.1 broadcast_add_fusion
  87.4 0.2 reduce-window.32
  87.5 0.1 convert_reduce_fusion
  87.6 0.4 select_reduce_fusion
  88.1 0.1 fusion.19
  88.2 12.8 %all-to-all-done = bf16[8,48,896]{2,1,0:T(8,128)(2,1)S(1)} async-done(((bf16[8,48,896]{2,1,0:T(8,128)(2,1)}), bf16[8,48,896]{2,1,0:T(8,128)(2,1)S(1)}, u32[]{:S(2)}, u32[]{:S(2)}) %all-to-all-start) | async-done | bytes 688160 | tf_op jit(solution)/shard_map/all_to_all | solution.py:137
  101.0 0.5 convolution_convert_fusion.1
  101.5 0.2 copy.31
  101.6 0.4 fusion.50
  102.0 0.2 fusion.7
  102.2 0.4 convolution_convert_fusion.2
  102.6 5.2 %fusion.51 = f32[256,5120]{1,0:T(8,128)S(1)} fusion(bf16[256,640]{0,1:T(8,128)(2,1)S(1)} %bitcast.126, bf16[640,5120]{1,0:T(8,128)(2,1)} %param.23), kind=kOutput, calls=%fused_computation.141 | convolution fusion | flops 1677721600 | bytes 12124160 | tf_op jit(solution)/shard_map/dot_general | solution.py:183
  107.8 0.3 select_bitcast_fusion.4
  108.1 0.2 pad_maximum_fusion
  108.2 0.1 collective-permute-start.2
  108.3 4.9 %collective-permute-done.2 = f32[2,256,1280]{2,1,0:T(8,128)S(1)} collective-permute-done((f32[2,256,1280]{2,1,0:T(8,128)S(1)}, f32[2,256,1280]{2,1,0:T(8,128)S(1)}, u32[]{:S(2)}, u32[]{:S(2)}) %collective-permute-start.2) | collective-permute-done | bytes 2621472 | tf_op jit(solution)/shard_map/ppermute | solution.py:201
  113.2 0.5 select_bitcast_fusion.2
  113.7 1.6 %collective-permute-start.3 = (f32[1,256,1280]{2,1,0:T(8,128)S(1)}, f32[1,256,1280]{2,1,0:T(8,128)S(1)}, u32[]{:S(2)}, u32[]{:S(2)}) collective-permute-start(f32[1,256,1280]{2,1,0:T(8,128)S(1)} %get-tuple-element.6), channel_id=1, source_target_pairs={{0,2},{1,3},{2,0},{3,1},{4,6},{5,7},{6,4},{7,5},{8,10},{9,11},{10,... | collective-permute-start | bytes 3932168 | tf_op jit(solution)/shard_map/ppermute | solution.py:201
  115.3 29.3 %collective-permute-done.3 = f32[1,256,1280]{2,1,0:T(8,128)S(1)} collective-permute-done((f32[1,256,1280]{2,1,0:T(8,128)S(1)}, f32[1,256,1280]{2,1,0:T(8,128)S(1)}, u32[]{:S(2)}, u32[]{:S(2)}) %collective-permute-start.3) | collective-permute-done | bytes 1310752 | tf_op jit(solution)/shard_map/ppermute | solution.py:201
  144.6 1.0 fusion.5
  (35 shorter events, 0.4 us)
Async XLA Ops:
  0.0 67.7 %copy-start = (bf16[5120,128]{1,0:T(8,128)(2,1)S(1)}, bf16[5120,128]{1,0:T(8,128)(2,1)}, u32[]{:S(2)}) copy-start(bf16[5120,128]{1,0:T(8,128)(2,1)} %param.19) | copy-start | bytes 3932164
  0.0 25.0 %collective-permute-start = (bf16[1,96,5120]{2,1,0:T(8,128)(2,1)}, bf16[1,96,5120]{2,1,0:T(8,128)(2,1)}, u32[]{:S(2)}, u32[]{:S(2)}) collective-permute-start(bf16[1,96,5120]{2,1,0:T(8,128)(2,1)} %bitcast.124), channel_id=1, source_target_pairs={{0,2},{1,3},{2,0},{3,1},{4,6},{5,7},{6,4},{7,5},{8,10},{9,11},{10,... | collective-permute-start | bytes 2949128 | tf_op jit(solution)/shard_map/ppermute | solution.py:215
  28.1 28.8 %collective-permute-start.1 = (bf16[2,96,5120]{2,1,0:T(8,128)(2,1)}, bf16[2,96,5120]{2,1,0:T(8,128)(2,1)}, u32[]{:S(2)}, u32[]{:S(2)}) collective-permute-start(bf16[2,96,5120]{2,1,0:T(8,128)(2,1)} %maximum_bitcast_fusion), channel_id=1, source_target_pairs={{0,1},{1,0},{2,3},{3,2},{4,5},{5,4},{6,7},{7,6},{8,9},{9,8},{10,11... | collective-permute-start | bytes 5898248 | tf_op jit(solution)/shard_map/ppermute | solution.py:215
  62.3 1.0 copy-start.4
  63.3 4.5 %copy-start.5 = (f32[128]{0:T(128)S(1)}, f32[128]{0:T(128)}, u32[]{:S(2)}) copy-start(f32[128]{0:T(128)} %param.20) | copy-start | bytes 1540
  67.8 2.4 %copy-start.1 = (bf16[384,5120]{1,0:T(8,128)(2,1)}, bf16[384,5120]{1,0:T(8,128)(2,1)S(1)}, u32[]{:S(2)}) copy-start(bf16[384,5120]{1,0:T(8,128)(2,1)S(1)} %fusion.1) | copy-start | bytes 11796484
  67.8 2.4 %copy-start.7 = (f32[640]{0:T(1024)S(1)}, f32[640]{0:T(1024)}, u32[]{:S(2)}) copy-start(f32[640]{0:T(1024)} %param.18) | copy-start | bytes 7684
  75.7 0.7 copy-start.6
  80.1 0.8 copy-start.2
  80.9 5.2 %copy-start.3 = (s32[3072]{0:T(1024)S(1)}, s32[3072]{0:T(1024)}, u32[]{:S(2)}) copy-start(s32[3072]{0:T(1024)} %param.14) | copy-start | bytes 36868
  80.9 6.5 %copy-start.8 = (s32[1,8]{1,0:T(1,128)S(1)}, s32[1,8]{1,0:T(1,128)}, u32[]{:S(2)}) copy-start(s32[1,8]{1,0:T(1,128)} %param.15) | copy-start | bytes 100
  82.3 18.6 %all-to-all-start = ((bf16[8,48,896]{2,1,0:T(8,128)(2,1)}), bf16[8,48,896]{2,1,0:T(8,128)(2,1)S(1)}, u32[]{:S(2)}, u32[]{:S(2)}) async-start(bf16[8,48,896]{2,1,0:T(8,128)(2,1)} %bitcast.16), calls=%async_computation | async-start | bytes 1376256 | tf_op jit(solution)/shard_map/all_to_all | solution.py:137
  108.2 5.0 %collective-permute-start.2 = (f32[2,256,1280]{2,1,0:T(8,128)S(1)}, f32[2,256,1280]{2,1,0:T(8,128)S(1)}, u32[]{:S(2)}, u32[]{:S(2)}) collective-permute-start(f32[2,256,1280]{2,1,0:T(8,128)S(1)} %pad_maximum_fusion), channel_id=1, source_target_pairs={{0,1},{1,0},{2,3},{3,2},{4,5},{5,4},{6,7},{7,6},{8,9},{9,8},{10,11... | collective-permute-start | bytes 7864328 | tf_op jit(solution)/shard_map/ppermute | solution.py:201
  113.7 30.9 %collective-permute-start.3 = (f32[1,256,1280]{2,1,0:T(8,128)S(1)}, f32[1,256,1280]{2,1,0:T(8,128)S(1)}, u32[]{:S(2)}, u32[]{:S(2)}) collective-permute-start(f32[1,256,1280]{2,1,0:T(8,128)S(1)} %get-tuple-element.6), channel_id=1, source_target_pairs={{0,2},{1,3},{2,0},{3,1},{4,6},{5,7},{6,4},{7,5},{8,10},{9,11},{10,... | collective-permute-start | bytes 3932168 | tf_op jit(solution)/shard_map/ppermute | solution.py:201

commit v4 on v3

--- a/solution.py
+++ b/solution.py
@@ -77,59 +77,71 @@
     head_dim = HEAD_SIZE
     ctx_index = lax.axis_index("ctx")
 
-    length_rows = jnp.where(
-        jnp.arange(ctx_count, dtype=jnp.int32)[:, None] == ctx_index,
-        seq_len.astype(jnp.float32),
-        0.0,
-    )
-    all_lengths = lax.psum(length_rows, "ctx").astype(jnp.int32)
-    group_x = doubling_gather(x_pool, "head", head_count)
+    all_lengths = doubling_gather(seq_len, "ctx", ctx_count)
+    near_x, far_x = split_gather(x_pool, "head", head_count)
+    half_rows = near_x.shape[0]
 
     dest_grid = pool_dest.reshape(ctx_count, group_rows)
     my_dest = lax.dynamic_index_in_dim(dest_grid, ctx_index, 0, keepdims=False)
-    is_filled = my_dest >= 0
-    owner = jnp.where(is_filled, my_dest // pack_len, 0)
-    slot = jnp.where(is_filled, my_dest % pack_len, 0)
+    upper = lax.axis_index("head") >= head_count - head_count // 2
+    if far_x.shape[0]:
+        to_work_order = lambda v: jnp.where(upper, jnp.roll(v, -half_rows), v)
+    else:
+        to_work_order = lambda v: v
+    work_dest = to_work_order(my_dest)
+    is_filled = work_dest >= 0
+    owner = jnp.where(is_filled, work_dest // pack_len, 0)
+    slot = jnp.where(is_filled, work_dest % pack_len, 0)
     seq_ends = jnp.cumsum(all_lengths, axis=1).astype(jnp.int32)
     row_ends = jnp.take(seq_ends, owner, axis=0)
     row_lengths = jnp.take(all_lengths, owner, axis=0)
     finished = (row_ends <= slot[:, None]).astype(jnp.int32)
     sequence_starts = slot - jnp.sum(finished * row_lengths, axis=1)
 
-    values_wide = group_x.astype(jnp.float32)
-    normalized_input = (
-        values_wide
-        * lax.rsqrt(jnp.mean(values_wide * values_wide, axis=-1, keepdims=True) + norm_eps)
-        * norm_gain
-    ).astype(jnp.bfloat16)
     local_heads = w_query.shape[1] // head_dim
     local_kv = key_projection_weight.shape[1] // head_dim
     query_group_count = local_heads // local_kv
-    query_matrix = jnp.dot(normalized_input, w_query, preferred_element_type=jnp.float32) + q_bias
-    query_matrix = apply_rotary(
-        query_matrix.reshape(group_rows, local_heads, head_dim), sequence_starts, head_dim
-    ).astype(jnp.bfloat16)
-    projected_key_rows = (
-        jnp.dot(normalized_input, key_projection_weight, preferred_element_type=jnp.float32)
-        + key_bias_vector
-    )
-    projected_key_rows = apply_rotary(
-        projected_key_rows.reshape(group_rows, local_kv, head_dim), sequence_starts, head_dim
-    ).astype(jnp.bfloat16)
-    projected_value_rows = (
-        jnp.dot(normalized_input, value_projection_weight, preferred_element_type=jnp.float32)
-        + value_bias_vector
-    ).astype(jnp.bfloat16)
-    qkv = jnp.concatenate(
-        [
-            query_matrix.reshape(group_rows, local_heads * head_dim),
-            projected_key_rows.reshape(group_rows, local_kv * head_dim),
-            projected_value_rows,
-        ],
-        axis=1,
-    )
-
-    places = send_places(my_dest, ctx_count, group_cap, pack_len)
+
+    def project(rows_x, starts):
+        count = rows_x.shape[0]
+        values_wide = rows_x.astype(jnp.float32)
+        normalized_input = (
+            values_wide
+            * lax.rsqrt(jnp.mean(values_wide * values_wide, axis=-1, keepdims=True) + norm_eps)
+            * norm_gain
+        ).astype(jnp.bfloat16)
+        query_matrix = (
+            jnp.dot(normalized_input, w_query, preferred_element_type=jnp.float32) + q_bias
+        )
+        query_matrix = apply_rotary(
+            query_matrix.reshape(count, local_heads, head_dim), starts, head_dim
+        ).astype(jnp.bfloat16)
+        key_rows = (
+            jnp.dot(normalized_input, key_projection_weight, preferred_element_type=jnp.float32)
+            + key_bias_vector
+        )
+        key_rows = apply_rotary(
+            key_rows.reshape(count, local_kv, head_dim), starts, head_dim
+        ).astype(jnp.bfloat16)
+        value_rows = (
+            jnp.dot(normalized_input, value_projection_weight, preferred_element_type=jnp.float32)
+            + value_bias_vector
+        ).astype(jnp.bfloat16)
+        return jnp.concatenate(
+            [
+                query_matrix.reshape(count, local_heads * head_dim),
+                key_rows.reshape(count, local_kv * head_dim),
+                value_rows,
+            ],
+            axis=1,
+        )
+
+    parts = [project(near_x, sequence_starts[:half_rows])]
+    if far_x.shape[0]:
+        parts.append(project(far_x, sequence_starts[half_rows:]))
+    qkv = jnp.concatenate(parts, axis=0)
+
+    places = to_work_order(send_places(my_dest, ctx_count, group_cap, pack_len))
     send_hot = (
         places[None, :] == jnp.arange(ctx_count * group_cap, dtype=jnp.int32)[:, None]
     ).astype(jnp.bfloat16)
@@ -217,6 +229,37 @@
         second = jnp.where(bit == 0, got, have)
         have = jnp.stack([first, second], axis=1).reshape((-1,) + part.shape)
     return have.reshape((count * part.shape[0],) + part.shape[1:])
+
+
+def split_gather(part, axis_name, count):
+    if count == 1:
+        return part, part[:0]
+    half = count // 2
+    if count % 2 or half & (half - 1):
+        gathered = lax.all_gather(part, axis_name, tiled=True)
+        return gathered, gathered[:0]
+    me = lax.axis_index(axis_name)
+    crossed = lax.ppermute(part, axis_name, [(i, (i + half) % count) for i in range(count)])
+    if half == 1:
+        return part, crossed
+    near = doubling_gather_within(part, axis_name, half)
+    far = doubling_gather_within(crossed, axis_name, half)
+    return near, far
+
+
+def doubling_gather_within(part, axis_name, span):
+    bits = span.bit_length() - 1
+    me = lax.axis_index(axis_name)
+    count = lax.axis_size(axis_name)
+    have = part[None]
+    for stage in reversed(range(bits)):
+        bit = (me >> stage) & 1
+        pairs = [(i, i ^ (1 << stage)) for i in range(count)]
+        got = lax.ppermute(have, axis_name, pairs)
+        first = jnp.where(bit == 0, have, got)
+        second = jnp.where(bit == 0, got, have)
+        have = jnp.stack([first, second], axis=1).reshape((-1,) + part.shape)
+    return have.reshape((span * part.shape[0],) + part.shape[1:])
 
 
 def solution(mesh):

time: 146 us -> 135 us (0.925)
  blocking collectives: 21.9 us -> 0 us
  starting transfers between devices: 8.29 us -> 16.3 us
  waiting for transfers between devices: 67.6 us -> 60 us
  local copies, waits for them, and re-layouts: 6.21 us -> 13.3 us
  other arithmetic: 22.9 us -> 26.7 us
    psum x1 -> x0, blocking collectives: 21.9 us -> none  [local(): all_lengths = lax.psum(length_rows, 'ctx').astype(jnp.int32)]
    ppermute x2 -> x3, waiting for transfers between devices: 20.6 us -> 3.98 us  [doubling_gather(): got = lax.ppermute(have, axis_name, pairs)]
    ppermute x0 -> x3, waiting for transfers between devices: none -> 4.85 us  [the longest x1 4.84 us: split_gather(): lax.ppermute(part, axis_name, [(i, (i + half) % count) for i in range(cou...]
    another operation x3, other arithmetic: 0.95 us -> 5.79 us  [halving_scatter(): jnp.stack([jnp.where(bit == 0, hi, lo) for (_, lo), hi in zip(lows, highs)])]
    all_to_all x1, waiting for transfers between devices: 12.8 us -> 16.6 us  [local(): lax.all_to_all(outgoing, 'ctx', split_axis=0, concat_axis=0, tiled=True)]
    another operation x8 -> x11, other arithmetic: 2.27 us -> 5.58 us  [the longest x2 3.26 us: doubling_gather_within(): have = jnp.stack([first, second], axis=1).reshape((-1,) + part.shape)]
    ppermute x0 -> x3, starting transfers between devices: none -> 2.94 us  [the longest x1 2.94 us: split_gather(): lax.ppermute(part, axis_name, [(i, (i + half) % count) for i in range(cou...]
    ppermute x2 -> x3, starting transfers between devices: 2.94 us -> 5.75 us  [doubling_gather(): got = lax.ppermute(have, axis_name, pairs)]
  transfers between devices with their start and end apart: 5 -> 9, of which waited for: 4 -> 6; matrix products, arithmetic and copies ran while one was open for 7% -> 10% of each run, Pallas kernels for 0% -> 0%
where the time goes in v4:
time: 135 us
  waiting for transfers between devices  60 us (44%)
  other arithmetic  26.7 us (20%)
  matrix products  18.1 us (13%)
  starting transfers between devices  16.3 us (12%)
  local copies, waits for them, and re-layouts  13.3 us (10%)
    ppermute x2, waiting for transfers between devices, halving_scatter(): got = lax.ppermute(send, axis_name, pairs)  34.6 us
    all_to_all x1, waiting for transfers between devices, local(): lax.all_to_all(outgoing, 'ctx', split_axis=0, concat_axis=0, tiled=True)  16.6 us
    dot_general x2, matrix products, project(): jnp.dot(normalized_input, w_query, preferred_element_type=jnp.float32)  7.49 us
    all_to_all x1, starting transfers between devices, local(): lax.all_to_all(outgoing, 'ctx', split_axis=0, concat_axis=0, tiled=True)  6.09 us
    another operation x3, other arithmetic, halving_scatter(): jnp.stack([jnp.where(bit == 0, hi, lo) for (_, lo), hi in zip(lows, highs)])  5.79 us
    ppermute x3, starting transfers between devices, doubling_gather(): got = lax.ppermute(have, axis_name, pairs)  5.75 us
    dot_general x1, matrix products, local(): jnp.dot(mixed_heads, w_out, preferred_element_type=jnp.float32)  5.19 us
    ppermute x1, waiting for transfers between devices, split_gather(): lax.ppermute(part, axis_name, [(i, (i + half) % count) for i in range(cou...  4.84 us
  transfers between devices with their start and end apart: 9, of which 6 were waited for; matrix products, arithmetic and copies ran while one was open for 10% of the time, Pallas kernels for 0%

profile of v4, /device:TPU:0, one launch (start us, length us, event | category | flops | bytes accessed | tf_op | source)
XLA Modules:
  0.0 134.9 jit_solution(1528038333576700677)
XLA Ops:
  0.0 2.9 %collective-permute-start.4 = (bf16[96,5120]{1,0:T(8,128)(2,1)}, bf16[96,5120]{1,0:T(8,128)(2,1)}, u32[]{:S(2)}, u32[]{:S(2)}) collective-permute-start(bf16[96,5120]{1,0:T(8,128)(2,1)} %param.13), channel_id=1, source_target_pairs={{0,2},{1,3},{2,0},{3,1},{4,6},{5,7},{6,4},{7,5},{8,10},{9,11},{10,... | collective-permute-start | bytes 2949128 | tf_op jit(solution)/shard_map/ppermute | solution.py:242
  2.9 2.6 %collective-permute-start.1 = (s32[1,1,8]{2,1,0:T(1,128)}, s32[1,1,8]{2,1,0:T(1,128)S(1)}, u32[]{:S(2)}, u32[]{:S(2)}) collective-permute-start(s32[1,1,8]{2,1,0:T(1,128)} %bitcast.178), channel_id=1, source_target_pairs={{0,16},{4,20},{8,24},{12,28},{16,0},{20,4},{24,8},{28,12},{1,17},{... | collective-permute-start | bytes 104 | tf_op jit(solution)/shard_map/ppermute | solution.py:227
  5.5 0.7 reshape.576
  6.3 0.9 reduce-window.30
  7.2 0.2 slice_reduce_fusion
  7.5 0.1 copy.34
  7.8 0.2 fusion.33
  8.3 0.7 fusion.70
  8.9 0.7 fusion.73
  9.6 1.6 %collective-permute-start.2 = (s32[2,1,8]{2,0,1:T(2,128)S(1)}, s32[2,1,8]{2,0,1:T(2,128)S(1)}, u32[]{:S(2)}, u32[]{:S(2)}) collective-permute-start(s32[2,1,8]{2,0,1:T(2,128)S(1)} %bitcast.176), channel_id=1, source_target_pairs={{0,8},{4,12},{8,0},{12,4},{16,24},{20,28},{24,16},{28,20},{1,9},{5... | collective-permute-start | bytes 200 | tf_op jit(solution)/shard_map/ppermute | solution.py:227
  11.3 1.9 %collective-permute-done.2 = s32[2,1,8]{2,0,1:T(2,128)S(1)} collective-permute-done((s32[2,1,8]{2,0,1:T(2,128)S(1)}, s32[2,1,8]{2,0,1:T(2,128)S(1)}, u32[]{:S(2)}, u32[]{:S(2)}) %collective-permute-start.2) | collective-permute-done | bytes 96 | tf_op jit(solution)/shard_map/ppermute | solution.py:227
  13.2 1.6 %collective-permute-start.3 = (s32[4,1,8]{2,0,1:T(4,128)S(1)}, s32[4,1,8]{2,0,1:T(4,128)S(1)}, u32[]{:S(2)}, u32[]{:S(2)}) collective-permute-start(s32[4,1,8]{2,0,1:T(4,128)S(1)} %bitcast.170), channel_id=1, source_target_pairs={{0,4},{4,0},{8,12},{12,8},{16,20},{20,16},{24,28},{28,24},{1,5},{5... | collective-permute-start | bytes 392 | tf_op jit(solution)/shard_map/ppermute | solution.py:227
  14.8 2.1 %collective-permute-done.3 = s32[4,1,8]{2,0,1:T(4,128)S(1)} collective-permute-done((s32[4,1,8]{2,0,1:T(4,128)S(1)}, s32[4,1,8]{2,0,1:T(4,128)S(1)}, u32[]{:S(2)}, u32[]{:S(2)}) %collective-permute-start.3) | collective-permute-done | bytes 160 | tf_op jit(solution)/shard_map/ppermute | solution.py:227
  16.9 0.2 reduce_window_sum.54
  17.0 1.1 gather_fusion.1
  18.1 1.1 gather_fusion
  19.3 0.3 fusion.34
  19.6 0.5 multiply_cosine_fusion.3
  20.2 4.8 %collective-permute-done.4 = bf16[96,5120]{1,0:T(8,128)(2,1)} collective-permute-done((bf16[96,5120]{1,0:T(8,128)(2,1)}, bf16[96,5120]{1,0:T(8,128)(2,1)}, u32[]{:S(2)}, u32[]{:S(2)}) %collective-permute-start.4) | collective-permute-done | bytes 983072 | tf_op jit(solution)/shard_map/ppermute | solution.py:242
  25.0 1.6 %select_bitcast_fusion.6 = (bf16[1,1,96,5120]{3,2,1,0:T(8,128)(2,1)S(1)}, bf16[1,1,96,5120]{3,2,1,0:T(8,128)(2,1)S(1)}) fusion(bf16[1,96,5120]{2,1,0:T(8,128)(2,1)} %collective-permute-done, pred[]{:T(512)S(6)} %eq.114, bf16[96,5120]{1,0:T(8,128)(2,1)} %param.13), kind=kLoop, calls=%fused_computation.46 | loop fusion | flops 983040 | bytes 3932161 | tf_op jit(solution)/shard_map/stack | solution.py:261
  26.7 0.5 multiply_reduce_fusion.1
  27.1 0.6 add_rsqrt_fusion.1
  27.7 1.3 rsqrt.23
  29.1 1.6 %select_bitcast_fusion.4 = (bf16[1,1,96,5120]{3,2,1,0:T(8,128)(2,1)S(1)}, bf16[1,1,96,5120]{3,2,1,0:T(8,128)(2,1)S(1)}) fusion(bf16[1,96,5120]{2,1,0:T(8,128)(2,1)} %collective-permute-done.5, pred[]{:T(512)S(6)} %eq.114, bf16[96,5120]{1,0:T(8,128)(2,1)} %collective-permute-done.4), kind=kLoop, calls=%fused_computation.44 | loop fusion | flops 983040 | bytes 3932161 | tf_op jit(solution)/shard_map/stack | solution.py:261
  30.7 3.6 %maximum_convert_fusion = (f32[1,2,96,5120]{3,2,1,0:T(8,128)}, f32[1,2,96,5120]{3,2,1,0:T(8,128)}) fusion(bf16[1,1,96,5120]{3,2,1,0:T(8,128)(2,1)S(1)} %get-tuple-element.16, bf16[1,1,96,5120]{3,2,1,0:T(8,128)(2,1)S(1)} %get-tuple-element.15, bf16[1,1,96,5120]{3,2,1,0:T(8,128)(2,1)S(1)} %get-tuple-element.18, bf16[1,1,96,5120]{3,2,1,0:T(8,128)(2,1)S(1)} %get-tuple-element.17), kind=kLoop, calls=%fused_computation.13 | loop fusion | flops 3932160 | bytes 11796480 | tf_op jit(solution)/shard_map/convert_element_type | solution.py:107
  34.3 0.5 multiply_reduce_fusion
  34.9 0.1 copy-done.8
  35.0 4.5 %fusion.3 = (bf16[192,5120]{1,0:T(8,128)(2,1)S(1)}, bf16[192,5120]{1,0:T(8,128)(2,1)S(1)}) fusion(f32[1,2,96,5120]{3,2,1,0:T(8,128)} %get-tuple-element.53, f32[5120]{0:T(1024)S(1)} %copy-done.8, f32[192]{0:T(256)S(1)} %copy-done.11, f32[192]{0:T(256)S(1)} %rsqrt.25, f32[1,2,96,5120]{3,2,1,0:T(8,128)} %get-tuple-element.54), kind=kLoop, calls=%fused_computation.7 | loop fusion | flops 5898240 | bytes 11818496 | tf_op jit(solution)/shard_map/convert_element_type | solution.py:112
  39.6 0.7 fusion.11
  40.3 0.7 fusion.10
  41.0 0.6 copy-done.2
  41.6 0.7 fusion.13
  42.3 0.7 fusion.12
  43.0 5.7 %convolution_add_fusion = f32[192,640]{1,0:T(8,128)} fusion(bf16[192,5120]{1,0:T(8,128)(2,1)S(1)} %get-tuple-element.28, bf16[5120,640]{1,0:T(8,128)(2,1)} %param.17, f32[640]{0:T(1024)S(1)} %copy-done.18), kind=kOutput, calls=%fused_computation.32 | convolution fusion | flops 1258414080 | bytes 9013760 | tf_op jit(solution)/shard_map/dot_general | solution.py:114
  48.8 1.7 %convolution_add_fusion.1 = f32[192,640]{1,0:T(8,128)S(1)} fusion(bf16[192,5120]{1,0:T(8,128)(2,1)S(1)} %get-tuple-element.27, bf16[5120,640]{1,0:T(8,128)(2,1)S(1)} %bitcast.181, f32[640]{0:T(1024)S(1)} %copy-done.18), kind=kOutput, calls=%fused_computation.33 | convolution fusion | flops 1258414080 | bytes 9013760 | tf_op jit(solution)/shard_map/dot_general | solution.py:114
  50.5 0.7 copy.44
  51.3 0.8 fusion.53
  52.1 0.7 copy.43
  52.8 0.7 copy.42
  53.5 1.3 copy.41
  54.8 0.7 copy.40
  55.7 0.2 copy.35
  56.3 0.5 copy-done.3
  56.9 1.5 %convolution_convert_fusion = bf16[384,896]{1,0:T(8,128)(2,1)} fusion(bf16[192,128]{0,1:T(8,128)(2,1)S(1)} %copy-done.3, bf16[192,64]{0,1:T(8,128)(2,1)S(1)} %copy-done.6, bf16[192,64]{0,1:T(8,128)(2,1)S(1)} %copy-done.7, bf16[192,640]{0,1:T(8,128)(2,1)S(1)} %bitcast.164, bf16[192,128]{0,1:T(8,128)(2,1)S(1)} %copy-done.4, bf16[192,64]{0,1:T(8,128)(2,1)S(1)} %copy.39, ...), kind=kOutput, calls=%fused_computation.17 | convolution fusion | flops 270237696 | bytes 1377792 | tf_op jit(solution)/shard_map/dot_general | solution.py:148
  58.4 6.1 %all-to-all-start = ((bf16[8,48,896]{2,1,0:T(8,128)(2,1)}), bf16[8,48,896]{2,1,0:T(8,128)(2,1)S(1)}, u32[]{:S(2)}, u32[]{:S(2)}) async-start(bf16[8,48,896]{2,1,0:T(8,128)(2,1)} %bitcast.34), calls=%async_computation | async-start | bytes 1376256 | tf_op jit(solution)/shard_map/all_to_all | solution.py:149
  64.5 0.9 reduce-window.21
  65.4 0.2 slice_reduce_fusion.1
  65.8 0.2 reduce-window.32
  66.0 0.4 select_reduce_fusion
  66.6 16.6 %all-to-all-done = bf16[8,48,896]{2,1,0:T(8,128)(2,1)S(1)} async-done(((bf16[8,48,896]{2,1,0:T(8,128)(2,1)}), bf16[8,48,896]{2,1,0:T(8,128)(2,1)S(1)}, u32[]{:S(2)}, u32[]{:S(2)}) %all-to-all-start) | async-done | bytes 688160 | tf_op jit(solution)/shard_map/all_to_all | solution.py:149
  83.2 0.5 convolution_convert_fusion.1
  83.7 0.2 copy.45
  83.8 0.3 fusion.80
  84.2 0.2 fusion.9
  84.4 0.4 convolution_convert_fusion.2
  84.8 5.2 %fusion.81 = f32[256,5120]{1,0:T(8,128)S(1)} fusion(bf16[256,640]{0,1:T(8,128)(2,1)S(1)} %bitcast.163, bf16[640,5120]{1,0:T(8,128)(2,1)} %param.23), kind=kOutput, calls=%fused_computation.200 | convolution fusion | flops 1677721600 | bytes 12124160 | tf_op jit(solution)/shard_map/dot_general | solution.py:195
  90.0 0.3 select_bitcast_fusion.2
  90.3 2.0 %copy-done.1 = f32[256,5120]{1,0:T(8,128)} copy-done((f32[256,5120]{1,0:T(8,128)}, f32[256,5120]{1,0:T(8,128)S(1)}, u32[]{:S(2)}) %copy-start.1) | copy-done | bytes 5242904
  92.3 1.7 %pad_maximum_fusion = f32[2,256,1280]{2,1,0:T(8,128)} fusion(f32[1,256,1280]{2,1,0:T(8,128)S(1)} %get-tuple-element.14, f32[1,256,1280]{2,1,0:T(8,128)S(1)} %get-tuple-element.13), kind=kLoop, calls=%fused_computation.12 | loop fusion | flops 655360 | bytes 5242880 | tf_op jit(solution)/shard_map/stack | solution.py:211
  94.0 5.2 %collective-permute-done.6 = f32[2,256,1280]{2,1,0:T(8,128)} collective-permute-done((f32[2,256,1280]{2,1,0:T(8,128)}, f32[2,256,1280]{2,1,0:T(8,128)}, u32[]{:S(2)}, u32[]{:S(2)}) %collective-permute-start.6) | collective-permute-done | bytes 2621472 | tf_op jit(solution)/shard_map/ppermute | solution.py:213
  99.3 3.8 %select_bitcast_fusion = (f32[1,256,1280]{2,1,0:T(8,128)S(1)}, f32[256,1280]{1,0:T(8,128)S(1)}, f32[256,1280]{1,0:T(8,128)S(1)}) fusion(pred[]{:T(512)S(6)} %eq.113, f32[2,256,1280]{2,1,0:T(8,128)} %collective-permute-done.6, f32[256,5120]{1,0:T(8,128)} %copy-done.1, pred[]{:T(512)S(6)} %eq.114), kind=kLoop, calls=%fused_computation.24 | loop fusion | flops 1638400 | bytes 11796482 | tf_op jit(solution)/shard_map/stack | solution.py:211
  103.0 1.6 %collective-permute-start.7 = (f32[1,256,1280]{2,1,0:T(8,128)S(1)}, f32[1,256,1280]{2,1,0:T(8,128)S(1)}, u32[]{:S(2)}, u32[]{:S(2)}) collective-permute-start(f32[1,256,1280]{2,1,0:T(8,128)S(1)} %get-tuple-element.6), channel_id=1, source_target_pairs={{0,2},{1,3},{2,0},{3,1},{4,6},{5,7},{6,4},{7,5},{8,10},{9,11},{10,... | collective-permute-start | bytes 3932168 | tf_op jit(solution)/shard_map/ppermute | solution.py:213
  104.6 29.3 %collective-permute-done.7 = f32[1,256,1280]{2,1,0:T(8,128)S(1)} collective-permute-done((f32[1,256,1280]{2,1,0:T(8,128)S(1)}, f32[1,256,1280]{2,1,0:T(8,128)S(1)}, u32[]{:S(2)}, u32[]{:S(2)}) %collective-permute-start.7) | collective-permute-done | bytes 1310752 | tf_op jit(solution)/shard_map/ppermute | solution.py:213
  133.9 1.0 fusion.7
  (89 shorter events, 1.8 us)
Async XLA Ops:
  0.0 39.6 %copy-start = (bf16[5120,128]{1,0:T(8,128)(2,1)S(1)}, bf16[5120,128]{1,0:T(8,128)(2,1)}, u32[]{:S(2)}) copy-start(bf16[5120,128]{1,0:T(8,128)(2,1)} %param.19) | copy-start | bytes 3932164
  0.0 25.0 %collective-permute-start.4 = (bf16[96,5120]{1,0:T(8,128)(2,1)}, bf16[96,5120]{1,0:T(8,128)(2,1)}, u32[]{:S(2)}, u32[]{:S(2)}) collective-permute-start(bf16[96,5120]{1,0:T(8,128)(2,1)} %param.13), channel_id=1, source_target_pairs={{0,2},{1,3},{2,0},{3,1},{4,6},{5,7},{6,4},{7,5},{8,10},{9,11},{10,... | collective-permute-start | bytes 2949128 | tf_op jit(solution)/shard_map/ppermute | solution.py:242
  2.9 22.1 %collective-permute-start = (bf16[1,96,5120]{2,1,0:T(8,128)(2,1)}, bf16[1,96,5120]{2,1,0:T(8,128)(2,1)}, u32[]{:S(2)}, u32[]{:S(2)}) collective-permute-start(bf16[1,96,5120]{2,1,0:T(8,128)(2,1)} %bitcast.162), channel_id=1, source_target_pairs={{0,1},{1,0},{2,3},{3,2},{4,5},{5,4},{6,7},{7,6},{8,9},{9,8},{10,11... | collective-permute-start | bytes 2949128 | tf_op jit(solution)/shard_map/ppermute | solution.py:258
  2.9 6.0 %collective-permute-start.1 = (s32[1,1,8]{2,1,0:T(1,128)}, s32[1,1,8]{2,1,0:T(1,128)S(1)}, u32[]{:S(2)}, u32[]{:S(2)}) collective-permute-start(s32[1,1,8]{2,1,0:T(1,128)} %bitcast.178), channel_id=1, source_target_pairs={{0,16},{4,20},{8,24},{12,28},{16,0},{20,4},{24,8},{28,12},{1,17},{... | collective-permute-start | bytes 104 | tf_op jit(solution)/shard_map/ppermute | solution.py:227
  5.5 14.1 %copy-start.13 = (f32[64]{0:T(128)}, f32[64]{0:T(128)S(1)}, u32[]{:S(2)}) copy-start(f32[64]{0:T(128)S(1)} %multiply_exponential_fusion) | copy-start | bytes 772
  9.6 3.6 %collective-permute-start.2 = (s32[2,1,8]{2,0,1:T(2,128)S(1)}, s32[2,1,8]{2,0,1:T(2,128)S(1)}, u32[]{:S(2)}, u32[]{:S(2)}) collective-permute-start(s32[2,1,8]{2,0,1:T(2,128)S(1)} %bitcast.176), channel_id=1, source_target_pairs={{0,8},{4,12},{8,0},{12,4},{16,24},{20,28},{24,16},{28,20},{1,9},{5... | collective-permute-start | bytes 200 | tf_op jit(solution)/shard_map/ppermute | solution.py:227
  13.2 3.7 %collective-permute-start.3 = (s32[4,1,8]{2,0,1:T(4,128)S(1)}, s32[4,1,8]{2,0,1:T(4,128)S(1)}, u32[]{:S(2)}, u32[]{:S(2)}) collective-permute-start(s32[4,1,8]{2,0,1:T(4,128)S(1)} %bitcast.170), channel_id=1, source_target_pairs={{0,4},{4,0},{8,12},{12,8},{16,20},{20,16},{24,28},{28,24},{1,5},{5... | collective-permute-start | bytes 392 | tf_op jit(solution)/shard_map/ppermute | solution.py:227
  19.6 5.4 %copy-start.9 = (f32[192]{0:T(256)}, f32[192]{0:T(256)S(1)}, u32[]{:S(2)}) copy-start(f32[192]{0:T(256)S(1)} %get-tuple-element.38) | copy-start | bytes 2308
  25.0 4.0 %collective-permute-start.5 = (bf16[1,96,5120]{2,1,0:T(8,128)(2,1)}, bf16[1,96,5120]{2,1,0:T(8,128)(2,1)}, u32[]{:S(2)}, u32[]{:S(2)}) collective-permute-start(bf16[1,96,5120]{2,1,0:T(8,128)(2,1)} %bitcast.25), channel_id=1, source_target_pairs={{0,1},{1,0},{2,3},{3,2},{4,5},{5,4},{6,7},{7,6},{8,9},{9,8},{10,11... | collective-permute-start | bytes 2949128 | tf_op jit(solution)/shard_map/ppermute | solution.py:258
  34.3 0.7 copy-start.8
  34.3 0.7 copy-start.11
  35.0 4.5 %copy-start.15 = (f32[128]{0:T(128)S(1)}, f32[128]{0:T(128)}, u32[]{:S(2)}) copy-start(f32[128]{0:T(128)} %param.20) | copy-start | bytes 1540
  40.3 1.3 copy-start.2
  40.3 1.3 copy-start.16
  41.6 1.4 %copy-start.18 = (f32[640]{0:T(1024)S(1)}, f32[640]{0:T(1024)}, u32[]{:S(2)}) copy-start(f32[640]{0:T(1024)} %param.18) | copy-start | bytes 7684
  42.3 6.5 %slice-start = ((s8[6553600]{0:T(1024)(128)(4,1)}), s8[4194304]{0:T(1024)(128)(4,1)S(1)}, s32[]{:S(2)}) async-start(s8[6553600]{0:T(1024)(128)(4,1)} %bitcast.180), calls=%async_computation.1 | async-start | bytes 8388608
  43.0 5.8 %slice-start.1 = ((s8[6553600]{0:T(1024)(128)(4,1)}), s8[2359296]{0:T(1024)(128)(4,1)S(1)}, s32[]{:S(2)}) async-start(s8[6553600]{0:T(1024)(128)(4,1)} %bitcast.180), calls=%async_computation.2 | async-start | bytes 4718592
  48.8 2.5 %copy-start.10 = (f32[192]{0:T(256)S(1)}, f32[192]{0:T(256)}, u32[]{:S(2)}) copy-start(f32[192]{0:T(256)} %copy-done.9) | copy-start | bytes 2308
  48.8 2.5 %copy-start.14 = (f32[64]{0:T(128)S(1)}, f32[64]{0:T(128)}, u32[]{:S(2)}) copy-start(f32[64]{0:T(128)} %copy-done.13) | copy-start | bytes 772
  55.9 0.8 copy-start.3
  56.0 0.9 copy-start.4
  56.0 0.9 copy-start.6
  56.0 0.8 copy-start.7
  56.0 0.8 copy-start.12
  56.8 7.6 %copy-start.5 = (s32[3072]{0:T(1024)S(1)}, s32[3072]{0:T(1024)}, u32[]{:S(2)}) copy-start(s32[3072]{0:T(1024)} %param.14) | copy-start | bytes 36868
  56.8 8.9 %copy-start.17 = (s32[1,8]{1,0:T(1,128)S(1)}, s32[1,8]{1,0:T(1,128)}, u32[]{:S(2)}) copy-start(s32[1,8]{1,0:T(1,128)} %param.15) | copy-start | bytes 100
  58.4 24.8 %all-to-all-start = ((bf16[8,48,896]{2,1,0:T(8,128)(2,1)}), bf16[8,48,896]{2,1,0:T(8,128)(2,1)S(1)}, u32[]{:S(2)}, u32[]{:S(2)}) async-start(bf16[8,48,896]{2,1,0:T(8,128)(2,1)} %bitcast.34), calls=%async_computation | async-start | bytes 1376256 | tf_op jit(solution)/shard_map/all_to_all | solution.py:149
  90.0 2.3 %copy-start.1 = (f32[256,5120]{1,0:T(8,128)}, f32[256,5120]{1,0:T(8,128)S(1)}, u32[]{:S(2)}) copy-start(f32[256,5120]{1,0:T(8,128)S(1)} %fusion.81) | copy-start | bytes 15728644
  94.0 5.3 %collective-permute-start.6 = (f32[2,256,1280]{2,1,0:T(8,128)}, f32[2,256,1280]{2,1,0:T(8,128)}, u32[]{:S(2)}, u32[]{:S(2)}) collective-permute-start(f32[2,256,1280]{2,1,0:T(8,128)} %pad_maximum_fusion), channel_id=1, source_target_pairs={{0,1},{1,0},{2,3},{3,2},{4,5},{5,4},{6,7},{7,6},{8,9},{9,8},{10,11... | collective-permute-start | bytes 7864328 | tf_op jit(solution)/shard_map/ppermute | solution.py:213
  103.0 30.9 %collective-permute-start.7 = (f32[1,256,1280]{2,1,0:T(8,128)S(1)}, f32[1,256,1280]{2,1,0:T(8,128)S(1)}, u32[]{:S(2)}, u32[]{:S(2)}) collective-permute-start(f32[1,256,1280]{2,1,0:T(8,128)S(1)} %get-tuple-element.6), channel_id=1, source_target_pairs={{0,2},{1,3},{2,0},{3,1},{4,6},{5,7},{6,4},{7,5},{8,10},{9,11},{10,... | collective-permute-start | bytes 3932168 | tf_op jit(solution)/shard_map/ppermute | solution.py:213

commit v5 on v4

--- a/solution.py
+++ b/solution.py
@@ -78,13 +78,13 @@
     ctx_index = lax.axis_index("ctx")
 
     all_lengths = doubling_gather(seq_len, "ctx", ctx_count)
-    near_x, far_x = split_gather(x_pool, "head", head_count)
+    near_x, crossed, finish_far = split_gather(x_pool, "head", head_count)
     half_rows = near_x.shape[0]
 
     dest_grid = pool_dest.reshape(ctx_count, group_rows)
     my_dest = lax.dynamic_index_in_dim(dest_grid, ctx_index, 0, keepdims=False)
     upper = lax.axis_index("head") >= head_count - head_count // 2
-    if far_x.shape[0]:
+    if crossed.shape[0]:
         to_work_order = lambda v: jnp.where(upper, jnp.roll(v, -half_rows), v)
     else:
         to_work_order = lambda v: v
@@ -136,24 +136,38 @@
             axis=1,
         )
 
-    parts = [project(near_x, sequence_starts[:half_rows])]
-    if far_x.shape[0]:
-        parts.append(project(far_x, sequence_starts[half_rows:]))
-    qkv = jnp.concatenate(parts, axis=0)
-
-    places = to_work_order(send_places(my_dest, ctx_count, group_cap, pack_len))
-    send_hot = (
-        places[None, :] == jnp.arange(ctx_count * group_cap, dtype=jnp.int32)[:, None]
-    ).astype(jnp.bfloat16)
-    outgoing = jnp.dot(send_hot, qkv, preferred_element_type=jnp.float32).astype(jnp.bfloat16)
-    arrived = lax.all_to_all(outgoing, "ctx", split_axis=0, concat_axis=0, tiled=True)
+    halves = [(near_x, work_dest[:half_rows], sequence_starts[:half_rows])]
+    if crossed.shape[0]:
+        halves.append((crossed, work_dest[half_rows:], sequence_starts[half_rows:]))
+    half_cap = group_cap // len(halves)
+    arrivals = []
+    for rows_x, rows_dest, starts in halves:
+        if arrivals:
+            rows_x, _ = lax.optimization_barrier((rows_x, outgoing))
+            rows_x = finish_far(rows_x)
+        part_qkv = project(rows_x, starts)
+        places = send_places(rows_dest, ctx_count, half_cap, pack_len)
+        send_hot = (
+            places[None, :] == jnp.arange(ctx_count * half_cap, dtype=jnp.int32)[:, None]
+        ).astype(jnp.bfloat16)
+        outgoing = jnp.dot(send_hot, part_qkv, preferred_element_type=jnp.float32).astype(
+            jnp.bfloat16
+        )
+        arrivals.append(lax.all_to_all(outgoing, "ctx", split_axis=0, concat_axis=0, tiled=True))
+    arrived = jnp.concatenate(arrivals, axis=0)
 
     mine = (pool_dest >= 0) & (pool_dest // pack_len == ctx_index)
-    mine_grid = mine.reshape(ctx_count, group_rows).astype(jnp.int32)
-    rank_in = jnp.cumsum(mine_grid, axis=1) - mine_grid
-    arrived_index = (
-        jnp.arange(ctx_count, dtype=jnp.int32)[:, None] * group_cap + rank_in
-    ).reshape(-1)
+    row_head = (jnp.arange(pool_dest.shape[0], dtype=jnp.int32) // pool_rows) % head_count
+    in_near = (row_head >= head_count - head_count // 2) == upper
+    if len(halves) == 1:
+        in_near = jnp.ones_like(in_near)
+    group_base = jnp.arange(ctx_count, dtype=jnp.int32)[:, None] * half_cap
+    arrived_index = 0
+    for k, member in enumerate([in_near, ~in_near][: len(halves)]):
+        taken = (mine & member).reshape(ctx_count, group_rows).astype(jnp.int32)
+        rank_in = jnp.cumsum(taken, axis=1) - taken
+        arrived_index = arrived_index + taken * (k * ctx_count * half_cap + group_base + rank_in)
+    arrived_index = arrived_index.reshape(-1)
     my_slot_of_row = jnp.where(mine, pool_dest - ctx_index * pack_len, -1)
     slot_ids = jnp.arange(pack_len, dtype=jnp.int32)
     names_slot = my_slot_of_row[None, :] == slot_ids[:, None]
@@ -233,18 +247,16 @@
 
 def split_gather(part, axis_name, count):
     if count == 1:
-        return part, part[:0]
+        return part, part[:0], lambda v: v
     half = count // 2
     if count % 2 or half & (half - 1):
         gathered = lax.all_gather(part, axis_name, tiled=True)
-        return gathered, gathered[:0]
-    me = lax.axis_index(axis_name)
+        return gathered, gathered[:0], lambda v: v
     crossed = lax.ppermute(part, axis_name, [(i, (i + half) % count) for i in range(count)])
     if half == 1:
-        return part, crossed
+        return part, crossed, lambda v: v
     near = doubling_gather_within(part, axis_name, half)
-    far = doubling_gather_within(crossed, axis_name, half)
-    return near, far
+    return near, crossed, lambda v: doubling_gather_within(v, axis_name, half)
 
 
 def doubling_gather_within(part, axis_name, span):

time: 135 us -> 139 us (1.030)
  waiting for transfers between devices: 60 us -> 48.4 us
  other arithmetic: 26.7 us -> 32.2 us
  matrix products: 18.1 us -> 23 us
  starting transfers between devices: 16.3 us -> 19.1 us
  local copies, waits for them, and re-layouts: 13.3 us -> 15.3 us
    all_to_all x1 -> x2, waiting for transfers between devices: 16.6 us -> 10.1 us  [local(): lax.all_to_all(outgoing, 'ctx', split_axis=0, concat_axis=0, tiled=True)]
    ppermute x1, waiting for transfers between devices: 4.84 us -> 0.01 us  [split_gather(): lax.ppermute(part, axis_name, [(i, (i + half) % count) for i in range(cou...]
    all_to_all x1 -> x2, starting transfers between devices: 6.09 us -> 9.8 us  [local(): lax.all_to_all(outgoing, 'ctx', split_axis=0, concat_axis=0, tiled=True)]
    another operation x9 -> x17, other arithmetic: 2.32 us -> 4.91 us
    dot_general x2, matrix products: 7.49 us -> 9.9 us  [project(): jnp.dot(normalized_input, w_query, preferred_element_type=jnp.float32)]
    another operation x2, other arithmetic: 3.26 us -> 1.47 us  [doubling_gather_within(): have = jnp.stack([first, second], axis=1).reshape((-1,) + part.shape)]
    concatenate x4, local copies, waits for them, and re-layouts: 1.57 us -> 3.16 us  [apply_rotary(): jnp.concatenate([first_half * cosine - second_half * sine_table, second_h...]
    ppermute x3, starting transfers between devices: 5.75 us -> 7.2 us  [doubling_gather(): got = lax.ppermute(have, axis_name, pairs)]
  transfers between devices with their start and end apart: 9 -> 10, of which waited for: 6 -> 5; matrix products, arithmetic and copies ran while one was open for 10% -> 39% of each run, Pallas kernels for 0% -> 0%
where the time goes in v5:
time: 139 us; the launch traced here: 138 us
  waiting for transfers between devices  48.4 us (35%)
  other arithmetic  32.2 us (23%)
  matrix products  23 us (17%)
  starting transfers between devices  19.1 us (14%)
  local copies, waits for them, and re-layouts  15.3 us (11%)
    ppermute x2, waiting for transfers between devices, halving_scatter(): got = lax.ppermute(send, axis_name, pairs)  35.5 us
    all_to_all x2, waiting for transfers between devices, local(): lax.all_to_all(outgoing, 'ctx', split_axis=0, concat_axis=0, tiled=True)  10.1 us
    dot_general x2, matrix products, project(): jnp.dot(normalized_input, w_query, preferred_element_type=jnp.float32)  9.9 us
    all_to_all x2, starting transfers between devices, local(): lax.all_to_all(outgoing, 'ctx', split_axis=0, concat_axis=0, tiled=True)  9.8 us
    ppermute x3, starting transfers between devices, doubling_gather(): got = lax.ppermute(have, axis_name, pairs)  7.2 us
    another operation x3, other arithmetic, halving_scatter(): jnp.stack([jnp.where(bit == 0, hi, lo) for (_, lo), hi in zip(lows, highs)])  5.79 us
    convert_element_type x2, other arithmetic, project(): normalized_input = (values_wide * lax.rsqrt(jnp.mean(values_wide * values...  5.28 us
    dot_general x1, matrix products, local(): jnp.dot(mixed_heads, w_out, preferred_element_type=jnp.float32)  5.19 us
  transfers between devices with their start and end apart: 10, of which 5 were waited for; matrix products, arithmetic and copies ran while one was open for 39% of the time, Pallas kernels for 0%

profile of v5, /device:TPU:0, one launch (start us, length us, event | category | flops | bytes accessed | tf_op | source)
XLA Modules:
  0.0 138.5 jit_solution(11224996291220689774)
XLA Ops:
  0.0 4.0 %collective-permute-start.1 = (s32[1,1,8]{2,1,0:T(1,128)}, s32[1,1,8]{2,1,0:T(1,128)S(1)}, u32[]{:S(2)}, u32[]{:S(2)}) collective-permute-start(s32[1,1,8]{2,1,0:T(1,128)} %bitcast.159), channel_id=1, source_target_pairs={{0,16},{4,20},{8,24},{12,28},{16,0},{20,4},{24,8},{28,12},{1,17},{... | collective-permute-start | bytes 104 | tf_op jit(solution)/shard_map/ppermute | solution.py:241
  4.0 1.5 %collective-permute-start.4 = (bf16[96,5120]{1,0:T(8,128)(2,1)}, bf16[96,5120]{1,0:T(8,128)(2,1)}, u32[]{:S(2)}, u32[]{:S(2)}) collective-permute-start(bf16[96,5120]{1,0:T(8,128)(2,1)} %param.13), channel_id=1, source_target_pairs={{0,2},{1,3},{2,0},{3,1},{4,6},{5,7},{6,4},{7,5},{8,10},{9,11},{10,... | collective-permute-start | bytes 2949128 | tf_op jit(solution)/shard_map/ppermute | solution.py:255
  5.5 0.5 multiply_exponential_fusion
  6.1 0.7 reshape.579
  7.1 1.3 reduce-window.56
  8.5 0.6 reduce-window.54
  9.4 0.6 add_select_fusion.6
  10.1 0.6 reduce-window.41
  11.0 0.6 add_select_fusion.7
  11.6 1.3 subtract_select_fusion
  12.9 0.7 fusion.78
  13.6 1.6 %collective-permute-start.2 = (s32[2,1,8]{2,0,1:T(2,128)S(1)}, s32[2,1,8]{2,0,1:T(2,128)S(1)}, u32[]{:S(2)}, u32[]{:S(2)}) collective-permute-start(s32[2,1,8]{2,0,1:T(2,128)S(1)} %bitcast.157), channel_id=1, source_target_pairs={{0,8},{4,12},{8,0},{12,4},{16,24},{20,28},{24,16},{28,20},{1,9},{5... | collective-permute-start | bytes 200 | tf_op jit(solution)/shard_map/ppermute | solution.py:241
  15.2 0.6 add.157
  15.8 1.3 collective-permute-done.2
  17.2 1.6 %collective-permute-start.3 = (s32[4,1,8]{2,0,1:T(4,128)S(1)}, s32[4,1,8]{2,0,1:T(4,128)S(1)}, u32[]{:S(2)}, u32[]{:S(2)}) collective-permute-start(s32[4,1,8]{2,0,1:T(4,128)S(1)} %bitcast.151), channel_id=1, source_target_pairs={{0,4},{4,0},{8,12},{12,8},{16,20},{20,16},{24,28},{28,24},{1,5},{5... | collective-permute-start | bytes 392 | tf_op jit(solution)/shard_map/ppermute | solution.py:241
  18.8 0.6 add.161
  19.4 1.4 %collective-permute-done.3 = s32[4,1,8]{2,0,1:T(4,128)S(1)} collective-permute-done((s32[4,1,8]{2,0,1:T(4,128)S(1)}, s32[4,1,8]{2,0,1:T(4,128)S(1)}, u32[]{:S(2)}, u32[]{:S(2)}) %collective-permute-start.3) | collective-permute-done | bytes 160 | tf_op jit(solution)/shard_map/ppermute | solution.py:241
  21.0 1.1 gather_fusion.1
  22.1 1.6 %gather_fusion = s32[384,8]{1,0:T(8,128)} fusion(s32[8,8]{1,0:T(8,128)S(1)} %reduce_window_sum.78, s32[1024]{0:T(1024)S(1)} %pad_clamp_fusion), kind=kCustom, calls=%fused_computation.clone | custom fusion | bytes 26112 | tf_op jit(solution)/shard_map/jit(_take)/gather | solution.py:96
  23.8 1.2 fusion.33
  25.1 0.5 multiply_cosine_fusion.2
  25.8 0.5 multiply_reduce_fusion.1
  26.3 2.1 %maximum_convert_fusion = f32[1,2,96,5120]{3,2,1,0:T(8,128)} fusion(bf16[1,1,96,5120]{3,2,1,0:T(8,128)(2,1)S(1)} %get-tuple-element.21, bf16[1,1,96,5120]{3,2,1,0:T(8,128)(2,1)S(1)} %get-tuple-element.20), kind=kLoop, calls=%fused_computation.13 | loop fusion | flops 1966080 | bytes 5898240 | tf_op jit(solution)/shard_map/convert_element_type | solution.py:107
  28.5 2.6 %fusion.3 = bf16[192,5120]{1,0:T(8,128)(2,1)S(1)} fusion(f32[1,2,96,5120]{3,2,1,0:T(8,128)} %maximum_convert_fusion, f32[5120]{0:T(1024)} %param.16, f32[192]{0:T(256)S(1)} %rsqrt.23), kind=kLoop, calls=%fused_computation.7 | loop fusion | flops 2949120 | bytes 5919488 | tf_op jit(solution)/shard_map/convert_element_type | solution.py:112
  31.2 1.3 fusion.12
  32.5 1.5 %copy.42 = bf16[192,128]{0,1:T(8,128)(2,1)} copy(bf16[192,128]{1,0:T(8,128)(2,1)} %fusion.12) | data formatting | bytes 98304 | tf_op jit(solution)/shard_map/convert_element_type | solution.py:129
  34.0 2.0 %fusion.11 = f32[192,1,128]{2,0,1:T(8,128)S(1)} fusion(bf16[192,5120]{1,0:T(8,128)(2,1)S(1)} %fusion.3, bf16[5120,128]{1,0:T(8,128)(2,1)} %param.19, f32[128]{0:T(128)} %param.20), kind=kOutput, calls=%fused_computation.41 | convolution fusion | flops 251682816 | bytes 3375616 | tf_op jit(solution)/shard_map/dot_general | solution.py:120
  36.0 1.1 fusion.54
  37.1 1.5 %copy.40 = bf16[192,64]{0,1:T(8,128)(2,1)} copy(bf16[192,64]{1,0:T(8,128)(2,1)} %get-tuple-element.28) | data formatting | bytes 49152 | tf_op jit(solution)/shard_map/concatenate | solution.py:48
  38.6 1.5 %copy.41 = bf16[192,64]{0,1:T(8,128)(2,1)} copy(bf16[192,64]{1,0:T(8,128)(2,1)} %get-tuple-element.29) | data formatting | bytes 49152 | tf_op jit(solution)/shard_map/concatenate | solution.py:48
  40.1 5.3 %convolution_add_fusion.1 = f32[192,640]{1,0:T(8,128)} fusion(bf16[192,5120]{1,0:T(8,128)(2,1)S(1)} %fusion.3, bf16[5120,640]{1,0:T(8,128)(2,1)} %param.17, f32[640]{0:T(1024)} %param.18), kind=kOutput, calls=%fused_computation.34 | convolution fusion | flops 1258414080 | bytes 9013760 | tf_op jit(solution)/shard_map/dot_general | solution.py:114
  45.4 1.3 copy.37
  46.9 1.1 convolution_convert_fusion.2
  48.0 0.9 reduce-window.35
  48.9 0.2 slice_reduce_fusion.1
  49.3 0.9 reduce-window.39
  50.2 0.2 slice_reduce_fusion
  50.6 3.8 %all-to-all-start = ((bf16[8,24,896]{2,1,0:T(8,128)(2,1)}), bf16[8,24,896]{2,1,0:T(8,128)(2,1)S(1)}, u32[]{:S(2)}, u32[]{:S(2)}) async-start(bf16[8,24,896]{2,1,0:T(8,128)(2,1)} %bitcast.24), calls=%async_computation | async-start | bytes 688128 | tf_op jit(solution)/shard_map/all_to_all | solution.py:156
  54.4 1.3 select_bitcast_fusion.4
  55.8 0.5 multiply_reduce_fusion
  56.3 2.1 %maximum_convert_fusion.1 = f32[1,2,96,5120]{3,2,1,0:T(8,128)} fusion(bf16[1,1,96,5120]{3,2,1,0:T(8,128)(2,1)S(1)} %get-tuple-element.19, bf16[1,1,96,5120]{3,2,1,0:T(8,128)(2,1)S(1)} %get-tuple-element.18), kind=kLoop, calls=%fused_computation.14 | loop fusion | flops 1966080 | bytes 5898240 | tf_op jit(solution)/shard_map/convert_element_type | solution.py:107
  58.5 2.6 %fusion.1 = bf16[192,5120]{1,0:T(8,128)(2,1)S(1)} fusion(f32[1,2,96,5120]{3,2,1,0:T(8,128)} %maximum_convert_fusion.1, f32[192]{0:T(256)S(1)} %rsqrt.25, f32[5120]{0:T(1024)S(1)} %copy-done.4), kind=kLoop, calls=%fused_computation.4 | loop fusion | flops 2949120 | bytes 5919488 | tf_op jit(solution)/shard_map/convert_element_type | solution.py:112
  61.2 0.7 fusion.13
  61.8 0.6 copy-done.2
  62.5 0.7 fusion.10
  63.2 4.6 %convolution_add_fusion = f32[192,640]{1,0:T(8,128)S(1)} fusion(bf16[192,5120]{1,0:T(8,128)(2,1)S(1)} %fusion.1, bf16[5120,640]{1,0:T(8,128)(2,1)} %param.17, f32[640]{0:T(1024)S(1)} %copy-done.20), kind=kOutput, calls=%fused_computation.33 | convolution fusion | flops 1258414080 | bytes 9013760 | tf_op jit(solution)/shard_map/dot_general | solution.py:114
  67.7 0.5 fusion.56
  68.5 0.2 copy.43
  68.9 1.1 convolution_convert_fusion.1
  70.0 6.0 %all-to-all-start.1 = ((bf16[8,24,896]{2,1,0:T(8,128)(2,1)}), bf16[8,24,896]{2,1,0:T(8,128)(2,1)S(1)}, u32[]{:S(2)}, u32[]{:S(2)}) async-start(bf16[8,24,896]{2,1,0:T(8,128)(2,1)} %bitcast.38), calls=%async_computation.1 | async-start | bytes 688128 | tf_op jit(solution)/shard_map/all_to_all | solution.py:156
  76.0 0.4 select_reduce_fusion
  76.6 10.1 %all-to-all-done.1 = bf16[8,24,896]{2,1,0:T(8,128)(2,1)S(1)} async-done(((bf16[8,24,896]{2,1,0:T(8,128)(2,1)}), bf16[8,24,896]{2,1,0:T(8,128)(2,1)S(1)}, u32[]{:S(2)}, u32[]{:S(2)}) %all-to-all-start.1) | async-done | bytes 344096 | tf_op jit(solution)/shard_map/all_to_all | solution.py:156
  86.7 0.5 convolution_convert_fusion
  87.4 0.3 fusion.87
  88.0 0.4 convolution_convert_fusion.3
  88.3 5.2 %fusion.88 = f32[256,5120]{1,0:T(8,128)S(1)} fusion(bf16[256,640]{0,1:T(8,128)(2,1)S(1)} %bitcast.146, bf16[640,5120]{1,0:T(8,128)(2,1)} %param.23), kind=kOutput, calls=%fused_computation.218 | convolution fusion | flops 1677721600 | bytes 12124160 | tf_op jit(solution)/shard_map/dot_general | solution.py:209
  93.5 0.3 select_bitcast_fusion.2
  93.8 2.0 %copy-done.1 = f32[256,5120]{1,0:T(8,128)} copy-done((f32[256,5120]{1,0:T(8,128)}, f32[256,5120]{1,0:T(8,128)S(1)}, u32[]{:S(2)}) %copy-start.1) | copy-done | bytes 5242904
  95.8 1.7 %pad_maximum_fusion = f32[2,256,1280]{2,1,0:T(8,128)} fusion(f32[1,256,1280]{2,1,0:T(8,128)S(1)} %get-tuple-element.17, f32[1,256,1280]{2,1,0:T(8,128)S(1)} %get-tuple-element.16), kind=kLoop, calls=%fused_computation.12 | loop fusion | flops 655360 | bytes 5242880 | tf_op jit(solution)/shard_map/stack | solution.py:225
  97.6 5.2 %collective-permute-done.6 = f32[2,256,1280]{2,1,0:T(8,128)} collective-permute-done((f32[2,256,1280]{2,1,0:T(8,128)}, f32[2,256,1280]{2,1,0:T(8,128)}, u32[]{:S(2)}, u32[]{:S(2)}) %collective-permute-start.6) | collective-permute-done | bytes 2621472 | tf_op jit(solution)/shard_map/ppermute | solution.py:227
  102.8 3.8 %select_bitcast_fusion = (f32[1,256,1280]{2,1,0:T(8,128)S(1)}, f32[256,1280]{1,0:T(8,128)S(1)}, f32[256,1280]{1,0:T(8,128)S(1)}) fusion(pred[]{:T(512)S(6)} %eq.151, f32[2,256,1280]{2,1,0:T(8,128)} %collective-permute-done.6, f32[256,5120]{1,0:T(8,128)} %copy-done.1, pred[]{:T(512)S(6)} %eq.152), kind=kLoop, calls=%fused_computation.23 | loop fusion | flops 1638400 | bytes 11796482 | tf_op jit(solution)/shard_map/stack | solution.py:225
  106.6 0.6 collective-permute-start.7
  107.2 30.3 %collective-permute-done.7 = f32[1,256,1280]{2,1,0:T(8,128)S(1)} collective-permute-done((f32[1,256,1280]{2,1,0:T(8,128)S(1)}, f32[1,256,1280]{2,1,0:T(8,128)S(1)}, u32[]{:S(2)}, u32[]{:S(2)}) %collective-permute-start.7) | collective-permute-done | bytes 1310752 | tf_op jit(solution)/shard_map/ppermute | solution.py:227
  137.5 1.0 fusion.7
  (115 shorter events, 3.4 us)
Async XLA Ops:
  0.0 31.1 %copy-start = (bf16[5120,128]{1,0:T(8,128)(2,1)S(1)}, bf16[5120,128]{1,0:T(8,128)(2,1)}, u32[]{:S(2)}) copy-start(bf16[5120,128]{1,0:T(8,128)(2,1)} %param.21) | copy-start | bytes 3932164
  0.0 12.9 %collective-permute-start.1 = (s32[1,1,8]{2,1,0:T(1,128)}, s32[1,1,8]{2,1,0:T(1,128)S(1)}, u32[]{:S(2)}, u32[]{:S(2)}) collective-permute-start(s32[1,1,8]{2,1,0:T(1,128)} %bitcast.159), channel_id=1, source_target_pairs={{0,16},{4,20},{8,24},{12,28},{16,0},{20,4},{24,8},{28,12},{1,17},{... | collective-permute-start | bytes 104 | tf_op jit(solution)/shard_map/ppermute | solution.py:241
  4.0 43.9 %collective-permute-start.4 = (bf16[96,5120]{1,0:T(8,128)(2,1)}, bf16[96,5120]{1,0:T(8,128)(2,1)}, u32[]{:S(2)}, u32[]{:S(2)}) collective-permute-start(bf16[96,5120]{1,0:T(8,128)(2,1)} %param.13), channel_id=1, source_target_pairs={{0,2},{1,3},{2,0},{3,1},{4,6},{5,7},{6,4},{7,5},{8,10},{9,11},{10,... | collective-permute-start | bytes 2949128 | tf_op jit(solution)/shard_map/ppermute | solution.py:255
  5.5 20.1 %collective-permute-start = (bf16[1,96,5120]{2,1,0:T(8,128)(2,1)}, bf16[1,96,5120]{2,1,0:T(8,128)(2,1)S(1)}, u32[]{:S(2)}, u32[]{:S(2)}) collective-permute-start(bf16[1,96,5120]{2,1,0:T(8,128)(2,1)} %bitcast.145), channel_id=1, source_target_pairs={{0,1},{1,0},{2,3},{3,2},{4,5},{5,4},{6,7},{7,6},{8,9},{9,8},{10,11... | collective-permute-start | bytes 2949128 | tf_op jit(solution)/shard_map/ppermute | solution.py:270
  13.6 3.6 %collective-permute-start.2 = (s32[2,1,8]{2,0,1:T(2,128)S(1)}, s32[2,1,8]{2,0,1:T(2,128)S(1)}, u32[]{:S(2)}, u32[]{:S(2)}) collective-permute-start(s32[2,1,8]{2,0,1:T(2,128)S(1)} %bitcast.157), channel_id=1, source_target_pairs={{0,8},{4,12},{8,0},{12,4},{16,24},{20,28},{24,16},{28,20},{1,9},{5... | collective-permute-start | bytes 200 | tf_op jit(solution)/shard_map/ppermute | solution.py:241
  17.2 3.7 %collective-permute-start.3 = (s32[4,1,8]{2,0,1:T(4,128)S(1)}, s32[4,1,8]{2,0,1:T(4,128)S(1)}, u32[]{:S(2)}, u32[]{:S(2)}) collective-permute-start(s32[4,1,8]{2,0,1:T(4,128)S(1)} %bitcast.151), channel_id=1, source_target_pairs={{0,4},{4,0},{8,12},{12,8},{16,20},{20,16},{24,28},{28,24},{1,5},{5... | collective-permute-start | bytes 392 | tf_op jit(solution)/shard_map/ppermute | solution.py:241
  21.0 4.6 %copy-start.3 = (bf16[96,5120]{1,0:T(8,128)(2,1)S(1)}, bf16[96,5120]{1,0:T(8,128)(2,1)}, u32[]{:S(2)}) copy-start(bf16[96,5120]{1,0:T(8,128)(2,1)} %param.13) | copy-start | bytes 2949124
  22.1 2.9 %copy-start.13 = (f32[64]{0:T(128)S(1)}, f32[64]{0:T(128)}, u32[]{:S(2)}) copy-start(f32[64]{0:T(128)} %multiply_exponential_fusion) | copy-start | bytes 772
  25.1 0.6 copy-start.11
  28.5 2.7 %copy-start.15 = (f32[128]{0:T(128)S(1)}, f32[128]{0:T(128)}, u32[]{:S(2)}) copy-start(f32[128]{0:T(128)} %param.22) | copy-start | bytes 1540
  32.5 3.5 %copy-start.12 = (f32[192]{0:T(256)S(1)}, f32[192]{0:T(256)}, u32[]{:S(2)}) copy-start(f32[192]{0:T(256)} %copy-done.11) | copy-start | bytes 2308
  32.5 3.5 %copy-start.14 = (f32[64]{0:T(128)S(1)}, f32[64]{0:T(128)}, u32[]{:S(2)}) copy-start(f32[64]{0:T(128)} %multiply_exponential_fusion) | copy-start | bytes 772
  45.4 1.5 %copy-start.5 = (bf16[192,128]{0,1:T(8,128)(2,1)S(1)}, bf16[192,128]{0,1:T(8,128)(2,1)}, u32[]{:S(2)}) copy-start(bf16[192,128]{0,1:T(8,128)(2,1)} %copy.42) | copy-start | bytes 147460
  45.4 1.5 %copy-start.9 = (bf16[192,64]{0,1:T(8,128)(2,1)S(1)}, bf16[192,64]{0,1:T(8,128)(2,1)}, u32[]{:S(2)}) copy-start(bf16[192,64]{0,1:T(8,128)(2,1)} %copy.40) | copy-start | bytes 73732
  45.4 1.5 %copy-start.10 = (bf16[192,64]{0,1:T(8,128)(2,1)S(1)}, bf16[192,64]{0,1:T(8,128)(2,1)}, u32[]{:S(2)}) copy-start(bf16[192,64]{0,1:T(8,128)(2,1)} %copy.41) | copy-start | bytes 73732
  45.4 1.5 %copy-start.19 = (s32[192]{0:T(256)S(1)}, s32[192]{0:T(256)}, u32[]{:S(2)}) copy-start(s32[192]{0:T(256)} %add_select_fusion.7) | copy-start | bytes 2308
  46.7 3.8 %copy-start.21 = (s32[8,1]{0,1:T(1,128)S(1)}, s32[8,1]{0,1:T(1,128)}, u32[]{:S(2)}) copy-start(s32[8,1]{0,1:T(1,128)} %reduce-window.56) | copy-start | bytes 100
  48.0 6.4 %collective-permute-start.5 = (bf16[1,96,5120]{2,1,0:T(8,128)(2,1)}, bf16[1,96,5120]{2,1,0:T(8,128)(2,1)S(1)}, u32[]{:S(2)}, u32[]{:S(2)}) collective-permute-start(bf16[1,96,5120]{2,1,0:T(8,128)(2,1)} %bitcast.29), channel_id=1, source_target_pairs={{0,1},{1,0},{2,3},{3,2},{4,5},{5,4},{6,7},{7,6},{8,9},{9,8},{10,11... | collective-permute-start | bytes 2949128 | tf_op jit(solution)/shard_map/ppermute | solution.py:270
  50.6 19.4 %all-to-all-start = ((bf16[8,24,896]{2,1,0:T(8,128)(2,1)}), bf16[8,24,896]{2,1,0:T(8,128)(2,1)S(1)}, u32[]{:S(2)}, u32[]{:S(2)}) async-start(bf16[8,24,896]{2,1,0:T(8,128)(2,1)} %bitcast.24), calls=%async_computation | async-start | bytes 688128 | tf_op jit(solution)/shard_map/all_to_all | solution.py:156
  56.2 2.2 %copy-start.4 = (f32[5120]{0:T(1024)S(1)}, f32[5120]{0:T(1024)}, u32[]{:S(2)}) copy-start(f32[5120]{0:T(1024)} %param.16) | copy-start | bytes 61444
  58.5 2.6 %copy-start.16 = (f32[128]{0:T(128)S(1)}, f32[128]{0:T(128)}, u32[]{:S(2)}) copy-start(f32[128]{0:T(128)} %param.22) | copy-start | bytes 1540
  61.1 1.3 copy-start.2
  61.2 1.3 copy-start.17
  62.5 0.7 copy-start.20
  67.7 1.2 copy-start.18
  68.7 7.2 %copy-start.7 = (s32[3072]{0:T(1024)S(1)}, s32[3072]{0:T(1024)}, u32[]{:S(2)}) copy-start(s32[3072]{0:T(1024)} %add.157) | copy-start | bytes 36868
  68.7 7.2 %copy-start.8 = (s32[3072]{0:T(1024)S(1)}, s32[3072]{0:T(1024)}, u32[]{:S(2)}) copy-start(s32[3072]{0:T(1024)} %add.161) | copy-start | bytes 36868
  68.8 7.3 %copy-start.6 = (s32[3072]{0:T(1024)S(1)}, s32[3072]{0:T(1024)}, u32[]{:S(2)}) copy-start(s32[3072]{0:T(1024)} %get-tuple-element.11) | copy-start | bytes 36868
  70.0 16.7 %all-to-all-start.1 = ((bf16[8,24,896]{2,1,0:T(8,128)(2,1)}), bf16[8,24,896]{2,1,0:T(8,128)(2,1)S(1)}, u32[]{:S(2)}, u32[]{:S(2)}) async-start(bf16[8,24,896]{2,1,0:T(8,128)(2,1)} %bitcast.38), calls=%async_computation.1 | async-start | bytes 688128 | tf_op jit(solution)/shard_map/all_to_all | solution.py:156
  93.5 2.3 %copy-start.1 = (f32[256,5120]{1,0:T(8,128)}, f32[256,5120]{1,0:T(8,128)S(1)}, u32[]{:S(2)}) copy-start(f32[256,5120]{1,0:T(8,128)S(1)} %fusion.88) | copy-start | bytes 15728644
  97.6 5.3 %collective-permute-start.6 = (f32[2,256,1280]{2,1,0:T(8,128)}, f32[2,256,1280]{2,1,0:T(8,128)}, u32[]{:S(2)}, u32[]{:S(2)}) collective-permute-start(f32[2,256,1280]{2,1,0:T(8,128)} %pad_maximum_fusion), channel_id=1, source_target_pairs={{0,1},{1,0},{2,3},{3,2},{4,5},{5,4},{6,7},{7,6},{8,9},{9,8},{10,11... | collective-permute-start | bytes 7864328 | tf_op jit(solution)/shard_map/ppermute | solution.py:227
  106.6 30.9 %collective-permute-start.7 = (f32[1,256,1280]{2,1,0:T(8,128)S(1)}, f32[1,256,1280]{2,1,0:T(8,128)S(1)}, u32[]{:S(2)}, u32[]{:S(2)}) collective-permute-start(f32[1,256,1280]{2,1,0:T(8,128)S(1)} %get-tuple-element.8), channel_id=1, source_target_pairs={{0,2},{1,3},{2,0},{3,1},{4,6},{5,7},{6,4},{7,5},{8,10},{9,11},{10,... | collective-permute-start | bytes 3932168 | tf_op jit(solution)/shard_map/ppermute | solution.py:227

commit v6 on v4

--- a/solution.py
+++ b/solution.py
@@ -173,27 +173,38 @@
     segment = jnp.sum((own_ends[None, :] <= slot_ids[:, None]).astype(jnp.int32), axis=1)
 
     score_scale = 1.0 / math.sqrt(head_dim)
-    scores = (
-        jnp.einsum(
-            "qkgd,tkd->kgqt",
-            query_matrix,
-            projected_key_rows,
+    chunk_count = 2 if pack_len % 16 == 0 else 1
+    chunk_len = pack_len // chunk_count
+    results = []
+    for chunk in range(chunk_count):
+        lo, hi = chunk * chunk_len, (chunk + 1) * chunk_len
+        scores = (
+            jnp.einsum(
+                "qkgd,tkd->kgqt",
+                query_matrix[lo:hi],
+                projected_key_rows[:hi],
+                preferred_element_type=jnp.float32,
+            )
+            * score_scale
+        )
+        allowed = (segment[lo:hi, None] == segment[None, :hi]) & (
+            slot_ids[None, :hi] <= slot_ids[lo:hi, None]
+        )
+        scores = jnp.where(allowed[None, None], scores, -1e30)
+        row_max = jnp.max(scores, axis=-1, keepdims=True)
+        weights = jnp.exp(scores - row_max)
+        row_total = jnp.sum(weights, axis=-1, keepdims=True)
+        probability = (weights / row_total).astype(jnp.bfloat16)
+        mixed_heads = jnp.einsum(
+            "kgqt,tkd->qkgd",
+            probability,
+            projected_value_rows[:hi],
             preferred_element_type=jnp.float32,
         )
-        * score_scale
-    )
-    allowed = (segment[:, None] == segment[None, :]) & (slot_ids[None, :] <= slot_ids[:, None])
-    scores = jnp.where(allowed[None, None], scores, -1e30)
-    row_max = jnp.max(scores, axis=-1, keepdims=True)
-    weights = jnp.exp(scores - row_max)
-    row_total = jnp.sum(weights, axis=-1, keepdims=True)
-    probability = (weights / row_total).astype(jnp.bfloat16)
-    mixed_heads = jnp.einsum(
-        "kgqt,tkd->qkgd", probability, projected_value_rows, preferred_element_type=jnp.float32
-    )
-    mixed_heads = mixed_heads.astype(jnp.bfloat16).reshape(pack_len, local_heads * head_dim)
-    partial_out = jnp.dot(mixed_heads, w_out, preferred_element_type=jnp.float32)
-    return halving_scatter(partial_out, "head", head_count).astype(jnp.bfloat16)
+        mixed_heads = mixed_heads.astype(jnp.bfloat16).reshape(chunk_len, local_heads * head_dim)
+        partial_out = jnp.dot(mixed_heads, w_out, preferred_element_type=jnp.float32)
+        results.append(halving_scatter(partial_out, "head", head_count).astype(jnp.bfloat16))
+    return jnp.concatenate(results, axis=0)
 
 
 def halving_scatter(partial, axis_name, count):

time: 135 us -> 133 us (0.985)
  waiting for transfers between devices: 60 us -> 50.9 us
  matrix products: 18.1 us -> 21.4 us
    ppermute x2 -> x4, waiting for transfers between devices: 34.6 us -> 26.9 us  [halving_scatter(): got = lax.ppermute(send, axis_name, pairs)]
    dot_general x1 -> x2, matrix products: 5.19 us -> 8.19 us  [local(): jnp.dot(mixed_heads, w_out, preferred_element_type=jnp.float32)]
    ppermute x1, waiting for transfers between devices: 4.84 us -> 2.28 us  [split_gather(): lax.ppermute(part, axis_name, [(i, (i + half) % count) for i in range(cou...]
    ppermute x2 -> x4, starting transfers between devices: 1.57 us -> 2.73 us  [halving_scatter(): got = lax.ppermute(send, axis_name, pairs)]
    unnamed x42 -> x50, local copies, waits for them, and re-layouts: 3.33 us -> 4.05 us
    another operation x3 -> x6, other arithmetic: 5.79 us -> 5.65 us  [halving_scatter(): jnp.stack([jnp.where(bit == 0, hi, lo) for (_, lo), hi in zip(lows, highs)])]
  transfers between devices with their start and end apart: 9 -> 11, of which waited for: 6 -> 6; matrix products, arithmetic and copies ran while one was open for 10% -> 18% of each run, Pallas kernels for 0% -> 0%
where the time goes in v6:
time: 133 us
  waiting for transfers between devices  50.9 us (38%)
  other arithmetic  28 us (21%)
  matrix products  21.4 us (16%)
  starting transfers between devices  17.5 us (13%)
  local copies, waits for them, and re-layouts  14.2 us (11%)
    ppermute x4, waiting for transfers between devices, halving_scatter(): got = lax.ppermute(send, axis_name, pairs)  26.9 us
    all_to_all x1, waiting for transfers between devices, local(): lax.all_to_all(outgoing, 'ctx', split_axis=0, concat_axis=0, tiled=True)  17.6 us
    dot_general x2, matrix products, local(): jnp.dot(mixed_heads, w_out, preferred_element_type=jnp.float32)  8.19 us
    dot_general x2, matrix products, project(): jnp.dot(normalized_input, w_query, preferred_element_type=jnp.float32)  7.49 us
    all_to_all x1, starting transfers between devices, local(): lax.all_to_all(outgoing, 'ctx', split_axis=0, concat_axis=0, tiled=True)  6.08 us
    ppermute x3, starting transfers between devices, doubling_gather(): got = lax.ppermute(have, axis_name, pairs)  5.75 us
    another operation x6, other arithmetic, halving_scatter(): jnp.stack([jnp.where(bit == 0, hi, lo) for (_, lo), hi in zip(lows, highs)])  5.65 us
    convert_element_type x1, other arithmetic, project(): normalized_input = (values_wide * lax.rsqrt(jnp.mean(values_wide * values...  4.52 us
  transfers between devices with their start and end apart: 11, of which 6 were waited for; matrix products, arithmetic and copies ran while one was open for 18% of the time, Pallas kernels for 0%

profile of v6, /device:TPU:0, one launch (start us, length us, event | category | flops | bytes accessed | tf_op | source)
XLA Modules:
  0.0 132.6 jit_solution(10167561408806445344)
XLA Ops:
  0.0 2.9 %collective-permute-start.4 = (bf16[96,5120]{1,0:T(8,128)(2,1)}, bf16[96,5120]{1,0:T(8,128)(2,1)}, u32[]{:S(2)}, u32[]{:S(2)}) collective-permute-start(bf16[96,5120]{1,0:T(8,128)(2,1)} %param.13), channel_id=1, source_target_pairs={{0,2},{1,3},{2,0},{3,1},{4,6},{5,7},{6,4},{7,5},{8,10},{9,11},{10,... | collective-permute-start | bytes 2949128 | tf_op jit(solution)/shard_map/ppermute | solution.py:253
  2.9 2.6 %collective-permute-start.1 = (s32[1,1,8]{2,1,0:T(1,128)}, s32[1,1,8]{2,1,0:T(1,128)S(1)}, u32[]{:S(2)}, u32[]{:S(2)}) collective-permute-start(s32[1,1,8]{2,1,0:T(1,128)} %bitcast.226), channel_id=1, source_target_pairs={{0,16},{4,20},{8,24},{12,28},{16,0},{20,4},{24,8},{28,12},{1,17},{... | collective-permute-start | bytes 104 | tf_op jit(solution)/shard_map/ppermute | solution.py:238
  5.5 0.7 reshape.672
  6.3 0.9 reduce-window.30
  7.8 0.2 fusion.38
  8.2 0.7 subtract_select_fusion
  9.0 0.9 reduce-window.21
  10.1 0.7 broadcast_add_fusion
  10.8 0.7 fusion.77
  11.5 0.7 fusion.80
  12.2 1.6 %collective-permute-start.2 = (s32[2,1,8]{2,0,1:T(2,128)S(1)}, s32[2,1,8]{2,0,1:T(2,128)S(1)}, u32[]{:S(2)}, u32[]{:S(2)}) collective-permute-start(s32[2,1,8]{2,0,1:T(2,128)S(1)} %bitcast.224), channel_id=1, source_target_pairs={{0,8},{4,12},{8,0},{12,4},{16,24},{20,28},{24,16},{28,20},{1,9},{5... | collective-permute-start | bytes 200 | tf_op jit(solution)/shard_map/ppermute | solution.py:238
  13.7 2.0 %collective-permute-done.2 = s32[2,1,8]{2,0,1:T(2,128)S(1)} collective-permute-done((s32[2,1,8]{2,0,1:T(2,128)S(1)}, s32[2,1,8]{2,0,1:T(2,128)S(1)}, u32[]{:S(2)}, u32[]{:S(2)}) %collective-permute-start.2) | collective-permute-done | bytes 96 | tf_op jit(solution)/shard_map/ppermute | solution.py:238
  15.8 1.6 %collective-permute-start.3 = (s32[4,1,8]{2,0,1:T(4,128)S(1)}, s32[4,1,8]{2,0,1:T(4,128)S(1)}, u32[]{:S(2)}, u32[]{:S(2)}) collective-permute-start(s32[4,1,8]{2,0,1:T(4,128)S(1)} %bitcast.218), channel_id=1, source_target_pairs={{0,4},{4,0},{8,12},{12,8},{16,20},{20,16},{24,28},{28,24},{1,5},{5... | collective-permute-start | bytes 392 | tf_op jit(solution)/shard_map/ppermute | solution.py:238
  17.3 2.1 %collective-permute-done.3 = s32[4,1,8]{2,0,1:T(4,128)S(1)} collective-permute-done((s32[4,1,8]{2,0,1:T(4,128)S(1)}, s32[4,1,8]{2,0,1:T(4,128)S(1)}, u32[]{:S(2)}, u32[]{:S(2)}) %collective-permute-start.3) | collective-permute-done | bytes 160 | tf_op jit(solution)/shard_map/ppermute | solution.py:238
  19.6 1.1 gather_fusion.1
  20.7 1.1 gather_fusion
  21.8 0.3 fusion.39
  22.2 0.5 multiply_cosine_fusion.3
  22.7 2.3 %collective-permute-done.4 = bf16[96,5120]{1,0:T(8,128)(2,1)} collective-permute-done((bf16[96,5120]{1,0:T(8,128)(2,1)}, bf16[96,5120]{1,0:T(8,128)(2,1)}, u32[]{:S(2)}, u32[]{:S(2)}) %collective-permute-start.4) | collective-permute-done | bytes 983072 | tf_op jit(solution)/shard_map/ppermute | solution.py:253
  25.0 1.6 %select_bitcast_fusion.3 = (bf16[1,1,96,5120]{3,2,1,0:T(8,128)(2,1)S(1)}, bf16[1,1,96,5120]{3,2,1,0:T(8,128)(2,1)S(1)}) fusion(bf16[1,96,5120]{2,1,0:T(8,128)(2,1)} %collective-permute-done, pred[]{:T(512)S(6)} %eq.137, bf16[96,5120]{1,0:T(8,128)(2,1)} %param.13), kind=kLoop, calls=%fused_computation.39 | loop fusion | flops 983040 | bytes 3932161 | tf_op jit(solution)/shard_map/stack | solution.py:272
  26.7 0.5 multiply_reduce_fusion.1
  27.1 0.6 add_rsqrt_fusion.1
  27.7 1.3 %rsqrt.23 = f32[192]{0:T(256)} reshape(f32[2,96]{1,0:T(2,128)} %add_rsqrt_fusion.1) | data formatting | bytes 1536 | tf_op jit(solution)/shard_map/rsqrt | solution.py:110
  29.1 1.6 %select_bitcast_fusion.1 = (bf16[1,1,96,5120]{3,2,1,0:T(8,128)(2,1)S(1)}, bf16[1,1,96,5120]{3,2,1,0:T(8,128)(2,1)S(1)}) fusion(bf16[1,96,5120]{2,1,0:T(8,128)(2,1)} %collective-permute-done.5, pred[]{:T(512)S(6)} %eq.137, bf16[96,5120]{1,0:T(8,128)(2,1)} %collective-permute-done.4), kind=kLoop, calls=%fused_computation.37 | loop fusion | flops 983040 | bytes 3932161 | tf_op jit(solution)/shard_map/stack | solution.py:272
  30.7 3.6 %maximum_convert_fusion = (f32[1,2,96,5120]{3,2,1,0:T(8,128)}, f32[1,2,96,5120]{3,2,1,0:T(8,128)}) fusion(bf16[1,1,96,5120]{3,2,1,0:T(8,128)(2,1)S(1)} %get-tuple-element.21, bf16[1,1,96,5120]{3,2,1,0:T(8,128)(2,1)S(1)} %get-tuple-element.20, bf16[1,1,96,5120]{3,2,1,0:T(8,128)(2,1)S(1)} %get-tuple-element.23, bf16[1,1,96,5120]{3,2,1,0:T(8,128)(2,1)S(1)} %get-tuple-element.22), kind=kLoop, calls=%fused_computation.12 | loop fusion | flops 3932160 | bytes 11796480 | tf_op jit(solution)/shard_map/convert_element_type | solution.py:107
  34.3 0.5 multiply_reduce_fusion
  35.1 4.5 %fusion.3 = (bf16[192,5120]{1,0:T(8,128)(2,1)S(1)}, bf16[192,5120]{1,0:T(8,128)(2,1)S(1)}) fusion(f32[1,2,96,5120]{3,2,1,0:T(8,128)} %get-tuple-element.64, f32[5120]{0:T(1024)S(1)} %copy-done.10, f32[192]{0:T(256)S(1)} %copy-done.15, f32[192]{0:T(256)S(1)} %rsqrt.25, f32[1,2,96,5120]{3,2,1,0:T(8,128)} %get-tuple-element.65), kind=kLoop, calls=%fused_computation.7 | loop fusion | flops 5898240 | bytes 11818496 | tf_op jit(solution)/shard_map/convert_element_type | solution.py:112
  39.6 0.7 fusion.9
  40.3 0.7 fusion.8
  41.0 0.6 copy-done.4
  41.6 0.7 fusion.11
  42.3 0.7 fusion.10
  43.1 5.7 %convolution_add_fusion = f32[192,640]{1,0:T(8,128)} fusion(bf16[192,5120]{1,0:T(8,128)(2,1)S(1)} %get-tuple-element.35, bf16[5120,640]{1,0:T(8,128)(2,1)} %param.17, f32[640]{0:T(1024)S(1)} %copy-done.22), kind=kOutput, calls=%fused_computation.20 | convolution fusion | flops 1258414080 | bytes 9013760 | tf_op jit(solution)/shard_map/dot_general | solution.py:114
  48.8 1.7 %convolution_add_fusion.1 = f32[192,640]{1,0:T(8,128)S(1)} fusion(bf16[192,5120]{1,0:T(8,128)(2,1)S(1)} %get-tuple-element.34, bf16[5120,640]{1,0:T(8,128)(2,1)S(1)} %bitcast.229, f32[640]{0:T(1024)S(1)} %copy-done.22), kind=kOutput, calls=%fused_computation.21 | convolution fusion | flops 1258414080 | bytes 9013760 | tf_op jit(solution)/shard_map/dot_general | solution.py:114
  50.6 0.7 copy.51
  51.3 0.8 fusion.60
  52.2 0.7 copy.50
  52.9 0.7 copy.49
  53.6 1.3 copy.48
  54.8 0.7 copy.47
  55.8 0.2 copy.42
  56.4 0.5 copy-done.5
  56.9 1.5 %convolution_convert_fusion = bf16[384,896]{1,0:T(8,128)(2,1)} fusion(bf16[192,128]{0,1:T(8,128)(2,1)S(1)} %copy-done.5, bf16[192,64]{0,1:T(8,128)(2,1)S(1)} %copy-done.8, bf16[192,64]{0,1:T(8,128)(2,1)S(1)} %copy-done.9, bf16[192,640]{0,1:T(8,128)(2,1)S(1)} %bitcast.212, bf16[192,128]{0,1:T(8,128)(2,1)S(1)} %copy-done.6, bf16[192,64]{0,1:T(8,128)(2,1)S(1)} %copy.46, ...), kind=kOutput, calls=%fused_computation.14 | convolution fusion | flops 270237696 | bytes 1377792 | tf_op jit(solution)/shard_map/dot_general | solution.py:148
  58.4 6.1 %all-to-all-start = ((bf16[8,48,896]{2,1,0:T(8,128)(2,1)}), bf16[8,48,896]{2,1,0:T(8,128)(2,1)S(1)}, u32[]{:S(2)}, u32[]{:S(2)}) async-start(bf16[8,48,896]{2,1,0:T(8,128)(2,1)} %bitcast.34), calls=%async_computation | async-start | bytes 1376256 | tf_op jit(solution)/shard_map/all_to_all | solution.py:149
  64.9 0.4 select_reduce_fusion
  65.6 17.6 %all-to-all-done = bf16[8,48,896]{2,1,0:T(8,128)(2,1)S(1)} async-done(((bf16[8,48,896]{2,1,0:T(8,128)(2,1)}), bf16[8,48,896]{2,1,0:T(8,128)(2,1)S(1)}, u32[]{:S(2)}, u32[]{:S(2)}) %all-to-all-start) | async-done | bytes 688160 | tf_op jit(solution)/shard_map/all_to_all | solution.py:149
  83.2 0.5 convolution_convert_fusion.1
  83.9 0.3 fusion.91
  84.2 0.3 convolution_convert_fusion.2
  84.5 4.1 %fusion.94 = f32[128,5120]{1,0:T(8,128)S(1)} fusion(bf16[128,640]{0,1:T(8,128)(2,1)S(1)} %bitcast.211, bf16[640,5120]{1,0:T(8,128)(2,1)} %param.23), kind=kOutput, calls=%fused_computation.226 | convolution fusion | flops 838860800 | bytes 9338880 | tf_op jit(solution)/shard_map/dot_general | solution.py:205
  88.8 1.3 %copy-done.1 = f32[128,5120]{1,0:T(8,128)} copy-done((f32[128,5120]{1,0:T(8,128)}, f32[128,5120]{1,0:T(8,128)S(1)}, u32[]{:S(2)}) %copy-start.1) | copy-done | bytes 2621464
  90.1 1.2 pad_maximum_fusion.1
  91.5 0.2 fusion.92
  91.8 0.2 convolution_convert_fusion.3
  92.0 4.1 %fusion.93 = f32[128,5120]{1,0:T(8,128)S(1)} fusion(bf16[128,640]{0,1:T(8,128)(2,1)S(1)} %bitcast.210, bf16[640,5120]{1,0:T(8,128)(2,1)} %param.23), kind=kOutput, calls=%fused_computation.225 | convolution fusion | flops 838860800 | bytes 9338880 | tf_op jit(solution)/shard_map/dot_general | solution.py:205
  96.3 1.4 %copy-done.2 = f32[128,5120]{1,0:T(8,128)} copy-done((f32[128,5120]{1,0:T(8,128)}, f32[128,5120]{1,0:T(8,128)S(1)}, u32[]{:S(2)}) %copy-start.2) | copy-done | bytes 2621464
  97.7 0.6 collective-permute-start.6
  98.3 2.5 %select_bitcast_fusion.4 = (f32[1,128,1280]{2,1,0:T(8,128)S(1)}, f32[128,1280]{1,0:T(8,128)S(1)}, f32[128,1280]{1,0:T(8,128)S(1)}) fusion(pred[]{:T(512)S(6)} %eq.136, f32[2,128,1280]{2,1,0:T(8,128)} %collective-permute-done.8, f32[128,5120]{1,0:T(8,128)} %copy-done.1, pred[]{:T(512)S(6)} %eq.137), kind=kLoop, calls=%fused_computation.68 | loop fusion | flops 819200 | bytes 5898242 | tf_op jit(solution)/shard_map/stack | solution.py:222
  100.8 1.6 %collective-permute-start.9 = (f32[1,128,1280]{2,1,0:T(8,128)S(1)}, f32[1,128,1280]{2,1,0:T(8,128)S(1)}, u32[]{:S(2)}, u32[]{:S(2)}) collective-permute-start(f32[1,128,1280]{2,1,0:T(8,128)S(1)} %get-tuple-element.9), channel_id=1, source_target_pairs={{0,2},{1,3},{2,0},{3,1},{4,6},{5,7},{6,4},{7,5},{8,10},{9,11},{10,... | collective-permute-start | bytes 1966088 | tf_op jit(solution)/shard_map/ppermute | solution.py:224
  102.3 1.6 %select_bitcast_fusion.7 = (f32[1,128,1280]{2,1,0:T(8,128)S(1)}, f32[128,1280]{1,0:T(8,128)S(1)}, f32[128,1280]{1,0:T(8,128)S(1)}) fusion(pred[]{:T(512)S(6)} %eq.136, f32[2,128,1280]{2,1,0:T(8,128)} %collective-permute-done.6, f32[128,5120]{1,0:T(8,128)S(1)} %copy-done.3, pred[]{:T(512)S(6)} %eq.137), kind=kLoop, calls=%fused_computation.73 | loop fusion | flops 819200 | bytes 5898242 | tf_op jit(solution)/shard_map/stack | solution.py:222
  103.9 0.6 collective-permute-start.7
  104.5 13.9 %collective-permute-done.9 = f32[1,128,1280]{2,1,0:T(8,128)S(1)} collective-permute-done((f32[1,128,1280]{2,1,0:T(8,128)S(1)}, f32[1,128,1280]{2,1,0:T(8,128)S(1)}, u32[]{:S(2)}, u32[]{:S(2)}) %collective-permute-start.9) | collective-permute-done | bytes 655392 | tf_op jit(solution)/shard_map/ppermute | solution.py:224
  118.5 13.0 %collective-permute-done.7 = f32[1,128,1280]{2,1,0:T(8,128)S(1)} collective-permute-done((f32[1,128,1280]{2,1,0:T(8,128)S(1)}, f32[1,128,1280]{2,1,0:T(8,128)S(1)}, u32[]{:S(2)}, u32[]{:S(2)}) %collective-permute-start.7) | collective-permute-done | bytes 655392 | tf_op jit(solution)/shard_map/ppermute | solution.py:224
  131.7 0.9 pad_maximum_fusion.2
  (117 shorter events, 3.9 us)
Async XLA Ops:
  0.0 39.6 %copy-start = (bf16[5120,128]{1,0:T(8,128)(2,1)S(1)}, bf16[5120,128]{1,0:T(8,128)(2,1)}, u32[]{:S(2)}) copy-start(bf16[5120,128]{1,0:T(8,128)(2,1)} %param.19) | copy-start | bytes 3932164
  0.0 25.0 %collective-permute-start.4 = (bf16[96,5120]{1,0:T(8,128)(2,1)}, bf16[96,5120]{1,0:T(8,128)(2,1)}, u32[]{:S(2)}, u32[]{:S(2)}) collective-permute-start(bf16[96,5120]{1,0:T(8,128)(2,1)} %param.13), channel_id=1, source_target_pairs={{0,2},{1,3},{2,0},{3,1},{4,6},{5,7},{6,4},{7,5},{8,10},{9,11},{10,... | collective-permute-start | bytes 2949128 | tf_op jit(solution)/shard_map/ppermute | solution.py:253
  2.9 22.1 %collective-permute-start = (bf16[1,96,5120]{2,1,0:T(8,128)(2,1)}, bf16[1,96,5120]{2,1,0:T(8,128)(2,1)}, u32[]{:S(2)}, u32[]{:S(2)}) collective-permute-start(bf16[1,96,5120]{2,1,0:T(8,128)(2,1)} %bitcast.207), channel_id=1, source_target_pairs={{0,1},{1,0},{2,3},{3,2},{4,5},{5,4},{6,7},{7,6},{8,9},{9,8},{10,11... | collective-permute-start | bytes 2949128 | tf_op jit(solution)/shard_map/ppermute | solution.py:269
  2.9 8.5 %collective-permute-start.1 = (s32[1,1,8]{2,1,0:T(1,128)}, s32[1,1,8]{2,1,0:T(1,128)S(1)}, u32[]{:S(2)}, u32[]{:S(2)}) collective-permute-start(s32[1,1,8]{2,1,0:T(1,128)} %bitcast.226), channel_id=1, source_target_pairs={{0,16},{4,20},{8,24},{12,28},{16,0},{20,4},{24,8},{28,12},{1,17},{... | collective-permute-start | bytes 104 | tf_op jit(solution)/shard_map/ppermute | solution.py:238
  5.5 16.6 %copy-start.17 = (f32[64]{0:T(128)}, f32[64]{0:T(128)S(1)}, u32[]{:S(2)}) copy-start(f32[64]{0:T(128)S(1)} %multiply_exponential_fusion) | copy-start | bytes 772
  12.2 3.6 %collective-permute-start.2 = (s32[2,1,8]{2,0,1:T(2,128)S(1)}, s32[2,1,8]{2,0,1:T(2,128)S(1)}, u32[]{:S(2)}, u32[]{:S(2)}) collective-permute-start(s32[2,1,8]{2,0,1:T(2,128)S(1)} %bitcast.224), channel_id=1, source_target_pairs={{0,8},{4,12},{8,0},{12,4},{16,24},{20,28},{24,16},{28,20},{1,9},{5... | collective-permute-start | bytes 200 | tf_op jit(solution)/shard_map/ppermute | solution.py:238
  15.8 3.7 %collective-permute-start.3 = (s32[4,1,8]{2,0,1:T(4,128)S(1)}, s32[4,1,8]{2,0,1:T(4,128)S(1)}, u32[]{:S(2)}, u32[]{:S(2)}) collective-permute-start(s32[4,1,8]{2,0,1:T(4,128)S(1)} %bitcast.218), channel_id=1, source_target_pairs={{0,4},{4,0},{8,12},{12,8},{16,20},{20,16},{24,28},{28,24},{1,5},{5... | collective-permute-start | bytes 392 | tf_op jit(solution)/shard_map/ppermute | solution.py:238
  22.2 2.8 %copy-start.11 = (f32[192]{0:T(256)}, f32[192]{0:T(256)S(1)}, u32[]{:S(2)}) copy-start(f32[192]{0:T(256)S(1)} %get-tuple-element.44) | copy-start | bytes 2308
  22.2 2.8 %copy-start.13 = (f32[192]{0:T(256)}, f32[192]{0:T(256)S(1)}, u32[]{:S(2)}) copy-start(f32[192]{0:T(256)S(1)} %get-tuple-element.45) | copy-start | bytes 2308
  25.0 4.1 %collective-permute-start.5 = (bf16[1,96,5120]{2,1,0:T(8,128)(2,1)}, bf16[1,96,5120]{2,1,0:T(8,128)(2,1)}, u32[]{:S(2)}, u32[]{:S(2)}) collective-permute-start(bf16[1,96,5120]{2,1,0:T(8,128)(2,1)} %bitcast.25), channel_id=1, source_target_pairs={{0,1},{1,0},{2,3},{3,2},{4,5},{5,4},{6,7},{7,6},{8,9},{9,8},{10,11... | collective-permute-start | bytes 2949128 | tf_op jit(solution)/shard_map/ppermute | solution.py:269
  34.3 0.7 copy-start.10
  34.3 0.7 copy-start.15
  35.1 4.5 %copy-start.19 = (f32[128]{0:T(128)S(1)}, f32[128]{0:T(128)}, u32[]{:S(2)}) copy-start(f32[128]{0:T(128)} %param.20) | copy-start | bytes 1540
  40.3 1.3 copy-start.4
  40.3 1.3 copy-start.20
  41.6 1.4 %copy-start.22 = (f32[640]{0:T(1024)S(1)}, f32[640]{0:T(1024)}, u32[]{:S(2)}) copy-start(f32[640]{0:T(1024)} %param.18) | copy-start | bytes 7684
  42.3 6.5 %slice-start = ((s8[6553600]{0:T(1024)(128)(4,1)}), s8[4194304]{0:T(1024)(128)(4,1)S(1)}, s32[]{:S(2)}) async-start(s8[6553600]{0:T(1024)(128)(4,1)} %bitcast.228), calls=%async_computation.1 | async-start | bytes 8388608
  43.0 5.8 %slice-start.1 = ((s8[6553600]{0:T(1024)(128)(4,1)}), s8[2359296]{0:T(1024)(128)(4,1)S(1)}, s32[]{:S(2)}) async-start(s8[6553600]{0:T(1024)(128)(4,1)} %bitcast.228), calls=%async_computation.2 | async-start | bytes 4718592
  48.8 2.5 %copy-start.12 = (f32[192]{0:T(256)S(1)}, f32[192]{0:T(256)}, u32[]{:S(2)}) copy-start(f32[192]{0:T(256)} %copy-done.11) | copy-start | bytes 2308
  48.8 2.5 %copy-start.14 = (f32[192]{0:T(256)S(1)}, f32[192]{0:T(256)}, u32[]{:S(2)}) copy-start(f32[192]{0:T(256)} %copy-done.13) | copy-start | bytes 2308
  48.8 2.5 %copy-start.18 = (f32[64]{0:T(128)S(1)}, f32[64]{0:T(128)}, u32[]{:S(2)}) copy-start(f32[64]{0:T(128)} %copy-done.17) | copy-start | bytes 772
  56.0 0.8 copy-start.5
  56.0 0.9 copy-start.6
  56.0 0.9 copy-start.8
  56.0 0.8 copy-start.9
  56.0 0.8 copy-start.16
  56.9 7.7 %copy-start.7 = (s32[8,3,128]{2,0,1:T(8,128)S(1)}, s32[8,3,128]{2,0,1:T(8,128)}, u32[]{:S(2)}) copy-start(s32[8,3,128]{2,0,1:T(8,128)} %broadcast_add_fusion) | copy-start | bytes 36868
  56.9 7.7 %copy-start.21 = (s32[1,8]{1,0:T(1,128)S(1)}, s32[1,8]{1,0:T(1,128)}, u32[]{:S(2)}) copy-start(s32[1,8]{1,0:T(1,128)} %param.15) | copy-start | bytes 100
  58.4 24.8 %all-to-all-start = ((bf16[8,48,896]{2,1,0:T(8,128)(2,1)}), bf16[8,48,896]{2,1,0:T(8,128)(2,1)S(1)}, u32[]{:S(2)}, u32[]{:S(2)}) async-start(bf16[8,48,896]{2,1,0:T(8,128)(2,1)} %bitcast.34), calls=%async_computation | async-start | bytes 1376256 | tf_op jit(solution)/shard_map/all_to_all | solution.py:149
  88.6 1.5 %copy-start.1 = (f32[128,5120]{1,0:T(8,128)}, f32[128,5120]{1,0:T(8,128)S(1)}, u32[]{:S(2)}) copy-start(f32[128,5120]{1,0:T(8,128)S(1)} %fusion.94) | copy-start | bytes 7864324
  91.4 7.0 %collective-permute-start.8 = (f32[2,128,1280]{2,1,0:T(8,128)}, f32[2,128,1280]{2,1,0:T(8,128)}, u32[]{:S(2)}, u32[]{:S(2)}) collective-permute-start(f32[2,128,1280]{2,1,0:T(8,128)} %pad_maximum_fusion.1), channel_id=1, source_target_pairs={{0,1},{1,0},{2,3},{3,2},{4,5},{5,4},{6,7},{7,6},{8,9},{9,8},{10,11... | collective-permute-start | bytes 3932168 | tf_op jit(solution)/shard_map/ppermute | solution.py:224
  96.1 1.5 %copy-start.2 = (f32[128,5120]{1,0:T(8,128)}, f32[128,5120]{1,0:T(8,128)S(1)}, u32[]{:S(2)}) copy-start(f32[128,5120]{1,0:T(8,128)S(1)} %fusion.93) | copy-start | bytes 7864324
  97.7 4.6 %collective-permute-start.6 = (f32[2,128,1280]{2,1,0:T(8,128)S(1)}, f32[2,128,1280]{2,1,0:T(8,128)}, u32[]{:S(2)}, u32[]{:S(2)}) collective-permute-start(f32[2,128,1280]{2,1,0:T(8,128)S(1)} %pad_maximum_fusion), channel_id=1, source_target_pairs={{0,1},{1,0},{2,3},{3,2},{4,5},{5,4},{6,7},{7,6},{8,9},{9,8},{10,11... | collective-permute-start | bytes 3932168 | tf_op jit(solution)/shard_map/ppermute | solution.py:224
  98.3 4.0 %copy-start.3 = (f32[128,5120]{1,0:T(8,128)S(1)}, f32[128,5120]{1,0:T(8,128)}, u32[]{:S(2)}) copy-start(f32[128,5120]{1,0:T(8,128)} %copy-done.2) | copy-start | bytes 7864324
  100.8 17.7 %collective-permute-start.9 = (f32[1,128,1280]{2,1,0:T(8,128)S(1)}, f32[1,128,1280]{2,1,0:T(8,128)S(1)}, u32[]{:S(2)}, u32[]{:S(2)}) collective-permute-start(f32[1,128,1280]{2,1,0:T(8,128)S(1)} %get-tuple-element.9), channel_id=1, source_target_pairs={{0,2},{1,3},{2,0},{3,1},{4,6},{5,7},{6,4},{7,5},{8,10},{9,11},{10,... | collective-permute-start | bytes 1966088 | tf_op jit(solution)/shard_map/ppermute | solution.py:224
  103.9 27.6 %collective-permute-start.7 = (f32[1,128,1280]{2,1,0:T(8,128)S(1)}, f32[1,128,1280]{2,1,0:T(8,128)S(1)}, u32[]{:S(2)}, u32[]{:S(2)}) collective-permute-start(f32[1,128,1280]{2,1,0:T(8,128)S(1)} %get-tuple-element.6), channel_id=1, source_target_pairs={{0,2},{1,3},{2,0},{3,1},{4,6},{5,7},{6,4},{7,5},{8,10},{9,11},{10,... | collective-permute-start | bytes 1966088 | tf_op jit(solution)/shard_map/ppermute | solution.py:224

commit v7 on v6

--- a/solution.py
+++ b/solution.py
@@ -146,7 +146,7 @@
         places[None, :] == jnp.arange(ctx_count * group_cap, dtype=jnp.int32)[:, None]
     ).astype(jnp.bfloat16)
     outgoing = jnp.dot(send_hot, qkv, preferred_element_type=jnp.float32).astype(jnp.bfloat16)
-    arrived = lax.all_to_all(outgoing, "ctx", split_axis=0, concat_axis=0, tiled=True)
+    arrived = exchange(outgoing, "ctx", ctx_count)
 
     mine = (pool_dest >= 0) & (pool_dest // pack_len == ctx_index)
     mine_grid = mine.reshape(ctx_count, group_rows).astype(jnp.int32)
@@ -207,6 +207,21 @@
     return jnp.concatenate(results, axis=0)
 
 
+def exchange(outgoing, axis_name, count):
+    if count > 8:
+        return lax.all_to_all(outgoing, axis_name, split_axis=0, concat_axis=0, tiled=True)
+    me = lax.axis_index(axis_name)
+    chunks = outgoing.reshape((count, -1) + outgoing.shape[1:])
+    by_shift = jnp.take(chunks, (me + jnp.arange(count)) % count, axis=0)
+    from_shift = [by_shift[0]]
+    for shift in range(1, count):
+        pairs = [(i, (i + shift) % count) for i in range(count)]
+        from_shift.append(lax.ppermute(by_shift[shift], axis_name, pairs))
+    from_shift = jnp.stack(from_shift)
+    arrived = jnp.take(from_shift, (me - jnp.arange(count)) % count, axis=0)
+    return arrived.reshape(outgoing.shape)
+
+
 def halving_scatter(partial, axis_name, count):
     bits = count.bit_length() - 1
     if count != 1 << bits or bits == 0:

time: 133 us -> 126 us (0.947)
  the two profiles are of different devices: /device:TPU:0 before, /device:TPU:12 now
where the time goes in v7:
time: 126 us; the launch traced here: 125 us
  waiting for transfers between devices  45.1 us (36%)
  other arithmetic  30.1 us (24%)
  matrix products  19.7 us (16%)
  starting transfers between devices  17 us (13%)
  local copies, waits for them, and re-layouts  12.4 us (10%)
    ppermute x4, waiting for transfers between devices, halving_scatter(): got = lax.ppermute(send, axis_name, pairs)  28.2 us
    ppermute x7, waiting for transfers between devices, exchange(): from_shift.append(lax.ppermute(by_shift[shift], axis_name, pairs))  10.7 us
    ppermute x7, starting transfers between devices, exchange(): from_shift.append(lax.ppermute(by_shift[shift], axis_name, pairs))  9.12 us
    dot_general x2, matrix products, local(): jnp.dot(mixed_heads, w_out, preferred_element_type=jnp.float32)  8.19 us
    dot_general x2, matrix products, project(): jnp.dot(normalized_input, w_query, preferred_element_type=jnp.float32)  6.71 us
    ppermute x3, waiting for transfers between devices, doubling_gather(): got = lax.ppermute(have, axis_name, pairs)  6.2 us
    convert_element_type x1, other arithmetic, project(): normalized_input = (values_wide * lax.rsqrt(jnp.mean(values_wide * values...  4.52 us
    another operation x6, other arithmetic, halving_scatter(): jnp.stack([jnp.where(bit == 0, hi, lo) for (_, lo), hi in zip(lows, highs)])  4.3 us
  transfers between devices with their start and end apart: 17, of which 8 were waited for; matrix products, arithmetic and copies ran while one was open for 22% of the time, Pallas kernels for 0%

profile of v7, /device:TPU:12, one launch (start us, length us, event | category | flops | bytes accessed | tf_op | source)
XLA Modules:
  0.0 125.1 jit_solution(15140914806865809641)
XLA Ops:
  0.0 1.5 %collective-permute-start.4 = (bf16[96,5120]{1,0:T(8,128)(2,1)}, bf16[96,5120]{1,0:T(8,128)(2,1)}, u32[]{:S(2)}, u32[]{:S(2)}) collective-permute-start(bf16[96,5120]{1,0:T(8,128)(2,1)} %param.15), channel_id=1, source_target_pairs={{0,2},{1,3},{2,0},{3,1},{4,6},{5,7},{6,4},{7,5},{8,10},{9,11},{10,... | collective-permute-start | bytes 2949128 | tf_op jit(solution)/shard_map/ppermute | solution.py:268
  1.5 2.6 %collective-permute-start.1 = (s32[1,1,8]{2,1,0:T(1,128)}, s32[1,1,8]{2,1,0:T(1,128)S(1)}, u32[]{:S(2)}, u32[]{:S(2)}) collective-permute-start(s32[1,1,8]{2,1,0:T(1,128)} %bitcast.255), channel_id=1, source_target_pairs={{0,16},{4,20},{8,24},{12,28},{16,0},{20,4},{24,8},{28,12},{1,17},{... | collective-permute-start | bytes 104 | tf_op jit(solution)/shard_map/ppermute | solution.py:253
  4.1 0.7 reshape.681
  4.9 0.5 compare_and_fusion.3
  5.5 0.9 reduce-window.30
  7.4 0.6 pad_clamp_fusion
  8.0 0.7 subtract_select_fusion
  8.8 0.9 reduce-window.21
  10.0 0.8 reduce-window.32
  11.0 0.6 pad_clamp_fusion.1
  11.6 0.7 fusion.77
  12.3 1.0 select_reduce_fusion
  13.3 0.7 fusion.50
  14.1 0.7 fusion.80
  14.8 0.4 collective-permute-start.2
  15.2 3.1 %collective-permute-done.2 = s32[2,1,8]{2,0,1:T(2,128)S(1)} collective-permute-done((s32[2,1,8]{2,0,1:T(2,128)S(1)}, s32[2,1,8]{2,0,1:T(2,128)S(1)}, u32[]{:S(2)}, u32[]{:S(2)}) %collective-permute-start.2) | collective-permute-done | bytes 96 | tf_op jit(solution)/shard_map/ppermute | solution.py:253
  18.4 0.6 collective-permute-start.3
  18.9 3.1 %collective-permute-done.3 = s32[4,1,8]{2,0,1:T(4,128)S(1)} collective-permute-done((s32[4,1,8]{2,0,1:T(4,128)S(1)}, s32[4,1,8]{2,0,1:T(4,128)S(1)}, u32[]{:S(2)}, u32[]{:S(2)}) %collective-permute-start.3) | collective-permute-done | bytes 160 | tf_op jit(solution)/shard_map/ppermute | solution.py:253
  22.2 1.1 gather_fusion.1
  23.3 1.3 %gather_fusion = s32[384,8]{1,0:T(8,128)S(1)} fusion(s32[8,8]{1,0:T(8,128)S(1)} %reduce_window_sum.54, s32[1024]{0:T(1024)S(1)} %get-tuple-element.76), kind=kCustom, calls=%fused_computation.clone | custom fusion | bytes 26112 | tf_op jit(solution)/shard_map/jit(_take)/gather | solution.py:96
  25.0 0.5 multiply_cosine_fusion.3
  25.7 1.6 %select_bitcast_fusion.3 = (bf16[1,1,96,5120]{3,2,1,0:T(8,128)(2,1)S(1)}, bf16[1,1,96,5120]{3,2,1,0:T(8,128)(2,1)S(1)}) fusion(bf16[1,96,5120]{2,1,0:T(8,128)(2,1)} %collective-permute-done, pred[]{:T(512)S(6)} %eq.140, bf16[96,5120]{1,0:T(8,128)(2,1)} %param.15), kind=kLoop, calls=%fused_computation.41 | loop fusion | flops 983040 | bytes 3932161 | tf_op jit(solution)/shard_map/stack | solution.py:287
  27.3 0.5 multiply_reduce_fusion.1
  27.8 0.6 add_rsqrt_fusion.1
  28.4 1.3 %rsqrt.23 = f32[192]{0:T(256)} reshape(f32[2,96]{1,0:T(2,128)} %add_rsqrt_fusion.1) | data formatting | bytes 1536 | tf_op jit(solution)/shard_map/rsqrt | solution.py:110
  29.7 1.6 %select_bitcast_fusion.1 = (bf16[1,1,96,5120]{3,2,1,0:T(8,128)(2,1)S(1)}, bf16[1,1,96,5120]{3,2,1,0:T(8,128)(2,1)S(1)}) fusion(bf16[1,96,5120]{2,1,0:T(8,128)(2,1)} %collective-permute-done.5, pred[]{:T(512)S(6)} %eq.140, bf16[96,5120]{1,0:T(8,128)(2,1)} %collective-permute-done.4), kind=kLoop, calls=%fused_computation.39 | loop fusion | flops 983040 | bytes 3932161 | tf_op jit(solution)/shard_map/stack | solution.py:287
  31.3 3.6 %maximum_convert_fusion = (f32[1,2,96,5120]{3,2,1,0:T(8,128)}, f32[1,2,96,5120]{3,2,1,0:T(8,128)}) fusion(bf16[1,1,96,5120]{3,2,1,0:T(8,128)(2,1)S(1)} %get-tuple-element.22, bf16[1,1,96,5120]{3,2,1,0:T(8,128)(2,1)S(1)} %get-tuple-element.21, bf16[1,1,96,5120]{3,2,1,0:T(8,128)(2,1)S(1)} %get-tuple-element.24, bf16[1,1,96,5120]{3,2,1,0:T(8,128)(2,1)S(1)} %get-tuple-element.23), kind=kLoop, calls=%fused_computation.14 | loop fusion | flops 3932160 | bytes 11796480 | tf_op jit(solution)/shard_map/convert_element_type | solution.py:107
  34.9 0.5 multiply_reduce_fusion
  35.6 4.5 %fusion.3 = (bf16[192,5120]{1,0:T(8,128)(2,1)S(1)}, bf16[192,5120]{1,0:T(8,128)(2,1)S(1)}) fusion(f32[1,2,96,5120]{3,2,1,0:T(8,128)} %get-tuple-element.73, f32[5120]{0:T(1024)S(1)} %copy-done.7, f32[192]{0:T(256)S(1)} %copy-done.12, f32[192]{0:T(256)S(1)} %rsqrt.25, f32[1,2,96,5120]{3,2,1,0:T(8,128)} %get-tuple-element.74), kind=kLoop, calls=%fused_computation.9 | loop fusion | flops 5898240 | bytes 11818496 | tf_op jit(solution)/shard_map/convert_element_type | solution.py:112
  40.2 0.7 fusion.9
  40.9 0.7 fusion.8
  41.6 0.6 copy-done.5
  42.2 0.7 fusion.11
  42.9 0.7 fusion.10
  43.6 5.0 %convolution_add_fusion = f32[192,640]{1,0:T(8,128)S(1)} fusion(bf16[192,5120]{1,0:T(8,128)(2,1)S(1)} %get-tuple-element.44, bf16[5120,640]{1,0:T(8,128)(2,1)} %param.19, f32[640]{0:T(1024)S(1)} %copy-done.20), kind=kOutput, calls=%fused_computation.22 | convolution fusion | flops 1258414080 | bytes 9013760 | tf_op jit(solution)/shard_map/dot_general | solution.py:114
  48.7 1.7 %convolution_add_fusion.1 = f32[192,640]{1,0:T(8,128)S(1)} fusion(bf16[192,5120]{1,0:T(8,128)(2,1)S(1)} %get-tuple-element.43, bf16[5120,640]{1,0:T(8,128)(2,1)S(1)} %bitcast.258, f32[640]{0:T(1024)S(1)} %copy-done.20), kind=kOutput, calls=%fused_computation.23 | convolution fusion | flops 1258414080 | bytes 9013760 | tf_op jit(solution)/shard_map/dot_general | solution.py:114
  50.5 0.8 fusion.60
  52.7 0.4 copy-done.14
  53.0 0.6 convolution_convert_fusion
  53.7 0.8 gather_fusion.2
  54.5 0.4 broadcast_select_fusion.1
  55.0 1.3 %collective-permute-start.7 = (bf16[48,896]{1,0:T(8,128)(2,1)S(1)}, bf16[48,896]{1,0:T(8,128)(2,1)S(1)}, u32[]{:S(2)}, u32[]{:S(2)}) collective-permute-start(bf16[48,896]{1,0:T(8,128)(2,1)S(1)} %get-tuple-element.34), channel_id=1, source_target_pairs={{0,8},{4,12},{8,16},{12,20},{16,24},{20,28},{24,0},{28,4},{1,9},{5... | collective-permute-start | bytes 258056 | tf_op jit(solution)/shard_map/ppermute | solution.py:219
  56.3 3.0 %collective-permute-start.8 = (bf16[48,896]{1,0:T(8,128)(2,1)S(1)}, bf16[48,896]{1,0:T(8,128)(2,1)S(1)}, u32[]{:S(2)}, u32[]{:S(2)}) collective-permute-start(bf16[48,896]{1,0:T(8,128)(2,1)S(1)} %get-tuple-element.33), channel_id=1, source_target_pairs={{0,12},{4,16},{8,20},{12,24},{16,28},{20,0},{24,4},{28,8},{1,13},{... | collective-permute-start | bytes 258056 | tf_op jit(solution)/shard_map/ppermute | solution.py:219
  59.5 2.8 %collective-permute-start.10 = (bf16[48,896]{1,0:T(8,128)(2,1)S(1)}, bf16[48,896]{1,0:T(8,128)(2,1)S(1)}, u32[]{:S(2)}, u32[]{:S(2)}) collective-permute-start(bf16[48,896]{1,0:T(8,128)(2,1)S(1)} %get-tuple-element.31), channel_id=1, source_target_pairs={{0,20},{4,24},{8,28},{12,0},{16,4},{20,8},{24,12},{28,16},{1,21},{... | collective-permute-start | bytes 258056 | tf_op jit(solution)/shard_map/ppermute | solution.py:219
  62.3 1.3 %collective-permute-start.11 = (bf16[48,896]{1,0:T(8,128)(2,1)S(1)}, bf16[48,896]{1,0:T(8,128)(2,1)S(1)}, u32[]{:S(2)}, u32[]{:S(2)}) collective-permute-start(bf16[48,896]{1,0:T(8,128)(2,1)S(1)} %get-tuple-element.30), channel_id=1, source_target_pairs={{0,24},{4,28},{8,0},{12,4},{16,8},{20,12},{24,16},{28,20},{1,25},{... | collective-permute-start | bytes 258056 | tf_op jit(solution)/shard_map/ppermute | solution.py:219
  63.7 0.4 collective-permute-start.12
  64.1 5.4 %collective-permute-done.8 = bf16[48,896]{1,0:T(8,128)(2,1)S(1)} collective-permute-done((bf16[48,896]{1,0:T(8,128)(2,1)S(1)}, bf16[48,896]{1,0:T(8,128)(2,1)S(1)}, u32[]{:S(2)}, u32[]{:S(2)}) %collective-permute-start.8) | collective-permute-done | bytes 86048 | tf_op jit(solution)/shard_map/ppermute | solution.py:219
  69.6 1.0 collective-permute-done.9
  70.7 2.9 %collective-permute-done.11 = bf16[48,896]{1,0:T(8,128)(2,1)S(1)} collective-permute-done((bf16[48,896]{1,0:T(8,128)(2,1)S(1)}, bf16[48,896]{1,0:T(8,128)(2,1)S(1)}, u32[]{:S(2)}, u32[]{:S(2)}) %collective-permute-start.11) | collective-permute-done | bytes 86048 | tf_op jit(solution)/shard_map/ppermute | solution.py:219
  73.6 1.3 %collective-permute-done.12 = bf16[48,896]{1,0:T(8,128)(2,1)S(1)} collective-permute-done((bf16[48,896]{1,0:T(8,128)(2,1)S(1)}, bf16[48,896]{1,0:T(8,128)(2,1)S(1)}, u32[]{:S(2)}, u32[]{:S(2)}) %collective-permute-start.12) | collective-permute-done | bytes 86048 | tf_op jit(solution)/shard_map/ppermute | solution.py:219
  74.9 0.8 gather_fusion.3
  75.9 0.5 convolution_convert_fusion.1
  77.2 4.1 %fusion.96 = f32[128,5120]{1,0:T(8,128)S(1)} fusion(bf16[128,640]{0,1:T(8,128)(2,1)S(1)} %bitcast.240, bf16[640,5120]{1,0:T(8,128)(2,1)} %param.25), kind=kOutput, calls=%fused_computation.259 | convolution fusion | flops 838860800 | bytes 9338880 | tf_op jit(solution)/shard_map/dot_general | solution.py:205
  81.4 1.3 %copy-done.2 = f32[128,5120]{1,0:T(8,128)} copy-done((f32[128,5120]{1,0:T(8,128)}, f32[128,5120]{1,0:T(8,128)S(1)}, u32[]{:S(2)}) %copy-start.2) | copy-done | bytes 2621464
  83.6 4.1 %fusion.95 = f32[128,5120]{1,0:T(8,128)S(1)} fusion(bf16[128,640]{0,1:T(8,128)(2,1)S(1)} %bitcast.239, bf16[640,5120]{1,0:T(8,128)(2,1)} %param.25), kind=kOutput, calls=%fused_computation.258 | convolution fusion | flops 838860800 | bytes 9338880 | tf_op jit(solution)/shard_map/dot_general | solution.py:205
  87.9 1.4 %copy-done.3 = f32[128,5120]{1,0:T(8,128)} copy-done((f32[128,5120]{1,0:T(8,128)}, f32[128,5120]{1,0:T(8,128)S(1)}, u32[]{:S(2)}) %copy-start.3) | copy-done | bytes 2621464
  89.2 1.1 pad_maximum_fusion
  90.4 0.5 collective-permute-start.13
  90.9 2.5 %select_bitcast_fusion.4 = (f32[1,128,1280]{2,1,0:T(8,128)S(1)}, f32[128,1280]{1,0:T(8,128)S(1)}, f32[128,1280]{1,0:T(8,128)S(1)}) fusion(pred[]{:T(512)S(6)} %eq.139, f32[2,128,1280]{2,1,0:T(8,128)} %collective-permute-done.15, f32[128,5120]{1,0:T(8,128)} %copy-done.2, pred[]{:T(512)S(6)} %eq.140), kind=kLoop, calls=%fused_computation.72 | loop fusion | flops 819200 | bytes 5898242 | tf_op jit(solution)/shard_map/stack | solution.py:237
  93.3 0.6 collective-permute-start.16
  94.3 1.5 %collective-permute-start.14 = (f32[1,128,1280]{2,1,0:T(8,128)S(1)}, f32[1,128,1280]{2,1,0:T(8,128)S(1)}, u32[]{:S(2)}, u32[]{:S(2)}) collective-permute-start(f32[1,128,1280]{2,1,0:T(8,128)S(1)} %get-tuple-element.6), channel_id=1, source_target_pairs={{0,2},{1,3},{2,0},{3,1},{4,6},{5,7},{6,4},{7,5},{8,10},{9,11},{10,... | collective-permute-start | bytes 1966088 | tf_op jit(solution)/shard_map/ppermute | solution.py:239
  95.8 15.1 %collective-permute-done.16 = f32[1,128,1280]{2,1,0:T(8,128)S(1)} collective-permute-done((f32[1,128,1280]{2,1,0:T(8,128)S(1)}, f32[1,128,1280]{2,1,0:T(8,128)S(1)}, u32[]{:S(2)}, u32[]{:S(2)}) %collective-permute-start.16) | collective-permute-done | bytes 655392 | tf_op jit(solution)/shard_map/ppermute | solution.py:239
  111.1 13.0 %collective-permute-done.14 = f32[1,128,1280]{2,1,0:T(8,128)S(1)} collective-permute-done((f32[1,128,1280]{2,1,0:T(8,128)S(1)}, f32[1,128,1280]{2,1,0:T(8,128)S(1)}, u32[]{:S(2)}, u32[]{:S(2)}) %collective-permute-start.14) | collective-permute-done | bytes 655392 | tf_op jit(solution)/shard_map/ppermute | solution.py:239
  124.2 0.9 pad_maximum_fusion.2
  (142 shorter events, 7.1 us)
Async XLA Ops:
  0.0 40.2 %copy-start = (bf16[5120,128]{1,0:T(8,128)(2,1)S(1)}, bf16[5120,128]{1,0:T(8,128)(2,1)}, u32[]{:S(2)}) copy-start(bf16[5120,128]{1,0:T(8,128)(2,1)} %param.21) | copy-start | bytes 3932164
  0.0 25.5 %collective-permute-start.4 = (bf16[96,5120]{1,0:T(8,128)(2,1)}, bf16[96,5120]{1,0:T(8,128)(2,1)}, u32[]{:S(2)}, u32[]{:S(2)}) collective-permute-start(bf16[96,5120]{1,0:T(8,128)(2,1)} %param.15), channel_id=1, source_target_pairs={{0,2},{1,3},{2,0},{3,1},{4,6},{5,7},{6,4},{7,5},{8,10},{9,11},{10,... | collective-permute-start | bytes 2949128 | tf_op jit(solution)/shard_map/ppermute | solution.py:268
  1.5 24.2 %collective-permute-start = (bf16[1,96,5120]{2,1,0:T(8,128)(2,1)}, bf16[1,96,5120]{2,1,0:T(8,128)(2,1)}, u32[]{:S(2)}, u32[]{:S(2)}) collective-permute-start(bf16[1,96,5120]{2,1,0:T(8,128)(2,1)} %bitcast.235), channel_id=1, source_target_pairs={{0,1},{1,0},{2,3},{3,2},{4,5},{5,4},{6,7},{7,6},{8,9},{9,8},{10,11... | collective-permute-start | bytes 2949128 | tf_op jit(solution)/shard_map/ppermute | solution.py:284
  1.5 12.6 %collective-permute-start.1 = (s32[1,1,8]{2,1,0:T(1,128)}, s32[1,1,8]{2,1,0:T(1,128)S(1)}, u32[]{:S(2)}, u32[]{:S(2)}) collective-permute-start(s32[1,1,8]{2,1,0:T(1,128)} %bitcast.255), channel_id=1, source_target_pairs={{0,16},{4,20},{8,24},{12,28},{16,0},{20,4},{24,8},{28,12},{1,17},{... | collective-permute-start | bytes 104 | tf_op jit(solution)/shard_map/ppermute | solution.py:253
  4.1 20.9 %copy-start.15 = (f32[64]{0:T(128)}, f32[64]{0:T(128)S(1)}, u32[]{:S(2)}) copy-start(f32[64]{0:T(128)S(1)} %multiply_exponential_fusion) | copy-start | bytes 772
  14.8 3.6 %collective-permute-start.2 = (s32[2,1,8]{2,0,1:T(2,128)S(1)}, s32[2,1,8]{2,0,1:T(2,128)S(1)}, u32[]{:S(2)}, u32[]{:S(2)}) collective-permute-start(s32[2,1,8]{2,0,1:T(2,128)S(1)} %bitcast.253), channel_id=1, source_target_pairs={{0,8},{4,12},{8,0},{12,4},{16,24},{20,28},{24,16},{28,20},{1,9},{5... | collective-permute-start | bytes 200 | tf_op jit(solution)/shard_map/ppermute | solution.py:253
  18.4 3.7 %collective-permute-start.3 = (s32[4,1,8]{2,0,1:T(4,128)S(1)}, s32[4,1,8]{2,0,1:T(4,128)S(1)}, u32[]{:S(2)}, u32[]{:S(2)}) collective-permute-start(s32[4,1,8]{2,0,1:T(4,128)S(1)} %bitcast.247), channel_id=1, source_target_pairs={{0,4},{4,0},{8,12},{12,8},{16,20},{20,16},{24,28},{28,24},{1,5},{5... | collective-permute-start | bytes 392 | tf_op jit(solution)/shard_map/ppermute | solution.py:253
  25.0 0.6 copy-start.8
  25.0 0.6 copy-start.10
  25.5 4.1 %collective-permute-start.5 = (bf16[1,96,5120]{2,1,0:T(8,128)(2,1)}, bf16[1,96,5120]{2,1,0:T(8,128)(2,1)}, u32[]{:S(2)}, u32[]{:S(2)}) collective-permute-start(bf16[1,96,5120]{2,1,0:T(8,128)(2,1)} %bitcast.25), channel_id=1, source_target_pairs={{0,1},{1,0},{2,3},{3,2},{4,5},{5,4},{6,7},{7,6},{8,9},{9,8},{10,11... | collective-permute-start | bytes 2949128 | tf_op jit(solution)/shard_map/ppermute | solution.py:284
  34.9 0.7 copy-start.7
  34.9 0.7 copy-start.12
  35.6 4.5 %copy-start.17 = (f32[128]{0:T(128)S(1)}, f32[128]{0:T(128)}, u32[]{:S(2)}) copy-start(f32[128]{0:T(128)} %param.22) | copy-start | bytes 1540
  40.9 1.3 %copy-start.5 = (bf16[5120,128]{1,0:T(8,128)(2,1)S(1)}, bf16[5120,128]{1,0:T(8,128)(2,1)}, u32[]{:S(2)}) copy-start(bf16[5120,128]{1,0:T(8,128)(2,1)} %param.23) | copy-start | bytes 3932164
  40.9 1.3 %copy-start.18 = (f32[128]{0:T(128)S(1)}, f32[128]{0:T(128)}, u32[]{:S(2)}) copy-start(f32[128]{0:T(128)} %param.24) | copy-start | bytes 1540
  42.2 1.4 %copy-start.20 = (f32[640]{0:T(1024)S(1)}, f32[640]{0:T(1024)}, u32[]{:S(2)}) copy-start(f32[640]{0:T(1024)} %param.20) | copy-start | bytes 7684
  42.9 5.7 %slice-start = ((s8[6553600]{0:T(1024)(128)(4,1)}), s8[4194304]{0:T(1024)(128)(4,1)S(1)}, s32[]{:S(2)}) async-start(s8[6553600]{0:T(1024)(128)(4,1)} %bitcast.257), calls=%async_computation | async-start | bytes 8388608
  43.6 5.0 %slice-start.1 = ((s8[6553600]{0:T(1024)(128)(4,1)}), s8[2359296]{0:T(1024)(128)(4,1)S(1)}, s32[]{:S(2)}) async-start(s8[6553600]{0:T(1024)(128)(4,1)} %bitcast.257), calls=%async_computation.1 | async-start | bytes 4718592
  48.6 1.9 %copy-start.9 = (f32[192]{0:T(256)S(1)}, f32[192]{0:T(256)}, u32[]{:S(2)}) copy-start(f32[192]{0:T(256)} %copy-done.8) | copy-start | bytes 2308
  48.6 1.9 %copy-start.11 = (f32[192]{0:T(256)S(1)}, f32[192]{0:T(256)}, u32[]{:S(2)}) copy-start(f32[192]{0:T(256)} %copy-done.10) | copy-start | bytes 2308
  48.6 1.9 %copy-start.16 = (f32[64]{0:T(128)S(1)}, f32[64]{0:T(128)}, u32[]{:S(2)}) copy-start(f32[64]{0:T(128)} %copy-done.15) | copy-start | bytes 772
  52.4 0.7 copy-start.14
  53.0 1.4 %copy-start.19 = (pred[8]{0:T(512)(128)(4,1)S(1)}, pred[8]{0:T(512)(128)(4,1)}, u32[]{:S(2)}) copy-start(pred[8]{0:T(512)(128)(4,1)} %compare_and_fusion.3) | copy-start | bytes 28
  54.9 7.4 %collective-permute-start.6 = (bf16[48,896]{1,0:T(8,128)(2,1)S(1)}, bf16[48,896]{1,0:T(8,128)(2,1)S(1)}, u32[]{:S(2)}, u32[]{:S(2)}) collective-permute-start(bf16[48,896]{1,0:T(8,128)(2,1)S(1)} %get-tuple-element.35), channel_id=1, source_target_pairs={{0,4},{4,8},{8,12},{12,16},{16,20},{20,24},{24,28},{28,0},{1,5},{5... | collective-permute-start | bytes 258056 | tf_op jit(solution)/shard_map/ppermute | solution.py:219
  55.0 8.7 %collective-permute-start.7 = (bf16[48,896]{1,0:T(8,128)(2,1)S(1)}, bf16[48,896]{1,0:T(8,128)(2,1)S(1)}, u32[]{:S(2)}, u32[]{:S(2)}) collective-permute-start(bf16[48,896]{1,0:T(8,128)(2,1)S(1)} %get-tuple-element.34), channel_id=1, source_target_pairs={{0,8},{4,12},{8,16},{12,20},{16,24},{20,28},{24,0},{28,4},{1,9},{5... | collective-permute-start | bytes 258056 | tf_op jit(solution)/shard_map/ppermute | solution.py:219
  56.3 13.2 %collective-permute-start.8 = (bf16[48,896]{1,0:T(8,128)(2,1)S(1)}, bf16[48,896]{1,0:T(8,128)(2,1)S(1)}, u32[]{:S(2)}, u32[]{:S(2)}) collective-permute-start(bf16[48,896]{1,0:T(8,128)(2,1)S(1)} %get-tuple-element.33), channel_id=1, source_target_pairs={{0,12},{4,16},{8,20},{12,24},{16,28},{20,0},{24,4},{28,8},{1,13},{... | collective-permute-start | bytes 258056 | tf_op jit(solution)/shard_map/ppermute | solution.py:219
  59.3 11.3 %collective-permute-start.9 = (bf16[48,896]{1,0:T(8,128)(2,1)S(1)}, bf16[48,896]{1,0:T(8,128)(2,1)S(1)}, u32[]{:S(2)}, u32[]{:S(2)}) collective-permute-start(bf16[48,896]{1,0:T(8,128)(2,1)S(1)} %get-tuple-element.32), channel_id=1, source_target_pairs={{0,16},{4,20},{8,24},{12,28},{16,0},{20,4},{24,8},{28,12},{1,17},{... | collective-permute-start | bytes 258056 | tf_op jit(solution)/shard_map/ppermute | solution.py:219
  59.5 11.1 %collective-permute-start.10 = (bf16[48,896]{1,0:T(8,128)(2,1)S(1)}, bf16[48,896]{1,0:T(8,128)(2,1)S(1)}, u32[]{:S(2)}, u32[]{:S(2)}) collective-permute-start(bf16[48,896]{1,0:T(8,128)(2,1)S(1)} %get-tuple-element.31), channel_id=1, source_target_pairs={{0,20},{4,24},{8,28},{12,0},{16,4},{20,8},{24,12},{28,16},{1,21},{... | collective-permute-start | bytes 258056 | tf_op jit(solution)/shard_map/ppermute | solution.py:219
  62.3 11.3 %collective-permute-start.11 = (bf16[48,896]{1,0:T(8,128)(2,1)S(1)}, bf16[48,896]{1,0:T(8,128)(2,1)S(1)}, u32[]{:S(2)}, u32[]{:S(2)}) collective-permute-start(bf16[48,896]{1,0:T(8,128)(2,1)S(1)} %get-tuple-element.30), channel_id=1, source_target_pairs={{0,24},{4,28},{8,0},{12,4},{16,8},{20,12},{24,16},{28,20},{1,25},{... | collective-permute-start | bytes 258056 | tf_op jit(solution)/shard_map/ppermute | solution.py:219
  63.7 12.2 %copy-start.13 = (s32[256]{0:T(256)S(1)}, s32[256]{0:T(256)}, u32[]{:S(2)}) copy-start(s32[256]{0:T(256)} %select_reduce_fusion) | copy-start | bytes 3076
  63.7 11.2 %collective-permute-start.12 = (bf16[48,896]{1,0:T(8,128)(2,1)S(1)}, bf16[48,896]{1,0:T(8,128)(2,1)S(1)}, u32[]{:S(2)}, u32[]{:S(2)}) collective-permute-start(bf16[48,896]{1,0:T(8,128)(2,1)S(1)} %get-tuple-element.29), channel_id=1, source_target_pairs={{0,28},{4,0},{8,4},{12,8},{16,12},{20,16},{24,20},{28,24},{1,29},{... | collective-permute-start | bytes 258056 | tf_op jit(solution)/shard_map/ppermute | solution.py:219
  75.7 0.8 copy-start.6
  81.3 1.5 %copy-start.2 = (f32[128,5120]{1,0:T(8,128)}, f32[128,5120]{1,0:T(8,128)S(1)}, u32[]{:S(2)}) copy-start(f32[128,5120]{1,0:T(8,128)S(1)} %fusion.96) | copy-start | bytes 7864324
  82.9 8.0 %collective-permute-start.15 = (f32[2,128,1280]{2,1,0:T(8,128)S(1)}, f32[2,128,1280]{2,1,0:T(8,128)}, u32[]{:S(2)}, u32[]{:S(2)}) collective-permute-start(f32[2,128,1280]{2,1,0:T(8,128)S(1)} %pad_maximum_fusion.1), channel_id=1, source_target_pairs={{0,1},{1,0},{2,3},{3,2},{4,5},{5,4},{6,7},{7,6},{8,9},{9,8},{10,11... | collective-permute-start | bytes 3932168 | tf_op jit(solution)/shard_map/ppermute | solution.py:239
  87.7 1.5 %copy-start.3 = (f32[128,5120]{1,0:T(8,128)}, f32[128,5120]{1,0:T(8,128)S(1)}, u32[]{:S(2)}) copy-start(f32[128,5120]{1,0:T(8,128)S(1)} %fusion.95) | copy-start | bytes 7864324
  90.4 3.6 %collective-permute-start.13 = (f32[2,128,1280]{2,1,0:T(8,128)}, f32[2,128,1280]{2,1,0:T(8,128)S(1)}, u32[]{:S(2)}, u32[]{:S(2)}) collective-permute-start(f32[2,128,1280]{2,1,0:T(8,128)} %pad_maximum_fusion), channel_id=1, source_target_pairs={{0,1},{1,0},{2,3},{3,2},{4,5},{5,4},{6,7},{7,6},{8,9},{9,8},{10,11... | collective-permute-start | bytes 3932168 | tf_op jit(solution)/shard_map/ppermute | solution.py:239
  90.9 3.1 %copy-start.4 = (f32[128,5120]{1,0:T(8,128)S(1)}, f32[128,5120]{1,0:T(8,128)}, u32[]{:S(2)}) copy-start(f32[128,5120]{1,0:T(8,128)} %copy-done.3) | copy-start | bytes 7864324
  93.3 17.7 %collective-permute-start.16 = (f32[1,128,1280]{2,1,0:T(8,128)S(1)}, f32[1,128,1280]{2,1,0:T(8,128)S(1)}, u32[]{:S(2)}, u32[]{:S(2)}) collective-permute-start(f32[1,128,1280]{2,1,0:T(8,128)S(1)} %get-tuple-element.10), channel_id=1, source_target_pairs={{0,2},{1,3},{2,0},{3,1},{4,6},{5,7},{6,4},{7,5},{8,10},{9,11},{10,... | collective-permute-start | bytes 1966088 | tf_op jit(solution)/shard_map/ppermute | solution.py:239
  94.3 29.8 %collective-permute-start.14 = (f32[1,128,1280]{2,1,0:T(8,128)S(1)}, f32[1,128,1280]{2,1,0:T(8,128)S(1)}, u32[]{:S(2)}, u32[]{:S(2)}) collective-permute-start(f32[1,128,1280]{2,1,0:T(8,128)S(1)} %get-tuple-element.6), channel_id=1, source_target_pairs={{0,2},{1,3},{2,0},{3,1},{4,6},{5,7},{6,4},{7,5},{8,10},{9,11},{10,... | collective-permute-start | bytes 1966088 | tf_op jit(solution)/shard_map/ppermute | solution.py:239
  111.0 14.1 %copy-start.1 = (bf16[5120,128]{1,0:T(8,128)(2,1)S(1)}, bf16[5120,128]{1,0:T(8,128)(2,1)}, u32[]{:S(2)}) copy-start(bf16[5120,128]{1,0:T(8,128)(2,1)} %param.21) | copy-start | bytes 3932164

commit v8 on v7

--- a/solution.py
+++ b/solution.py
@@ -78,16 +78,13 @@
     ctx_index = lax.axis_index("ctx")
 
     all_lengths = doubling_gather(seq_len, "ctx", ctx_count)
-    near_x, far_x = split_gather(x_pool, "head", head_count)
-    half_rows = near_x.shape[0]
+    pieces, work_heads = xor_gather(x_pool, "head", head_count)
 
     dest_grid = pool_dest.reshape(ctx_count, group_rows)
     my_dest = lax.dynamic_index_in_dim(dest_grid, ctx_index, 0, keepdims=False)
-    upper = lax.axis_index("head") >= head_count - head_count // 2
-    if far_x.shape[0]:
-        to_work_order = lambda v: jnp.where(upper, jnp.roll(v, -half_rows), v)
-    else:
-        to_work_order = lambda v: v
+    to_work_order = lambda v: jnp.take(
+        v.reshape(head_count, pool_rows), work_heads, axis=0
+    ).reshape(-1)
     work_dest = to_work_order(my_dest)
     is_filled = work_dest >= 0
     owner = jnp.where(is_filled, work_dest // pack_len, 0)
@@ -136,10 +133,7 @@
             axis=1,
         )
 
-    parts = [project(near_x, sequence_starts[:half_rows])]
-    if far_x.shape[0]:
-        parts.append(project(far_x, sequence_starts[half_rows:]))
-    qkv = jnp.concatenate(parts, axis=0)
+    qkv = project(jnp.concatenate(pieces, axis=0), sequence_starts)
 
     places = to_work_order(send_places(my_dest, ctx_count, group_cap, pack_len))
     send_hot = (
@@ -257,35 +251,17 @@
     return have.reshape((count * part.shape[0],) + part.shape[1:])
 
 
-def split_gather(part, axis_name, count):
-    if count == 1:
-        return part, part[:0]
-    half = count // 2
-    if count % 2 or half & (half - 1):
-        gathered = lax.all_gather(part, axis_name, tiled=True)
-        return gathered, gathered[:0]
-    me = lax.axis_index(axis_name)
-    crossed = lax.ppermute(part, axis_name, [(i, (i + half) % count) for i in range(count)])
-    if half == 1:
-        return part, crossed
-    near = doubling_gather_within(part, axis_name, half)
-    far = doubling_gather_within(crossed, axis_name, half)
-    return near, far
-
-
-def doubling_gather_within(part, axis_name, span):
-    bits = span.bit_length() - 1
-    me = lax.axis_index(axis_name)
-    count = lax.axis_size(axis_name)
-    have = part[None]
+def xor_gather(part, axis_name, count):
+    me = lax.axis_index(axis_name)
+    bits = count.bit_length() - 1
+    if count != 1 << bits:
+        return [lax.all_gather(part, axis_name, tiled=True)], jnp.arange(count, dtype=jnp.int32)
+    pieces, masks = [part], [0]
     for stage in reversed(range(bits)):
-        bit = (me >> stage) & 1
         pairs = [(i, i ^ (1 << stage)) for i in range(count)]
-        got = lax.ppermute(have, axis_name, pairs)
-        first = jnp.where(bit == 0, have, got)
-        second = jnp.where(bit == 0, got, have)
-        have = jnp.stack([first, second], axis=1).reshape((-1,) + part.shape)
-    return have.reshape((span * part.shape[0],) + part.shape[1:])
+        pieces = pieces + [lax.ppermute(p, axis_name, pairs) for p in pieces]
+        masks = masks + [m ^ (1 << stage) for m in masks]
+    return pieces, me ^ jnp.asarray(masks, dtype=jnp.int32)
 
 
 def solution(mesh):

time: 126 us -> 125 us (level)
  the two profiles are of different devices: /device:TPU:12 before, /device:TPU:0 now
where the time goes in v8:
time: 125 us; the launch traced here: 124 us
  waiting for transfers between devices  34.7 us (28%)
  other arithmetic  27.8 us (22%)
  starting transfers between devices  24.2 us (19%)
  matrix products  18.5 us (15%)
  local copies, waits for them, and re-layouts  18.2 us (15%)
    ppermute x4, waiting for transfers between devices, halving_scatter(): got = lax.ppermute(send, axis_name, pairs)  26.9 us
    ppermute x7, starting transfers between devices, exchange(): from_shift.append(lax.ppermute(by_shift[shift], axis_name, pairs))  12.5 us
    dot_general x2, matrix products, local(): jnp.dot(mixed_heads, w_out, preferred_element_type=jnp.float32)  8.19 us
    unnamed x42, local copies, waits for them, and re-layouts  6.9 us
    ppermute x3, starting transfers between devices, doubling_gather(): got = lax.ppermute(have, axis_name, pairs)  5.97 us
    another operation x6, other arithmetic, halving_scatter(): jnp.stack([jnp.where(bit == 0, hi, lo) for (_, lo), hi in zip(lows, highs)])  5.63 us
    convert_element_type x1, other arithmetic, project(): normalized_input = (values_wide * lax.rsqrt(jnp.mean(values_wide * values...  4.65 us
    dot_general x1, matrix products, project(): jnp.dot(normalized_input, value_projection_weight, preferred_element_type...  3.76 us
  transfers between devices with their start and end apart: 17, of which 8 were waited for; matrix products, arithmetic and copies ran while one was open for 27% of the time, Pallas kernels for 0%

profile of v8, /device:TPU:0, one launch (start us, length us, event | category | flops | bytes accessed | tf_op | source)
XLA Modules:
  0.0 124.0 jit_solution(17199012276962955671)
XLA Ops:
  0.0 2.9 %collective-permute-start = (bf16[96,5120]{1,0:T(8,128)(2,1)}, bf16[96,5120]{1,0:T(8,128)(2,1)S(1)}, u32[]{:S(2)}, u32[]{:S(2)}) collective-permute-start(bf16[96,5120]{1,0:T(8,128)(2,1)} %param.18), channel_id=1, source_target_pairs={{0,2},{1,3},{2,0},{3,1},{4,6},{5,7},{6,4},{7,5},{8,10},{9,11},{10,... | collective-permute-start | bytes 2949128 | tf_op jit(solution)/shard_map/ppermute | solution.py:262
  2.9 2.6 %collective-permute-start.3 = (s32[1,1,8]{2,1,0:T(1,128)}, s32[1,1,8]{2,1,0:T(1,128)S(1)}, u32[]{:S(2)}, u32[]{:S(2)}) collective-permute-start(s32[1,1,8]{2,1,0:T(1,128)} %bitcast.202), channel_id=1, source_target_pairs={{0,16},{4,20},{8,24},{12,28},{16,0},{20,4},{24,8},{28,12},{1,17},{... | collective-permute-start | bytes 104 | tf_op jit(solution)/shard_map/ppermute | solution.py:247
  6.1 0.7 reshape.493
  6.9 0.9 reduce-window.30
  8.6 0.7 compare_and_fusion.5
  9.3 0.6 gather_fusion.1
  9.8 0.6 gather_fusion
  10.6 0.6 compare_and_fusion.4
  11.1 0.6 fusion.55
  11.7 0.6 pad_clamp_fusion
  12.4 0.7 subtract_select_fusion
  13.2 0.9 reduce-window.21
  14.4 0.8 reduce-window.32
  15.3 0.6 pad_clamp_fusion.1
  16.1 0.6 compare_and_fusion.3
  16.7 1.0 select_reduce_fusion
  17.8 0.7 fusion.62
  18.5 1.6 %collective-permute-start.4 = (s32[2,1,8]{2,0,1:T(2,128)S(1)}, s32[2,1,8]{2,0,1:T(2,128)S(1)}, u32[]{:S(2)}, u32[]{:S(2)}) collective-permute-start(s32[2,1,8]{2,0,1:T(2,128)S(1)} %bitcast.200), channel_id=1, source_target_pairs={{0,8},{4,12},{8,0},{12,4},{16,24},{20,28},{24,16},{28,20},{1,9},{5... | collective-permute-start | bytes 200 | tf_op jit(solution)/shard_map/ppermute | solution.py:247
  20.0 0.7 eq.151
  20.7 1.3 %collective-permute-done.4 = s32[2,1,8]{2,0,1:T(2,128)S(1)} collective-permute-done((s32[2,1,8]{2,0,1:T(2,128)S(1)}, s32[2,1,8]{2,0,1:T(2,128)S(1)}, u32[]{:S(2)}, u32[]{:S(2)}) %collective-permute-start.4) | collective-permute-done | bytes 96 | tf_op jit(solution)/shard_map/ppermute | solution.py:247
  22.0 2.9 %collective-permute-done = bf16[96,5120]{1,0:T(8,128)(2,1)S(1)} collective-permute-done((bf16[96,5120]{1,0:T(8,128)(2,1)}, bf16[96,5120]{1,0:T(8,128)(2,1)S(1)}, u32[]{:S(2)}, u32[]{:S(2)}) %collective-permute-start) | collective-permute-done | bytes 983072 | tf_op jit(solution)/shard_map/ppermute | solution.py:262
  25.0 1.8 %collective-permute-start.5 = (s32[4,1,8]{2,0,1:T(4,128)S(1)}, s32[4,1,8]{2,0,1:T(4,128)S(1)}, u32[]{:S(2)}, u32[]{:S(2)}) collective-permute-start(s32[4,1,8]{2,0,1:T(4,128)S(1)} %bitcast.196), channel_id=1, source_target_pairs={{0,4},{4,0},{8,12},{12,8},{16,20},{20,16},{24,28},{28,24},{1,5},{5... | collective-permute-start | bytes 392 | tf_op jit(solution)/shard_map/ppermute | solution.py:247
  26.8 1.8 %collective-permute-done.5 = s32[4,1,8]{2,0,1:T(4,128)S(1)} collective-permute-done((s32[4,1,8]{2,0,1:T(4,128)S(1)}, s32[4,1,8]{2,0,1:T(4,128)S(1)}, u32[]{:S(2)}, u32[]{:S(2)}) %collective-permute-start.5) | collective-permute-done | bytes 160 | tf_op jit(solution)/shard_map/ppermute | solution.py:247
  28.8 1.4 %gather_fusion.3 = s32[384,8]{1,0:T(8,128)S(1)} fusion(s32[8,8]{1,0:T(8,128)S(1)} %bitcast.187, s32[1024]{0:T(1024)} %get-tuple-element.55), kind=kCustom, calls=%fused_computation.4.clone | custom fusion | bytes 26112 | tf_op jit(solution)/shard_map/jit(_take)/gather | solution.py:94
  30.2 1.8 %gather_fusion.2 = s32[384,8]{1,0:T(8,128)} fusion(s32[8,8]{1,0:T(8,128)S(1)} %reduce_window_sum.54, s32[1024]{0:T(1024)} %get-tuple-element.55), kind=kCustom, calls=%fused_computation.1.clone | custom fusion | bytes 26112 | tf_op jit(solution)/shard_map/jit(_take)/gather | solution.py:93
  31.9 1.2 fusion.28
  33.2 1.0 multiply_cosine_fusion.1
  34.2 2.3 %fusion = f32[384]{0:T(512)S(1)} fusion(bf16[96,5120]{1,0:T(8,128)(2,1)} %collective-permute-done.2, bf16[96,5120]{1,0:T(8,128)(2,1)} %collective-permute-done.1, bf16[96,5120]{1,0:T(8,128)(2,1)S(1)} %collective-permute-done, bf16[96,5120]{1,0:T(8,128)(2,1)S(1)} %copy-done.5), kind=kLoop, calls=%fused_computation.8 | loop fusion | flops 19660416 | bytes 3933696 | tf_op jit(solution)/shard_map/reduce_sum | solution.py:107
  36.5 4.7 %fusion.2 = bf16[384,5120]{1,0:T(8,128)(2,1)S(1)} fusion(f32[5120]{0:T(1024)S(1)} %copy-done.8, f32[384]{0:T(512)S(1)} %add_rsqrt_fusion, bf16[96,5120]{1,0:T(8,128)(2,1)} %collective-permute-done.2, bf16[96,5120]{1,0:T(8,128)(2,1)} %collective-permute-done.1, bf16[96,5120]{1,0:T(8,128)(2,1)S(1)} %collective-permute-done, bf16[96,5120]{1,0:T(8,128)(2,1)S(1)} %copy-done.5), kind=kLoop, calls=%fused_computation.10 | loop fusion | flops 21626880 | bytes 7886336 | tf_op jit(solution)/shard_map/convert_element_type | solution.py:109
  41.3 1.2 %fusion.6 = f32[384,1,128]{0,2,1:T(8,128)S(1)} fusion(bf16[384,5120]{1,0:T(8,128)(2,1)S(1)} %fusion.2, bf16[5120,128]{1,0:T(8,128)(2,1)S(1)} %copy-done, f32[128]{0:T(128)S(1)} %copy-done.12), kind=kOutput, calls=%fused_computation.28 | convolution fusion | flops 503365632 | bytes 5440000 | tf_op jit(solution)/shard_map/dot_general | solution.py:117
  42.5 1.1 fusion.41
  43.6 3.3 %convolution_add_fusion = f32[384,640]{1,0:T(8,128)S(1)} fusion(bf16[384,5120]{1,0:T(8,128)(2,1)S(1)} %fusion.2, bf16[5120,640]{1,0:T(8,128)(2,1)S(1)} %bitcast.205, f32[640]{0:T(1024)S(1)} %copy-done.15), kind=kOutput, calls=%fused_computation.17 | convolution fusion | flops 2516828160 | bytes 11471360 | tf_op jit(solution)/shard_map/dot_general | solution.py:111
  47.3 3.8 %fusion.8 = bf16[384,128]{0,1:T(8,128)(2,1)S(1)} fusion(bf16[384,5120]{1,0:T(8,128)(2,1)} %copy-done.1, bf16[5120,128]{1,0:T(8,128)(2,1)} %param.26, f32[128]{0:T(128)S(1)} %copy-done.13), kind=kOutput, calls=%fused_computation.30 | convolution fusion | flops 503414784 | bytes 5341696 | tf_op jit(solution)/shard_map/dot_general | solution.py:124
  51.3 0.6 convolution_convert_fusion
  51.9 0.8 gather_fusion.4
  52.9 0.7 slice_bitcast_fusion.4
  53.5 1.7 %collective-permute-start.6 = (bf16[48,896]{1,0:T(8,128)(2,1)S(1)}, bf16[48,896]{1,0:T(8,128)(2,1)S(1)}, u32[]{:S(2)}, u32[]{:S(2)}) collective-permute-start(bf16[48,896]{1,0:T(8,128)(2,1)S(1)} %get-tuple-element.32), channel_id=1, source_target_pairs={{0,4},{4,8},{8,12},{12,16},{16,20},{20,24},{24,28},{28,0},{1,5},{5... | collective-permute-start | bytes 258056 | tf_op jit(solution)/shard_map/ppermute | solution.py:213
  55.3 1.6 %collective-permute-start.7 = (bf16[48,896]{1,0:T(8,128)(2,1)S(1)}, bf16[48,896]{1,0:T(8,128)(2,1)S(1)}, u32[]{:S(2)}, u32[]{:S(2)}) collective-permute-start(bf16[48,896]{1,0:T(8,128)(2,1)S(1)} %get-tuple-element.31), channel_id=1, source_target_pairs={{0,8},{4,12},{8,16},{12,20},{16,24},{20,28},{24,0},{28,4},{1,9},{5... | collective-permute-start | bytes 258056 | tf_op jit(solution)/shard_map/ppermute | solution.py:213
  56.9 2.5 %collective-permute-start.8 = (bf16[48,896]{1,0:T(8,128)(2,1)S(1)}, bf16[48,896]{1,0:T(8,128)(2,1)S(1)}, u32[]{:S(2)}, u32[]{:S(2)}) collective-permute-start(bf16[48,896]{1,0:T(8,128)(2,1)S(1)} %get-tuple-element.30), channel_id=1, source_target_pairs={{0,12},{4,16},{8,20},{12,24},{16,28},{20,0},{24,4},{28,8},{1,13},{... | collective-permute-start | bytes 258056 | tf_op jit(solution)/shard_map/ppermute | solution.py:213
  59.5 1.2 collective-permute-start.9
  60.7 2.6 %collective-permute-start.10 = (bf16[48,896]{1,0:T(8,128)(2,1)S(1)}, bf16[48,896]{1,0:T(8,128)(2,1)S(1)}, u32[]{:S(2)}, u32[]{:S(2)}) collective-permute-start(bf16[48,896]{1,0:T(8,128)(2,1)S(1)} %get-tuple-element.28), channel_id=1, source_target_pairs={{0,20},{4,24},{8,28},{12,0},{16,4},{20,8},{24,12},{28,16},{1,21},{... | collective-permute-start | bytes 258056 | tf_op jit(solution)/shard_map/ppermute | solution.py:213
  63.3 1.3 %collective-permute-start.11 = (bf16[48,896]{1,0:T(8,128)(2,1)S(1)}, bf16[48,896]{1,0:T(8,128)(2,1)S(1)}, u32[]{:S(2)}, u32[]{:S(2)}) collective-permute-start(bf16[48,896]{1,0:T(8,128)(2,1)S(1)} %get-tuple-element.27), channel_id=1, source_target_pairs={{0,24},{4,28},{8,0},{12,4},{16,8},{20,12},{24,16},{28,20},{1,25},{... | collective-permute-start | bytes 258056 | tf_op jit(solution)/shard_map/ppermute | solution.py:213
  64.7 0.6 bitcast_dynamic-update-slice_fusion.6
  65.3 1.4 %collective-permute-start.12 = (bf16[48,896]{1,0:T(8,128)(2,1)S(1)}, bf16[48,896]{1,0:T(8,128)(2,1)S(1)}, u32[]{:S(2)}, u32[]{:S(2)}) collective-permute-start(bf16[48,896]{1,0:T(8,128)(2,1)S(1)} %get-tuple-element.26), channel_id=1, source_target_pairs={{0,28},{4,0},{8,4},{12,8},{16,12},{20,16},{24,20},{28,24},{1,29},{... | collective-permute-start | bytes 258056 | tf_op jit(solution)/shard_map/ppermute | solution.py:213
  66.7 0.6 bitcast_dynamic-update-slice_fusion.5
  67.4 0.8 collective-permute-done.8
  68.2 0.6 bitcast_dynamic-update-slice_fusion.4
  69.2 0.6 bitcast_dynamic-update-slice_fusion.3
  69.8 0.6 bitcast_dynamic-update-slice_fusion.2
  71.0 0.6 bitcast_dynamic-update-slice_fusion.1
  71.7 0.6 bitcast_dynamic-update-slice_fusion
  72.3 1.9 %gather_fusion.5 = bf16[8,48,896]{2,1,0:T(8,128)(2,1)S(1)} fusion(bf16[8,48,896]{2,1,0:T(8,128)(2,1)} %bitcast_dynamic-update-slice_fusion, s32[1024]{0:T(1024)} %pad_clamp_fusion), kind=kCustom, calls=%fused_computation.5.clone | custom fusion | bytes 1376288 | tf_op jit(solution)/shard_map/jit(_take)/gather | solution.py:215
  75.7 4.1 %fusion.76 = f32[128,5120]{1,0:T(8,128)S(1)} fusion(bf16[128,640]{0,1:T(8,128)(2,1)S(1)} %bitcast.195, bf16[640,5120]{1,0:T(8,128)(2,1)} %param.28), kind=kOutput, calls=%fused_computation.221 | convolution fusion | flops 838860800 | bytes 9338880 | tf_op jit(solution)/shard_map/dot_general | solution.py:199
  79.8 1.5 %copy-done.2 = f32[128,5120]{1,0:T(8,128)} copy-done((f32[128,5120]{1,0:T(8,128)}, f32[128,5120]{1,0:T(8,128)S(1)}, u32[]{:S(2)}) %copy-start.2) | copy-done | bytes 2621464
  82.3 4.1 %fusion.75 = f32[128,5120]{1,0:T(8,128)S(1)} fusion(bf16[128,640]{0,1:T(8,128)(2,1)S(1)} %bitcast.194, bf16[640,5120]{1,0:T(8,128)(2,1)} %param.28), kind=kOutput, calls=%fused_computation.220 | convolution fusion | flops 838860800 | bytes 9338880 | tf_op jit(solution)/shard_map/dot_general | solution.py:199
  86.4 1.5 %copy-done.3 = f32[128,5120]{1,0:T(8,128)} copy-done((f32[128,5120]{1,0:T(8,128)}, f32[128,5120]{1,0:T(8,128)S(1)}, u32[]{:S(2)}) %copy-start.3) | copy-done | bytes 2621464
  88.0 1.2 pad_maximum_fusion.1
  89.7 2.5 %select_bitcast_fusion = (f32[1,128,1280]{2,1,0:T(8,128)S(1)}, f32[128,1280]{1,0:T(8,128)S(1)}, f32[128,1280]{1,0:T(8,128)S(1)}) fusion(pred[]{:T(512)S(6)} %eq.135, f32[2,128,1280]{2,1,0:T(8,128)} %collective-permute-done.15, f32[128,5120]{1,0:T(8,128)} %copy-done.2, pred[]{:T(512)S(6)} %eq.136), kind=kLoop, calls=%fused_computation.53 | loop fusion | flops 819200 | bytes 5898242 | tf_op jit(solution)/shard_map/stack | solution.py:231
  92.2 1.6 %collective-permute-start.16 = (f32[1,128,1280]{2,1,0:T(8,128)S(1)}, f32[1,128,1280]{2,1,0:T(8,128)S(1)}, u32[]{:S(2)}, u32[]{:S(2)}) collective-permute-start(f32[1,128,1280]{2,1,0:T(8,128)S(1)} %get-tuple-element.11), channel_id=1, source_target_pairs={{0,2},{1,3},{2,0},{3,1},{4,6},{5,7},{6,4},{7,5},{8,10},{9,11},{10,... | collective-permute-start | bytes 1966088 | tf_op jit(solution)/shard_map/ppermute | solution.py:233
  93.8 1.6 %select_bitcast_fusion.3 = (f32[1,128,1280]{2,1,0:T(8,128)S(1)}, f32[128,1280]{1,0:T(8,128)S(1)}, f32[128,1280]{1,0:T(8,128)S(1)}) fusion(pred[]{:T(512)S(6)} %eq.135, f32[2,128,1280]{2,1,0:T(8,128)} %collective-permute-done.13, f32[128,5120]{1,0:T(8,128)S(1)} %copy-done.4, pred[]{:T(512)S(6)} %eq.136), kind=kLoop, calls=%fused_computation.58 | loop fusion | flops 819200 | bytes 5898242 | tf_op jit(solution)/shard_map/stack | solution.py:231
  95.4 0.6 collective-permute-start.14
  96.0 13.9 %collective-permute-done.16 = f32[1,128,1280]{2,1,0:T(8,128)S(1)} collective-permute-done((f32[1,128,1280]{2,1,0:T(8,128)S(1)}, f32[1,128,1280]{2,1,0:T(8,128)S(1)}, u32[]{:S(2)}, u32[]{:S(2)}) %collective-permute-start.16) | collective-permute-done | bytes 655392 | tf_op jit(solution)/shard_map/ppermute | solution.py:233
  110.0 13.0 %collective-permute-done.14 = f32[1,128,1280]{2,1,0:T(8,128)S(1)} collective-permute-done((f32[1,128,1280]{2,1,0:T(8,128)S(1)}, f32[1,128,1280]{2,1,0:T(8,128)S(1)}, u32[]{:S(2)}, u32[]{:S(2)}) %collective-permute-start.14) | collective-permute-done | bytes 655392 | tf_op jit(solution)/shard_map/ppermute | solution.py:233
  123.1 0.9 pad_maximum_fusion.3
  (119 shorter events, 7.5 us)
Async XLA Ops:
  0.0 41.2 %copy-start = (bf16[5120,128]{1,0:T(8,128)(2,1)S(1)}, bf16[5120,128]{1,0:T(8,128)(2,1)}, u32[]{:S(2)}) copy-start(bf16[5120,128]{1,0:T(8,128)(2,1)} %param.24) | copy-start | bytes 3932164
  0.0 34.2 %copy-start.5 = (bf16[96,5120]{1,0:T(8,128)(2,1)S(1)}, bf16[96,5120]{1,0:T(8,128)(2,1)}, u32[]{:S(2)}) copy-start(bf16[96,5120]{1,0:T(8,128)(2,1)} %param.18) | copy-start | bytes 2949124
  0.0 24.9 %collective-permute-start = (bf16[96,5120]{1,0:T(8,128)(2,1)}, bf16[96,5120]{1,0:T(8,128)(2,1)S(1)}, u32[]{:S(2)}, u32[]{:S(2)}) collective-permute-start(bf16[96,5120]{1,0:T(8,128)(2,1)} %param.18), channel_id=1, source_target_pairs={{0,2},{1,3},{2,0},{3,1},{4,6},{5,7},{6,4},{7,5},{8,10},{9,11},{10,... | collective-permute-start | bytes 2949128 | tf_op jit(solution)/shard_map/ppermute | solution.py:262
  2.9 31.2 %collective-permute-start.1 = (bf16[96,5120]{1,0:T(8,128)(2,1)}, bf16[96,5120]{1,0:T(8,128)(2,1)}, u32[]{:S(2)}, u32[]{:S(2)}) collective-permute-start(bf16[96,5120]{1,0:T(8,128)(2,1)} %param.18), channel_id=1, source_target_pairs={{0,1},{1,0},{2,3},{3,2},{4,5},{5,4},{6,7},{7,6},{8,9},{9,8},{10,11... | collective-permute-start | bytes 2949128 | tf_op jit(solution)/shard_map/ppermute | solution.py:262
  2.9 14.8 %collective-permute-start.3 = (s32[1,1,8]{2,1,0:T(1,128)}, s32[1,1,8]{2,1,0:T(1,128)S(1)}, u32[]{:S(2)}, u32[]{:S(2)}) collective-permute-start(s32[1,1,8]{2,1,0:T(1,128)} %bitcast.202), channel_id=1, source_target_pairs={{0,16},{4,20},{8,24},{12,28},{16,0},{20,4},{24,8},{28,12},{1,17},{... | collective-permute-start | bytes 104 | tf_op jit(solution)/shard_map/ppermute | solution.py:247
  18.5 3.6 %collective-permute-start.4 = (s32[2,1,8]{2,0,1:T(2,128)S(1)}, s32[2,1,8]{2,0,1:T(2,128)S(1)}, u32[]{:S(2)}, u32[]{:S(2)}) collective-permute-start(s32[2,1,8]{2,0,1:T(2,128)S(1)} %bitcast.200), channel_id=1, source_target_pairs={{0,8},{4,12},{8,0},{12,4},{16,24},{20,28},{24,16},{28,20},{1,9},{5... | collective-permute-start | bytes 200 | tf_op jit(solution)/shard_map/ppermute | solution.py:247
  24.9 9.3 %collective-permute-start.2 = (bf16[96,5120]{1,0:T(8,128)(2,1)S(1)}, bf16[96,5120]{1,0:T(8,128)(2,1)}, u32[]{:S(2)}, u32[]{:S(2)}) collective-permute-start(bf16[96,5120]{1,0:T(8,128)(2,1)S(1)} %collective-permute-done), channel_id=1, source_target_pairs={{0,1},{1,0},{2,3},{3,2},{4,5},{5,4},{6,7},{7,6},{8,9},{9,8},{10,11... | collective-permute-start | bytes 2949128 | tf_op jit(solution)/shard_map/ppermute | solution.py:262
  25.0 3.7 %collective-permute-start.5 = (s32[4,1,8]{2,0,1:T(4,128)S(1)}, s32[4,1,8]{2,0,1:T(4,128)S(1)}, u32[]{:S(2)}, u32[]{:S(2)}) collective-permute-start(s32[4,1,8]{2,0,1:T(4,128)S(1)} %bitcast.196), channel_id=1, source_target_pairs={{0,4},{4,0},{8,12},{12,8},{16,20},{20,16},{24,28},{28,24},{1,5},{5... | collective-permute-start | bytes 392 | tf_op jit(solution)/shard_map/ppermute | solution.py:247
  28.8 7.7 %copy-start.8 = (f32[5120]{0:T(1024)S(1)}, f32[5120]{0:T(1024)}, u32[]{:S(2)}) copy-start(f32[5120]{0:T(1024)} %param.21) | copy-start | bytes 61444
  34.2 9.4 %slice-start = ((s8[6553600]{0:T(1024)(128)(4,1)}), s8[4194304]{0:T(1024)(128)(4,1)S(1)}, s32[]{:S(2)}) async-start(s8[6553600]{0:T(1024)(128)(4,1)} %bitcast.204), calls=%async_computation | async-start | bytes 8388608
  36.5 4.7 %copy-start.12 = (f32[128]{0:T(128)S(1)}, f32[128]{0:T(128)}, u32[]{:S(2)}) copy-start(f32[128]{0:T(128)} %param.25) | copy-start | bytes 1540
  36.5 7.1 %slice-start.1 = ((s8[6553600]{0:T(1024)(128)(4,1)}), s8[2359296]{0:T(1024)(128)(4,1)S(1)}, s32[]{:S(2)}) async-start(s8[6553600]{0:T(1024)(128)(4,1)} %bitcast.204), calls=%async_computation.1 | async-start | bytes 4718592
  41.2 2.4 %copy-start.1 = (bf16[384,5120]{1,0:T(8,128)(2,1)}, bf16[384,5120]{1,0:T(8,128)(2,1)S(1)}, u32[]{:S(2)}) copy-start(bf16[384,5120]{1,0:T(8,128)(2,1)S(1)} %fusion.2) | copy-start | bytes 11796484
  41.2 1.3 %copy-start.10 = (f32[64]{0:T(128)S(1)}, f32[64]{0:T(128)}, u32[]{:S(2)}) copy-start(f32[64]{0:T(128)} %multiply_exponential_fusion) | copy-start | bytes 772
  41.2 2.4 %copy-start.15 = (f32[640]{0:T(1024)S(1)}, f32[640]{0:T(1024)}, u32[]{:S(2)}) copy-start(f32[640]{0:T(1024)} %param.23) | copy-start | bytes 7684
  43.6 3.7 %copy-start.13 = (f32[128]{0:T(128)S(1)}, f32[128]{0:T(128)}, u32[]{:S(2)}) copy-start(f32[128]{0:T(128)} %param.27) | copy-start | bytes 1540
  47.3 4.0 %copy-start.6 = (bf16[384,64]{0,1:T(8,128)(2,1)S(1)}, bf16[384,64]{0,1:T(8,128)(2,1)}, u32[]{:S(2)}) copy-start(bf16[384,64]{0,1:T(8,128)(2,1)} %get-tuple-element.36) | copy-start | bytes 147460
  47.3 4.0 %copy-start.7 = (bf16[384,64]{0,1:T(8,128)(2,1)S(1)}, bf16[384,64]{0,1:T(8,128)(2,1)}, u32[]{:S(2)}) copy-start(bf16[384,64]{0,1:T(8,128)(2,1)} %get-tuple-element.37) | copy-start | bytes 147460
  47.3 4.0 %copy-start.11 = (s32[384]{0:T(512)S(1)}, s32[384]{0:T(512)}, u32[]{:S(2)}) copy-start(s32[384]{0:T(512)} %eq.151) | copy-start | bytes 4612
  51.1 1.6 %copy-start.14 = (pred[8]{0:T(512)(128)(4,1)S(1)}, pred[8]{0:T(512)(128)(4,1)}, u32[]{:S(2)}) copy-start(pred[8]{0:T(512)(128)(4,1)} %compare_and_fusion.3) | copy-start | bytes 28
  51.9 22.4 %copy-start.9 = (s32[256]{0:T(256)S(1)}, s32[256]{0:T(256)}, u32[]{:S(2)}) copy-start(s32[256]{0:T(256)} %select_reduce_fusion) | copy-start | bytes 3076
  53.5 9.8 %collective-permute-start.6 = (bf16[48,896]{1,0:T(8,128)(2,1)S(1)}, bf16[48,896]{1,0:T(8,128)(2,1)S(1)}, u32[]{:S(2)}, u32[]{:S(2)}) collective-permute-start(bf16[48,896]{1,0:T(8,128)(2,1)S(1)} %get-tuple-element.32), channel_id=1, source_target_pairs={{0,4},{4,8},{8,12},{12,16},{16,20},{20,24},{24,28},{28,0},{1,5},{5... | collective-permute-start | bytes 258056 | tf_op jit(solution)/shard_map/ppermute | solution.py:213
  55.3 10.0 %collective-permute-start.7 = (bf16[48,896]{1,0:T(8,128)(2,1)S(1)}, bf16[48,896]{1,0:T(8,128)(2,1)S(1)}, u32[]{:S(2)}, u32[]{:S(2)}) collective-permute-start(bf16[48,896]{1,0:T(8,128)(2,1)S(1)} %get-tuple-element.31), channel_id=1, source_target_pairs={{0,8},{4,12},{8,16},{12,20},{16,24},{20,28},{24,0},{28,4},{1,9},{5... | collective-permute-start | bytes 258056 | tf_op jit(solution)/shard_map/ppermute | solution.py:213
  56.9 11.3 %collective-permute-start.8 = (bf16[48,896]{1,0:T(8,128)(2,1)S(1)}, bf16[48,896]{1,0:T(8,128)(2,1)S(1)}, u32[]{:S(2)}, u32[]{:S(2)}) collective-permute-start(bf16[48,896]{1,0:T(8,128)(2,1)S(1)} %get-tuple-element.30), channel_id=1, source_target_pairs={{0,12},{4,16},{8,20},{12,24},{16,28},{20,0},{24,4},{28,8},{1,13},{... | collective-permute-start | bytes 258056 | tf_op jit(solution)/shard_map/ppermute | solution.py:213
  59.5 9.7 %collective-permute-start.9 = (bf16[48,896]{1,0:T(8,128)(2,1)S(1)}, bf16[48,896]{1,0:T(8,128)(2,1)S(1)}, u32[]{:S(2)}, u32[]{:S(2)}) collective-permute-start(bf16[48,896]{1,0:T(8,128)(2,1)S(1)} %get-tuple-element.29), channel_id=1, source_target_pairs={{0,16},{4,20},{8,24},{12,28},{16,0},{20,4},{24,8},{28,12},{1,17},{... | collective-permute-start | bytes 258056 | tf_op jit(solution)/shard_map/ppermute | solution.py:213
  60.7 9.2 %collective-permute-start.10 = (bf16[48,896]{1,0:T(8,128)(2,1)S(1)}, bf16[48,896]{1,0:T(8,128)(2,1)S(1)}, u32[]{:S(2)}, u32[]{:S(2)}) collective-permute-start(bf16[48,896]{1,0:T(8,128)(2,1)S(1)} %get-tuple-element.28), channel_id=1, source_target_pairs={{0,20},{4,24},{8,28},{12,0},{16,4},{20,8},{24,12},{28,16},{1,21},{... | collective-permute-start | bytes 258056 | tf_op jit(solution)/shard_map/ppermute | solution.py:213
  63.3 7.7 %collective-permute-start.11 = (bf16[48,896]{1,0:T(8,128)(2,1)S(1)}, bf16[48,896]{1,0:T(8,128)(2,1)S(1)}, u32[]{:S(2)}, u32[]{:S(2)}) collective-permute-start(bf16[48,896]{1,0:T(8,128)(2,1)S(1)} %get-tuple-element.27), channel_id=1, source_target_pairs={{0,24},{4,28},{8,0},{12,4},{16,8},{20,12},{24,16},{28,20},{1,25},{... | collective-permute-start | bytes 258056 | tf_op jit(solution)/shard_map/ppermute | solution.py:213
  65.3 6.3 %collective-permute-start.12 = (bf16[48,896]{1,0:T(8,128)(2,1)S(1)}, bf16[48,896]{1,0:T(8,128)(2,1)S(1)}, u32[]{:S(2)}, u32[]{:S(2)}) collective-permute-start(bf16[48,896]{1,0:T(8,128)(2,1)S(1)} %get-tuple-element.26), channel_id=1, source_target_pairs={{0,28},{4,0},{8,4},{12,8},{16,12},{20,16},{24,20},{28,24},{1,29},{... | collective-permute-start | bytes 258056 | tf_op jit(solution)/shard_map/ppermute | solution.py:213
  79.8 1.5 %copy-start.2 = (f32[128,5120]{1,0:T(8,128)}, f32[128,5120]{1,0:T(8,128)S(1)}, u32[]{:S(2)}) copy-start(f32[128,5120]{1,0:T(8,128)S(1)} %fusion.76) | copy-start | bytes 7864324
  81.5 8.2 %collective-permute-start.15 = (f32[2,128,1280]{2,1,0:T(8,128)S(1)}, f32[2,128,1280]{2,1,0:T(8,128)}, u32[]{:S(2)}, u32[]{:S(2)}) collective-permute-start(f32[2,128,1280]{2,1,0:T(8,128)S(1)} %pad_maximum_fusion.2), channel_id=1, source_target_pairs={{0,1},{1,0},{2,3},{3,2},{4,5},{5,4},{6,7},{7,6},{8,9},{9,8},{10,11... | collective-permute-start | bytes 3932168 | tf_op jit(solution)/shard_map/ppermute | solution.py:233
  86.4 1.5 %copy-start.3 = (f32[128,5120]{1,0:T(8,128)}, f32[128,5120]{1,0:T(8,128)S(1)}, u32[]{:S(2)}) copy-start(f32[128,5120]{1,0:T(8,128)S(1)} %fusion.75) | copy-start | bytes 7864324
  89.2 4.5 %collective-permute-start.13 = (f32[2,128,1280]{2,1,0:T(8,128)}, f32[2,128,1280]{2,1,0:T(8,128)}, u32[]{:S(2)}, u32[]{:S(2)}) collective-permute-start(f32[2,128,1280]{2,1,0:T(8,128)} %pad_maximum_fusion.1), channel_id=1, source_target_pairs={{0,1},{1,0},{2,3},{3,2},{4,5},{5,4},{6,7},{7,6},{8,9},{9,8},{10,11... | collective-permute-start | bytes 3932168 | tf_op jit(solution)/shard_map/ppermute | solution.py:233
  89.7 4.0 %copy-start.4 = (f32[128,5120]{1,0:T(8,128)S(1)}, f32[128,5120]{1,0:T(8,128)}, u32[]{:S(2)}) copy-start(f32[128,5120]{1,0:T(8,128)} %copy-done.3) | copy-start | bytes 7864324
  92.2 17.7 %collective-permute-start.16 = (f32[1,128,1280]{2,1,0:T(8,128)S(1)}, f32[1,128,1280]{2,1,0:T(8,128)S(1)}, u32[]{:S(2)}, u32[]{:S(2)}) collective-permute-start(f32[1,128,1280]{2,1,0:T(8,128)S(1)} %get-tuple-element.11), channel_id=1, source_target_pairs={{0,2},{1,3},{2,0},{3,1},{4,6},{5,7},{6,4},{7,5},{8,10},{9,11},{10,... | collective-permute-start | bytes 1966088 | tf_op jit(solution)/shard_map/ppermute | solution.py:233
  95.4 27.6 %collective-permute-start.14 = (f32[1,128,1280]{2,1,0:T(8,128)S(1)}, f32[1,128,1280]{2,1,0:T(8,128)S(1)}, u32[]{:S(2)}, u32[]{:S(2)}) collective-permute-start(f32[1,128,1280]{2,1,0:T(8,128)S(1)} %get-tuple-element.6), channel_id=1, source_target_pairs={{0,2},{1,3},{2,0},{3,1},{4,6},{5,7},{6,4},{7,5},{8,10},{9,11},{10,... | collective-permute-start | bytes 1966088 | tf_op jit(solution)/shard_map/ppermute | solution.py:233

commit v9 on v8

--- a/solution.py
+++ b/solution.py
@@ -110,13 +110,14 @@
         query_matrix = (
             jnp.dot(normalized_input, w_query, preferred_element_type=jnp.float32) + q_bias
         )
-        query_matrix = apply_rotary(
-            query_matrix.reshape(count, local_heads, head_dim), starts, head_dim
-        ).astype(jnp.bfloat16)
         key_rows = (
             jnp.dot(normalized_input, key_projection_weight, preferred_element_type=jnp.float32)
             + key_bias_vector
         )
+        query_matrix, key_rows = lax.optimization_barrier((query_matrix, key_rows))
+        query_matrix = apply_rotary(
+            query_matrix.reshape(count, local_heads, head_dim), starts, head_dim
+        ).astype(jnp.bfloat16)
         key_rows = apply_rotary(
             key_rows.reshape(count, local_kv, head_dim), starts, head_dim
         ).astype(jnp.bfloat16)
@@ -135,7 +136,16 @@
 
     qkv = project(jnp.concatenate(pieces, axis=0), sequence_starts)
 
-    places = to_work_order(send_places(my_dest, ctx_count, group_cap, pack_len))
+    shift_order = ctx_count <= 8
+    if shift_order:
+        shifted_dest = jnp.where(
+            my_dest >= 0,
+            ((my_dest // pack_len - ctx_index) % ctx_count) * pack_len + my_dest % pack_len,
+            -1,
+        )
+    else:
+        shifted_dest = my_dest
+    places = to_work_order(send_places(shifted_dest, ctx_count, group_cap, pack_len))
     send_hot = (
         places[None, :] == jnp.arange(ctx_count * group_cap, dtype=jnp.int32)[:, None]
     ).astype(jnp.bfloat16)
@@ -145,8 +155,11 @@
     mine = (pool_dest >= 0) & (pool_dest // pack_len == ctx_index)
     mine_grid = mine.reshape(ctx_count, group_rows).astype(jnp.int32)
     rank_in = jnp.cumsum(mine_grid, axis=1) - mine_grid
+    source_ctx = jnp.arange(ctx_count, dtype=jnp.int32)[:, None]
+    if shift_order:
+        source_ctx = (ctx_index - source_ctx) % ctx_count
     arrived_index = (
-        jnp.arange(ctx_count, dtype=jnp.int32)[:, None] * group_cap + rank_in
+        source_ctx * group_cap + rank_in
     ).reshape(-1)
     my_slot_of_row = jnp.where(mine, pool_dest - ctx_index * pack_len, -1)
     slot_ids = jnp.arange(pack_len, dtype=jnp.int32)
@@ -167,7 +180,7 @@
     segment = jnp.sum((own_ends[None, :] <= slot_ids[:, None]).astype(jnp.int32), axis=1)
 
     score_scale = 1.0 / math.sqrt(head_dim)
-    chunk_count = 2 if pack_len % 16 == 0 else 1
+    chunk_count = 4 if pack_len % 32 == 0 else 1
     chunk_len = pack_len // chunk_count
     results = []
     for chunk in range(chunk_count):
@@ -204,16 +217,12 @@
 def exchange(outgoing, axis_name, count):
     if count > 8:
         return lax.all_to_all(outgoing, axis_name, split_axis=0, concat_axis=0, tiled=True)
-    me = lax.axis_index(axis_name)
     chunks = outgoing.reshape((count, -1) + outgoing.shape[1:])
-    by_shift = jnp.take(chunks, (me + jnp.arange(count)) % count, axis=0)
-    from_shift = [by_shift[0]]
+    arrived = [chunks[0]]
     for shift in range(1, count):
         pairs = [(i, (i + shift) % count) for i in range(count)]
-        from_shift.append(lax.ppermute(by_shift[shift], axis_name, pairs))
-    from_shift = jnp.stack(from_shift)
-    arrived = jnp.take(from_shift, (me - jnp.arange(count)) % count, axis=0)
-    return arrived.reshape(outgoing.shape)
+        arrived.append(lax.ppermute(chunks[shift], axis_name, pairs))
+    return jnp.concatenate(arrived, axis=0)
 
 
 def halving_scatter(partial, axis_name, count):

time: 125 us -> 118 us (0.944)
  the two profiles are of different devices: /device:TPU:0 before, /device:TPU:20 now
where the time goes in v9:
time: 118 us; the launch traced here: 117 us
  waiting for transfers between devices  48.3 us (41%)
  other arithmetic  21 us (18%)
  matrix products  19.5 us (17%)
  starting transfers between devices  17.4 us (15%)
  local copies, waits for them, and re-layouts  10.3 us (9%)
    ppermute x8, waiting for transfers between devices, halving_scatter(): got = lax.ppermute(send, axis_name, pairs)  25.9 us
    ppermute x7, waiting for transfers between devices, exchange(): arrived.append(lax.ppermute(chunks[shift], axis_name, pairs))  11.9 us
    dot_general x4, matrix products, local(): jnp.dot(mixed_heads, w_out, preferred_element_type=jnp.float32)  8.08 us
    ppermute x7, starting transfers between devices, exchange(): arrived.append(lax.ppermute(chunks[shift], axis_name, pairs))  7.81 us
    ppermute x3, waiting for transfers between devices, xor_gather(): pieces = pieces + [lax.ppermute(p, axis_name, pairs) for p in pieces]  6.08 us
    ppermute x8, starting transfers between devices, halving_scatter(): got = lax.ppermute(send, axis_name, pairs)  5.59 us
    convert_element_type x1, other arithmetic, project(): normalized_input = (values_wide * lax.rsqrt(jnp.mean(values_wide * values...  4.65 us
    ppermute x3, waiting for transfers between devices, doubling_gather(): got = lax.ppermute(have, axis_name, pairs)  4.4 us
  transfers between devices with their start and end apart: 21, of which 10 were waited for; matrix products, arithmetic and copies ran while one was open for 22% of the time, Pallas kernels for 0%

profile of v9, /device:TPU:20, one launch (start us, length us, event | category | flops | bytes accessed | tf_op | source)
XLA Modules:
  0.0 117.2 jit_solution(6746018777367696398)
XLA Ops:
  0.0 1.5 %collective-permute-start = (bf16[96,5120]{1,0:T(8,128)(2,1)}, bf16[96,5120]{1,0:T(8,128)(2,1)S(1)}, u32[]{:S(2)}, u32[]{:S(2)}) collective-permute-start(bf16[96,5120]{1,0:T(8,128)(2,1)} %param.16), channel_id=1, source_target_pairs={{0,2},{1,3},{2,0},{3,1},{4,6},{5,7},{6,4},{7,5},{8,10},{9,11},{10,... | collective-permute-start | bytes 2949128 | tf_op jit(solution)/shard_map/ppermute | solution.py:271
  1.5 0.3 collective-permute-start.3
  1.8 0.6 multiply_exponential_fusion
  2.4 0.7 reshape.750
  3.3 0.8 reduce-window.32
  4.3 0.5 slice.252
  4.8 0.5 slice.253
  5.3 0.6 slice.254
  5.9 0.8 reduce-window.30
  7.5 0.7 compare_and_fusion.5
  8.3 0.6 gather_fusion.1
  8.8 0.6 gather_fusion
  9.6 0.7 subtract_select_fusion
  10.4 0.9 reduce-window.21
  11.7 0.7 fusion.78
  12.6 0.7 compare_and_fusion.1
  13.4 0.7 fusion.117
  14.1 1.6 %collective-permute-start.4 = (s32[2,1,8]{2,0,1:T(2,128)S(1)}, s32[2,1,8]{2,0,1:T(2,128)S(1)}, u32[]{:S(2)}, u32[]{:S(2)}) collective-permute-start(s32[2,1,8]{2,0,1:T(2,128)S(1)} %bitcast.305), channel_id=1, source_target_pairs={{0,8},{4,12},{8,0},{12,4},{16,24},{20,28},{24,16},{28,20},{1,9},{5... | collective-permute-start | bytes 200 | tf_op jit(solution)/shard_map/ppermute | solution.py:256
  15.6 2.0 %collective-permute-done.4 = s32[2,1,8]{2,0,1:T(2,128)S(1)} collective-permute-done((s32[2,1,8]{2,0,1:T(2,128)S(1)}, s32[2,1,8]{2,0,1:T(2,128)S(1)}, u32[]{:S(2)}, u32[]{:S(2)}) %collective-permute-start.4) | collective-permute-done | bytes 96 | tf_op jit(solution)/shard_map/ppermute | solution.py:256
  17.6 6.1 %collective-permute-done = bf16[96,5120]{1,0:T(8,128)(2,1)S(1)} collective-permute-done((bf16[96,5120]{1,0:T(8,128)(2,1)}, bf16[96,5120]{1,0:T(8,128)(2,1)S(1)}, u32[]{:S(2)}, u32[]{:S(2)}) %collective-permute-start) | collective-permute-done | bytes 983072 | tf_op jit(solution)/shard_map/ppermute | solution.py:271
  23.7 0.6 collective-permute-start.5
  24.3 0.7 eq.198
  25.0 2.4 %collective-permute-done.5 = s32[4,1,8]{2,0,1:T(4,128)S(1)} collective-permute-done((s32[4,1,8]{2,0,1:T(4,128)S(1)}, s32[4,1,8]{2,0,1:T(4,128)S(1)}, u32[]{:S(2)}, u32[]{:S(2)}) %collective-permute-start.5) | collective-permute-done | bytes 160 | tf_op jit(solution)/shard_map/ppermute | solution.py:256
  27.6 1.1 gather_fusion.3
  28.7 1.6 %gather_fusion.2 = s32[384,8]{1,0:T(8,128)} fusion(s32[8,8]{1,0:T(8,128)S(1)} %reduce_window_sum.54, s32[1024]{0:T(1024)S(1)} %pad_clamp_fusion), kind=kCustom, calls=%fused_computation.1.clone | custom fusion | bytes 26112 | tf_op jit(solution)/shard_map/jit(_take)/gather | solution.py:93
  30.3 1.2 %fusion.48 = s32[384]{0:T(512)S(1)} fusion(s32[384,8]{1,0:T(8,128)S(1)} %gather_fusion.3, s32[384,8]{1,0:T(8,128)} %gather_fusion.2, s32[384]{0:T(512)S(1)} %fusion.107, pred[384]{0:T(512)(128)(4,1)S(1)} %get-tuple-element.25), kind=kLoop, calls=%fused_computation.112 | loop fusion | flops 14976 | bytes 28032 | tf_op jit(solution)/shard_map/reduce_sum | solution.py:96
  31.5 1.1 multiply_cosine_fusion.1
  32.6 2.3 %fusion = f32[384]{0:T(512)S(1)} fusion(bf16[96,5120]{1,0:T(8,128)(2,1)} %collective-permute-done.2, bf16[96,5120]{1,0:T(8,128)(2,1)} %collective-permute-done.1, bf16[96,5120]{1,0:T(8,128)(2,1)S(1)} %collective-permute-done, bf16[96,5120]{1,0:T(8,128)(2,1)S(1)} %copy-done.2), kind=kLoop, calls=%fused_computation.6 | loop fusion | flops 19660416 | bytes 3933696 | tf_op jit(solution)/shard_map/reduce_sum | solution.py:107
  34.9 4.7 %fusion.2 = bf16[384,5120]{1,0:T(8,128)(2,1)S(1)} fusion(f32[5120]{0:T(1024)S(1)} %copy-done.5, f32[384]{0:T(512)S(1)} %add_rsqrt_fusion, bf16[96,5120]{1,0:T(8,128)(2,1)} %collective-permute-done.2, bf16[96,5120]{1,0:T(8,128)(2,1)} %collective-permute-done.1, bf16[96,5120]{1,0:T(8,128)(2,1)S(1)} %collective-permute-done, bf16[96,5120]{1,0:T(8,128)(2,1)S(1)} %copy-done.2), kind=kLoop, calls=%fused_computation.8 | loop fusion | flops 21626880 | bytes 7886336 | tf_op jit(solution)/shard_map/convert_element_type | solution.py:109
  39.7 3.3 %convolution_add_fusion = f32[384,640]{1,0:T(8,128)S(1)} fusion(bf16[384,5120]{1,0:T(8,128)(2,1)S(1)} %fusion.2, bf16[5120,640]{1,0:T(8,128)(2,1)S(1)} %bitcast.311, f32[640]{0:T(1024)S(1)} %copy-done.11), kind=kOutput, calls=%fused_computation.13 | convolution fusion | flops 2516828160 | bytes 11471360 | tf_op jit(solution)/shard_map/dot_general | solution.py:111
  43.0 1.2 %convolution_add_fusion.2 = f32[384,128]{1,0:T(8,128)S(1)} fusion(bf16[384,5120]{1,0:T(8,128)(2,1)S(1)} %fusion.2, bf16[5120,128]{1,0:T(8,128)(2,1)S(1)} %copy-done, f32[128]{0:T(128)S(1)} %copy-done.7), kind=kOutput, calls=%fused_computation.20 | convolution fusion | flops 503365632 | bytes 5440000 | tf_op jit(solution)/shard_map/dot_general | solution.py:114
  44.2 0.8 fusion.55
  45.1 0.7 copy.44
  45.8 0.7 copy.43
  46.5 0.3 copy.40
  46.9 3.8 %fusion.9 = bf16[384,128]{0,1:T(8,128)(2,1)S(1)} fusion(bf16[384,5120]{1,0:T(8,128)(2,1)} %copy-done.1, bf16[5120,128]{1,0:T(8,128)(2,1)} %param.24, f32[128]{0:T(128)S(1)} %copy-done.10), kind=kOutput, calls=%fused_computation.27 | convolution fusion | flops 503414784 | bytes 5341696 | tf_op jit(solution)/shard_map/dot_general | solution.py:125
  50.9 0.6 convolution_convert_fusion
  51.5 1.6 %collective-permute-start.6 = (bf16[48,896]{1,0:T(8,128)(2,1)S(1)}, bf16[48,896]{1,0:T(8,128)(2,1)S(1)}, u32[]{:S(2)}, u32[]{:S(2)}) collective-permute-start(bf16[48,896]{1,0:T(8,128)(2,1)S(1)} %get-tuple-element.45), channel_id=1, source_target_pairs={{0,4},{4,8},{8,12},{12,16},{16,20},{20,24},{24,28},{28,0},{1,5},{5... | collective-permute-start | bytes 258056 | tf_op jit(solution)/shard_map/ppermute | solution.py:224
  53.1 0.4 select_reduce_fusion
  53.6 1.8 %collective-permute-start.8 = (bf16[48,896]{1,0:T(8,128)(2,1)S(1)}, bf16[48,896]{1,0:T(8,128)(2,1)S(1)}, u32[]{:S(2)}, u32[]{:S(2)}) collective-permute-start(bf16[48,896]{1,0:T(8,128)(2,1)S(1)} %get-tuple-element.43), channel_id=1, source_target_pairs={{0,12},{4,16},{8,20},{12,24},{16,28},{20,0},{24,4},{28,8},{1,13},{... | collective-permute-start | bytes 258056 | tf_op jit(solution)/shard_map/ppermute | solution.py:224
  55.4 2.6 %collective-permute-start.9 = (bf16[48,896]{1,0:T(8,128)(2,1)S(1)}, bf16[48,896]{1,0:T(8,128)(2,1)S(1)}, u32[]{:S(2)}, u32[]{:S(2)}) collective-permute-start(bf16[48,896]{1,0:T(8,128)(2,1)S(1)} %get-tuple-element.42), channel_id=1, source_target_pairs={{0,16},{4,20},{8,24},{12,28},{16,0},{20,4},{24,8},{28,12},{1,17},{... | collective-permute-start | bytes 258056 | tf_op jit(solution)/shard_map/ppermute | solution.py:224
  58.0 1.3 %collective-permute-start.10 = (bf16[48,896]{1,0:T(8,128)(2,1)S(1)}, bf16[48,896]{1,0:T(8,128)(2,1)S(1)}, u32[]{:S(2)}, u32[]{:S(2)}) collective-permute-start(bf16[48,896]{1,0:T(8,128)(2,1)S(1)} %get-tuple-element.41), channel_id=1, source_target_pairs={{0,20},{4,24},{8,28},{12,0},{16,4},{20,8},{24,12},{28,16},{1,21},{... | collective-permute-start | bytes 258056 | tf_op jit(solution)/shard_map/ppermute | solution.py:224
  59.3 0.5 collective-permute-start.11
  59.8 6.6 %collective-permute-done.7 = bf16[48,896]{1,0:T(8,128)(2,1)S(1)} collective-permute-done((bf16[48,896]{1,0:T(8,128)(2,1)S(1)}, bf16[48,896]{1,0:T(8,128)(2,1)S(1)}, u32[]{:S(2)}, u32[]{:S(2)}) %collective-permute-start.7) | collective-permute-done | bytes 86048 | tf_op jit(solution)/shard_map/ppermute | solution.py:224
  66.5 1.0 collective-permute-done.11
  67.5 4.3 %collective-permute-done.12 = bf16[48,896]{1,0:T(8,128)(2,1)S(1)} collective-permute-done((bf16[48,896]{1,0:T(8,128)(2,1)S(1)}, bf16[48,896]{1,0:T(8,128)(2,1)S(1)}, u32[]{:S(2)}, u32[]{:S(2)}) %collective-permute-start.12) | collective-permute-done | bytes 86048 | tf_op jit(solution)/shard_map/ppermute | solution.py:224
  71.8 0.5 convolution_convert_fusion.1
  73.2 4.3 %fusion.56 = f32[64,5120]{1,0:T(8,128)S(1)} fusion(bf16[640,5120]{1,0:T(8,128)(2,1)} %param.26, bf16[8,8,5,128]{3,2,1,0:T(8,128)(2,1)S(1)} %bitcast.295), kind=kOutput, calls=%fused_computation.129 | convolution fusion | flops 419430400 | bytes 7946240 | tf_op jit(solution)/shard_map/dot_general | solution.py:212
  77.7 0.3 fusion.133
  78.2 0.3 fusion.12
  78.6 1.3 %fusion.59 = f32[64,5120]{1,0:T(8,128)S(1)} fusion(bf16[640,5120]{1,0:T(8,128)(2,1)S(1)} %bitcast.292, bf16[8,8,5,128]{3,2,1,0:T(8,128)(2,1)S(1)} %bitcast.296), kind=kOutput, calls=%fused_computation.132 | convolution fusion | flops 419430400 | bytes 7946240 | tf_op jit(solution)/shard_map/dot_general | solution.py:212
  80.0 0.6 collective-permute-start.17
  81.4 1.3 %fusion.62 = f32[64,5120]{1,0:T(8,128)S(1)} fusion(bf16[640,5120]{1,0:T(8,128)(2,1)S(1)} %bitcast.292, bf16[8,8,5,128]{3,2,1,0:T(8,128)(2,1)S(1)} %bitcast.297), kind=kOutput, calls=%fused_computation.135 | convolution fusion | flops 419430400 | bytes 7946240 | tf_op jit(solution)/shard_map/dot_general | solution.py:212
  83.4 1.3 %fusion.65 = f32[64,5120]{1,0:T(8,128)S(1)} fusion(bf16[640,5120]{1,0:T(8,128)(2,1)S(1)} %bitcast.292, bf16[8,8,5,128]{3,2,1,0:T(8,128)(2,1)S(1)} %bitcast.298), kind=kOutput, calls=%fused_computation.138 | convolution fusion | flops 419430400 | bytes 7946240 | tf_op jit(solution)/shard_map/dot_general | solution.py:212
  84.8 0.6 collective-permute-start.13
  85.5 1.6 %collective-permute-start.20 = (f32[1,64,1280]{2,1,0:T(8,128)S(1)}, f32[1,64,1280]{2,1,0:T(8,128)S(1)}, u32[]{:S(2)}, u32[]{:S(2)}) collective-permute-start(f32[1,64,1280]{2,1,0:T(8,128)S(1)} %get-tuple-element.20), channel_id=1, source_target_pairs={{0,2},{1,3},{2,0},{3,1},{4,6},{5,7},{6,4},{7,5},{8,10},{9,11},{10,... | collective-permute-start | bytes 983048 | tf_op jit(solution)/shard_map/ppermute | solution.py:242
  87.1 0.6 collective-permute-start.18
  87.9 1.6 %collective-permute-start.16 = (f32[1,64,1280]{2,1,0:T(8,128)S(1)}, f32[1,64,1280]{2,1,0:T(8,128)S(1)}, u32[]{:S(2)}, u32[]{:S(2)}) collective-permute-start(f32[1,64,1280]{2,1,0:T(8,128)S(1)} %get-tuple-element.14), channel_id=1, source_target_pairs={{0,2},{1,3},{2,0},{3,1},{4,6},{5,7},{6,4},{7,5},{8,10},{9,11},{10,... | collective-permute-start | bytes 983048 | tf_op jit(solution)/shard_map/ppermute | solution.py:242
  89.6 0.6 collective-permute-start.14
  90.2 6.0 %collective-permute-done.20 = f32[1,64,1280]{2,1,0:T(8,128)S(1)} collective-permute-done((f32[1,64,1280]{2,1,0:T(8,128)S(1)}, f32[1,64,1280]{2,1,0:T(8,128)S(1)}, u32[]{:S(2)}, u32[]{:S(2)}) %collective-permute-start.20) | collective-permute-done | bytes 327712 | tf_op jit(solution)/shard_map/ppermute | solution.py:242
  96.2 7.0 %collective-permute-done.18 = f32[1,64,1280]{2,1,0:T(8,128)S(1)} collective-permute-done((f32[1,64,1280]{2,1,0:T(8,128)S(1)}, f32[1,64,1280]{2,1,0:T(8,128)S(1)}, u32[]{:S(2)}, u32[]{:S(2)}) %collective-permute-start.18) | collective-permute-done | bytes 327712 | tf_op jit(solution)/shard_map/ppermute | solution.py:242
  103.2 7.0 %collective-permute-done.16 = f32[1,64,1280]{2,1,0:T(8,128)S(1)} collective-permute-done((f32[1,64,1280]{2,1,0:T(8,128)S(1)}, f32[1,64,1280]{2,1,0:T(8,128)S(1)}, u32[]{:S(2)}, u32[]{:S(2)}) %collective-permute-start.16) | collective-permute-done | bytes 327712 | tf_op jit(solution)/shard_map/ppermute | solution.py:242
  110.2 6.0 %collective-permute-done.14 = f32[1,64,1280]{2,1,0:T(8,128)S(1)} collective-permute-done((f32[1,64,1280]{2,1,0:T(8,128)S(1)}, f32[1,64,1280]{2,1,0:T(8,128)S(1)}, u32[]{:S(2)}, u32[]{:S(2)}) %collective-permute-start.14) | collective-permute-done | bytes 327712 | tf_op jit(solution)/shard_map/ppermute | solution.py:242
  116.3 0.9 pad_maximum_fusion.5
  (143 shorter events, 6.6 us)
Async XLA Ops:
  0.0 43.0 %copy-start = (bf16[5120,128]{1,0:T(8,128)(2,1)S(1)}, bf16[5120,128]{1,0:T(8,128)(2,1)}, u32[]{:S(2)}) copy-start(bf16[5120,128]{1,0:T(8,128)(2,1)} %param.22) | copy-start | bytes 3932164
  0.0 32.6 %copy-start.2 = (bf16[96,5120]{1,0:T(8,128)(2,1)S(1)}, bf16[96,5120]{1,0:T(8,128)(2,1)}, u32[]{:S(2)}) copy-start(bf16[96,5120]{1,0:T(8,128)(2,1)} %param.16) | copy-start | bytes 2949124
  0.0 23.7 %collective-permute-start = (bf16[96,5120]{1,0:T(8,128)(2,1)}, bf16[96,5120]{1,0:T(8,128)(2,1)S(1)}, u32[]{:S(2)}, u32[]{:S(2)}) collective-permute-start(bf16[96,5120]{1,0:T(8,128)(2,1)} %param.16), channel_id=1, source_target_pairs={{0,2},{1,3},{2,0},{3,1},{4,6},{5,7},{6,4},{7,5},{8,10},{9,11},{10,... | collective-permute-start | bytes 2949128 | tf_op jit(solution)/shard_map/ppermute | solution.py:271
  1.5 31.1 %collective-permute-start.1 = (bf16[96,5120]{1,0:T(8,128)(2,1)}, bf16[96,5120]{1,0:T(8,128)(2,1)}, u32[]{:S(2)}, u32[]{:S(2)}) collective-permute-start(bf16[96,5120]{1,0:T(8,128)(2,1)} %param.16), channel_id=1, source_target_pairs={{0,1},{1,0},{2,3},{3,2},{4,5},{5,4},{6,7},{7,6},{8,9},{9,8},{10,11... | collective-permute-start | bytes 2949128 | tf_op jit(solution)/shard_map/ppermute | solution.py:271
  1.5 11.9 %collective-permute-start.3 = (s32[1,1,8]{2,1,0:T(1,128)}, s32[1,1,8]{2,1,0:T(1,128)}, u32[]{:S(2)}, u32[]{:S(2)}) collective-permute-start(s32[1,1,8]{2,1,0:T(1,128)} %bitcast.308), channel_id=1, source_target_pairs={{0,16},{4,20},{8,24},{12,28},{16,0},{20,4},{24,8},{28,12},{1,17},{... | collective-permute-start | bytes 104 | tf_op jit(solution)/shard_map/ppermute | solution.py:256
  14.1 3.6 %collective-permute-start.4 = (s32[2,1,8]{2,0,1:T(2,128)S(1)}, s32[2,1,8]{2,0,1:T(2,128)S(1)}, u32[]{:S(2)}, u32[]{:S(2)}) collective-permute-start(s32[2,1,8]{2,0,1:T(2,128)S(1)} %bitcast.305), channel_id=1, source_target_pairs={{0,8},{4,12},{8,0},{12,4},{16,24},{20,28},{24,16},{28,20},{1,9},{5... | collective-permute-start | bytes 200 | tf_op jit(solution)/shard_map/ppermute | solution.py:256
  23.7 8.9 %collective-permute-start.2 = (bf16[96,5120]{1,0:T(8,128)(2,1)S(1)}, bf16[96,5120]{1,0:T(8,128)(2,1)}, u32[]{:S(2)}, u32[]{:S(2)}) collective-permute-start(bf16[96,5120]{1,0:T(8,128)(2,1)S(1)} %collective-permute-done), channel_id=1, source_target_pairs={{0,1},{1,0},{2,3},{3,2},{4,5},{5,4},{6,7},{7,6},{8,9},{9,8},{10,11... | collective-permute-start | bytes 2949128 | tf_op jit(solution)/shard_map/ppermute | solution.py:271
  23.7 3.7 %collective-permute-start.5 = (s32[4,1,8]{2,0,1:T(4,128)S(1)}, s32[4,1,8]{2,0,1:T(4,128)S(1)}, u32[]{:S(2)}, u32[]{:S(2)}) collective-permute-start(s32[4,1,8]{2,0,1:T(4,128)S(1)} %bitcast.301), channel_id=1, source_target_pairs={{0,4},{4,0},{8,12},{12,8},{16,20},{20,16},{24,28},{28,24},{1,5},{5... | collective-permute-start | bytes 392 | tf_op jit(solution)/shard_map/ppermute | solution.py:256
  30.3 4.6 %copy-start.5 = (f32[5120]{0:T(1024)S(1)}, f32[5120]{0:T(1024)}, u32[]{:S(2)}) copy-start(f32[5120]{0:T(1024)} %param.19) | copy-start | bytes 61444
  32.6 7.0 %slice-start.2 = ((s8[6553600]{0:T(1024)(128)(4,1)}), s8[4194304]{0:T(1024)(128)(4,1)S(1)}, s32[]{:S(2)}) async-start(s8[6553600]{0:T(1024)(128)(4,1)} %bitcast.310), calls=%async_computation.2 | async-start | bytes 8388608
  34.9 4.7 %slice-start.3 = ((s8[6553600]{0:T(1024)(128)(4,1)}), s8[2359296]{0:T(1024)(128)(4,1)S(1)}, s32[]{:S(2)}) async-start(s8[6553600]{0:T(1024)(128)(4,1)} %bitcast.310), calls=%async_computation.3 | async-start | bytes 4718592
  34.9 4.7 %copy-start.11 = (f32[640]{0:T(1024)S(1)}, f32[640]{0:T(1024)}, u32[]{:S(2)}) copy-start(f32[640]{0:T(1024)} %param.21) | copy-start | bytes 7684
  39.6 3.3 %copy-start.1 = (bf16[384,5120]{1,0:T(8,128)(2,1)}, bf16[384,5120]{1,0:T(8,128)(2,1)S(1)}, u32[]{:S(2)}) copy-start(bf16[384,5120]{1,0:T(8,128)(2,1)S(1)} %fusion.2) | copy-start | bytes 11796484
  39.7 3.3 %copy-start.7 = (f32[128]{0:T(128)S(1)}, f32[128]{0:T(128)}, u32[]{:S(2)}) copy-start(f32[128]{0:T(128)} %param.23) | copy-start | bytes 1540
  43.0 1.2 %copy-start.9 = (f32[64]{0:T(128)S(1)}, f32[64]{0:T(128)}, u32[]{:S(2)}) copy-start(f32[64]{0:T(128)} %multiply_exponential_fusion) | copy-start | bytes 772
  43.0 3.8 %copy-start.10 = (f32[128]{0:T(128)S(1)}, f32[128]{0:T(128)}, u32[]{:S(2)}) copy-start(f32[128]{0:T(128)} %param.25) | copy-start | bytes 1540
  46.8 4.0 %copy-start.3 = (bf16[384,64]{0,1:T(8,128)(2,1)S(1)}, bf16[384,64]{0,1:T(8,128)(2,1)}, u32[]{:S(2)}) copy-start(bf16[384,64]{0,1:T(8,128)(2,1)} %copy.44) | copy-start | bytes 147460
  46.8 4.0 %copy-start.4 = (bf16[384,64]{0,1:T(8,128)(2,1)S(1)}, bf16[384,64]{0,1:T(8,128)(2,1)}, u32[]{:S(2)}) copy-start(bf16[384,64]{0,1:T(8,128)(2,1)} %copy.43) | copy-start | bytes 147460
  46.9 4.0 %copy-start.8 = (s32[384]{0:T(512)S(1)}, s32[384]{0:T(512)}, u32[]{:S(2)}) copy-start(s32[384]{0:T(512)} %eq.198) | copy-start | bytes 4612
  50.8 21.5 %copy-start.6 = (pred[64,256]{1,0:T(8,128)(4,1)S(1)}, pred[64,256]{1,0:T(8,128)(4,1)}, u32[]{:S(2)}) copy-start(pred[64,256]{1,0:T(8,128)(4,1)} %fusion.78) | copy-start | bytes 49156
  51.5 7.8 %collective-permute-start.6 = (bf16[48,896]{1,0:T(8,128)(2,1)S(1)}, bf16[48,896]{1,0:T(8,128)(2,1)S(1)}, u32[]{:S(2)}, u32[]{:S(2)}) collective-permute-start(bf16[48,896]{1,0:T(8,128)(2,1)S(1)} %get-tuple-element.45), channel_id=1, source_target_pairs={{0,4},{4,8},{8,12},{12,16},{16,20},{20,24},{24,28},{28,0},{1,5},{5... | collective-permute-start | bytes 258056 | tf_op jit(solution)/shard_map/ppermute | solution.py:224
  53.5 12.9 %collective-permute-start.7 = (bf16[48,896]{1,0:T(8,128)(2,1)S(1)}, bf16[48,896]{1,0:T(8,128)(2,1)S(1)}, u32[]{:S(2)}, u32[]{:S(2)}) collective-permute-start(bf16[48,896]{1,0:T(8,128)(2,1)S(1)} %get-tuple-element.44), channel_id=1, source_target_pairs={{0,8},{4,12},{8,16},{12,20},{16,24},{20,28},{24,0},{28,4},{1,9},{5... | collective-permute-start | bytes 258056 | tf_op jit(solution)/shard_map/ppermute | solution.py:224
  53.6 12.8 %collective-permute-start.8 = (bf16[48,896]{1,0:T(8,128)(2,1)S(1)}, bf16[48,896]{1,0:T(8,128)(2,1)S(1)}, u32[]{:S(2)}, u32[]{:S(2)}) collective-permute-start(bf16[48,896]{1,0:T(8,128)(2,1)S(1)} %get-tuple-element.43), channel_id=1, source_target_pairs={{0,12},{4,16},{8,20},{12,24},{16,28},{20,0},{24,4},{28,8},{1,13},{... | collective-permute-start | bytes 258056 | tf_op jit(solution)/shard_map/ppermute | solution.py:224
  55.4 11.0 %collective-permute-start.9 = (bf16[48,896]{1,0:T(8,128)(2,1)S(1)}, bf16[48,896]{1,0:T(8,128)(2,1)S(1)}, u32[]{:S(2)}, u32[]{:S(2)}) collective-permute-start(bf16[48,896]{1,0:T(8,128)(2,1)S(1)} %get-tuple-element.42), channel_id=1, source_target_pairs={{0,16},{4,20},{8,24},{12,28},{16,0},{20,4},{24,8},{28,12},{1,17},{... | collective-permute-start | bytes 258056 | tf_op jit(solution)/shard_map/ppermute | solution.py:224
  58.0 8.5 %collective-permute-start.10 = (bf16[48,896]{1,0:T(8,128)(2,1)S(1)}, bf16[48,896]{1,0:T(8,128)(2,1)S(1)}, u32[]{:S(2)}, u32[]{:S(2)}) collective-permute-start(bf16[48,896]{1,0:T(8,128)(2,1)S(1)} %get-tuple-element.41), channel_id=1, source_target_pairs={{0,20},{4,24},{8,28},{12,0},{16,4},{20,8},{24,12},{28,16},{1,21},{... | collective-permute-start | bytes 258056 | tf_op jit(solution)/shard_map/ppermute | solution.py:224
  59.3 8.2 %collective-permute-start.11 = (bf16[48,896]{1,0:T(8,128)(2,1)S(1)}, bf16[48,896]{1,0:T(8,128)(2,1)S(1)}, u32[]{:S(2)}, u32[]{:S(2)}) collective-permute-start(bf16[48,896]{1,0:T(8,128)(2,1)S(1)} %get-tuple-element.40), channel_id=1, source_target_pairs={{0,24},{4,28},{8,0},{12,4},{16,8},{20,12},{24,16},{28,20},{1,25},{... | collective-permute-start | bytes 258056 | tf_op jit(solution)/shard_map/ppermute | solution.py:224
  66.4 5.4 %collective-permute-start.12 = (bf16[48,896]{1,0:T(8,128)(2,1)S(1)}, bf16[48,896]{1,0:T(8,128)(2,1)S(1)}, u32[]{:S(2)}, u32[]{:S(2)}) collective-permute-start(bf16[48,896]{1,0:T(8,128)(2,1)S(1)} %get-tuple-element.39), channel_id=1, source_target_pairs={{0,28},{4,0},{8,4},{12,8},{16,12},{20,16},{24,20},{28,24},{1,29},{... | collective-permute-start | bytes 258056 | tf_op jit(solution)/shard_map/ppermute | solution.py:224
  73.2 5.4 %slice-start = ((s8[6553600]{0:T(1024)(128)(4,1)}), s8[4194304]{0:T(1024)(128)(4,1)S(1)}, s32[]{:S(2)}) async-start(s8[6553600]{0:T(1024)(128)(4,1)} %bitcast.291), calls=%async_computation | async-start | bytes 8388608
  73.2 5.4 %slice-start.1 = ((s8[6553600]{0:T(1024)(128)(4,1)}), s8[2359296]{0:T(1024)(128)(4,1)S(1)}, s32[]{:S(2)}) async-start(s8[6553600]{0:T(1024)(128)(4,1)} %bitcast.291), calls=%async_computation.1 | async-start | bytes 4718592
  77.6 7.8 %collective-permute-start.19 = (f32[2,64,1280]{2,1,0:T(8,128)S(1)}, f32[2,64,1280]{2,1,0:T(8,128)S(1)}, u32[]{:S(2)}, u32[]{:S(2)}) collective-permute-start(f32[2,64,1280]{2,1,0:T(8,128)S(1)} %pad_maximum_fusion.4), channel_id=1, source_target_pairs={{0,1},{1,0},{2,3},{3,2},{4,5},{5,4},{6,7},{7,6},{8,9},{9,8},{10,11... | collective-permute-start | bytes 1966088 | tf_op jit(solution)/shard_map/ppermute | solution.py:242
  80.0 7.1 %collective-permute-start.17 = (f32[2,64,1280]{2,1,0:T(8,128)S(1)}, f32[2,64,1280]{2,1,0:T(8,128)S(1)}, u32[]{:S(2)}, u32[]{:S(2)}) collective-permute-start(f32[2,64,1280]{2,1,0:T(8,128)S(1)} %pad_maximum_fusion.3), channel_id=1, source_target_pairs={{0,1},{1,0},{2,3},{3,2},{4,5},{5,4},{6,7},{7,6},{8,9},{9,8},{10,11... | collective-permute-start | bytes 1966088 | tf_op jit(solution)/shard_map/ppermute | solution.py:242
  82.8 5.0 %collective-permute-start.15 = (f32[2,64,1280]{2,1,0:T(8,128)S(1)}, f32[2,64,1280]{2,1,0:T(8,128)S(1)}, u32[]{:S(2)}, u32[]{:S(2)}) collective-permute-start(f32[2,64,1280]{2,1,0:T(8,128)S(1)} %pad_maximum_fusion.2), channel_id=1, source_target_pairs={{0,1},{1,0},{2,3},{3,2},{4,5},{5,4},{6,7},{7,6},{8,9},{9,8},{10,11... | collective-permute-start | bytes 1966088 | tf_op jit(solution)/shard_map/ppermute | solution.py:242
  84.8 4.6 %collective-permute-start.13 = (f32[2,64,1280]{2,1,0:T(8,128)S(1)}, f32[2,64,1280]{2,1,0:T(8,128)S(1)}, u32[]{:S(2)}, u32[]{:S(2)}) collective-permute-start(f32[2,64,1280]{2,1,0:T(8,128)S(1)} %pad_maximum_fusion.1), channel_id=1, source_target_pairs={{0,1},{1,0},{2,3},{3,2},{4,5},{5,4},{6,7},{7,6},{8,9},{9,8},{10,11... | collective-permute-start | bytes 1966088 | tf_op jit(solution)/shard_map/ppermute | solution.py:242
  85.5 10.6 %collective-permute-start.20 = (f32[1,64,1280]{2,1,0:T(8,128)S(1)}, f32[1,64,1280]{2,1,0:T(8,128)S(1)}, u32[]{:S(2)}, u32[]{:S(2)}) collective-permute-start(f32[1,64,1280]{2,1,0:T(8,128)S(1)} %get-tuple-element.20), channel_id=1, source_target_pairs={{0,2},{1,3},{2,0},{3,1},{4,6},{5,7},{6,4},{7,5},{8,10},{9,11},{10,... | collective-permute-start | bytes 983048 | tf_op jit(solution)/shard_map/ppermute | solution.py:242
  87.1 16.0 %collective-permute-start.18 = (f32[1,64,1280]{2,1,0:T(8,128)S(1)}, f32[1,64,1280]{2,1,0:T(8,128)S(1)}, u32[]{:S(2)}, u32[]{:S(2)}) collective-permute-start(f32[1,64,1280]{2,1,0:T(8,128)S(1)} %get-tuple-element.17), channel_id=1, source_target_pairs={{0,2},{1,3},{2,0},{3,1},{4,6},{5,7},{6,4},{7,5},{8,10},{9,11},{10,... | collective-permute-start | bytes 983048 | tf_op jit(solution)/shard_map/ppermute | solution.py:242
  87.9 22.3 %collective-permute-start.16 = (f32[1,64,1280]{2,1,0:T(8,128)S(1)}, f32[1,64,1280]{2,1,0:T(8,128)S(1)}, u32[]{:S(2)}, u32[]{:S(2)}) collective-permute-start(f32[1,64,1280]{2,1,0:T(8,128)S(1)} %get-tuple-element.14), channel_id=1, source_target_pairs={{0,2},{1,3},{2,0},{3,1},{4,6},{5,7},{6,4},{7,5},{8,10},{9,11},{10,... | collective-permute-start | bytes 983048 | tf_op jit(solution)/shard_map/ppermute | solution.py:242
  89.6 26.7 %collective-permute-start.14 = (f32[1,64,1280]{2,1,0:T(8,128)S(1)}, f32[1,64,1280]{2,1,0:T(8,128)S(1)}, u32[]{:S(2)}, u32[]{:S(2)}) collective-permute-start(f32[1,64,1280]{2,1,0:T(8,128)S(1)} %get-tuple-element.11), channel_id=1, source_target_pairs={{0,2},{1,3},{2,0},{3,1},{4,6},{5,7},{6,4},{7,5},{8,10},{9,11},{10,... | collective-permute-start | bytes 983048 | tf_op jit(solution)/shard_map/ppermute | solution.py:242

commit v10 on v9

--- a/solution.py
+++ b/solution.py
@@ -77,7 +77,7 @@
     head_dim = HEAD_SIZE
     ctx_index = lax.axis_index("ctx")
 
-    all_lengths = doubling_gather(seq_len, "ctx", ctx_count)
+    all_lengths = shift_gather(seq_len, "ctx", ctx_count)
     pieces, work_heads = xor_gather(x_pool, "head", head_count)
 
     dest_grid = pool_dest.reshape(ctx_count, group_rows)
@@ -90,8 +90,9 @@
     owner = jnp.where(is_filled, work_dest // pack_len, 0)
     slot = jnp.where(is_filled, work_dest % pack_len, 0)
     seq_ends = jnp.cumsum(all_lengths, axis=1).astype(jnp.int32)
-    row_ends = jnp.take(seq_ends, owner, axis=0)
-    row_lengths = jnp.take(all_lengths, owner, axis=0)
+    owner_hot = owner[:, None, None] == jnp.arange(ctx_count, dtype=jnp.int32)[None, :, None]
+    row_ends = jnp.sum(jnp.where(owner_hot, seq_ends[None], 0), axis=1)
+    row_lengths = jnp.sum(jnp.where(owner_hot, all_lengths[None], 0), axis=1)
     finished = (row_ends <= slot[:, None]).astype(jnp.int32)
     sequence_starts = slot - jnp.sum(finished * row_lengths, axis=1)
 
@@ -214,6 +215,20 @@
     return jnp.concatenate(results, axis=0)
 
 
+def shift_gather(part, axis_name, count):
+    if count > 8:
+        return doubling_gather(part, axis_name, count)
+    me = lax.axis_index(axis_name)
+    by_shift = [part] + [
+        lax.ppermute(part, axis_name, [(i, (i + shift) % count) for i in range(count)])
+        for shift in range(1, count)
+    ]
+    stacked = jnp.stack(by_shift)
+    return jnp.take(stacked, (me - jnp.arange(count)) % count, axis=0).reshape(
+        (count * part.shape[0],) + part.shape[1:]
+    )
+
+
 def exchange(outgoing, axis_name, count):
     if count > 8:
         return lax.all_to_all(outgoing, axis_name, split_axis=0, concat_axis=0, tiled=True)

time: 118 us -> 112 us (0.949)
  the two profiles are of different devices: /device:TPU:20 before, /device:TPU:0 now
where the time goes in v10:
time: 112 us; the launch traced here: 111 us
  waiting for transfers between devices  33.6 us (30%)
  starting transfers between devices  32.2 us (29%)
  matrix products  19.5 us (17%)
  other arithmetic  18.4 us (16%)
  local copies, waits for them, and re-layouts  6.52 us (6%)
    ppermute x8, waiting for transfers between devices, halving_scatter(): got = lax.ppermute(send, axis_name, pairs)  25.9 us
    ppermute x7, starting transfers between devices, shift_gather(): lax.ppermute(part, axis_name, [(i, (i + shift) % count) for i in range(co...  12.5 us
    ppermute x7, starting transfers between devices, exchange(): arrived.append(lax.ppermute(chunks[shift], axis_name, pairs))  11.1 us
    dot_general x4, matrix products, local(): jnp.dot(mixed_heads, w_out, preferred_element_type=jnp.float32)  8.08 us
    ppermute x7, waiting for transfers between devices, exchange(): arrived.append(lax.ppermute(chunks[shift], axis_name, pairs))  5.65 us
    ppermute x8, starting transfers between devices, halving_scatter(): got = lax.ppermute(send, axis_name, pairs)  5.59 us
    convert_element_type x1, other arithmetic, project(): normalized_input = (values_wide * lax.rsqrt(jnp.mean(values_wide * values...  4.47 us
    dot_general x1, matrix products, project(): jnp.dot(normalized_input, value_projection_weight, preferred_element_type...  3.77 us
  transfers between devices with their start and end apart: 25, of which 9 were waited for; matrix products, arithmetic and copies ran while one was open for 17% of the time, Pallas kernels for 0%

profile of v10, /device:TPU:0, one launch (start us, length us, event | category | flops | bytes accessed | tf_op | source)
XLA Modules:
  0.0 111.0 jit_solution(13097332404586831298)
XLA Ops:
  0.0 3.0 %collective-permute-start = (bf16[96,5120]{1,0:T(8,128)(2,1)}, bf16[96,5120]{1,0:T(8,128)(2,1)S(1)}, u32[]{:S(2)}, u32[]{:S(2)}) collective-permute-start(bf16[96,5120]{1,0:T(8,128)(2,1)} %param.14), channel_id=1, source_target_pairs={{0,2},{1,3},{2,0},{3,1},{4,6},{5,7},{6,4},{7,5},{8,10},{9,11},{10,... | collective-permute-start | bytes 2949128 | tf_op jit(solution)/shard_map/ppermute | solution.py:286
  3.0 1.5 %collective-permute-start.3 = (s32[1,8]{1,0:T(1,128)}, s32[1,8]{1,0:T(1,128)S(1)}, u32[]{:S(2)}, u32[]{:S(2)}) collective-permute-start(s32[1,8]{1,0:T(1,128)} %param.16), channel_id=1, source_target_pairs={{0,4},{4,8},{8,12},{12,16},{16,20},{20,24},{24,28},{28,0},{1,5},{5... | collective-permute-start | bytes 104 | tf_op jit(solution)/shard_map/ppermute | solution.py:223
  4.5 1.6 %collective-permute-start.4 = (s32[1,8]{1,0:T(1,128)}, s32[1,8]{1,0:T(1,128)S(1)}, u32[]{:S(2)}, u32[]{:S(2)}) collective-permute-start(s32[1,8]{1,0:T(1,128)} %param.16), channel_id=1, source_target_pairs={{0,8},{4,12},{8,16},{12,20},{16,24},{20,28},{24,0},{28,4},{1,9},{5... | collective-permute-start | bytes 104 | tf_op jit(solution)/shard_map/ppermute | solution.py:223
  6.1 2.5 %collective-permute-start.5 = (s32[1,8]{1,0:T(1,128)}, s32[1,8]{1,0:T(1,128)S(1)}, u32[]{:S(2)}, u32[]{:S(2)}) collective-permute-start(s32[1,8]{1,0:T(1,128)} %param.16), channel_id=1, source_target_pairs={{0,12},{4,16},{8,20},{12,24},{16,28},{20,0},{24,4},{28,8},{1,13},{... | collective-permute-start | bytes 104 | tf_op jit(solution)/shard_map/ppermute | solution.py:223
  8.6 0.5 multiply_exponential_fusion
  9.2 0.7 constant_dynamic-update-slice_fusion.7
  9.9 0.7 reshape.875
  10.8 0.8 reduce-window.32
  11.8 0.9 reduce-window.30
  13.1 0.7 compare_and_fusion.4
  13.9 0.6 gather_fusion.2
  14.4 0.6 gather_fusion.1
  15.3 0.7 subtract_select_fusion
  16.1 0.9 reduce-window.21
  17.4 0.7 fusion.75
  18.4 1.3 %collective-permute-start.6 = (s32[1,8]{1,0:T(1,128)}, s32[1,8]{1,0:T(1,128)S(1)}, u32[]{:S(2)}, u32[]{:S(2)}) collective-permute-start(s32[1,8]{1,0:T(1,128)} %param.16), channel_id=1, source_target_pairs={{0,16},{4,20},{8,24},{12,28},{16,0},{20,4},{24,8},{28,12},{1,17},{... | collective-permute-start | bytes 104 | tf_op jit(solution)/shard_map/ppermute | solution.py:223
  19.7 2.6 %collective-permute-start.7 = (s32[1,8]{1,0:T(1,128)}, s32[1,8]{1,0:T(1,128)S(1)}, u32[]{:S(2)}, u32[]{:S(2)}) collective-permute-start(s32[1,8]{1,0:T(1,128)} %param.16), channel_id=1, source_target_pairs={{0,20},{4,24},{8,28},{12,0},{16,4},{20,8},{24,12},{28,16},{1,21},{... | collective-permute-start | bytes 104 | tf_op jit(solution)/shard_map/ppermute | solution.py:223
  22.4 1.3 %collective-permute-start.8 = (s32[1,8]{1,0:T(1,128)}, s32[1,8]{1,0:T(1,128)S(1)}, u32[]{:S(2)}, u32[]{:S(2)}) collective-permute-start(s32[1,8]{1,0:T(1,128)} %param.16), channel_id=1, source_target_pairs={{0,24},{4,28},{8,0},{12,4},{16,8},{20,12},{24,16},{28,20},{1,25},{... | collective-permute-start | bytes 104 | tf_op jit(solution)/shard_map/ppermute | solution.py:223
  23.7 1.6 %collective-permute-start.9 = (s32[1,8]{1,0:T(1,128)}, s32[1,8]{1,0:T(1,128)S(1)}, u32[]{:S(2)}, u32[]{:S(2)}) collective-permute-start(s32[1,8]{1,0:T(1,128)} %param.16), channel_id=1, source_target_pairs={{0,28},{4,0},{8,4},{12,8},{16,12},{20,16},{24,20},{28,24},{1,29},{... | collective-permute-start | bytes 104 | tf_op jit(solution)/shard_map/ppermute | solution.py:223
  25.4 0.7 collective-permute-done.8
  26.1 1.3 %collective-permute-done.9 = s32[1,8]{1,0:T(1,128)S(1)} collective-permute-done((s32[1,8]{1,0:T(1,128)}, s32[1,8]{1,0:T(1,128)S(1)}, u32[]{:S(2)}, u32[]{:S(2)}) %collective-permute-start.9) | collective-permute-done | bytes 64 | tf_op jit(solution)/shard_map/ppermute | solution.py:223
  27.4 0.6 gather_fusion
  28.3 1.1 multiply_cosine_fusion.1
  29.4 2.4 %fusion = f32[384]{0:T(512)S(1)} fusion(bf16[96,5120]{1,0:T(8,128)(2,1)} %collective-permute-done.2, bf16[96,5120]{1,0:T(8,128)(2,1)} %collective-permute-done.1, bf16[96,5120]{1,0:T(8,128)(2,1)S(1)} %collective-permute-done, bf16[96,5120]{1,0:T(8,128)(2,1)} %param.14), kind=kLoop, calls=%fused_computation.5 | loop fusion | flops 19660416 | bytes 3933696 | tf_op jit(solution)/shard_map/reduce_sum | solution.py:108
  31.9 4.5 %fusion.2 = bf16[384,5120]{1,0:T(8,128)(2,1)S(1)} fusion(f32[5120]{0:T(1024)S(1)} %copy-done.5, f32[384]{0:T(512)S(1)} %add_rsqrt_fusion, bf16[96,5120]{1,0:T(8,128)(2,1)} %collective-permute-done.2, bf16[96,5120]{1,0:T(8,128)(2,1)} %collective-permute-done.1, bf16[96,5120]{1,0:T(8,128)(2,1)S(1)} %collective-permute-done, bf16[96,5120]{1,0:T(8,128)(2,1)S(1)} %copy-done.2), kind=kLoop, calls=%fused_computation.7 | loop fusion | flops 21626880 | bytes 7886336 | tf_op jit(solution)/shard_map/convert_element_type | solution.py:110
  36.5 3.3 %convolution_add_fusion = f32[384,640]{1,0:T(8,128)S(1)} fusion(bf16[384,5120]{1,0:T(8,128)(2,1)S(1)} %fusion.2, bf16[5120,640]{1,0:T(8,128)(2,1)S(1)} %bitcast.305, f32[640]{0:T(1024)S(1)} %copy-done.10), kind=kOutput, calls=%fused_computation.12 | convolution fusion | flops 2516828160 | bytes 11471360 | tf_op jit(solution)/shard_map/dot_general | solution.py:112
  39.8 1.2 %convolution_add_fusion.2 = f32[384,128]{1,0:T(8,128)S(1)} fusion(bf16[384,5120]{1,0:T(8,128)(2,1)S(1)} %fusion.2, bf16[5120,128]{1,0:T(8,128)(2,1)S(1)} %copy-done, f32[128]{0:T(128)S(1)} %copy-done.7), kind=kOutput, calls=%fused_computation.19 | convolution fusion | flops 503365632 | bytes 5440000 | tf_op jit(solution)/shard_map/dot_general | solution.py:115
  41.0 0.8 fusion.52
  41.9 0.7 copy.36
  42.6 0.7 copy.35
  43.3 0.3 copy.34
  43.7 3.8 %fusion.9 = bf16[384,128]{0,1:T(8,128)(2,1)S(1)} fusion(bf16[384,5120]{1,0:T(8,128)(2,1)} %copy-done.1, bf16[5120,128]{1,0:T(8,128)(2,1)} %param.22, f32[128]{0:T(128)S(1)} %copy-done.9), kind=kOutput, calls=%fused_computation.26 | convolution fusion | flops 503414784 | bytes 5341696 | tf_op jit(solution)/shard_map/dot_general | solution.py:126
  47.7 0.6 convolution_convert_fusion
  48.3 1.8 %collective-permute-start.10 = (bf16[48,896]{1,0:T(8,128)(2,1)S(1)}, bf16[48,896]{1,0:T(8,128)(2,1)S(1)}, u32[]{:S(2)}, u32[]{:S(2)}) collective-permute-start(bf16[48,896]{1,0:T(8,128)(2,1)S(1)} %get-tuple-element.44), channel_id=1, source_target_pairs={{0,4},{4,8},{8,12},{12,16},{16,20},{20,24},{24,28},{28,0},{1,5},{5... | collective-permute-start | bytes 258056 | tf_op jit(solution)/shard_map/ppermute | solution.py:239
  50.1 0.4 select_reduce_fusion
  50.5 0.3 collective-permute-start.11
  50.8 2.5 %collective-permute-start.12 = (bf16[48,896]{1,0:T(8,128)(2,1)S(1)}, bf16[48,896]{1,0:T(8,128)(2,1)S(1)}, u32[]{:S(2)}, u32[]{:S(2)}) collective-permute-start(bf16[48,896]{1,0:T(8,128)(2,1)S(1)} %get-tuple-element.42), channel_id=1, source_target_pairs={{0,12},{4,16},{8,20},{12,24},{16,28},{20,0},{24,4},{28,8},{1,13},{... | collective-permute-start | bytes 258056 | tf_op jit(solution)/shard_map/ppermute | solution.py:239
  53.3 1.5 %collective-permute-start.13 = (bf16[48,896]{1,0:T(8,128)(2,1)S(1)}, bf16[48,896]{1,0:T(8,128)(2,1)S(1)}, u32[]{:S(2)}, u32[]{:S(2)}) collective-permute-start(bf16[48,896]{1,0:T(8,128)(2,1)S(1)} %get-tuple-element.41), channel_id=1, source_target_pairs={{0,16},{4,20},{8,24},{12,28},{16,0},{20,4},{24,8},{28,12},{1,17},{... | collective-permute-start | bytes 258056 | tf_op jit(solution)/shard_map/ppermute | solution.py:239
  54.8 3.3 %collective-permute-start.14 = (bf16[48,896]{1,0:T(8,128)(2,1)S(1)}, bf16[48,896]{1,0:T(8,128)(2,1)S(1)}, u32[]{:S(2)}, u32[]{:S(2)}) collective-permute-start(bf16[48,896]{1,0:T(8,128)(2,1)S(1)} %get-tuple-element.40), channel_id=1, source_target_pairs={{0,20},{4,24},{8,28},{12,0},{16,4},{20,8},{24,12},{28,16},{1,21},{... | collective-permute-start | bytes 258056 | tf_op jit(solution)/shard_map/ppermute | solution.py:239
  58.2 1.6 %collective-permute-start.16 = (bf16[48,896]{1,0:T(8,128)(2,1)S(1)}, bf16[48,896]{1,0:T(8,128)(2,1)S(1)}, u32[]{:S(2)}, u32[]{:S(2)}) collective-permute-start(bf16[48,896]{1,0:T(8,128)(2,1)S(1)} %get-tuple-element.38), channel_id=1, source_target_pairs={{0,28},{4,0},{8,4},{12,8},{16,12},{20,16},{24,20},{28,24},{1,29},{... | collective-permute-start | bytes 258056 | tf_op jit(solution)/shard_map/ppermute | solution.py:239
  59.8 2.7 %collective-permute-done.12 = bf16[48,896]{1,0:T(8,128)(2,1)S(1)} collective-permute-done((bf16[48,896]{1,0:T(8,128)(2,1)S(1)}, bf16[48,896]{1,0:T(8,128)(2,1)S(1)}, u32[]{:S(2)}, u32[]{:S(2)}) %collective-permute-start.12) | collective-permute-done | bytes 86048 | tf_op jit(solution)/shard_map/ppermute | solution.py:239
  62.5 1.3 %collective-permute-done.13 = bf16[48,896]{1,0:T(8,128)(2,1)S(1)} collective-permute-done((bf16[48,896]{1,0:T(8,128)(2,1)S(1)}, bf16[48,896]{1,0:T(8,128)(2,1)S(1)}, u32[]{:S(2)}, u32[]{:S(2)}) %collective-permute-start.13) | collective-permute-done | bytes 86048 | tf_op jit(solution)/shard_map/ppermute | solution.py:239
  63.9 1.7 %collective-permute-done.15 = bf16[48,896]{1,0:T(8,128)(2,1)S(1)} collective-permute-done((bf16[48,896]{1,0:T(8,128)(2,1)S(1)}, bf16[48,896]{1,0:T(8,128)(2,1)S(1)}, u32[]{:S(2)}, u32[]{:S(2)}) %collective-permute-start.15) | collective-permute-done | bytes 86048 | tf_op jit(solution)/shard_map/ppermute | solution.py:239
  65.6 0.5 convolution_convert_fusion.1
  66.1 0.3 fusion.130
  66.6 0.3 fusion.13
  67.0 4.3 %fusion.53 = f32[64,5120]{1,0:T(8,128)S(1)} fusion(bf16[640,5120]{1,0:T(8,128)(2,1)} %param.24, bf16[8,8,5,128]{3,2,1,0:T(8,128)(2,1)S(1)} %bitcast.294), kind=kOutput, calls=%fused_computation.123 | convolution fusion | flops 419430400 | bytes 7946240 | tf_op jit(solution)/shard_map/dot_general | solution.py:213
  71.4 0.3 fusion.131
  71.9 0.3 fusion.12
  72.3 1.3 %fusion.56 = f32[64,5120]{1,0:T(8,128)S(1)} fusion(bf16[640,5120]{1,0:T(8,128)(2,1)S(1)} %bitcast.291, bf16[8,8,5,128]{3,2,1,0:T(8,128)(2,1)S(1)} %bitcast.295), kind=kOutput, calls=%fused_computation.126 | convolution fusion | flops 419430400 | bytes 7946240 | tf_op jit(solution)/shard_map/dot_general | solution.py:213
  73.7 0.6 collective-permute-start.21
  74.3 0.3 fusion.132
  75.1 1.3 %fusion.59 = f32[64,5120]{1,0:T(8,128)S(1)} fusion(bf16[640,5120]{1,0:T(8,128)(2,1)S(1)} %bitcast.291, bf16[8,8,5,128]{3,2,1,0:T(8,128)(2,1)S(1)} %bitcast.296), kind=kOutput, calls=%fused_computation.129 | convolution fusion | flops 419430400 | bytes 7946240 | tf_op jit(solution)/shard_map/dot_general | solution.py:213
  77.2 1.3 %fusion.62 = f32[64,5120]{1,0:T(8,128)S(1)} fusion(bf16[640,5120]{1,0:T(8,128)(2,1)S(1)} %bitcast.291, bf16[8,8,5,128]{3,2,1,0:T(8,128)(2,1)S(1)} %bitcast.297), kind=kOutput, calls=%fused_computation.132 | convolution fusion | flops 419430400 | bytes 7946240 | tf_op jit(solution)/shard_map/dot_general | solution.py:213
  78.6 0.6 collective-permute-start.17
  79.2 1.1 %collective-permute-start.24 = (f32[1,64,1280]{2,1,0:T(8,128)S(1)}, f32[1,64,1280]{2,1,0:T(8,128)S(1)}, u32[]{:S(2)}, u32[]{:S(2)}) collective-permute-start(f32[1,64,1280]{2,1,0:T(8,128)S(1)} %get-tuple-element.21), channel_id=1, source_target_pairs={{0,2},{1,3},{2,0},{3,1},{4,6},{5,7},{6,4},{7,5},{8,10},{9,11},{10,... | collective-permute-start | bytes 983048 | tf_op jit(solution)/shard_map/ppermute | solution.py:257
  80.5 1.0 collective-permute-start.22
  81.6 1.1 %collective-permute-start.20 = (f32[1,64,1280]{2,1,0:T(8,128)S(1)}, f32[1,64,1280]{2,1,0:T(8,128)S(1)}, u32[]{:S(2)}, u32[]{:S(2)}) collective-permute-start(f32[1,64,1280]{2,1,0:T(8,128)S(1)} %get-tuple-element.15), channel_id=1, source_target_pairs={{0,2},{1,3},{2,0},{3,1},{4,6},{5,7},{6,4},{7,5},{8,10},{9,11},{10,... | collective-permute-start | bytes 983048 | tf_op jit(solution)/shard_map/ppermute | solution.py:257
  82.9 1.0 collective-permute-start.18
  83.9 6.0 %collective-permute-done.24 = f32[1,64,1280]{2,1,0:T(8,128)S(1)} collective-permute-done((f32[1,64,1280]{2,1,0:T(8,128)S(1)}, f32[1,64,1280]{2,1,0:T(8,128)S(1)}, u32[]{:S(2)}, u32[]{:S(2)}) %collective-permute-start.24) | collective-permute-done | bytes 327712 | tf_op jit(solution)/shard_map/ppermute | solution.py:257
  89.9 7.0 %collective-permute-done.22 = f32[1,64,1280]{2,1,0:T(8,128)S(1)} collective-permute-done((f32[1,64,1280]{2,1,0:T(8,128)S(1)}, f32[1,64,1280]{2,1,0:T(8,128)S(1)}, u32[]{:S(2)}, u32[]{:S(2)}) %collective-permute-start.22) | collective-permute-done | bytes 327712 | tf_op jit(solution)/shard_map/ppermute | solution.py:257
  97.0 7.0 %collective-permute-done.20 = f32[1,64,1280]{2,1,0:T(8,128)S(1)} collective-permute-done((f32[1,64,1280]{2,1,0:T(8,128)S(1)}, f32[1,64,1280]{2,1,0:T(8,128)S(1)}, u32[]{:S(2)}, u32[]{:S(2)}) %collective-permute-start.20) | collective-permute-done | bytes 327712 | tf_op jit(solution)/shard_map/ppermute | solution.py:257
  104.0 6.0 %collective-permute-done.18 = f32[1,64,1280]{2,1,0:T(8,128)S(1)} collective-permute-done((f32[1,64,1280]{2,1,0:T(8,128)S(1)}, f32[1,64,1280]{2,1,0:T(8,128)S(1)}, u32[]{:S(2)}, u32[]{:S(2)}) %collective-permute-start.18) | collective-permute-done | bytes 327712 | tf_op jit(solution)/shard_map/ppermute | solution.py:257
  110.1 0.9 pad_maximum_fusion.5
  (150 shorter events, 5.9 us)
Async XLA Ops:
  0.0 39.8 %copy-start = (bf16[5120,128]{1,0:T(8,128)(2,1)S(1)}, bf16[5120,128]{1,0:T(8,128)(2,1)}, u32[]{:S(2)}) copy-start(bf16[5120,128]{1,0:T(8,128)(2,1)} %param.20) | copy-start | bytes 3932164
  0.0 31.9 %copy-start.2 = (bf16[96,5120]{1,0:T(8,128)(2,1)S(1)}, bf16[96,5120]{1,0:T(8,128)(2,1)}, u32[]{:S(2)}) copy-start(bf16[96,5120]{1,0:T(8,128)(2,1)} %param.14) | copy-start | bytes 2949124
  0.0 31.9 %copy-start.5 = (f32[5120]{0:T(1024)S(1)}, f32[5120]{0:T(1024)}, u32[]{:S(2)}) copy-start(f32[5120]{0:T(1024)} %param.17) | copy-start | bytes 61444
  0.0 26.0 %collective-permute-start = (bf16[96,5120]{1,0:T(8,128)(2,1)}, bf16[96,5120]{1,0:T(8,128)(2,1)S(1)}, u32[]{:S(2)}, u32[]{:S(2)}) collective-permute-start(bf16[96,5120]{1,0:T(8,128)(2,1)} %param.14), channel_id=1, source_target_pairs={{0,2},{1,3},{2,0},{3,1},{4,6},{5,7},{6,4},{7,5},{8,10},{9,11},{10,... | collective-permute-start | bytes 2949128 | tf_op jit(solution)/shard_map/ppermute | solution.py:286
  3.0 26.4 %collective-permute-start.1 = (bf16[96,5120]{1,0:T(8,128)(2,1)}, bf16[96,5120]{1,0:T(8,128)(2,1)}, u32[]{:S(2)}, u32[]{:S(2)}) collective-permute-start(bf16[96,5120]{1,0:T(8,128)(2,1)} %param.14), channel_id=1, source_target_pairs={{0,1},{1,0},{2,3},{3,2},{4,5},{5,4},{6,7},{7,6},{8,9},{9,8},{10,11... | collective-permute-start | bytes 2949128 | tf_op jit(solution)/shard_map/ppermute | solution.py:286
  3.0 15.4 %collective-permute-start.3 = (s32[1,8]{1,0:T(1,128)}, s32[1,8]{1,0:T(1,128)S(1)}, u32[]{:S(2)}, u32[]{:S(2)}) collective-permute-start(s32[1,8]{1,0:T(1,128)} %param.16), channel_id=1, source_target_pairs={{0,4},{4,8},{8,12},{12,16},{16,20},{20,24},{24,28},{28,0},{1,5},{5... | collective-permute-start | bytes 104 | tf_op jit(solution)/shard_map/ppermute | solution.py:223
  4.5 15.2 %collective-permute-start.4 = (s32[1,8]{1,0:T(1,128)}, s32[1,8]{1,0:T(1,128)S(1)}, u32[]{:S(2)}, u32[]{:S(2)}) collective-permute-start(s32[1,8]{1,0:T(1,128)} %param.16), channel_id=1, source_target_pairs={{0,8},{4,12},{8,16},{12,20},{16,24},{20,28},{24,0},{28,4},{1,9},{5... | collective-permute-start | bytes 104 | tf_op jit(solution)/shard_map/ppermute | solution.py:223
  6.1 16.3 %collective-permute-start.5 = (s32[1,8]{1,0:T(1,128)}, s32[1,8]{1,0:T(1,128)S(1)}, u32[]{:S(2)}, u32[]{:S(2)}) collective-permute-start(s32[1,8]{1,0:T(1,128)} %param.16), channel_id=1, source_target_pairs={{0,12},{4,16},{8,20},{12,24},{16,28},{20,0},{24,4},{28,8},{1,13},{... | collective-permute-start | bytes 104 | tf_op jit(solution)/shard_map/ppermute | solution.py:223
  18.4 5.3 %collective-permute-start.6 = (s32[1,8]{1,0:T(1,128)}, s32[1,8]{1,0:T(1,128)S(1)}, u32[]{:S(2)}, u32[]{:S(2)}) collective-permute-start(s32[1,8]{1,0:T(1,128)} %param.16), channel_id=1, source_target_pairs={{0,16},{4,20},{8,24},{12,28},{16,0},{20,4},{24,8},{28,12},{1,17},{... | collective-permute-start | bytes 104 | tf_op jit(solution)/shard_map/ppermute | solution.py:223
  19.7 5.6 %collective-permute-start.7 = (s32[1,8]{1,0:T(1,128)}, s32[1,8]{1,0:T(1,128)S(1)}, u32[]{:S(2)}, u32[]{:S(2)}) collective-permute-start(s32[1,8]{1,0:T(1,128)} %param.16), channel_id=1, source_target_pairs={{0,20},{4,24},{8,28},{12,0},{16,4},{20,8},{24,12},{28,16},{1,21},{... | collective-permute-start | bytes 104 | tf_op jit(solution)/shard_map/ppermute | solution.py:223
  22.4 3.7 %collective-permute-start.8 = (s32[1,8]{1,0:T(1,128)}, s32[1,8]{1,0:T(1,128)S(1)}, u32[]{:S(2)}, u32[]{:S(2)}) collective-permute-start(s32[1,8]{1,0:T(1,128)} %param.16), channel_id=1, source_target_pairs={{0,24},{4,28},{8,0},{12,4},{16,8},{20,12},{24,16},{28,20},{1,25},{... | collective-permute-start | bytes 104 | tf_op jit(solution)/shard_map/ppermute | solution.py:223
  23.7 3.7 %collective-permute-start.9 = (s32[1,8]{1,0:T(1,128)}, s32[1,8]{1,0:T(1,128)S(1)}, u32[]{:S(2)}, u32[]{:S(2)}) collective-permute-start(s32[1,8]{1,0:T(1,128)} %param.16), channel_id=1, source_target_pairs={{0,28},{4,0},{8,4},{12,8},{16,12},{20,16},{24,20},{28,24},{1,29},{... | collective-permute-start | bytes 104 | tf_op jit(solution)/shard_map/ppermute | solution.py:223
  26.1 3.4 %collective-permute-start.2 = (bf16[96,5120]{1,0:T(8,128)(2,1)S(1)}, bf16[96,5120]{1,0:T(8,128)(2,1)}, u32[]{:S(2)}, u32[]{:S(2)}) collective-permute-start(bf16[96,5120]{1,0:T(8,128)(2,1)S(1)} %collective-permute-done), channel_id=1, source_target_pairs={{0,1},{1,0},{2,3},{3,2},{4,5},{5,4},{6,7},{7,6},{8,9},{9,8},{10,11... | collective-permute-start | bytes 2949128 | tf_op jit(solution)/shard_map/ppermute | solution.py:286
  29.4 7.0 %slice-start.2 = ((s8[6553600]{0:T(1024)(128)(4,1)}), s8[4194304]{0:T(1024)(128)(4,1)S(1)}, s32[]{:S(2)}) async-start(s8[6553600]{0:T(1024)(128)(4,1)} %bitcast.304), calls=%async_computation.2 | async-start | bytes 8388608
  31.9 4.5 %slice-start.3 = ((s8[6553600]{0:T(1024)(128)(4,1)}), s8[2359296]{0:T(1024)(128)(4,1)S(1)}, s32[]{:S(2)}) async-start(s8[6553600]{0:T(1024)(128)(4,1)} %bitcast.304), calls=%async_computation.3 | async-start | bytes 4718592
  31.9 4.5 %copy-start.10 = (f32[640]{0:T(1024)S(1)}, f32[640]{0:T(1024)}, u32[]{:S(2)}) copy-start(f32[640]{0:T(1024)} %param.19) | copy-start | bytes 7684
  36.4 3.3 %copy-start.1 = (bf16[384,5120]{1,0:T(8,128)(2,1)}, bf16[384,5120]{1,0:T(8,128)(2,1)S(1)}, u32[]{:S(2)}) copy-start(bf16[384,5120]{1,0:T(8,128)(2,1)S(1)} %fusion.2) | copy-start | bytes 11796484
  36.4 3.3 %copy-start.7 = (f32[128]{0:T(128)S(1)}, f32[128]{0:T(128)}, u32[]{:S(2)}) copy-start(f32[128]{0:T(128)} %param.21) | copy-start | bytes 1540
  39.8 1.2 %copy-start.8 = (f32[64]{0:T(128)S(1)}, f32[64]{0:T(128)}, u32[]{:S(2)}) copy-start(f32[64]{0:T(128)} %multiply_exponential_fusion) | copy-start | bytes 772
  39.8 3.8 %copy-start.9 = (f32[128]{0:T(128)S(1)}, f32[128]{0:T(128)}, u32[]{:S(2)}) copy-start(f32[128]{0:T(128)} %param.23) | copy-start | bytes 1540
  43.6 4.0 %copy-start.3 = (bf16[384,64]{0,1:T(8,128)(2,1)S(1)}, bf16[384,64]{0,1:T(8,128)(2,1)}, u32[]{:S(2)}) copy-start(bf16[384,64]{0,1:T(8,128)(2,1)} %copy.36) | copy-start | bytes 147460
  43.6 4.0 %copy-start.4 = (bf16[384,64]{0,1:T(8,128)(2,1)S(1)}, bf16[384,64]{0,1:T(8,128)(2,1)}, u32[]{:S(2)}) copy-start(bf16[384,64]{0,1:T(8,128)(2,1)} %copy.35) | copy-start | bytes 147460
  47.6 18.5 %copy-start.6 = (pred[64,256]{1,0:T(8,128)(4,1)S(1)}, pred[64,256]{1,0:T(8,128)(4,1)}, u32[]{:S(2)}) copy-start(pred[64,256]{1,0:T(8,128)(4,1)} %fusion.75) | copy-start | bytes 49156
  48.3 9.8 %collective-permute-start.10 = (bf16[48,896]{1,0:T(8,128)(2,1)S(1)}, bf16[48,896]{1,0:T(8,128)(2,1)S(1)}, u32[]{:S(2)}, u32[]{:S(2)}) collective-permute-start(bf16[48,896]{1,0:T(8,128)(2,1)S(1)} %get-tuple-element.44), channel_id=1, source_target_pairs={{0,4},{4,8},{8,12},{12,16},{16,20},{20,24},{24,28},{28,0},{1,5},{5... | collective-permute-start | bytes 258056 | tf_op jit(solution)/shard_map/ppermute | solution.py:239
  50.5 7.7 %collective-permute-start.11 = (bf16[48,896]{1,0:T(8,128)(2,1)S(1)}, bf16[48,896]{1,0:T(8,128)(2,1)S(1)}, u32[]{:S(2)}, u32[]{:S(2)}) collective-permute-start(bf16[48,896]{1,0:T(8,128)(2,1)S(1)} %get-tuple-element.43), channel_id=1, source_target_pairs={{0,8},{4,12},{8,16},{12,20},{16,24},{20,28},{24,0},{28,4},{1,9},{5... | collective-permute-start | bytes 258056 | tf_op jit(solution)/shard_map/ppermute | solution.py:239
  50.8 11.7 %collective-permute-start.12 = (bf16[48,896]{1,0:T(8,128)(2,1)S(1)}, bf16[48,896]{1,0:T(8,128)(2,1)S(1)}, u32[]{:S(2)}, u32[]{:S(2)}) collective-permute-start(bf16[48,896]{1,0:T(8,128)(2,1)S(1)} %get-tuple-element.42), channel_id=1, source_target_pairs={{0,12},{4,16},{8,20},{12,24},{16,28},{20,0},{24,4},{28,8},{1,13},{... | collective-permute-start | bytes 258056 | tf_op jit(solution)/shard_map/ppermute | solution.py:239
  53.3 10.5 %collective-permute-start.13 = (bf16[48,896]{1,0:T(8,128)(2,1)S(1)}, bf16[48,896]{1,0:T(8,128)(2,1)S(1)}, u32[]{:S(2)}, u32[]{:S(2)}) collective-permute-start(bf16[48,896]{1,0:T(8,128)(2,1)S(1)} %get-tuple-element.41), channel_id=1, source_target_pairs={{0,16},{4,20},{8,24},{12,28},{16,0},{20,4},{24,8},{28,12},{1,17},{... | collective-permute-start | bytes 258056 | tf_op jit(solution)/shard_map/ppermute | solution.py:239
  54.8 9.0 %collective-permute-start.14 = (bf16[48,896]{1,0:T(8,128)(2,1)S(1)}, bf16[48,896]{1,0:T(8,128)(2,1)S(1)}, u32[]{:S(2)}, u32[]{:S(2)}) collective-permute-start(bf16[48,896]{1,0:T(8,128)(2,1)S(1)} %get-tuple-element.40), channel_id=1, source_target_pairs={{0,20},{4,24},{8,28},{12,0},{16,4},{20,8},{24,12},{28,16},{1,21},{... | collective-permute-start | bytes 258056 | tf_op jit(solution)/shard_map/ppermute | solution.py:239
  58.1 7.4 %collective-permute-start.15 = (bf16[48,896]{1,0:T(8,128)(2,1)S(1)}, bf16[48,896]{1,0:T(8,128)(2,1)S(1)}, u32[]{:S(2)}, u32[]{:S(2)}) collective-permute-start(bf16[48,896]{1,0:T(8,128)(2,1)S(1)} %get-tuple-element.39), channel_id=1, source_target_pairs={{0,24},{4,28},{8,0},{12,4},{16,8},{20,12},{24,16},{28,20},{1,25},{... | collective-permute-start | bytes 258056 | tf_op jit(solution)/shard_map/ppermute | solution.py:239
  58.2 7.3 %collective-permute-start.16 = (bf16[48,896]{1,0:T(8,128)(2,1)S(1)}, bf16[48,896]{1,0:T(8,128)(2,1)S(1)}, u32[]{:S(2)}, u32[]{:S(2)}) collective-permute-start(bf16[48,896]{1,0:T(8,128)(2,1)S(1)} %get-tuple-element.38), channel_id=1, source_target_pairs={{0,28},{4,0},{8,4},{12,8},{16,12},{20,16},{24,20},{28,24},{1,29},{... | collective-permute-start | bytes 258056 | tf_op jit(solution)/shard_map/ppermute | solution.py:239
  66.9 5.4 %slice-start = ((s8[6553600]{0:T(1024)(128)(4,1)}), s8[4194304]{0:T(1024)(128)(4,1)S(1)}, s32[]{:S(2)}) async-start(s8[6553600]{0:T(1024)(128)(4,1)} %bitcast.290), calls=%async_computation | async-start | bytes 8388608
  66.9 5.4 %slice-start.1 = ((s8[6553600]{0:T(1024)(128)(4,1)}), s8[2359296]{0:T(1024)(128)(4,1)S(1)}, s32[]{:S(2)}) async-start(s8[6553600]{0:T(1024)(128)(4,1)} %bitcast.290), calls=%async_computation.1 | async-start | bytes 4718592
  71.4 7.8 %collective-permute-start.23 = (f32[2,64,1280]{2,1,0:T(8,128)S(1)}, f32[2,64,1280]{2,1,0:T(8,128)S(1)}, u32[]{:S(2)}, u32[]{:S(2)}) collective-permute-start(f32[2,64,1280]{2,1,0:T(8,128)S(1)} %pad_maximum_fusion.4), channel_id=1, source_target_pairs={{0,1},{1,0},{2,3},{3,2},{4,5},{5,4},{6,7},{7,6},{8,9},{9,8},{10,11... | collective-permute-start | bytes 1966088 | tf_op jit(solution)/shard_map/ppermute | solution.py:257
  73.7 6.7 %collective-permute-start.21 = (f32[2,64,1280]{2,1,0:T(8,128)S(1)}, f32[2,64,1280]{2,1,0:T(8,128)S(1)}, u32[]{:S(2)}, u32[]{:S(2)}) collective-permute-start(f32[2,64,1280]{2,1,0:T(8,128)S(1)} %pad_maximum_fusion.3), channel_id=1, source_target_pairs={{0,1},{1,0},{2,3},{3,2},{4,5},{5,4},{6,7},{7,6},{8,9},{9,8},{10,11... | collective-permute-start | bytes 1966088 | tf_op jit(solution)/shard_map/ppermute | solution.py:257
  76.5 5.0 %collective-permute-start.19 = (f32[2,64,1280]{2,1,0:T(8,128)S(1)}, f32[2,64,1280]{2,1,0:T(8,128)S(1)}, u32[]{:S(2)}, u32[]{:S(2)}) collective-permute-start(f32[2,64,1280]{2,1,0:T(8,128)S(1)} %pad_maximum_fusion.2), channel_id=1, source_target_pairs={{0,1},{1,0},{2,3},{3,2},{4,5},{5,4},{6,7},{7,6},{8,9},{9,8},{10,11... | collective-permute-start | bytes 1966088 | tf_op jit(solution)/shard_map/ppermute | solution.py:257
  78.6 4.2 %collective-permute-start.17 = (f32[2,64,1280]{2,1,0:T(8,128)S(1)}, f32[2,64,1280]{2,1,0:T(8,128)S(1)}, u32[]{:S(2)}, u32[]{:S(2)}) collective-permute-start(f32[2,64,1280]{2,1,0:T(8,128)S(1)} %pad_maximum_fusion.1), channel_id=1, source_target_pairs={{0,1},{1,0},{2,3},{3,2},{4,5},{5,4},{6,7},{7,6},{8,9},{9,8},{10,11... | collective-permute-start | bytes 1966088 | tf_op jit(solution)/shard_map/ppermute | solution.py:257
  79.2 10.6 %collective-permute-start.24 = (f32[1,64,1280]{2,1,0:T(8,128)S(1)}, f32[1,64,1280]{2,1,0:T(8,128)S(1)}, u32[]{:S(2)}, u32[]{:S(2)}) collective-permute-start(f32[1,64,1280]{2,1,0:T(8,128)S(1)} %get-tuple-element.21), channel_id=1, source_target_pairs={{0,2},{1,3},{2,0},{3,1},{4,6},{5,7},{6,4},{7,5},{8,10},{9,11},{10,... | collective-permute-start | bytes 983048 | tf_op jit(solution)/shard_map/ppermute | solution.py:257
  80.5 16.4 %collective-permute-start.22 = (f32[1,64,1280]{2,1,0:T(8,128)S(1)}, f32[1,64,1280]{2,1,0:T(8,128)S(1)}, u32[]{:S(2)}, u32[]{:S(2)}) collective-permute-start(f32[1,64,1280]{2,1,0:T(8,128)S(1)} %get-tuple-element.18), channel_id=1, source_target_pairs={{0,2},{1,3},{2,0},{3,1},{4,6},{5,7},{6,4},{7,5},{8,10},{9,11},{10,... | collective-permute-start | bytes 983048 | tf_op jit(solution)/shard_map/ppermute | solution.py:257
  81.6 22.3 %collective-permute-start.20 = (f32[1,64,1280]{2,1,0:T(8,128)S(1)}, f32[1,64,1280]{2,1,0:T(8,128)S(1)}, u32[]{:S(2)}, u32[]{:S(2)}) collective-permute-start(f32[1,64,1280]{2,1,0:T(8,128)S(1)} %get-tuple-element.15), channel_id=1, source_target_pairs={{0,2},{1,3},{2,0},{3,1},{4,6},{5,7},{6,4},{7,5},{8,10},{9,11},{10,... | collective-permute-start | bytes 983048 | tf_op jit(solution)/shard_map/ppermute | solution.py:257
  82.9 27.1 %collective-permute-start.18 = (f32[1,64,1280]{2,1,0:T(8,128)S(1)}, f32[1,64,1280]{2,1,0:T(8,128)S(1)}, u32[]{:S(2)}, u32[]{:S(2)}) collective-permute-start(f32[1,64,1280]{2,1,0:T(8,128)S(1)} %get-tuple-element.12), channel_id=1, source_target_pairs={{0,2},{1,3},{2,0},{3,1},{4,6},{5,7},{6,4},{7,5},{8,10},{9,11},{10,... | collective-permute-start | bytes 983048 | tf_op jit(solution)/shard_map/ppermute | solution.py:257

commit v11 on v10

--- a/solution.py
+++ b/solution.py
@@ -166,15 +166,8 @@
     slot_ids = jnp.arange(pack_len, dtype=jnp.int32)
     names_slot = my_slot_of_row[None, :] == slot_ids[:, None]
     source_of_slot = jnp.sum(jnp.where(names_slot, arrived_index[None, :], 0), axis=1)
-    packed_qkv = select_rows(source_of_slot, arrived)
-
     q_width = local_heads * head_dim
     kv_width = local_kv * head_dim
-    query_matrix = packed_qkv[:, :q_width].reshape(pack_len, local_kv, query_group_count, head_dim)
-    projected_key_rows = packed_qkv[:, q_width : q_width + kv_width].reshape(
-        pack_len, local_kv, head_dim
-    )
-    projected_value_rows = packed_qkv[:, q_width + kv_width :].reshape(pack_len, local_kv, head_dim)
 
     own_lengths = seq_len[0]
     own_ends = jnp.cumsum(own_lengths).astype(jnp.int32)
@@ -184,13 +177,29 @@
     chunk_count = 4 if pack_len % 32 == 0 else 1
     chunk_len = pack_len // chunk_count
     results = []
+    key_parts, value_parts = [], []
+    pending = None
     for chunk in range(chunk_count):
         lo, hi = chunk * chunk_len, (chunk + 1) * chunk_len
+        chunk_qkv = select_rows(source_of_slot[lo:hi], arrived)
+        if pending is not None:
+            chunk_qkv, held = lax.optimization_barrier((chunk_qkv, [x for _, x in pending]))
+            pending = [(b, x) for (b, _), x in zip(pending, held)]
+            results.append(finish_scatter(pending, "head", head_count).astype(jnp.bfloat16))
+        query_matrix = chunk_qkv[:, :q_width].reshape(
+            chunk_len, local_kv, query_group_count, head_dim
+        )
+        key_parts.append(chunk_qkv[:, q_width : q_width + kv_width])
+        value_parts.append(chunk_qkv[:, q_width + kv_width :])
+        projected_key_rows = jnp.concatenate(key_parts, axis=0).reshape(hi, local_kv, head_dim)
+        projected_value_rows = jnp.concatenate(value_parts, axis=0).reshape(
+            hi, local_kv, head_dim
+        )
         scores = (
             jnp.einsum(
                 "qkgd,tkd->kgqt",
-                query_matrix[lo:hi],
-                projected_key_rows[:hi],
+                query_matrix,
+                projected_key_rows,
                 preferred_element_type=jnp.float32,
             )
             * score_scale
@@ -206,12 +215,13 @@
         mixed_heads = jnp.einsum(
             "kgqt,tkd->qkgd",
             probability,
-            projected_value_rows[:hi],
+            projected_value_rows,
             preferred_element_type=jnp.float32,
         )
         mixed_heads = mixed_heads.astype(jnp.bfloat16).reshape(chunk_len, local_heads * head_dim)
         partial_out = jnp.dot(mixed_heads, w_out, preferred_element_type=jnp.float32)
-        results.append(halving_scatter(partial_out, "head", head_count).astype(jnp.bfloat16))
+        pending = start_scatter(partial_out, "head", head_count)
+    results.append(finish_scatter(pending, "head", head_count).astype(jnp.bfloat16))
     return jnp.concatenate(results, axis=0)
 
 
@@ -240,22 +250,38 @@
     return jnp.concatenate(arrived, axis=0)
 
 
-def halving_scatter(partial, axis_name, count):
+def scatter_bits(count):
     bits = count.bit_length() - 1
-    if count != 1 << bits or bits == 0:
-        return lax.psum_scatter(partial, axis_name, scatter_dimension=1, tiled=True)
+    return bits if count == 1 << bits else 0
+
+
+def halving_stage(pieces, stage, axis_name, count):
+    me = lax.axis_index(axis_name)
+    bit = (me >> stage) & 1
+    lows = [(b, x) for b, x in pieces if not (b >> stage) & 1]
+    highs = [x for b, x in pieces if (b >> stage) & 1]
+    keep = [jnp.where(bit == 0, lo, hi) for (_, lo), hi in zip(lows, highs)]
+    send = jnp.stack([jnp.where(bit == 0, hi, lo) for (_, lo), hi in zip(lows, highs)])
+    pairs = [(i, i ^ (1 << stage)) for i in range(count)]
+    got = lax.ppermute(send, axis_name, pairs)
+    return [(b, k + got[i]) for i, ((b, _), k) in enumerate(zip(lows, keep))]
+
+
+def start_scatter(partial, axis_name, count):
+    bits = scatter_bits(count)
+    if bits == 0:
+        return [(0, partial)]
     block = partial.shape[1] // count
-    me = lax.axis_index(axis_name)
     pieces = [(b, partial[:, b * block : (b + 1) * block]) for b in range(count)]
-    for stage in range(bits):
-        bit = (me >> stage) & 1
-        lows = [(b, x) for b, x in pieces if not (b >> stage) & 1]
-        highs = [x for b, x in pieces if (b >> stage) & 1]
-        keep = [jnp.where(bit == 0, lo, hi) for (_, lo), hi in zip(lows, highs)]
-        send = jnp.stack([jnp.where(bit == 0, hi, lo) for (_, lo), hi in zip(lows, highs)])
-        pairs = [(i, i ^ (1 << stage)) for i in range(count)]
-        got = lax.ppermute(send, axis_name, pairs)
-        pieces = [(b, k + got[i]) for i, ((b, _), k) in enumerate(zip(lows, keep))]
+    return halving_stage(pieces, 0, axis_name, count)
+
+
+def finish_scatter(pieces, axis_name, count):
+    bits = scatter_bits(count)
+    if bits == 0:
+        return lax.psum_scatter(pieces[0][1], axis_name, scatter_dimension=1, tiled=True)
+    for stage in range(1, bits):
+        pieces = halving_stage(pieces, stage, axis_name, count)
     return pieces[0][1]
 
 

time: 112 us -> 113 us (level)
  waiting for transfers between devices: 33.6 us -> 35.6 us
  starting transfers between devices: 32.2 us -> 30.5 us
    ppermute x8, starting transfers between devices: 5.59 us -> 3.93 us  [halving_stage(): got = lax.ppermute(send, axis_name, pairs)]
    ppermute x8, waiting for transfers between devices: 25.9 us -> 27.4 us  [halving_stage(): got = lax.ppermute(send, axis_name, pairs)]
  transfers between devices with their start and end apart: 25 -> 25, of which waited for: 9 -> 10; matrix products, arithmetic and copies ran while one was open for 17% -> 17% of each run, Pallas kernels for 0% -> 0%
where the time goes in v11:
time: 113 us; the launch traced here: 112 us
  waiting for transfers between devices  35.6 us (32%)
  starting transfers between devices  30.5 us (27%)
  matrix products  20.3 us (18%)
  other arithmetic  18.5 us (16%)
  local copies, waits for them, and re-layouts  6.59 us (6%)
    ppermute x8, waiting for transfers between devices, halving_stage(): got = lax.ppermute(send, axis_name, pairs)  27.4 us
    ppermute x7, starting transfers between devices, shift_gather(): lax.ppermute(part, axis_name, [(i, (i + shift) % count) for i in range(co...  12.5 us
    ppermute x7, starting transfers between devices, exchange(): arrived.append(lax.ppermute(chunks[shift], axis_name, pairs))  11.1 us
    dot_general x4, matrix products, local(): jnp.dot(mixed_heads, w_out, preferred_element_type=jnp.float32)  8.1 us
    ppermute x7, waiting for transfers between devices, exchange(): arrived.append(lax.ppermute(chunks[shift], axis_name, pairs))  6.09 us
    convert_element_type x1, other arithmetic, project(): normalized_input = (values_wide * lax.rsqrt(jnp.mean(values_wide * values...  4.47 us
    ppermute x8, starting transfers between devices, halving_stage(): got = lax.ppermute(send, axis_name, pairs)  3.93 us
    dot_general x1, matrix products, project(): jnp.dot(normalized_input, value_projection_weight, preferred_element_type...  3.77 us
  transfers between devices with their start and end apart: 25, of which 10 were waited for; matrix products, arithmetic and copies ran while one was open for 17% of the time, Pallas kernels for 0%

profile of v11, /device:TPU:0, one launch (start us, length us, event | category | flops | bytes accessed | tf_op | source)
XLA Modules:
  0.0 112.3 jit_solution(14455809129095838735)
XLA Ops:
  0.0 3.0 %collective-permute-start = (bf16[96,5120]{1,0:T(8,128)(2,1)}, bf16[96,5120]{1,0:T(8,128)(2,1)S(1)}, u32[]{:S(2)}, u32[]{:S(2)}) collective-permute-start(bf16[96,5120]{1,0:T(8,128)(2,1)} %param.14), channel_id=1, source_target_pairs={{0,2},{1,3},{2,0},{3,1},{4,6},{5,7},{6,4},{7,5},{8,10},{9,11},{10,... | collective-permute-start | bytes 2949128 | tf_op jit(solution)/shard_map/ppermute | solution.py:312
  3.0 1.5 %collective-permute-start.3 = (s32[1,8]{1,0:T(1,128)}, s32[1,8]{1,0:T(1,128)S(1)}, u32[]{:S(2)}, u32[]{:S(2)}) collective-permute-start(s32[1,8]{1,0:T(1,128)} %param.16), channel_id=1, source_target_pairs={{0,4},{4,8},{8,12},{12,16},{16,20},{20,24},{24,28},{28,0},{1,5},{5... | collective-permute-start | bytes 104 | tf_op jit(solution)/shard_map/ppermute | solution.py:233
  4.5 1.6 %collective-permute-start.4 = (s32[1,8]{1,0:T(1,128)}, s32[1,8]{1,0:T(1,128)S(1)}, u32[]{:S(2)}, u32[]{:S(2)}) collective-permute-start(s32[1,8]{1,0:T(1,128)} %param.16), channel_id=1, source_target_pairs={{0,8},{4,12},{8,16},{12,20},{16,24},{20,28},{24,0},{28,4},{1,9},{5... | collective-permute-start | bytes 104 | tf_op jit(solution)/shard_map/ppermute | solution.py:233
  6.1 2.5 %collective-permute-start.5 = (s32[1,8]{1,0:T(1,128)}, s32[1,8]{1,0:T(1,128)S(1)}, u32[]{:S(2)}, u32[]{:S(2)}) collective-permute-start(s32[1,8]{1,0:T(1,128)} %param.16), channel_id=1, source_target_pairs={{0,12},{4,16},{8,20},{12,24},{16,28},{20,0},{24,4},{28,8},{1,13},{... | collective-permute-start | bytes 104 | tf_op jit(solution)/shard_map/ppermute | solution.py:233
  8.7 0.7 constant_dynamic-update-slice_fusion.7
  9.4 0.7 reshape.877
  10.3 0.8 reduce-window.32
  11.4 0.9 reduce-window.30
  12.7 0.7 compare_and_fusion.4
  13.4 0.6 gather_fusion.2
  13.9 0.6 gather_fusion.1
  14.7 0.7 eq.244
  15.4 0.7 subtract_select_fusion
  16.2 0.9 reduce-window.21
  17.5 1.0 select_reduce_fusion
  18.5 0.7 compare_and_fusion.2
  19.3 0.7 compare_and_fusion.1
  20.1 1.3 %collective-permute-start.6 = (s32[1,8]{1,0:T(1,128)}, s32[1,8]{1,0:T(1,128)S(1)}, u32[]{:S(2)}, u32[]{:S(2)}) collective-permute-start(s32[1,8]{1,0:T(1,128)} %param.16), channel_id=1, source_target_pairs={{0,16},{4,20},{8,24},{12,28},{16,0},{20,4},{24,8},{28,12},{1,17},{... | collective-permute-start | bytes 104 | tf_op jit(solution)/shard_map/ppermute | solution.py:233
  21.4 2.6 %collective-permute-start.7 = (s32[1,8]{1,0:T(1,128)}, s32[1,8]{1,0:T(1,128)S(1)}, u32[]{:S(2)}, u32[]{:S(2)}) collective-permute-start(s32[1,8]{1,0:T(1,128)} %param.16), channel_id=1, source_target_pairs={{0,20},{4,24},{8,28},{12,0},{16,4},{20,8},{24,12},{28,16},{1,21},{... | collective-permute-start | bytes 104 | tf_op jit(solution)/shard_map/ppermute | solution.py:233
  24.0 1.3 %collective-permute-start.8 = (s32[1,8]{1,0:T(1,128)}, s32[1,8]{1,0:T(1,128)S(1)}, u32[]{:S(2)}, u32[]{:S(2)}) collective-permute-start(s32[1,8]{1,0:T(1,128)} %param.16), channel_id=1, source_target_pairs={{0,24},{4,28},{8,0},{12,4},{16,8},{20,12},{24,16},{28,20},{1,25},{... | collective-permute-start | bytes 104 | tf_op jit(solution)/shard_map/ppermute | solution.py:233
  25.4 1.6 %collective-permute-start.9 = (s32[1,8]{1,0:T(1,128)}, s32[1,8]{1,0:T(1,128)S(1)}, u32[]{:S(2)}, u32[]{:S(2)}) collective-permute-start(s32[1,8]{1,0:T(1,128)} %param.16), channel_id=1, source_target_pairs={{0,28},{4,0},{8,4},{12,8},{16,12},{20,16},{24,20},{28,24},{1,29},{... | collective-permute-start | bytes 104 | tf_op jit(solution)/shard_map/ppermute | solution.py:233
  27.0 0.7 collective-permute-done.8
  27.7 1.3 %collective-permute-done.9 = s32[1,8]{1,0:T(1,128)S(1)} collective-permute-done((s32[1,8]{1,0:T(1,128)}, s32[1,8]{1,0:T(1,128)S(1)}, u32[]{:S(2)}, u32[]{:S(2)}) %collective-permute-start.9) | collective-permute-done | bytes 64 | tf_op jit(solution)/shard_map/ppermute | solution.py:233
  29.1 0.6 gather_fusion
  30.0 0.4 multiply_cosine_fusion.1
  30.5 2.4 %fusion = f32[384]{0:T(512)S(1)} fusion(bf16[96,5120]{1,0:T(8,128)(2,1)} %collective-permute-done.2, bf16[96,5120]{1,0:T(8,128)(2,1)} %collective-permute-done.1, bf16[96,5120]{1,0:T(8,128)(2,1)S(1)} %collective-permute-done, bf16[96,5120]{1,0:T(8,128)(2,1)} %param.14), kind=kLoop, calls=%fused_computation.5 | loop fusion | flops 19660416 | bytes 3933696 | tf_op jit(solution)/shard_map/reduce_sum | solution.py:108
  32.9 4.5 %fusion.2 = bf16[384,5120]{1,0:T(8,128)(2,1)S(1)} fusion(f32[5120]{0:T(1024)S(1)} %copy-done.4, f32[384]{0:T(512)S(1)} %add_rsqrt_fusion, bf16[96,5120]{1,0:T(8,128)(2,1)} %collective-permute-done.2, bf16[96,5120]{1,0:T(8,128)(2,1)} %collective-permute-done.1, bf16[96,5120]{1,0:T(8,128)(2,1)S(1)} %collective-permute-done, bf16[96,5120]{1,0:T(8,128)(2,1)S(1)} %copy-done.2), kind=kLoop, calls=%fused_computation.7 | loop fusion | flops 21626880 | bytes 7886336 | tf_op jit(solution)/shard_map/convert_element_type | solution.py:110
  37.5 3.3 %convolution_add_fusion = f32[384,640]{1,0:T(8,128)S(1)} fusion(bf16[384,5120]{1,0:T(8,128)(2,1)S(1)} %fusion.2, bf16[5120,640]{1,0:T(8,128)(2,1)S(1)} %bitcast.310, f32[640]{0:T(1024)S(1)} %copy-done.10), kind=kOutput, calls=%fused_computation.12 | convolution fusion | flops 2516828160 | bytes 11471360 | tf_op jit(solution)/shard_map/dot_general | solution.py:112
  40.8 1.2 %convolution_add_fusion.2 = f32[384,128]{1,0:T(8,128)S(1)} fusion(bf16[384,5120]{1,0:T(8,128)(2,1)S(1)} %fusion.2, bf16[5120,128]{1,0:T(8,128)(2,1)S(1)} %copy-done, f32[128]{0:T(128)S(1)} %copy-done.8), kind=kOutput, calls=%fused_computation.18 | convolution fusion | flops 503365632 | bytes 5440000 | tf_op jit(solution)/shard_map/dot_general | solution.py:115
  42.0 0.8 fusion.51
  43.0 0.7 copy.35
  43.7 0.3 copy.34
  44.1 3.8 %fusion.9 = bf16[384,128]{0,1:T(8,128)(2,1)S(1)} fusion(bf16[384,5120]{1,0:T(8,128)(2,1)} %copy-done.1, bf16[5120,128]{1,0:T(8,128)(2,1)} %param.22, f32[128]{0:T(128)} %param.23), kind=kOutput, calls=%fused_computation.29 | convolution fusion | flops 503414784 | bytes 5341696 | tf_op jit(solution)/shard_map/dot_general | solution.py:126
  48.1 0.6 convolution_convert_fusion
  48.7 1.8 %collective-permute-start.10 = (bf16[48,896]{1,0:T(8,128)(2,1)S(1)}, bf16[48,896]{1,0:T(8,128)(2,1)S(1)}, u32[]{:S(2)}, u32[]{:S(2)}) collective-permute-start(bf16[48,896]{1,0:T(8,128)(2,1)S(1)} %get-tuple-element.59), channel_id=1, source_target_pairs={{0,4},{4,8},{8,12},{12,16},{16,20},{20,24},{24,28},{28,0},{1,5},{5... | collective-permute-start | bytes 258056 | tf_op jit(solution)/shard_map/ppermute | solution.py:249
  50.8 3.2 %collective-permute-start.12 = (bf16[48,896]{1,0:T(8,128)(2,1)S(1)}, bf16[48,896]{1,0:T(8,128)(2,1)S(1)}, u32[]{:S(2)}, u32[]{:S(2)}) collective-permute-start(bf16[48,896]{1,0:T(8,128)(2,1)S(1)} %get-tuple-element.57), channel_id=1, source_target_pairs={{0,12},{4,16},{8,20},{12,24},{16,28},{20,0},{24,4},{28,8},{1,13},{... | collective-permute-start | bytes 258056 | tf_op jit(solution)/shard_map/ppermute | solution.py:249
  54.0 0.8 collective-permute-start.13
  54.8 3.3 %collective-permute-start.14 = (bf16[48,896]{1,0:T(8,128)(2,1)S(1)}, bf16[48,896]{1,0:T(8,128)(2,1)S(1)}, u32[]{:S(2)}, u32[]{:S(2)}) collective-permute-start(bf16[48,896]{1,0:T(8,128)(2,1)S(1)} %get-tuple-element.55), channel_id=1, source_target_pairs={{0,20},{4,24},{8,28},{12,0},{16,4},{20,8},{24,12},{28,16},{1,21},{... | collective-permute-start | bytes 258056 | tf_op jit(solution)/shard_map/ppermute | solution.py:249
  58.1 0.4 collective-permute-start.15
  58.5 1.4 %collective-permute-start.16 = (bf16[48,896]{1,0:T(8,128)(2,1)S(1)}, bf16[48,896]{1,0:T(8,128)(2,1)S(1)}, u32[]{:S(2)}, u32[]{:S(2)}) collective-permute-start(bf16[48,896]{1,0:T(8,128)(2,1)S(1)} %get-tuple-element.53), channel_id=1, source_target_pairs={{0,28},{4,0},{8,4},{12,8},{16,12},{20,16},{24,20},{28,24},{1,29},{... | collective-permute-start | bytes 258056 | tf_op jit(solution)/shard_map/ppermute | solution.py:249
  59.9 3.7 %collective-permute-done.12 = bf16[48,896]{1,0:T(8,128)(2,1)S(1)} collective-permute-done((bf16[48,896]{1,0:T(8,128)(2,1)S(1)}, bf16[48,896]{1,0:T(8,128)(2,1)S(1)}, u32[]{:S(2)}, u32[]{:S(2)}) %collective-permute-start.12) | collective-permute-done | bytes 86048 | tf_op jit(solution)/shard_map/ppermute | solution.py:249
  63.6 2.4 %collective-permute-done.15 = bf16[48,896]{1,0:T(8,128)(2,1)S(1)} collective-permute-done((bf16[48,896]{1,0:T(8,128)(2,1)S(1)}, bf16[48,896]{1,0:T(8,128)(2,1)S(1)}, u32[]{:S(2)}, u32[]{:S(2)}) %collective-permute-start.15) | collective-permute-done | bytes 86048 | tf_op jit(solution)/shard_map/ppermute | solution.py:249
  66.1 0.3 convolution_convert_fusion.3
  67.0 4.3 %fusion.61 = f32[64,5120]{1,0:T(8,128)S(1)} fusion(bf16[640,5120]{1,0:T(8,128)(2,1)} %param.24, bf16[8,8,5,128]{3,2,1,0:T(8,128)(2,1)S(1)} %bitcast.299), kind=kOutput, calls=%fused_computation.137 | convolution fusion | flops 419430400 | bytes 7946240 | tf_op jit(solution)/shard_map/dot_general | solution.py:222
  71.5 0.3 convolution_convert_fusion.1
  71.8 0.3 convolution_convert_fusion.4
  72.1 1.5 %collective-permute-done.17 = f32[2,64,1280]{2,1,0:T(8,128)S(1)} collective-permute-done((f32[2,64,1280]{2,1,0:T(8,128)S(1)}, f32[2,64,1280]{2,1,0:T(8,128)S(1)}, u32[]{:S(2)}, u32[]{:S(2)}) %collective-permute-start.17) | collective-permute-done | bytes 655392 | tf_op jit(solution)/shard_map/ppermute | solution.py:266
  74.6 1.3 %fusion.58 = f32[64,5120]{1,0:T(8,128)S(1)} fusion(bf16[640,5120]{1,0:T(8,128)(2,1)S(1)} %bitcast.296, bf16[8,8,5,128]{3,2,1,0:T(8,128)(2,1)S(1)} %bitcast.300), kind=kOutput, calls=%fused_computation.134 | convolution fusion | flops 419430400 | bytes 7946240 | tf_op jit(solution)/shard_map/dot_general | solution.py:222
  76.2 0.3 convolution_convert_fusion.2
  76.5 0.6 collective-permute-start.18
  77.2 1.0 collective-permute-done.19
  78.3 0.3 fusion.168
  79.2 1.3 %fusion.55 = f32[64,5120]{1,0:T(8,128)S(1)} fusion(bf16[640,5120]{1,0:T(8,128)(2,1)S(1)} %bitcast.296, bf16[8,8,5,128]{3,2,1,0:T(8,128)(2,1)S(1)} %bitcast.301), kind=kOutput, calls=%fused_computation.131 | convolution fusion | flops 419430400 | bytes 7946240 | tf_op jit(solution)/shard_map/dot_general | solution.py:222
  80.8 5.8 %collective-permute-done.18 = f32[1,64,1280]{2,1,0:T(8,128)S(1)} collective-permute-done((f32[1,64,1280]{2,1,0:T(8,128)S(1)}, f32[1,64,1280]{2,1,0:T(8,128)S(1)}, u32[]{:S(2)}, u32[]{:S(2)}) %collective-permute-start.18) | collective-permute-done | bytes 327712 | tf_op jit(solution)/shard_map/ppermute | solution.py:266
  86.7 0.6 collective-permute-start.20
  87.4 0.3 fusion.169
  87.9 0.3 fusion.13
  88.3 1.3 %fusion.52 = f32[64,5120]{1,0:T(8,128)S(1)} fusion(bf16[640,5120]{1,0:T(8,128)(2,1)S(1)} %bitcast.296, bf16[8,8,5,128]{3,2,1,0:T(8,128)(2,1)S(1)} %bitcast.302), kind=kOutput, calls=%fused_computation.128 | convolution fusion | flops 419430400 | bytes 7946240 | tf_op jit(solution)/shard_map/dot_general | solution.py:222
  89.8 6.2 %collective-permute-done.20 = f32[1,64,1280]{2,1,0:T(8,128)S(1)} collective-permute-done((f32[1,64,1280]{2,1,0:T(8,128)S(1)}, f32[1,64,1280]{2,1,0:T(8,128)S(1)}, u32[]{:S(2)}, u32[]{:S(2)}) %collective-permute-start.20) | collective-permute-done | bytes 327712 | tf_op jit(solution)/shard_map/ppermute | solution.py:266
  96.0 0.6 collective-permute-start.22
  96.8 1.6 %collective-permute-start.24 = (f32[1,64,1280]{2,1,0:T(8,128)S(1)}, f32[1,64,1280]{2,1,0:T(8,128)S(1)}, u32[]{:S(2)}, u32[]{:S(2)}) collective-permute-start(f32[1,64,1280]{2,1,0:T(8,128)S(1)} %get-tuple-element.30), channel_id=1, source_target_pairs={{0,2},{1,3},{2,0},{3,1},{4,6},{5,7},{6,4},{7,5},{8,10},{9,11},{10,... | collective-permute-start | bytes 983048 | tf_op jit(solution)/shard_map/ppermute | solution.py:266
  98.3 8.4 %collective-permute-done.22 = f32[1,64,1280]{2,1,0:T(8,128)S(1)} collective-permute-done((f32[1,64,1280]{2,1,0:T(8,128)S(1)}, f32[1,64,1280]{2,1,0:T(8,128)S(1)}, u32[]{:S(2)}, u32[]{:S(2)}) %collective-permute-start.22) | collective-permute-done | bytes 327712 | tf_op jit(solution)/shard_map/ppermute | solution.py:266
  106.8 4.6 %collective-permute-done.24 = f32[1,64,1280]{2,1,0:T(8,128)S(1)} collective-permute-done((f32[1,64,1280]{2,1,0:T(8,128)S(1)}, f32[1,64,1280]{2,1,0:T(8,128)S(1)}, u32[]{:S(2)}, u32[]{:S(2)}) %collective-permute-start.24) | collective-permute-done | bytes 327712 | tf_op jit(solution)/shard_map/ppermute | solution.py:266
  111.4 0.9 pad_maximum_fusion.5
  (160 shorter events, 7.1 us)
Async XLA Ops:
  0.0 40.8 %copy-start = (bf16[5120,128]{1,0:T(8,128)(2,1)S(1)}, bf16[5120,128]{1,0:T(8,128)(2,1)}, u32[]{:S(2)}) copy-start(bf16[5120,128]{1,0:T(8,128)(2,1)} %param.20) | copy-start | bytes 3932164
  0.0 32.9 %copy-start.2 = (bf16[96,5120]{1,0:T(8,128)(2,1)S(1)}, bf16[96,5120]{1,0:T(8,128)(2,1)}, u32[]{:S(2)}) copy-start(bf16[96,5120]{1,0:T(8,128)(2,1)} %param.14) | copy-start | bytes 2949124
  0.0 32.9 %copy-start.4 = (f32[5120]{0:T(1024)S(1)}, f32[5120]{0:T(1024)}, u32[]{:S(2)}) copy-start(f32[5120]{0:T(1024)} %param.17) | copy-start | bytes 61444
  0.0 27.7 %collective-permute-start = (bf16[96,5120]{1,0:T(8,128)(2,1)}, bf16[96,5120]{1,0:T(8,128)(2,1)S(1)}, u32[]{:S(2)}, u32[]{:S(2)}) collective-permute-start(bf16[96,5120]{1,0:T(8,128)(2,1)} %param.14), channel_id=1, source_target_pairs={{0,2},{1,3},{2,0},{3,1},{4,6},{5,7},{6,4},{7,5},{8,10},{9,11},{10,... | collective-permute-start | bytes 2949128 | tf_op jit(solution)/shard_map/ppermute | solution.py:312
  3.0 27.4 %collective-permute-start.1 = (bf16[96,5120]{1,0:T(8,128)(2,1)}, bf16[96,5120]{1,0:T(8,128)(2,1)}, u32[]{:S(2)}, u32[]{:S(2)}) collective-permute-start(bf16[96,5120]{1,0:T(8,128)(2,1)} %param.14), channel_id=1, source_target_pairs={{0,1},{1,0},{2,3},{3,2},{4,5},{5,4},{6,7},{7,6},{8,9},{9,8},{10,11... | collective-permute-start | bytes 2949128 | tf_op jit(solution)/shard_map/ppermute | solution.py:312
  3.0 17.0 %collective-permute-start.3 = (s32[1,8]{1,0:T(1,128)}, s32[1,8]{1,0:T(1,128)S(1)}, u32[]{:S(2)}, u32[]{:S(2)}) collective-permute-start(s32[1,8]{1,0:T(1,128)} %param.16), channel_id=1, source_target_pairs={{0,4},{4,8},{8,12},{12,16},{16,20},{20,24},{24,28},{28,0},{1,5},{5... | collective-permute-start | bytes 104 | tf_op jit(solution)/shard_map/ppermute | solution.py:233
  4.5 16.8 %collective-permute-start.4 = (s32[1,8]{1,0:T(1,128)}, s32[1,8]{1,0:T(1,128)S(1)}, u32[]{:S(2)}, u32[]{:S(2)}) collective-permute-start(s32[1,8]{1,0:T(1,128)} %param.16), channel_id=1, source_target_pairs={{0,8},{4,12},{8,16},{12,20},{16,24},{20,28},{24,0},{28,4},{1,9},{5... | collective-permute-start | bytes 104 | tf_op jit(solution)/shard_map/ppermute | solution.py:233
  6.1 17.9 %collective-permute-start.5 = (s32[1,8]{1,0:T(1,128)}, s32[1,8]{1,0:T(1,128)S(1)}, u32[]{:S(2)}, u32[]{:S(2)}) collective-permute-start(s32[1,8]{1,0:T(1,128)} %param.16), channel_id=1, source_target_pairs={{0,12},{4,16},{8,20},{12,24},{16,28},{20,0},{24,4},{28,8},{1,13},{... | collective-permute-start | bytes 104 | tf_op jit(solution)/shard_map/ppermute | solution.py:233
  20.1 5.3 %collective-permute-start.6 = (s32[1,8]{1,0:T(1,128)}, s32[1,8]{1,0:T(1,128)S(1)}, u32[]{:S(2)}, u32[]{:S(2)}) collective-permute-start(s32[1,8]{1,0:T(1,128)} %param.16), channel_id=1, source_target_pairs={{0,16},{4,20},{8,24},{12,28},{16,0},{20,4},{24,8},{28,12},{1,17},{... | collective-permute-start | bytes 104 | tf_op jit(solution)/shard_map/ppermute | solution.py:233
  21.4 5.6 %collective-permute-start.7 = (s32[1,8]{1,0:T(1,128)}, s32[1,8]{1,0:T(1,128)S(1)}, u32[]{:S(2)}, u32[]{:S(2)}) collective-permute-start(s32[1,8]{1,0:T(1,128)} %param.16), channel_id=1, source_target_pairs={{0,20},{4,24},{8,28},{12,0},{16,4},{20,8},{24,12},{28,16},{1,21},{... | collective-permute-start | bytes 104 | tf_op jit(solution)/shard_map/ppermute | solution.py:233
  24.0 3.7 %collective-permute-start.8 = (s32[1,8]{1,0:T(1,128)}, s32[1,8]{1,0:T(1,128)S(1)}, u32[]{:S(2)}, u32[]{:S(2)}) collective-permute-start(s32[1,8]{1,0:T(1,128)} %param.16), channel_id=1, source_target_pairs={{0,24},{4,28},{8,0},{12,4},{16,8},{20,12},{24,16},{28,20},{1,25},{... | collective-permute-start | bytes 104 | tf_op jit(solution)/shard_map/ppermute | solution.py:233
  25.4 3.7 %collective-permute-start.9 = (s32[1,8]{1,0:T(1,128)}, s32[1,8]{1,0:T(1,128)S(1)}, u32[]{:S(2)}, u32[]{:S(2)}) collective-permute-start(s32[1,8]{1,0:T(1,128)} %param.16), channel_id=1, source_target_pairs={{0,28},{4,0},{8,4},{12,8},{16,12},{20,16},{24,20},{28,24},{1,29},{... | collective-permute-start | bytes 104 | tf_op jit(solution)/shard_map/ppermute | solution.py:233
  27.7 2.7 %collective-permute-start.2 = (bf16[96,5120]{1,0:T(8,128)(2,1)S(1)}, bf16[96,5120]{1,0:T(8,128)(2,1)}, u32[]{:S(2)}, u32[]{:S(2)}) collective-permute-start(bf16[96,5120]{1,0:T(8,128)(2,1)S(1)} %collective-permute-done), channel_id=1, source_target_pairs={{0,1},{1,0},{2,3},{3,2},{4,5},{5,4},{6,7},{7,6},{8,9},{9,8},{10,11... | collective-permute-start | bytes 2949128 | tf_op jit(solution)/shard_map/ppermute | solution.py:312
  30.5 7.0 %slice-start.2 = ((s8[6553600]{0:T(1024)(128)(4,1)}), s8[4194304]{0:T(1024)(128)(4,1)S(1)}, s32[]{:S(2)}) async-start(s8[6553600]{0:T(1024)(128)(4,1)} %bitcast.309), calls=%async_computation.2 | async-start | bytes 8388608
  32.9 4.5 %slice-start.3 = ((s8[6553600]{0:T(1024)(128)(4,1)}), s8[2359296]{0:T(1024)(128)(4,1)S(1)}, s32[]{:S(2)}) async-start(s8[6553600]{0:T(1024)(128)(4,1)} %bitcast.309), calls=%async_computation.3 | async-start | bytes 4718592
  32.9 4.5 %copy-start.10 = (f32[640]{0:T(1024)S(1)}, f32[640]{0:T(1024)}, u32[]{:S(2)}) copy-start(f32[640]{0:T(1024)} %param.19) | copy-start | bytes 7684
  37.5 3.3 %copy-start.1 = (bf16[384,5120]{1,0:T(8,128)(2,1)}, bf16[384,5120]{1,0:T(8,128)(2,1)S(1)}, u32[]{:S(2)}) copy-start(bf16[384,5120]{1,0:T(8,128)(2,1)S(1)} %fusion.2) | copy-start | bytes 11796484
  37.5 3.4 %copy-start.8 = (f32[128]{0:T(128)S(1)}, f32[128]{0:T(128)}, u32[]{:S(2)}) copy-start(f32[128]{0:T(128)} %param.21) | copy-start | bytes 1540
  44.0 4.0 %copy-start.3 = (bf16[384,64]{0,1:T(8,128)(2,1)S(1)}, bf16[384,64]{0,1:T(8,128)(2,1)}, u32[]{:S(2)}) copy-start(bf16[384,64]{0,1:T(8,128)(2,1)} %copy.35) | copy-start | bytes 147460
  44.1 4.0 %copy-start.9 = (s32[384]{0:T(512)S(1)}, s32[384]{0:T(512)}, u32[]{:S(2)}) copy-start(s32[384]{0:T(512)} %eq.244) | copy-start | bytes 4612
  47.8 2.7 %copy-start.5 = (s32[256]{0:T(256)S(1)}, s32[256]{0:T(256)}, u32[]{:S(2)}) copy-start(s32[256]{0:T(256)} %select_reduce_fusion) | copy-start | bytes 3076
  48.0 18.4 %copy-start.7 = (pred[64,64]{0,1:T(8,128)(4,1)S(1)}, pred[64,64]{0,1:T(8,128)(4,1)}, u32[]{:S(2)}) copy-start(pred[64,64]{0,1:T(8,128)(4,1)} %compare_and_fusion.2) | copy-start | bytes 12292
  48.7 9.4 %collective-permute-start.10 = (bf16[48,896]{1,0:T(8,128)(2,1)S(1)}, bf16[48,896]{1,0:T(8,128)(2,1)S(1)}, u32[]{:S(2)}, u32[]{:S(2)}) collective-permute-start(bf16[48,896]{1,0:T(8,128)(2,1)S(1)} %get-tuple-element.59), channel_id=1, source_target_pairs={{0,4},{4,8},{8,12},{12,16},{16,20},{20,24},{24,28},{28,0},{1,5},{5... | collective-permute-start | bytes 258056 | tf_op jit(solution)/shard_map/ppermute | solution.py:249
  50.6 7.9 %collective-permute-start.11 = (bf16[48,896]{1,0:T(8,128)(2,1)S(1)}, bf16[48,896]{1,0:T(8,128)(2,1)S(1)}, u32[]{:S(2)}, u32[]{:S(2)}) collective-permute-start(bf16[48,896]{1,0:T(8,128)(2,1)S(1)} %get-tuple-element.58), channel_id=1, source_target_pairs={{0,8},{4,12},{8,16},{12,20},{16,24},{20,28},{24,0},{28,4},{1,9},{5... | collective-permute-start | bytes 258056 | tf_op jit(solution)/shard_map/ppermute | solution.py:249
  50.8 12.8 %collective-permute-start.12 = (bf16[48,896]{1,0:T(8,128)(2,1)S(1)}, bf16[48,896]{1,0:T(8,128)(2,1)S(1)}, u32[]{:S(2)}, u32[]{:S(2)}) collective-permute-start(bf16[48,896]{1,0:T(8,128)(2,1)S(1)} %get-tuple-element.57), channel_id=1, source_target_pairs={{0,12},{4,16},{8,20},{12,24},{16,28},{20,0},{24,4},{28,8},{1,13},{... | collective-permute-start | bytes 258056 | tf_op jit(solution)/shard_map/ppermute | solution.py:249
  54.0 9.6 %collective-permute-start.13 = (bf16[48,896]{1,0:T(8,128)(2,1)S(1)}, bf16[48,896]{1,0:T(8,128)(2,1)S(1)}, u32[]{:S(2)}, u32[]{:S(2)}) collective-permute-start(bf16[48,896]{1,0:T(8,128)(2,1)S(1)} %get-tuple-element.56), channel_id=1, source_target_pairs={{0,16},{4,20},{8,24},{12,28},{16,0},{20,4},{24,8},{28,12},{1,17},{... | collective-permute-start | bytes 258056 | tf_op jit(solution)/shard_map/ppermute | solution.py:249
  54.8 8.8 %collective-permute-start.14 = (bf16[48,896]{1,0:T(8,128)(2,1)S(1)}, bf16[48,896]{1,0:T(8,128)(2,1)S(1)}, u32[]{:S(2)}, u32[]{:S(2)}) collective-permute-start(bf16[48,896]{1,0:T(8,128)(2,1)S(1)} %get-tuple-element.55), channel_id=1, source_target_pairs={{0,20},{4,24},{8,28},{12,0},{16,4},{20,8},{24,12},{28,16},{1,21},{... | collective-permute-start | bytes 258056 | tf_op jit(solution)/shard_map/ppermute | solution.py:249
  58.1 7.9 %collective-permute-start.15 = (bf16[48,896]{1,0:T(8,128)(2,1)S(1)}, bf16[48,896]{1,0:T(8,128)(2,1)S(1)}, u32[]{:S(2)}, u32[]{:S(2)}) collective-permute-start(bf16[48,896]{1,0:T(8,128)(2,1)S(1)} %get-tuple-element.54), channel_id=1, source_target_pairs={{0,24},{4,28},{8,0},{12,4},{16,8},{20,12},{24,16},{28,20},{1,25},{... | collective-permute-start | bytes 258056 | tf_op jit(solution)/shard_map/ppermute | solution.py:249
  58.5 7.6 %collective-permute-start.16 = (bf16[48,896]{1,0:T(8,128)(2,1)S(1)}, bf16[48,896]{1,0:T(8,128)(2,1)S(1)}, u32[]{:S(2)}, u32[]{:S(2)}) collective-permute-start(bf16[48,896]{1,0:T(8,128)(2,1)S(1)} %get-tuple-element.53), channel_id=1, source_target_pairs={{0,28},{4,0},{8,4},{12,8},{16,12},{20,16},{24,20},{28,24},{1,29},{... | collective-permute-start | bytes 258056 | tf_op jit(solution)/shard_map/ppermute | solution.py:249
  67.0 7.6 %slice-start = ((s8[6553600]{0:T(1024)(128)(4,1)}), s8[4194304]{0:T(1024)(128)(4,1)S(1)}, s32[]{:S(2)}) async-start(s8[6553600]{0:T(1024)(128)(4,1)} %bitcast.295), calls=%async_computation | async-start | bytes 8388608
  67.0 7.6 %slice-start.1 = ((s8[6553600]{0:T(1024)(128)(4,1)}), s8[2359296]{0:T(1024)(128)(4,1)S(1)}, s32[]{:S(2)}) async-start(s8[6553600]{0:T(1024)(128)(4,1)} %bitcast.295), calls=%async_computation.1 | async-start | bytes 4718592
  71.3 2.4 %copy-start.6 = (pred[64,128]{1,0:T(8,128)(4,1)S(1)}, pred[64,128]{1,0:T(8,128)(4,1)}, u32[]{:S(2)}) copy-start(pred[64,128]{1,0:T(8,128)(4,1)} %compare_and_fusion.1) | copy-start | bytes 24580
  71.4 2.2 %collective-permute-start.17 = (f32[2,64,1280]{2,1,0:T(8,128)S(1)}, f32[2,64,1280]{2,1,0:T(8,128)S(1)}, u32[]{:S(2)}, u32[]{:S(2)}) collective-permute-start(f32[2,64,1280]{2,1,0:T(8,128)S(1)} %pad_maximum_fusion.1), channel_id=1, source_target_pairs={{0,1},{1,0},{2,3},{3,2},{4,5},{5,4},{6,7},{7,6},{8,9},{9,8},{10,11... | collective-permute-start | bytes 1966088 | tf_op jit(solution)/shard_map/ppermute | solution.py:266
  76.0 2.2 %collective-permute-start.19 = (f32[2,64,1280]{2,1,0:T(8,128)S(1)}, f32[2,64,1280]{2,1,0:T(8,128)S(1)}, u32[]{:S(2)}, u32[]{:S(2)}) collective-permute-start(f32[2,64,1280]{2,1,0:T(8,128)S(1)} %pad_maximum_fusion.2), channel_id=1, source_target_pairs={{0,1},{1,0},{2,3},{3,2},{4,5},{5,4},{6,7},{7,6},{8,9},{9,8},{10,11... | collective-permute-start | bytes 1966088 | tf_op jit(solution)/shard_map/ppermute | solution.py:266
  76.5 10.1 %collective-permute-start.18 = (f32[1,64,1280]{2,1,0:T(8,128)S(1)}, f32[1,64,1280]{2,1,0:T(8,128)S(1)}, u32[]{:S(2)}, u32[]{:S(2)}) collective-permute-start(f32[1,64,1280]{2,1,0:T(8,128)S(1)} %select_bitcast_fusion.9), channel_id=1, source_target_pairs={{0,2},{1,3},{2,0},{3,1},{4,6},{5,7},{6,4},{7,5},{8,10},{9,11},{10,... | collective-permute-start | bytes 983048 | tf_op jit(solution)/shard_map/ppermute | solution.py:266
  80.6 6.7 %collective-permute-start.21 = (f32[2,64,1280]{2,1,0:T(8,128)S(1)}, f32[2,64,1280]{2,1,0:T(8,128)S(1)}, u32[]{:S(2)}, u32[]{:S(2)}) collective-permute-start(f32[2,64,1280]{2,1,0:T(8,128)S(1)} %pad_maximum_fusion.3), channel_id=1, source_target_pairs={{0,1},{1,0},{2,3},{3,2},{4,5},{5,4},{6,7},{7,6},{8,9},{9,8},{10,11... | collective-permute-start | bytes 1966088 | tf_op jit(solution)/shard_map/ppermute | solution.py:266
  86.7 9.2 %collective-permute-start.20 = (f32[1,64,1280]{2,1,0:T(8,128)S(1)}, f32[1,64,1280]{2,1,0:T(8,128)S(1)}, u32[]{:S(2)}, u32[]{:S(2)}) collective-permute-start(f32[1,64,1280]{2,1,0:T(8,128)S(1)} %select_bitcast_fusion.6), channel_id=1, source_target_pairs={{0,2},{1,3},{2,0},{3,1},{4,6},{5,7},{6,4},{7,5},{8,10},{9,11},{10,... | collective-permute-start | bytes 983048 | tf_op jit(solution)/shard_map/ppermute | solution.py:266
  89.7 6.9 %collective-permute-start.23 = (f32[2,64,1280]{2,1,0:T(8,128)S(1)}, f32[2,64,1280]{2,1,0:T(8,128)S(1)}, u32[]{:S(2)}, u32[]{:S(2)}) collective-permute-start(f32[2,64,1280]{2,1,0:T(8,128)S(1)} %pad_maximum_fusion.4), channel_id=1, source_target_pairs={{0,1},{1,0},{2,3},{3,2},{4,5},{5,4},{6,7},{7,6},{8,9},{9,8},{10,11... | collective-permute-start | bytes 1966088 | tf_op jit(solution)/shard_map/ppermute | solution.py:266
  96.0 10.7 %collective-permute-start.22 = (f32[1,64,1280]{2,1,0:T(8,128)S(1)}, f32[1,64,1280]{2,1,0:T(8,128)S(1)}, u32[]{:S(2)}, u32[]{:S(2)}) collective-permute-start(f32[1,64,1280]{2,1,0:T(8,128)S(1)} %select_bitcast_fusion.3), channel_id=1, source_target_pairs={{0,2},{1,3},{2,0},{3,1},{4,6},{5,7},{6,4},{7,5},{8,10},{9,11},{10,... | collective-permute-start | bytes 983048 | tf_op jit(solution)/shard_map/ppermute | solution.py:266
  96.8 14.6 %collective-permute-start.24 = (f32[1,64,1280]{2,1,0:T(8,128)S(1)}, f32[1,64,1280]{2,1,0:T(8,128)S(1)}, u32[]{:S(2)}, u32[]{:S(2)}) collective-permute-start(f32[1,64,1280]{2,1,0:T(8,128)S(1)} %get-tuple-element.30), channel_id=1, source_target_pairs={{0,2},{1,3},{2,0},{3,1},{4,6},{5,7},{6,4},{7,5},{8,10},{9,11},{10,... | collective-permute-start | bytes 983048 | tf_op jit(solution)/shard_map/ppermute | solution.py:266

commit v12 on v10

--- a/solution.py
+++ b/solution.py
@@ -135,7 +135,11 @@
             axis=1,
         )
 
-    qkv = project(jnp.concatenate(pieces, axis=0), sequence_starts)
+    own_rows = pieces[0].shape[0]
+    qkv_parts = [project(pieces[0], sequence_starts[:own_rows])]
+    if len(pieces) > 1:
+        qkv_parts.append(project(jnp.concatenate(pieces[1:], axis=0), sequence_starts[own_rows:]))
+    qkv = jnp.concatenate(qkv_parts, axis=0)
 
     shift_order = ctx_count <= 8
     if shift_order:
@@ -166,15 +170,8 @@
     slot_ids = jnp.arange(pack_len, dtype=jnp.int32)
     names_slot = my_slot_of_row[None, :] == slot_ids[:, None]
     source_of_slot = jnp.sum(jnp.where(names_slot, arrived_index[None, :], 0), axis=1)
-    packed_qkv = select_rows(source_of_slot, arrived)
-
     q_width = local_heads * head_dim
     kv_width = local_kv * head_dim
-    query_matrix = packed_qkv[:, :q_width].reshape(pack_len, local_kv, query_group_count, head_dim)
-    projected_key_rows = packed_qkv[:, q_width : q_width + kv_width].reshape(
-        pack_len, local_kv, head_dim
-    )
-    projected_value_rows = packed_qkv[:, q_width + kv_width :].reshape(pack_len, local_kv, head_dim)
 
     own_lengths = seq_len[0]
     own_ends = jnp.cumsum(own_lengths).astype(jnp.int32)
@@ -184,13 +181,24 @@
     chunk_count = 4 if pack_len % 32 == 0 else 1
     chunk_len = pack_len // chunk_count
     results = []
+    key_parts, value_parts = [], []
     for chunk in range(chunk_count):
         lo, hi = chunk * chunk_len, (chunk + 1) * chunk_len
+        chunk_qkv = select_rows(source_of_slot[lo:hi], arrived)
+        query_matrix = chunk_qkv[:, :q_width].reshape(
+            chunk_len, local_kv, query_group_count, head_dim
+        )
+        key_parts.append(chunk_qkv[:, q_width : q_width + kv_width])
+        value_parts.append(chunk_qkv[:, q_width + kv_width :])
+        projected_key_rows = jnp.concatenate(key_parts, axis=0).reshape(hi, local_kv, head_dim)
+        projected_value_rows = jnp.concatenate(value_parts, axis=0).reshape(
+            hi, local_kv, head_dim
+        )
         scores = (
             jnp.einsum(
                 "qkgd,tkd->kgqt",
-                query_matrix[lo:hi],
-                projected_key_rows[:hi],
+                query_matrix,
+                projected_key_rows,
                 preferred_element_type=jnp.float32,
             )
             * score_scale
@@ -206,7 +214,7 @@
         mixed_heads = jnp.einsum(
             "kgqt,tkd->qkgd",
             probability,
-            projected_value_rows[:hi],
+            projected_value_rows,
             preferred_element_type=jnp.float32,
         )
         mixed_heads = mixed_heads.astype(jnp.bfloat16).reshape(chunk_len, local_heads * head_dim)

time: 112 us -> 140 us (1.25)
  the two profiles are of different devices: /device:TPU:0 before, /device:TPU:12 now
where the time goes in v12:
time: 140 us; the launch traced here: 139 us
  waiting for transfers between devices  38.6 us (28%)
  matrix products  30.6 us (22%)
  starting transfers between devices  28.4 us (20%)
  other arithmetic  25.4 us (18%)
  local copies, waits for them, and re-layouts  15.4 us (11%)
    ppermute x8, waiting for transfers between devices, halving_scatter(): got = lax.ppermute(send, axis_name, pairs)  26.4 us
    ppermute x7, starting transfers between devices, exchange(): arrived.append(lax.ppermute(chunks[shift], axis_name, pairs))  11.7 us
    ppermute x7, starting transfers between devices, shift_gather(): lax.ppermute(part, axis_name, [(i, (i + shift) % count) for i in range(co...  10.5 us
    dot_general x2, matrix products, project(): jnp.dot(normalized_input, w_query, preferred_element_type=jnp.float32)  10.4 us
    ppermute x7, waiting for transfers between devices, exchange(): arrived.append(lax.ppermute(chunks[shift], axis_name, pairs))  9.1 us
    dot_general x4, matrix products, local(): jnp.dot(mixed_heads, w_out, preferred_element_type=jnp.float32)  8.09 us
    and x4, other arithmetic, local(): (segment[lo:hi, None] == segment[None, :hi]) & (slot_ids[None, :hi] <= sl...  5.27 us
    ppermute x8, starting transfers between devices, halving_scatter(): got = lax.ppermute(send, axis_name, pairs)  4.66 us
  transfers between devices with their start and end apart: 25, of which 10 were waited for; matrix products, arithmetic and copies ran while one was open for 33% of the time, Pallas kernels for 0%

profile of v12, /device:TPU:12, one launch (start us, length us, event | category | flops | bytes accessed | tf_op | source)
XLA Modules:
  0.0 139.2 jit_solution(5442559056521665980)
XLA Ops:
  0.0 1.6 %collective-permute-start.7 = (bf16[96,5120]{1,0:T(8,128)(2,1)}, bf16[96,5120]{1,0:T(8,128)(2,1)S(1)}, u32[]{:S(2)}, u32[]{:S(2)}) collective-permute-start(bf16[96,5120]{1,0:T(8,128)(2,1)} %param.14), channel_id=1, source_target_pairs={{0,2},{1,3},{2,0},{3,1},{4,6},{5,7},{6,4},{7,5},{8,10},{9,11},{10,... | collective-permute-start | bytes 2949128 | tf_op jit(solution)/shard_map/ppermute | solution.py:294
  1.6 1.5 %collective-permute-start = (s32[1,8]{1,0:T(1,128)}, s32[1,8]{1,0:T(1,128)}, u32[]{:S(2)}, u32[]{:S(2)}) collective-permute-start(s32[1,8]{1,0:T(1,128)} %param.16), channel_id=1, source_target_pairs={{0,4},{4,8},{8,12},{12,16},{16,20},{20,24},{24,28},{28,0},{1,5},{5... | collective-permute-start | bytes 104 | tf_op jit(solution)/shard_map/ppermute | solution.py:231
  3.1 1.6 %collective-permute-start.1 = (s32[1,8]{1,0:T(1,128)}, s32[1,8]{1,0:T(1,128)}, u32[]{:S(2)}, u32[]{:S(2)}) collective-permute-start(s32[1,8]{1,0:T(1,128)} %param.16), channel_id=1, source_target_pairs={{0,8},{4,12},{8,16},{12,20},{16,24},{20,28},{24,0},{28,4},{1,9},{5... | collective-permute-start | bytes 104 | tf_op jit(solution)/shard_map/ppermute | solution.py:231
  4.7 1.2 collective-permute-start.2
  6.4 0.7 constant_dynamic-update-slice_fusion.7
  7.7 0.7 reshape.984
  8.5 1.5 %fusion.3 = f32[96]{0:T(128)S(1)} fusion(bf16[96,5120]{1,0:T(8,128)(2,1)} %param.14), kind=kLoop, calls=%fused_computation.13 | loop fusion | flops 1474464 | bytes 983424 | tf_op jit(solution)/shard_map/reduce_sum | solution.py:108
  10.6 0.8 reduce-window.32
  13.2 0.7 slice.271
  14.5 0.8 reduce-window.30
  15.7 0.7 compare_and_fusion.4
  17.6 0.7 broadcast_select_fusion.2
  19.5 1.7 %fusion.19 = bf16[96,128]{1,0:T(8,128)(2,1)S(1)} fusion(bf16[5120,128]{1,0:T(8,128)(2,1)S(1)} %copy-done, f32[128]{0:T(128)} %param.23, bf16[96,5120]{1,0:T(8,128)(2,1)} %param.14, f32[5120]{0:T(1024)} %param.17, f32[96]{0:T(128)S(1)} %add_rsqrt_fusion.1), kind=kOutput, calls=%fused_computation.48 | convolution fusion | flops 127819776 | bytes 2339712 | tf_op jit(solution)/shard_map/dot_general | solution.py:126
  21.3 0.7 copy.40
  22.0 4.3 %convolution_add_fusion.1 = f32[96,640]{1,0:T(8,128)S(1)} fusion(bf16[5120,640]{1,0:T(8,128)(2,1)} %param.18, f32[640]{0:T(1024)} %param.19, bf16[96,5120]{1,0:T(8,128)(2,1)S(1)} %copy-done.1, f32[5120]{0:T(1024)S(1)} %copy-done.5, f32[96]{0:T(128)} %copy-done.18), kind=kOutput, calls=%fused_computation.22 | convolution fusion | flops 631173120 | bytes 7805824 | tf_op jit(solution)/shard_map/dot_general | solution.py:112
  26.4 1.1 convolution_add_fusion.5
  27.7 1.3 eq.245
  29.0 0.7 add.253
  29.8 0.9 reduce-window.21
  31.2 1.0 select_reduce_fusion
  32.2 1.3 fusion.102
  33.5 1.3 compare_and_fusion.2
  34.8 1.3 compare_and_fusion
  36.1 1.4 compare_and_fusion.1
  37.5 1.7 %collective-permute-start.3 = (s32[1,8]{1,0:T(1,128)}, s32[1,8]{1,0:T(1,128)S(1)}, u32[]{:S(2)}, u32[]{:S(2)}) collective-permute-start(s32[1,8]{1,0:T(1,128)} %param.16), channel_id=1, source_target_pairs={{0,16},{4,20},{8,24},{12,28},{16,0},{20,4},{24,8},{28,12},{1,17},{... | collective-permute-start | bytes 104 | tf_op jit(solution)/shard_map/ppermute | solution.py:231
  39.1 0.7 constant_dynamic-update-slice_fusion.6
  39.8 1.3 collective-permute-start.4
  41.7 1.3 collective-permute-start.5
  43.1 0.7 constant_dynamic-update-slice_fusion.4
  43.8 1.9 %collective-permute-start.6 = (s32[1,8]{1,0:T(1,128)}, s32[1,8]{1,0:T(1,128)S(1)}, u32[]{:S(2)}, u32[]{:S(2)}) collective-permute-start(s32[1,8]{1,0:T(1,128)} %param.16), channel_id=1, source_target_pairs={{0,28},{4,0},{8,4},{12,8},{16,12},{20,16},{24,20},{28,24},{1,29},{... | collective-permute-start | bytes 104 | tf_op jit(solution)/shard_map/ppermute | solution.py:231
  45.7 2.7 %collective-permute-done.6 = s32[1,8]{1,0:T(1,128)S(1)} collective-permute-done((s32[1,8]{1,0:T(1,128)}, s32[1,8]{1,0:T(1,128)S(1)}, u32[]{:S(2)}, u32[]{:S(2)}) %collective-permute-start.6) | collective-permute-done | bytes 64 | tf_op jit(solution)/shard_map/ppermute | solution.py:231
  48.3 0.7 gather_fusion
  49.0 0.7 broadcast_select_fusion
  50.0 1.1 fusion.124
  51.3 0.7 copy.38
  52.0 0.9 multiply_cosine_fusion.3
  53.0 1.1 multiply_cosine_fusion.1
  54.5 2.1 %fusion = f32[288]{0:T(512)S(1)} fusion(bf16[96,5120]{1,0:T(8,128)(2,1)S(1)} %collective-permute-done.9, bf16[96,5120]{1,0:T(8,128)(2,1)} %collective-permute-done.8, bf16[96,5120]{1,0:T(8,128)(2,1)S(1)} %collective-permute-done.7), kind=kLoop, calls=%fused_computation.5 | loop fusion | flops 11796192 | bytes 2950272 | tf_op jit(solution)/shard_map/reduce_sum | solution.py:108
  56.7 2.2 %fusion.12 = bf16[288,128]{1,0:T(8,128)(2,1)S(1)} fusion(bf16[5120,128]{1,0:T(8,128)(2,1)S(1)} %copy-done, f32[128]{0:T(128)S(1)} %copy-done.22, f32[5120]{0:T(1024)S(1)} %copy-done.7, f32[288]{0:T(512)S(1)} %add_rsqrt_fusion, bf16[96,5120]{1,0:T(8,128)(2,1)S(1)} %collective-permute-done.9, bf16[96,5120]{1,0:T(8,128)(2,1)} %collective-permute-done.8, ...), kind=kOutput, calls=%fused_computation.39 | convolution fusion | flops 390832128 | bytes 4355712 | tf_op jit(solution)/shard_map/dot_general | solution.py:126
  59.1 6.1 %convolution_add_fusion = f32[288,640]{1,0:T(8,128)S(1)} fusion(bf16[5120,640]{1,0:T(8,128)(2,1)} %param.18, f32[640]{0:T(1024)S(1)} %copy-done.17, f32[5120]{0:T(1024)S(1)} %copy-done.8, f32[288]{0:T(512)S(1)} %add_rsqrt_fusion, bf16[96,5120]{1,0:T(8,128)(2,1)} %copy-done.2, bf16[96,5120]{1,0:T(8,128)(2,1)} %collective-permute-done.8, ...), kind=kOutput, calls=%fused_computation.17 | convolution fusion | flops 1900892160 | bytes 10264192 | tf_op jit(solution)/shard_map/dot_general | solution.py:112
  65.3 2.2 %convolution_add_fusion.3 = f32[288,128]{1,0:T(8,128)S(1)} fusion(bf16[5120,128]{1,0:T(8,128)(2,1)S(1)} %copy-done.21, f32[128]{0:T(128)S(1)} %copy-done.24, f32[5120]{0:T(1024)S(1)} %copy-done.8, f32[288]{0:T(512)S(1)} %add_rsqrt_fusion, bf16[96,5120]{1,0:T(8,128)(2,1)S(1)} %copy-done.3, bf16[96,5120]{1,0:T(8,128)(2,1)} %collective-permute-done.8, ...), kind=kOutput, calls=%fused_computation.34 | convolution fusion | flops 390795264 | bytes 4429440 | tf_op jit(solution)/shard_map/dot_general | solution.py:115
  68.3 0.7 copy.42
  69.5 1.5 %convolution_convert_fusion = bf16[384,896]{1,0:T(8,128)(2,1)S(1)} fusion(bf16[288,128]{0,1:T(8,128)(2,1)S(1)} %copy.44, bf16[288,64]{0,1:T(8,128)(2,1)S(1)} %copy.43, bf16[288,64]{0,1:T(8,128)(2,1)} %copy.42, bf16[288,640]{0,1:T(8,128)(2,1)S(1)} %bitcast.317, bf16[96,128]{0,1:T(8,128)(2,1)} %copy.40, bf16[96,64]{0,1:T(8,128)(2,1)S(1)} %copy.39, ...), kind=kOutput, calls=%fused_computation.16 | convolution fusion | flops 270237696 | bytes 1377792 | tf_op jit(solution)/shard_map/dot_general | solution.py:157
  71.1 0.7 collective-permute-start.10
  71.8 1.4 collective-permute-start.11
  73.2 3.6 %collective-permute-start.12 = (bf16[48,896]{1,0:T(8,128)(2,1)S(1)}, bf16[48,896]{1,0:T(8,128)(2,1)S(1)}, u32[]{:S(2)}, u32[]{:S(2)}) collective-permute-start(bf16[48,896]{1,0:T(8,128)(2,1)S(1)} %get-tuple-element.46), channel_id=1, source_target_pairs={{0,12},{4,16},{8,20},{12,24},{16,28},{20,0},{24,4},{28,8},{1,13},{... | collective-permute-start | bytes 258056 | tf_op jit(solution)/shard_map/ppermute | solution.py:247
  76.9 2.1 %collective-permute-start.14 = (bf16[48,896]{1,0:T(8,128)(2,1)S(1)}, bf16[48,896]{1,0:T(8,128)(2,1)S(1)}, u32[]{:S(2)}, u32[]{:S(2)}) collective-permute-start(bf16[48,896]{1,0:T(8,128)(2,1)S(1)} %get-tuple-element.44), channel_id=1, source_target_pairs={{0,20},{4,24},{8,28},{12,0},{16,4},{20,8},{24,12},{28,16},{1,21},{... | collective-permute-start | bytes 258056 | tf_op jit(solution)/shard_map/ppermute | solution.py:247
  78.9 2.3 %collective-permute-start.15 = (bf16[48,896]{1,0:T(8,128)(2,1)S(1)}, bf16[48,896]{1,0:T(8,128)(2,1)S(1)}, u32[]{:S(2)}, u32[]{:S(2)}) collective-permute-start(bf16[48,896]{1,0:T(8,128)(2,1)S(1)} %get-tuple-element.43), channel_id=1, source_target_pairs={{0,24},{4,28},{8,0},{12,4},{16,8},{20,12},{24,16},{28,20},{1,25},{... | collective-permute-start | bytes 258056 | tf_op jit(solution)/shard_map/ppermute | solution.py:247
  81.2 1.7 %collective-permute-start.16 = (bf16[48,896]{1,0:T(8,128)(2,1)S(1)}, bf16[48,896]{1,0:T(8,128)(2,1)S(1)}, u32[]{:S(2)}, u32[]{:S(2)}) collective-permute-start(bf16[48,896]{1,0:T(8,128)(2,1)S(1)} %get-tuple-element.42), channel_id=1, source_target_pairs={{0,28},{4,0},{8,4},{12,8},{16,12},{20,16},{24,20},{28,24},{1,29},{... | collective-permute-start | bytes 258056 | tf_op jit(solution)/shard_map/ppermute | solution.py:247
  82.9 3.8 %collective-permute-done.12 = bf16[48,896]{1,0:T(8,128)(2,1)S(1)} collective-permute-done((bf16[48,896]{1,0:T(8,128)(2,1)S(1)}, bf16[48,896]{1,0:T(8,128)(2,1)S(1)}, u32[]{:S(2)}, u32[]{:S(2)}) %collective-permute-start.12) | collective-permute-done | bytes 86048 | tf_op jit(solution)/shard_map/ppermute | solution.py:247
  86.7 0.9 collective-permute-done.13
  87.6 3.1 %collective-permute-done.15 = bf16[48,896]{1,0:T(8,128)(2,1)S(1)} collective-permute-done((bf16[48,896]{1,0:T(8,128)(2,1)S(1)}, bf16[48,896]{1,0:T(8,128)(2,1)S(1)}, u32[]{:S(2)}, u32[]{:S(2)}) %collective-permute-start.15) | collective-permute-done | bytes 86048 | tf_op jit(solution)/shard_map/ppermute | solution.py:247
  90.8 1.3 collective-permute-done.16
  94.2 4.3 %fusion.62 = f32[64,5120]{1,0:T(8,128)S(1)} fusion(bf16[640,5120]{1,0:T(8,128)(2,1)} %param.24, bf16[8,8,5,128]{3,2,1,0:T(8,128)(2,1)S(1)} %bitcast.313), kind=kOutput, calls=%fused_computation.146 | convolution fusion | flops 419430400 | bytes 7946240 | tf_op jit(solution)/shard_map/dot_general | solution.py:221
  100.1 1.3 fusion.65
  102.9 1.3 fusion.68
  105.5 1.3 fusion.71
  107.8 1.5 %collective-permute-start.22 = (f32[1,64,1280]{2,1,0:T(8,128)S(1)}, f32[1,64,1280]{2,1,0:T(8,128)S(1)}, u32[]{:S(2)}, u32[]{:S(2)}) collective-permute-start(f32[1,64,1280]{2,1,0:T(8,128)S(1)} %get-tuple-element.22), channel_id=1, source_target_pairs={{0,2},{1,3},{2,0},{3,1},{4,6},{5,7},{6,4},{7,5},{8,10},{9,11},{10,... | collective-permute-start | bytes 983048 | tf_op jit(solution)/shard_map/ppermute | solution.py:265
  110.2 1.5 %collective-permute-start.18 = (f32[1,64,1280]{2,1,0:T(8,128)S(1)}, f32[1,64,1280]{2,1,0:T(8,128)S(1)}, u32[]{:S(2)}, u32[]{:S(2)}) collective-permute-start(f32[1,64,1280]{2,1,0:T(8,128)S(1)} %get-tuple-element.16), channel_id=1, source_target_pairs={{0,2},{1,3},{2,0},{3,1},{4,6},{5,7},{6,4},{7,5},{8,10},{9,11},{10,... | collective-permute-start | bytes 983048 | tf_op jit(solution)/shard_map/ppermute | solution.py:265
  111.7 5.9 %collective-permute-done.24 = f32[1,64,1280]{2,1,0:T(8,128)S(1)} collective-permute-done((f32[1,64,1280]{2,1,0:T(8,128)S(1)}, f32[1,64,1280]{2,1,0:T(8,128)S(1)}, u32[]{:S(2)}, u32[]{:S(2)}) %collective-permute-start.24) | collective-permute-done | bytes 327712 | tf_op jit(solution)/shard_map/ppermute | solution.py:265
  117.7 7.0 %collective-permute-done.22 = f32[1,64,1280]{2,1,0:T(8,128)S(1)} collective-permute-done((f32[1,64,1280]{2,1,0:T(8,128)S(1)}, f32[1,64,1280]{2,1,0:T(8,128)S(1)}, u32[]{:S(2)}, u32[]{:S(2)}) %collective-permute-start.22) | collective-permute-done | bytes 327712 | tf_op jit(solution)/shard_map/ppermute | solution.py:265
  124.7 7.0 %collective-permute-done.20 = f32[1,64,1280]{2,1,0:T(8,128)S(1)} collective-permute-done((f32[1,64,1280]{2,1,0:T(8,128)S(1)}, f32[1,64,1280]{2,1,0:T(8,128)S(1)}, u32[]{:S(2)}, u32[]{:S(2)}) %collective-permute-start.20) | collective-permute-done | bytes 327712 | tf_op jit(solution)/shard_map/ppermute | solution.py:265
  131.7 6.6 %collective-permute-done.18 = f32[1,64,1280]{2,1,0:T(8,128)S(1)} collective-permute-done((f32[1,64,1280]{2,1,0:T(8,128)S(1)}, f32[1,64,1280]{2,1,0:T(8,128)S(1)}, u32[]{:S(2)}, u32[]{:S(2)}) %collective-permute-start.18) | collective-permute-done | bytes 327712 | tf_op jit(solution)/shard_map/ppermute | solution.py:265
  138.4 0.9 pad_maximum_fusion.5
  (193 shorter events, 19.5 us)
Async XLA Ops:
  0.0 19.5 %copy-start = (bf16[5120,128]{1,0:T(8,128)(2,1)S(1)}, bf16[5120,128]{1,0:T(8,128)(2,1)}, u32[]{:S(2)}) copy-start(bf16[5120,128]{1,0:T(8,128)(2,1)} %param.22) | copy-start | bytes 3932164
  0.0 22.0 %copy-start.1 = (bf16[96,5120]{1,0:T(8,128)(2,1)S(1)}, bf16[96,5120]{1,0:T(8,128)(2,1)}, u32[]{:S(2)}) copy-start(bf16[96,5120]{1,0:T(8,128)(2,1)} %param.14) | copy-start | bytes 2949124
  0.0 22.0 %copy-start.5 = (f32[5120]{0:T(1024)S(1)}, f32[5120]{0:T(1024)}, u32[]{:S(2)}) copy-start(f32[5120]{0:T(1024)} %param.17) | copy-start | bytes 61444
  0.0 51.9 %collective-permute-start.7 = (bf16[96,5120]{1,0:T(8,128)(2,1)}, bf16[96,5120]{1,0:T(8,128)(2,1)S(1)}, u32[]{:S(2)}, u32[]{:S(2)}) collective-permute-start(bf16[96,5120]{1,0:T(8,128)(2,1)} %param.14), channel_id=1, source_target_pairs={{0,2},{1,3},{2,0},{3,1},{4,6},{5,7},{6,4},{7,5},{8,10},{9,11},{10,... | collective-permute-start | bytes 2949128 | tf_op jit(solution)/shard_map/ppermute | solution.py:294
  1.6 52.5 %collective-permute-start.8 = (bf16[96,5120]{1,0:T(8,128)(2,1)}, bf16[96,5120]{1,0:T(8,128)(2,1)}, u32[]{:S(2)}, u32[]{:S(2)}) collective-permute-start(bf16[96,5120]{1,0:T(8,128)(2,1)} %param.14), channel_id=1, source_target_pairs={{0,1},{1,0},{2,3},{3,2},{4,5},{5,4},{6,7},{7,6},{8,9},{9,8},{10,11... | collective-permute-start | bytes 2949128 | tf_op jit(solution)/shard_map/ppermute | solution.py:294
  1.6 35.9 %collective-permute-start = (s32[1,8]{1,0:T(1,128)}, s32[1,8]{1,0:T(1,128)}, u32[]{:S(2)}, u32[]{:S(2)}) collective-permute-start(s32[1,8]{1,0:T(1,128)} %param.16), channel_id=1, source_target_pairs={{0,4},{4,8},{8,12},{12,16},{16,20},{20,24},{24,28},{28,0},{1,5},{5... | collective-permute-start | bytes 104 | tf_op jit(solution)/shard_map/ppermute | solution.py:231
  3.1 36.7 %collective-permute-start.1 = (s32[1,8]{1,0:T(1,128)}, s32[1,8]{1,0:T(1,128)}, u32[]{:S(2)}, u32[]{:S(2)}) collective-permute-start(s32[1,8]{1,0:T(1,128)} %param.16), channel_id=1, source_target_pairs={{0,8},{4,12},{8,16},{12,20},{16,24},{20,28},{24,0},{28,4},{1,9},{5... | collective-permute-start | bytes 104 | tf_op jit(solution)/shard_map/ppermute | solution.py:231
  4.7 37.1 %collective-permute-start.2 = (s32[1,8]{1,0:T(1,128)}, s32[1,8]{1,0:T(1,128)}, u32[]{:S(2)}, u32[]{:S(2)}) collective-permute-start(s32[1,8]{1,0:T(1,128)} %param.16), channel_id=1, source_target_pairs={{0,12},{4,16},{8,20},{12,24},{16,28},{20,0},{24,4},{28,8},{1,13},{... | collective-permute-start | bytes 104 | tf_op jit(solution)/shard_map/ppermute | solution.py:231
  19.5 1.7 %copy-start.18 = (f32[96]{0:T(128)}, f32[96]{0:T(128)S(1)}, u32[]{:S(2)}) copy-start(f32[96]{0:T(128)S(1)} %add_rsqrt_fusion.1) | copy-start | bytes 1156
  22.0 4.3 %copy-start.6 = (f32[5120]{0:T(1024)S(1)}, f32[5120]{0:T(1024)}, u32[]{:S(2)}) copy-start(f32[5120]{0:T(1024)} %param.17) | copy-start | bytes 61444
  22.0 4.3 %copy-start.19 = (f32[96]{0:T(128)S(1)}, f32[96]{0:T(128)}, u32[]{:S(2)}) copy-start(f32[96]{0:T(128)} %copy-done.18) | copy-start | bytes 1156
  22.0 4.3 %copy-start.20 = (bf16[5120,128]{1,0:T(8,128)(2,1)S(1)}, bf16[5120,128]{1,0:T(8,128)(2,1)}, u32[]{:S(2)}) copy-start(bf16[5120,128]{1,0:T(8,128)(2,1)} %param.20) | copy-start | bytes 3932164
  22.0 4.3 %copy-start.23 = (f32[128]{0:T(128)S(1)}, f32[128]{0:T(128)}, u32[]{:S(2)}) copy-start(f32[128]{0:T(128)} %param.21) | copy-start | bytes 1540
  26.3 3.4 %copy-start.4 = (s32[3072]{0:T(1024)S(1)}, s32[3072]{0:T(1024)}, u32[]{:S(2)}) copy-start(s32[3072]{0:T(1024)} %param.15) | copy-start | bytes 36868
  26.3 23.5 %copy-start.11 = (pred[384,8]{0,1:T(8,128)(4,1)S(1)}, pred[384,8]{0,1:T(8,128)(4,1)}, u32[]{:S(2)}) copy-start(pred[384,8]{0,1:T(8,128)(4,1)} %iota_compare_fusion.12) | copy-start | bytes 9220
  26.3 23.6 %copy-start.13 = (s32[384]{0:T(512)S(1)}, s32[384]{0:T(512)}, u32[]{:S(2)}) copy-start(s32[384]{0:T(512)} %get-tuple-element.66) | copy-start | bytes 4612
  27.5 29.2 %copy-start.7 = (f32[5120]{0:T(1024)S(1)}, f32[5120]{0:T(1024)}, u32[]{:S(2)}) copy-start(f32[5120]{0:T(1024)} %param.17) | copy-start | bytes 61444
  27.5 29.2 %copy-start.22 = (f32[128]{0:T(128)S(1)}, f32[128]{0:T(128)}, u32[]{:S(2)}) copy-start(f32[128]{0:T(128)} %param.23) | copy-start | bytes 1540
  37.5 6.3 %collective-permute-start.3 = (s32[1,8]{1,0:T(1,128)}, s32[1,8]{1,0:T(1,128)S(1)}, u32[]{:S(2)}, u32[]{:S(2)}) collective-permute-start(s32[1,8]{1,0:T(1,128)} %param.16), channel_id=1, source_target_pairs={{0,16},{4,20},{8,24},{12,28},{16,0},{20,4},{24,8},{28,12},{1,17},{... | collective-permute-start | bytes 104 | tf_op jit(solution)/shard_map/ppermute | solution.py:231
  39.8 5.8 %collective-permute-start.4 = (s32[1,8]{1,0:T(1,128)}, s32[1,8]{1,0:T(1,128)S(1)}, u32[]{:S(2)}, u32[]{:S(2)}) collective-permute-start(s32[1,8]{1,0:T(1,128)} %param.16), channel_id=1, source_target_pairs={{0,20},{4,24},{8,28},{12,0},{16,4},{20,8},{24,12},{28,16},{1,21},{... | collective-permute-start | bytes 104 | tf_op jit(solution)/shard_map/ppermute | solution.py:231
  41.7 3.9 %collective-permute-start.5 = (s32[1,8]{1,0:T(1,128)}, s32[1,8]{1,0:T(1,128)S(1)}, u32[]{:S(2)}, u32[]{:S(2)}) collective-permute-start(s32[1,8]{1,0:T(1,128)} %param.16), channel_id=1, source_target_pairs={{0,24},{4,28},{8,0},{12,4},{16,8},{20,12},{24,16},{28,20},{1,25},{... | collective-permute-start | bytes 104 | tf_op jit(solution)/shard_map/ppermute | solution.py:231
  43.8 4.6 %collective-permute-start.6 = (s32[1,8]{1,0:T(1,128)}, s32[1,8]{1,0:T(1,128)S(1)}, u32[]{:S(2)}, u32[]{:S(2)}) collective-permute-start(s32[1,8]{1,0:T(1,128)} %param.16), channel_id=1, source_target_pairs={{0,28},{4,0},{8,4},{12,8},{16,12},{20,16},{24,20},{28,24},{1,29},{... | collective-permute-start | bytes 104 | tf_op jit(solution)/shard_map/ppermute | solution.py:231
  52.0 2.6 %collective-permute-start.9 = (bf16[96,5120]{1,0:T(8,128)(2,1)S(1)}, bf16[96,5120]{1,0:T(8,128)(2,1)S(1)}, u32[]{:S(2)}, u32[]{:S(2)}) collective-permute-start(bf16[96,5120]{1,0:T(8,128)(2,1)S(1)} %collective-permute-done.7), channel_id=1, source_target_pairs={{0,1},{1,0},{2,3},{3,2},{4,5},{5,4},{6,7},{7,6},{8,9},{9,8},{10,11... | collective-permute-start | bytes 2949128 | tf_op jit(solution)/shard_map/ppermute | solution.py:294
  54.5 2.1 %copy-start.2 = (bf16[96,5120]{1,0:T(8,128)(2,1)}, bf16[96,5120]{1,0:T(8,128)(2,1)S(1)}, u32[]{:S(2)}) copy-start(bf16[96,5120]{1,0:T(8,128)(2,1)S(1)} %collective-permute-done.9) | copy-start | bytes 2949124
  56.7 2.4 %copy-start.8 = (f32[5120]{0:T(1024)S(1)}, f32[5120]{0:T(1024)}, u32[]{:S(2)}) copy-start(f32[5120]{0:T(1024)} %param.17) | copy-start | bytes 61444
  56.7 2.4 %copy-start.17 = (f32[640]{0:T(1024)S(1)}, f32[640]{0:T(1024)}, u32[]{:S(2)}) copy-start(f32[640]{0:T(1024)} %param.19) | copy-start | bytes 7684
  59.1 6.2 %copy-start.3 = (bf16[96,5120]{1,0:T(8,128)(2,1)S(1)}, bf16[96,5120]{1,0:T(8,128)(2,1)}, u32[]{:S(2)}) copy-start(bf16[96,5120]{1,0:T(8,128)(2,1)} %copy-done.2) | copy-start | bytes 2949124
  59.1 6.2 %copy-start.21 = (bf16[5120,128]{1,0:T(8,128)(2,1)S(1)}, bf16[5120,128]{1,0:T(8,128)(2,1)}, u32[]{:S(2)}) copy-start(bf16[5120,128]{1,0:T(8,128)(2,1)} %param.20) | copy-start | bytes 3932164
  59.1 6.2 %copy-start.24 = (f32[128]{0:T(128)S(1)}, f32[128]{0:T(128)}, u32[]{:S(2)}) copy-start(f32[128]{0:T(128)} %param.21) | copy-start | bytes 1540
  65.3 2.2 %copy-start.16 = (f32[64]{0:T(128)S(1)}, f32[64]{0:T(128)}, u32[]{:S(2)}) copy-start(f32[64]{0:T(128)} %multiply_exponential_fusion) | copy-start | bytes 772
  69.5 2.2 %copy-start.12 = (s32[256]{0:T(256)S(1)}, s32[256]{0:T(256)}, u32[]{:S(2)}) copy-start(s32[256]{0:T(256)} %select_reduce_fusion) | copy-start | bytes 3076
  71.0 22.3 %copy-start.10 = (pred[64,256]{1,0:T(8,128)(4,1)S(1)}, pred[64,256]{1,0:T(8,128)(4,1)}, u32[]{:S(2)}) copy-start(pred[64,256]{1,0:T(8,128)(4,1)} %fusion.102) | copy-start | bytes 49156
  71.1 7.8 %collective-permute-start.10 = (bf16[48,896]{1,0:T(8,128)(2,1)S(1)}, bf16[48,896]{1,0:T(8,128)(2,1)S(1)}, u32[]{:S(2)}, u32[]{:S(2)}) collective-permute-start(bf16[48,896]{1,0:T(8,128)(2,1)S(1)} %get-tuple-element.48), channel_id=1, source_target_pairs={{0,4},{4,8},{8,12},{12,16},{16,20},{20,24},{24,28},{28,0},{1,5},{5... | collective-permute-start | bytes 258056 | tf_op jit(solution)/shard_map/ppermute | solution.py:247
  71.8 9.4 %collective-permute-start.11 = (bf16[48,896]{1,0:T(8,128)(2,1)S(1)}, bf16[48,896]{1,0:T(8,128)(2,1)S(1)}, u32[]{:S(2)}, u32[]{:S(2)}) collective-permute-start(bf16[48,896]{1,0:T(8,128)(2,1)S(1)} %get-tuple-element.47), channel_id=1, source_target_pairs={{0,8},{4,12},{8,16},{12,20},{16,24},{20,28},{24,0},{28,4},{1,9},{5... | collective-permute-start | bytes 258056 | tf_op jit(solution)/shard_map/ppermute | solution.py:247
  73.2 13.5 %collective-permute-start.12 = (bf16[48,896]{1,0:T(8,128)(2,1)S(1)}, bf16[48,896]{1,0:T(8,128)(2,1)S(1)}, u32[]{:S(2)}, u32[]{:S(2)}) collective-permute-start(bf16[48,896]{1,0:T(8,128)(2,1)S(1)} %get-tuple-element.46), channel_id=1, source_target_pairs={{0,12},{4,16},{8,20},{12,24},{16,28},{20,0},{24,4},{28,8},{1,13},{... | collective-permute-start | bytes 258056 | tf_op jit(solution)/shard_map/ppermute | solution.py:247
  76.9 10.8 %collective-permute-start.13 = (bf16[48,896]{1,0:T(8,128)(2,1)S(1)}, bf16[48,896]{1,0:T(8,128)(2,1)S(1)}, u32[]{:S(2)}, u32[]{:S(2)}) collective-permute-start(bf16[48,896]{1,0:T(8,128)(2,1)S(1)} %get-tuple-element.45), channel_id=1, source_target_pairs={{0,16},{4,20},{8,24},{12,28},{16,0},{20,4},{24,8},{28,12},{1,17},{... | collective-permute-start | bytes 258056 | tf_op jit(solution)/shard_map/ppermute | solution.py:247
  76.9 10.8 %collective-permute-start.14 = (bf16[48,896]{1,0:T(8,128)(2,1)S(1)}, bf16[48,896]{1,0:T(8,128)(2,1)S(1)}, u32[]{:S(2)}, u32[]{:S(2)}) collective-permute-start(bf16[48,896]{1,0:T(8,128)(2,1)S(1)} %get-tuple-element.44), channel_id=1, source_target_pairs={{0,20},{4,24},{8,28},{12,0},{16,4},{20,8},{24,12},{28,16},{1,21},{... | collective-permute-start | bytes 258056 | tf_op jit(solution)/shard_map/ppermute | solution.py:247
  78.9 11.8 %collective-permute-start.15 = (bf16[48,896]{1,0:T(8,128)(2,1)S(1)}, bf16[48,896]{1,0:T(8,128)(2,1)S(1)}, u32[]{:S(2)}, u32[]{:S(2)}) collective-permute-start(bf16[48,896]{1,0:T(8,128)(2,1)S(1)} %get-tuple-element.43), channel_id=1, source_target_pairs={{0,24},{4,28},{8,0},{12,4},{16,8},{20,12},{24,16},{28,20},{1,25},{... | collective-permute-start | bytes 258056 | tf_op jit(solution)/shard_map/ppermute | solution.py:247
  81.2 10.9 %collective-permute-start.16 = (bf16[48,896]{1,0:T(8,128)(2,1)S(1)}, bf16[48,896]{1,0:T(8,128)(2,1)S(1)}, u32[]{:S(2)}, u32[]{:S(2)}) collective-permute-start(bf16[48,896]{1,0:T(8,128)(2,1)S(1)} %get-tuple-element.42), channel_id=1, source_target_pairs={{0,28},{4,0},{8,4},{12,8},{16,12},{20,16},{24,20},{28,24},{1,29},{... | collective-permute-start | bytes 258056 | tf_op jit(solution)/shard_map/ppermute | solution.py:247
  94.2 5.9 %slice-start = ((s8[6553600]{0:T(1024)(128)(4,1)}), s8[4194304]{0:T(1024)(128)(4,1)S(1)}, s32[]{:S(2)}) async-start(s8[6553600]{0:T(1024)(128)(4,1)} %bitcast.308), calls=%async_computation | async-start | bytes 8388608
  94.2 5.9 %slice-start.1 = ((s8[6553600]{0:T(1024)(128)(4,1)}), s8[2359296]{0:T(1024)(128)(4,1)S(1)}, s32[]{:S(2)}) async-start(s8[6553600]{0:T(1024)(128)(4,1)} %bitcast.308), calls=%async_computation.1 | async-start | bytes 4718592
  98.5 0.7 copy-start.9
  98.7 8.3 %collective-permute-start.23 = (f32[2,64,1280]{2,1,0:T(8,128)S(1)}, f32[2,64,1280]{2,1,0:T(8,128)S(1)}, u32[]{:S(2)}, u32[]{:S(2)}) collective-permute-start(f32[2,64,1280]{2,1,0:T(8,128)S(1)} %pad_maximum_fusion.4), channel_id=1, source_target_pairs={{0,1},{1,0},{2,3},{3,2},{4,5},{5,4},{6,7},{7,6},{8,9},{9,8},{10,11... | collective-permute-start | bytes 1966088 | tf_op jit(solution)/shard_map/ppermute | solution.py:265
  101.4 0.7 copy-start.15
  101.5 6.1 %collective-permute-start.21 = (f32[2,64,1280]{2,1,0:T(8,128)S(1)}, f32[2,64,1280]{2,1,0:T(8,128)S(1)}, u32[]{:S(2)}, u32[]{:S(2)}) collective-permute-start(f32[2,64,1280]{2,1,0:T(8,128)S(1)} %pad_maximum_fusion.3), channel_id=1, source_target_pairs={{0,1},{1,0},{2,3},{3,2},{4,5},{5,4},{6,7},{7,6},{8,9},{9,8},{10,11... | collective-permute-start | bytes 1966088 | tf_op jit(solution)/shard_map/ppermute | solution.py:265
  104.2 0.7 copy-start.14
  104.3 5.0 %collective-permute-start.19 = (f32[2,64,1280]{2,1,0:T(8,128)S(1)}, f32[2,64,1280]{2,1,0:T(8,128)S(1)}, u32[]{:S(2)}, u32[]{:S(2)}) collective-permute-start(f32[2,64,1280]{2,1,0:T(8,128)S(1)} %pad_maximum_fusion.2), channel_id=1, source_target_pairs={{0,1},{1,0},{2,3},{3,2},{4,5},{5,4},{6,7},{7,6},{8,9},{9,8},{10,11... | collective-permute-start | bytes 1966088 | tf_op jit(solution)/shard_map/ppermute | solution.py:265
  106.9 3.2 %collective-permute-start.17 = (f32[2,64,1280]{2,1,0:T(8,128)S(1)}, f32[2,64,1280]{2,1,0:T(8,128)S(1)}, u32[]{:S(2)}, u32[]{:S(2)}) collective-permute-start(f32[2,64,1280]{2,1,0:T(8,128)S(1)} %pad_maximum_fusion.1), channel_id=1, source_target_pairs={{0,1},{1,0},{2,3},{3,2},{4,5},{5,4},{6,7},{7,6},{8,9},{9,8},{10,11... | collective-permute-start | bytes 1966088 | tf_op jit(solution)/shard_map/ppermute | solution.py:265
  107.1 10.6 %collective-permute-start.24 = (f32[1,64,1280]{2,1,0:T(8,128)S(1)}, f32[1,64,1280]{2,1,0:T(8,128)S(1)}, u32[]{:S(2)}, u32[]{:S(2)}) collective-permute-start(f32[1,64,1280]{2,1,0:T(8,128)S(1)} %get-tuple-element.25), channel_id=1, source_target_pairs={{0,2},{1,3},{2,0},{3,1},{4,6},{5,7},{6,4},{7,5},{8,10},{9,11},{10,... | collective-permute-start | bytes 983048 | tf_op jit(solution)/shard_map/ppermute | solution.py:265
  107.8 16.9 %collective-permute-start.22 = (f32[1,64,1280]{2,1,0:T(8,128)S(1)}, f32[1,64,1280]{2,1,0:T(8,128)S(1)}, u32[]{:S(2)}, u32[]{:S(2)}) collective-permute-start(f32[1,64,1280]{2,1,0:T(8,128)S(1)} %get-tuple-element.22), channel_id=1, source_target_pairs={{0,2},{1,3},{2,0},{3,1},{4,6},{5,7},{6,4},{7,5},{8,10},{9,11},{10,... | collective-permute-start | bytes 983048 | tf_op jit(solution)/shard_map/ppermute | solution.py:265
  109.4 22.2 %collective-permute-start.20 = (f32[1,64,1280]{2,1,0:T(8,128)S(1)}, f32[1,64,1280]{2,1,0:T(8,128)S(1)}, u32[]{:S(2)}, u32[]{:S(2)}) collective-permute-start(f32[1,64,1280]{2,1,0:T(8,128)S(1)} %get-tuple-element.19), channel_id=1, source_target_pairs={{0,2},{1,3},{2,0},{3,1},{4,6},{5,7},{6,4},{7,5},{8,10},{9,11},{10,... | collective-permute-start | bytes 983048 | tf_op jit(solution)/shard_map/ppermute | solution.py:265
  110.2 28.1 %collective-permute-start.18 = (f32[1,64,1280]{2,1,0:T(8,128)S(1)}, f32[1,64,1280]{2,1,0:T(8,128)S(1)}, u32[]{:S(2)}, u32[]{:S(2)}) collective-permute-start(f32[1,64,1280]{2,1,0:T(8,128)S(1)} %get-tuple-element.16), channel_id=1, source_target_pairs={{0,2},{1,3},{2,0},{3,1},{4,6},{5,7},{6,4},{7,5},{8,10},{9,11},{10,... | collective-permute-start | bytes 983048 | tf_op jit(solution)/shard_map/ppermute | solution.py:265

commit v13 on v12

--- a/solution.py
+++ b/solution.py
@@ -135,11 +135,7 @@
             axis=1,
         )
 
-    own_rows = pieces[0].shape[0]
-    qkv_parts = [project(pieces[0], sequence_starts[:own_rows])]
-    if len(pieces) > 1:
-        qkv_parts.append(project(jnp.concatenate(pieces[1:], axis=0), sequence_starts[own_rows:]))
-    qkv = jnp.concatenate(qkv_parts, axis=0)
+    qkv = project(jnp.concatenate(pieces, axis=0), sequence_starts)
 
     shift_order = ctx_count <= 8
     if shift_order:

time: 140 us -> 114 us (0.81)
  the two profiles are of different devices: /device:TPU:12 before, /device:TPU:0 now
where the time goes in v13:
time: 114 us; the launch traced here: 113 us
  waiting for transfers between devices  33.4 us (29%)
  starting transfers between devices  32.1 us (28%)
  matrix products  20.3 us (18%)
  other arithmetic  19.5 us (17%)
  local copies, waits for them, and re-layouts  6.58 us (6%)
    ppermute x8, waiting for transfers between devices, halving_scatter(): got = lax.ppermute(send, axis_name, pairs)  25.9 us
    ppermute x7, starting transfers between devices, shift_gather(): lax.ppermute(part, axis_name, [(i, (i + shift) % count) for i in range(co...  12.5 us
    ppermute x7, starting transfers between devices, exchange(): arrived.append(lax.ppermute(chunks[shift], axis_name, pairs))  11 us
    dot_general x4, matrix products, local(): jnp.dot(mixed_heads, w_out, preferred_element_type=jnp.float32)  8.09 us
    ppermute x8, starting transfers between devices, halving_scatter(): got = lax.ppermute(send, axis_name, pairs)  5.58 us
    ppermute x7, waiting for transfers between devices, exchange(): arrived.append(lax.ppermute(chunks[shift], axis_name, pairs))  5.44 us
    convert_element_type x1, other arithmetic, project(): normalized_input = (values_wide * lax.rsqrt(jnp.mean(values_wide * values...  4.47 us
    dot_general x1, matrix products, project(): jnp.dot(normalized_input, value_projection_weight, preferred_element_type...  3.77 us
  transfers between devices with their start and end apart: 25, of which 9 were waited for; matrix products, arithmetic and copies ran while one was open for 19% of the time, Pallas kernels for 0%

profile of v13, /device:TPU:0, one launch (start us, length us, event | category | flops | bytes accessed | tf_op | source)
XLA Modules:
  0.0 112.6 jit_solution(13503544098878177055)
XLA Ops:
  0.0 3.0 %collective-permute-start = (bf16[96,5120]{1,0:T(8,128)(2,1)}, bf16[96,5120]{1,0:T(8,128)(2,1)S(1)}, u32[]{:S(2)}, u32[]{:S(2)}) collective-permute-start(bf16[96,5120]{1,0:T(8,128)(2,1)} %param.14), channel_id=1, source_target_pairs={{0,2},{1,3},{2,0},{3,1},{4,6},{5,7},{6,4},{7,5},{8,10},{9,11},{10,... | collective-permute-start | bytes 2949128 | tf_op jit(solution)/shard_map/ppermute | solution.py:290
  3.0 1.5 %collective-permute-start.3 = (s32[1,8]{1,0:T(1,128)}, s32[1,8]{1,0:T(1,128)S(1)}, u32[]{:S(2)}, u32[]{:S(2)}) collective-permute-start(s32[1,8]{1,0:T(1,128)} %param.16), channel_id=1, source_target_pairs={{0,4},{4,8},{8,12},{12,16},{16,20},{20,24},{24,28},{28,0},{1,5},{5... | collective-permute-start | bytes 104 | tf_op jit(solution)/shard_map/ppermute | solution.py:227
  4.5 1.6 %collective-permute-start.4 = (s32[1,8]{1,0:T(1,128)}, s32[1,8]{1,0:T(1,128)S(1)}, u32[]{:S(2)}, u32[]{:S(2)}) collective-permute-start(s32[1,8]{1,0:T(1,128)} %param.16), channel_id=1, source_target_pairs={{0,8},{4,12},{8,16},{12,20},{16,24},{20,28},{24,0},{28,4},{1,9},{5... | collective-permute-start | bytes 104 | tf_op jit(solution)/shard_map/ppermute | solution.py:227
  6.1 2.5 %collective-permute-start.5 = (s32[1,8]{1,0:T(1,128)}, s32[1,8]{1,0:T(1,128)S(1)}, u32[]{:S(2)}, u32[]{:S(2)}) collective-permute-start(s32[1,8]{1,0:T(1,128)} %param.16), channel_id=1, source_target_pairs={{0,12},{4,16},{8,20},{12,24},{16,28},{20,0},{24,4},{28,8},{1,13},{... | collective-permute-start | bytes 104 | tf_op jit(solution)/shard_map/ppermute | solution.py:227
  8.6 0.5 multiply_exponential_fusion
  9.2 0.7 constant_dynamic-update-slice_fusion.7
  9.9 0.7 reshape.877
  10.8 0.8 reduce-window.32
  11.8 0.9 reduce-window.30
  13.1 0.7 compare_and_fusion.4
  13.9 0.6 gather_fusion.2
  14.4 0.6 gather_fusion.1
  15.2 0.7 eq.245
  15.9 0.7 subtract_select_fusion
  16.7 0.9 reduce-window.21
  18.0 1.0 select_reduce_fusion
  19.1 0.7 compare_and_fusion.2
  19.8 0.7 compare_and_fusion.1
  20.5 1.2 %collective-permute-start.6 = (s32[1,8]{1,0:T(1,128)}, s32[1,8]{1,0:T(1,128)S(1)}, u32[]{:S(2)}, u32[]{:S(2)}) collective-permute-start(s32[1,8]{1,0:T(1,128)} %param.16), channel_id=1, source_target_pairs={{0,16},{4,20},{8,24},{12,28},{16,0},{20,4},{24,8},{28,12},{1,17},{... | collective-permute-start | bytes 104 | tf_op jit(solution)/shard_map/ppermute | solution.py:227
  21.8 2.6 %collective-permute-start.7 = (s32[1,8]{1,0:T(1,128)}, s32[1,8]{1,0:T(1,128)S(1)}, u32[]{:S(2)}, u32[]{:S(2)}) collective-permute-start(s32[1,8]{1,0:T(1,128)} %param.16), channel_id=1, source_target_pairs={{0,20},{4,24},{8,28},{12,0},{16,4},{20,8},{24,12},{28,16},{1,21},{... | collective-permute-start | bytes 104 | tf_op jit(solution)/shard_map/ppermute | solution.py:227
  24.4 1.3 %collective-permute-start.8 = (s32[1,8]{1,0:T(1,128)}, s32[1,8]{1,0:T(1,128)S(1)}, u32[]{:S(2)}, u32[]{:S(2)}) collective-permute-start(s32[1,8]{1,0:T(1,128)} %param.16), channel_id=1, source_target_pairs={{0,24},{4,28},{8,0},{12,4},{16,8},{20,12},{24,16},{28,20},{1,25},{... | collective-permute-start | bytes 104 | tf_op jit(solution)/shard_map/ppermute | solution.py:227
  25.8 1.6 %collective-permute-start.9 = (s32[1,8]{1,0:T(1,128)}, s32[1,8]{1,0:T(1,128)S(1)}, u32[]{:S(2)}, u32[]{:S(2)}) collective-permute-start(s32[1,8]{1,0:T(1,128)} %param.16), channel_id=1, source_target_pairs={{0,28},{4,0},{8,4},{12,8},{16,12},{20,16},{24,20},{28,24},{1,29},{... | collective-permute-start | bytes 104 | tf_op jit(solution)/shard_map/ppermute | solution.py:227
  27.4 0.7 collective-permute-done.8
  28.1 1.3 %collective-permute-done.9 = s32[1,8]{1,0:T(1,128)S(1)} collective-permute-done((s32[1,8]{1,0:T(1,128)}, s32[1,8]{1,0:T(1,128)S(1)}, u32[]{:S(2)}, u32[]{:S(2)}) %collective-permute-start.9) | collective-permute-done | bytes 64 | tf_op jit(solution)/shard_map/ppermute | solution.py:227
  29.5 0.6 gather_fusion
  30.4 1.1 multiply_cosine_fusion.1
  31.5 2.4 %fusion = f32[384]{0:T(512)S(1)} fusion(bf16[96,5120]{1,0:T(8,128)(2,1)} %collective-permute-done.2, bf16[96,5120]{1,0:T(8,128)(2,1)} %collective-permute-done.1, bf16[96,5120]{1,0:T(8,128)(2,1)S(1)} %collective-permute-done, bf16[96,5120]{1,0:T(8,128)(2,1)} %param.14), kind=kLoop, calls=%fused_computation.5 | loop fusion | flops 19660416 | bytes 3933696 | tf_op jit(solution)/shard_map/reduce_sum | solution.py:108
  34.0 4.5 %fusion.2 = bf16[384,5120]{1,0:T(8,128)(2,1)S(1)} fusion(f32[5120]{0:T(1024)S(1)} %copy-done.4, f32[384]{0:T(512)S(1)} %add_rsqrt_fusion, bf16[96,5120]{1,0:T(8,128)(2,1)} %collective-permute-done.2, bf16[96,5120]{1,0:T(8,128)(2,1)} %collective-permute-done.1, bf16[96,5120]{1,0:T(8,128)(2,1)S(1)} %collective-permute-done, bf16[96,5120]{1,0:T(8,128)(2,1)S(1)} %copy-done.2), kind=kLoop, calls=%fused_computation.7 | loop fusion | flops 21626880 | bytes 7886336 | tf_op jit(solution)/shard_map/convert_element_type | solution.py:110
  38.5 3.3 %convolution_add_fusion = f32[384,640]{1,0:T(8,128)S(1)} fusion(bf16[384,5120]{1,0:T(8,128)(2,1)S(1)} %fusion.2, bf16[5120,640]{1,0:T(8,128)(2,1)S(1)} %bitcast.316, f32[640]{0:T(1024)S(1)} %copy-done.11), kind=kOutput, calls=%fused_computation.12 | convolution fusion | flops 2516828160 | bytes 11471360 | tf_op jit(solution)/shard_map/dot_general | solution.py:112
  41.9 1.2 %convolution_add_fusion.2 = f32[384,128]{1,0:T(8,128)S(1)} fusion(bf16[384,5120]{1,0:T(8,128)(2,1)S(1)} %fusion.2, bf16[5120,128]{1,0:T(8,128)(2,1)S(1)} %copy-done, f32[128]{0:T(128)S(1)} %copy-done.8), kind=kOutput, calls=%fused_computation.18 | convolution fusion | flops 503365632 | bytes 5440000 | tf_op jit(solution)/shard_map/dot_general | solution.py:115
  43.1 0.8 fusion.51
  44.1 0.7 copy.35
  44.8 0.3 copy.34
  45.1 3.8 %fusion.9 = bf16[384,128]{0,1:T(8,128)(2,1)S(1)} fusion(bf16[384,5120]{1,0:T(8,128)(2,1)} %copy-done.1, bf16[5120,128]{1,0:T(8,128)(2,1)} %param.22, f32[128]{0:T(128)} %param.23), kind=kOutput, calls=%fused_computation.29 | convolution fusion | flops 503414784 | bytes 5341696 | tf_op jit(solution)/shard_map/dot_general | solution.py:126
  49.1 0.6 convolution_convert_fusion
  49.8 1.8 %collective-permute-start.10 = (bf16[48,896]{1,0:T(8,128)(2,1)S(1)}, bf16[48,896]{1,0:T(8,128)(2,1)S(1)}, u32[]{:S(2)}, u32[]{:S(2)}) collective-permute-start(bf16[48,896]{1,0:T(8,128)(2,1)S(1)} %get-tuple-element.44), channel_id=1, source_target_pairs={{0,4},{4,8},{8,12},{12,16},{16,20},{20,24},{24,28},{28,0},{1,5},{5... | collective-permute-start | bytes 258056 | tf_op jit(solution)/shard_map/ppermute | solution.py:243
  51.9 2.5 %collective-permute-start.12 = (bf16[48,896]{1,0:T(8,128)(2,1)S(1)}, bf16[48,896]{1,0:T(8,128)(2,1)S(1)}, u32[]{:S(2)}, u32[]{:S(2)}) collective-permute-start(bf16[48,896]{1,0:T(8,128)(2,1)S(1)} %get-tuple-element.42), channel_id=1, source_target_pairs={{0,12},{4,16},{8,20},{12,24},{16,28},{20,0},{24,4},{28,8},{1,13},{... | collective-permute-start | bytes 258056 | tf_op jit(solution)/shard_map/ppermute | solution.py:243
  54.4 1.5 %collective-permute-start.13 = (bf16[48,896]{1,0:T(8,128)(2,1)S(1)}, bf16[48,896]{1,0:T(8,128)(2,1)S(1)}, u32[]{:S(2)}, u32[]{:S(2)}) collective-permute-start(bf16[48,896]{1,0:T(8,128)(2,1)S(1)} %get-tuple-element.41), channel_id=1, source_target_pairs={{0,16},{4,20},{8,24},{12,28},{16,0},{20,4},{24,8},{28,12},{1,17},{... | collective-permute-start | bytes 258056 | tf_op jit(solution)/shard_map/ppermute | solution.py:243
  55.9 3.3 %collective-permute-start.14 = (bf16[48,896]{1,0:T(8,128)(2,1)S(1)}, bf16[48,896]{1,0:T(8,128)(2,1)S(1)}, u32[]{:S(2)}, u32[]{:S(2)}) collective-permute-start(bf16[48,896]{1,0:T(8,128)(2,1)S(1)} %get-tuple-element.40), channel_id=1, source_target_pairs={{0,20},{4,24},{8,28},{12,0},{16,4},{20,8},{24,12},{28,16},{1,21},{... | collective-permute-start | bytes 258056 | tf_op jit(solution)/shard_map/ppermute | solution.py:243
  59.3 1.6 %collective-permute-start.16 = (bf16[48,896]{1,0:T(8,128)(2,1)S(1)}, bf16[48,896]{1,0:T(8,128)(2,1)S(1)}, u32[]{:S(2)}, u32[]{:S(2)}) collective-permute-start(bf16[48,896]{1,0:T(8,128)(2,1)S(1)} %get-tuple-element.38), channel_id=1, source_target_pairs={{0,28},{4,0},{8,4},{12,8},{16,12},{20,16},{24,20},{28,24},{1,29},{... | collective-permute-start | bytes 258056 | tf_op jit(solution)/shard_map/ppermute | solution.py:243
  60.9 3.0 %collective-permute-done.12 = bf16[48,896]{1,0:T(8,128)(2,1)S(1)} collective-permute-done((bf16[48,896]{1,0:T(8,128)(2,1)S(1)}, bf16[48,896]{1,0:T(8,128)(2,1)S(1)}, u32[]{:S(2)}, u32[]{:S(2)}) %collective-permute-start.12) | collective-permute-done | bytes 86048 | tf_op jit(solution)/shard_map/ppermute | solution.py:243
  64.0 0.6 collective-permute-done.13
  64.6 1.8 %collective-permute-done.15 = bf16[48,896]{1,0:T(8,128)(2,1)S(1)} collective-permute-done((bf16[48,896]{1,0:T(8,128)(2,1)S(1)}, bf16[48,896]{1,0:T(8,128)(2,1)S(1)}, u32[]{:S(2)}, u32[]{:S(2)}) %collective-permute-start.15) | collective-permute-done | bytes 86048 | tf_op jit(solution)/shard_map/ppermute | solution.py:243
  66.5 0.3 convolution_convert_fusion.2
  66.8 0.3 convolution_convert_fusion.1
  67.1 0.3 convolution_convert_fusion.4
  67.4 0.3 convolution_convert_fusion.3
  68.2 0.3 fusion.13
  68.6 4.3 %fusion.52 = f32[64,5120]{1,0:T(8,128)S(1)} fusion(bf16[640,5120]{1,0:T(8,128)(2,1)} %param.24, bf16[8,8,5,128]{3,2,1,0:T(8,128)(2,1)S(1)} %bitcast.305), kind=kOutput, calls=%fused_computation.128 | convolution fusion | flops 419430400 | bytes 7946240 | tf_op jit(solution)/shard_map/dot_general | solution.py:217
  73.1 0.3 fusion.173
  74.0 1.3 %fusion.55 = f32[64,5120]{1,0:T(8,128)S(1)} fusion(bf16[640,5120]{1,0:T(8,128)(2,1)S(1)} %bitcast.302, bf16[8,8,5,128]{3,2,1,0:T(8,128)(2,1)S(1)} %bitcast.306), kind=kOutput, calls=%fused_computation.131 | convolution fusion | flops 419430400 | bytes 7946240 | tf_op jit(solution)/shard_map/dot_general | solution.py:217
  75.4 0.6 collective-permute-start.21
  76.8 1.3 %fusion.58 = f32[64,5120]{1,0:T(8,128)S(1)} fusion(bf16[640,5120]{1,0:T(8,128)(2,1)S(1)} %bitcast.302, bf16[8,8,5,128]{3,2,1,0:T(8,128)(2,1)S(1)} %bitcast.307), kind=kOutput, calls=%fused_computation.134 | convolution fusion | flops 419430400 | bytes 7946240 | tf_op jit(solution)/shard_map/dot_general | solution.py:217
  78.9 1.3 %fusion.61 = f32[64,5120]{1,0:T(8,128)S(1)} fusion(bf16[640,5120]{1,0:T(8,128)(2,1)S(1)} %bitcast.302, bf16[8,8,5,128]{3,2,1,0:T(8,128)(2,1)S(1)} %bitcast.308), kind=kOutput, calls=%fused_computation.137 | convolution fusion | flops 419430400 | bytes 7946240 | tf_op jit(solution)/shard_map/dot_general | solution.py:217
  80.3 0.6 collective-permute-start.17
  80.9 0.6 collective-permute-start.24
  81.6 1.6 %collective-permute-start.22 = (f32[1,64,1280]{2,1,0:T(8,128)S(1)}, f32[1,64,1280]{2,1,0:T(8,128)S(1)}, u32[]{:S(2)}, u32[]{:S(2)}) collective-permute-start(f32[1,64,1280]{2,1,0:T(8,128)S(1)} %get-tuple-element.18), channel_id=1, source_target_pairs={{0,2},{1,3},{2,0},{3,1},{4,6},{5,7},{6,4},{7,5},{8,10},{9,11},{10,... | collective-permute-start | bytes 983048 | tf_op jit(solution)/shard_map/ppermute | solution.py:261
  83.3 0.6 collective-permute-start.20
  84.1 1.6 %collective-permute-start.18 = (f32[1,64,1280]{2,1,0:T(8,128)S(1)}, f32[1,64,1280]{2,1,0:T(8,128)S(1)}, u32[]{:S(2)}, u32[]{:S(2)}) collective-permute-start(f32[1,64,1280]{2,1,0:T(8,128)S(1)} %get-tuple-element.12), channel_id=1, source_target_pairs={{0,2},{1,3},{2,0},{3,1},{4,6},{5,7},{6,4},{7,5},{8,10},{9,11},{10,... | collective-permute-start | bytes 983048 | tf_op jit(solution)/shard_map/ppermute | solution.py:261
  85.6 6.0 %collective-permute-done.24 = f32[1,64,1280]{2,1,0:T(8,128)S(1)} collective-permute-done((f32[1,64,1280]{2,1,0:T(8,128)S(1)}, f32[1,64,1280]{2,1,0:T(8,128)S(1)}, u32[]{:S(2)}, u32[]{:S(2)}) %collective-permute-start.24) | collective-permute-done | bytes 327712 | tf_op jit(solution)/shard_map/ppermute | solution.py:261
  91.6 7.0 %collective-permute-done.22 = f32[1,64,1280]{2,1,0:T(8,128)S(1)} collective-permute-done((f32[1,64,1280]{2,1,0:T(8,128)S(1)}, f32[1,64,1280]{2,1,0:T(8,128)S(1)}, u32[]{:S(2)}, u32[]{:S(2)}) %collective-permute-start.22) | collective-permute-done | bytes 327712 | tf_op jit(solution)/shard_map/ppermute | solution.py:261
  98.6 7.0 %collective-permute-done.20 = f32[1,64,1280]{2,1,0:T(8,128)S(1)} collective-permute-done((f32[1,64,1280]{2,1,0:T(8,128)S(1)}, f32[1,64,1280]{2,1,0:T(8,128)S(1)}, u32[]{:S(2)}, u32[]{:S(2)}) %collective-permute-start.20) | collective-permute-done | bytes 327712 | tf_op jit(solution)/shard_map/ppermute | solution.py:261
  105.7 6.0 %collective-permute-done.18 = f32[1,64,1280]{2,1,0:T(8,128)S(1)} collective-permute-done((f32[1,64,1280]{2,1,0:T(8,128)S(1)}, f32[1,64,1280]{2,1,0:T(8,128)S(1)}, u32[]{:S(2)}, u32[]{:S(2)}) %collective-permute-start.18) | collective-permute-done | bytes 327712 | tf_op jit(solution)/shard_map/ppermute | solution.py:261
  111.8 0.9 pad_maximum_fusion.5
  (157 shorter events, 6.9 us)
Async XLA Ops:
  0.0 41.9 %copy-start = (bf16[5120,128]{1,0:T(8,128)(2,1)S(1)}, bf16[5120,128]{1,0:T(8,128)(2,1)}, u32[]{:S(2)}) copy-start(bf16[5120,128]{1,0:T(8,128)(2,1)} %param.20) | copy-start | bytes 3932164
  0.0 33.9 %copy-start.2 = (bf16[96,5120]{1,0:T(8,128)(2,1)S(1)}, bf16[96,5120]{1,0:T(8,128)(2,1)}, u32[]{:S(2)}) copy-start(bf16[96,5120]{1,0:T(8,128)(2,1)} %param.14) | copy-start | bytes 2949124
  0.0 34.0 %copy-start.4 = (f32[5120]{0:T(1024)S(1)}, f32[5120]{0:T(1024)}, u32[]{:S(2)}) copy-start(f32[5120]{0:T(1024)} %param.17) | copy-start | bytes 61444
  0.0 28.1 %collective-permute-start = (bf16[96,5120]{1,0:T(8,128)(2,1)}, bf16[96,5120]{1,0:T(8,128)(2,1)S(1)}, u32[]{:S(2)}, u32[]{:S(2)}) collective-permute-start(bf16[96,5120]{1,0:T(8,128)(2,1)} %param.14), channel_id=1, source_target_pairs={{0,2},{1,3},{2,0},{3,1},{4,6},{5,7},{6,4},{7,5},{8,10},{9,11},{10,... | collective-permute-start | bytes 2949128 | tf_op jit(solution)/shard_map/ppermute | solution.py:290
  3.0 28.5 %collective-permute-start.1 = (bf16[96,5120]{1,0:T(8,128)(2,1)}, bf16[96,5120]{1,0:T(8,128)(2,1)}, u32[]{:S(2)}, u32[]{:S(2)}) collective-permute-start(bf16[96,5120]{1,0:T(8,128)(2,1)} %param.14), channel_id=1, source_target_pairs={{0,1},{1,0},{2,3},{3,2},{4,5},{5,4},{6,7},{7,6},{8,9},{9,8},{10,11... | collective-permute-start | bytes 2949128 | tf_op jit(solution)/shard_map/ppermute | solution.py:290
  3.0 17.5 %collective-permute-start.3 = (s32[1,8]{1,0:T(1,128)}, s32[1,8]{1,0:T(1,128)S(1)}, u32[]{:S(2)}, u32[]{:S(2)}) collective-permute-start(s32[1,8]{1,0:T(1,128)} %param.16), channel_id=1, source_target_pairs={{0,4},{4,8},{8,12},{12,16},{16,20},{20,24},{24,28},{28,0},{1,5},{5... | collective-permute-start | bytes 104 | tf_op jit(solution)/shard_map/ppermute | solution.py:227
  4.5 17.2 %collective-permute-start.4 = (s32[1,8]{1,0:T(1,128)}, s32[1,8]{1,0:T(1,128)S(1)}, u32[]{:S(2)}, u32[]{:S(2)}) collective-permute-start(s32[1,8]{1,0:T(1,128)} %param.16), channel_id=1, source_target_pairs={{0,8},{4,12},{8,16},{12,20},{16,24},{20,28},{24,0},{28,4},{1,9},{5... | collective-permute-start | bytes 104 | tf_op jit(solution)/shard_map/ppermute | solution.py:227
  6.1 18.3 %collective-permute-start.5 = (s32[1,8]{1,0:T(1,128)}, s32[1,8]{1,0:T(1,128)S(1)}, u32[]{:S(2)}, u32[]{:S(2)}) collective-permute-start(s32[1,8]{1,0:T(1,128)} %param.16), channel_id=1, source_target_pairs={{0,12},{4,16},{8,20},{12,24},{16,28},{20,0},{24,4},{28,8},{1,13},{... | collective-permute-start | bytes 104 | tf_op jit(solution)/shard_map/ppermute | solution.py:227
  20.5 5.3 %collective-permute-start.6 = (s32[1,8]{1,0:T(1,128)}, s32[1,8]{1,0:T(1,128)S(1)}, u32[]{:S(2)}, u32[]{:S(2)}) collective-permute-start(s32[1,8]{1,0:T(1,128)} %param.16), channel_id=1, source_target_pairs={{0,16},{4,20},{8,24},{12,28},{16,0},{20,4},{24,8},{28,12},{1,17},{... | collective-permute-start | bytes 104 | tf_op jit(solution)/shard_map/ppermute | solution.py:227
  21.8 5.6 %collective-permute-start.7 = (s32[1,8]{1,0:T(1,128)}, s32[1,8]{1,0:T(1,128)S(1)}, u32[]{:S(2)}, u32[]{:S(2)}) collective-permute-start(s32[1,8]{1,0:T(1,128)} %param.16), channel_id=1, source_target_pairs={{0,20},{4,24},{8,28},{12,0},{16,4},{20,8},{24,12},{28,16},{1,21},{... | collective-permute-start | bytes 104 | tf_op jit(solution)/shard_map/ppermute | solution.py:227
  24.4 3.7 %collective-permute-start.8 = (s32[1,8]{1,0:T(1,128)}, s32[1,8]{1,0:T(1,128)S(1)}, u32[]{:S(2)}, u32[]{:S(2)}) collective-permute-start(s32[1,8]{1,0:T(1,128)} %param.16), channel_id=1, source_target_pairs={{0,24},{4,28},{8,0},{12,4},{16,8},{20,12},{24,16},{28,20},{1,25},{... | collective-permute-start | bytes 104 | tf_op jit(solution)/shard_map/ppermute | solution.py:227
  25.8 3.7 %collective-permute-start.9 = (s32[1,8]{1,0:T(1,128)}, s32[1,8]{1,0:T(1,128)S(1)}, u32[]{:S(2)}, u32[]{:S(2)}) collective-permute-start(s32[1,8]{1,0:T(1,128)} %param.16), channel_id=1, source_target_pairs={{0,28},{4,0},{8,4},{12,8},{16,12},{20,16},{24,20},{28,24},{1,29},{... | collective-permute-start | bytes 104 | tf_op jit(solution)/shard_map/ppermute | solution.py:227
  28.1 3.4 %collective-permute-start.2 = (bf16[96,5120]{1,0:T(8,128)(2,1)S(1)}, bf16[96,5120]{1,0:T(8,128)(2,1)}, u32[]{:S(2)}, u32[]{:S(2)}) collective-permute-start(bf16[96,5120]{1,0:T(8,128)(2,1)S(1)} %collective-permute-done), channel_id=1, source_target_pairs={{0,1},{1,0},{2,3},{3,2},{4,5},{5,4},{6,7},{7,6},{8,9},{9,8},{10,11... | collective-permute-start | bytes 2949128 | tf_op jit(solution)/shard_map/ppermute | solution.py:290
  31.5 7.0 %slice-start.2 = ((s8[6553600]{0:T(1024)(128)(4,1)}), s8[4194304]{0:T(1024)(128)(4,1)S(1)}, s32[]{:S(2)}) async-start(s8[6553600]{0:T(1024)(128)(4,1)} %bitcast.315), calls=%async_computation.2 | async-start | bytes 8388608
  34.0 4.5 %slice-start.3 = ((s8[6553600]{0:T(1024)(128)(4,1)}), s8[2359296]{0:T(1024)(128)(4,1)S(1)}, s32[]{:S(2)}) async-start(s8[6553600]{0:T(1024)(128)(4,1)} %bitcast.315), calls=%async_computation.3 | async-start | bytes 4718592
  34.0 4.5 %copy-start.11 = (f32[640]{0:T(1024)S(1)}, f32[640]{0:T(1024)}, u32[]{:S(2)}) copy-start(f32[640]{0:T(1024)} %param.19) | copy-start | bytes 7684
  38.5 3.3 %copy-start.1 = (bf16[384,5120]{1,0:T(8,128)(2,1)}, bf16[384,5120]{1,0:T(8,128)(2,1)S(1)}, u32[]{:S(2)}) copy-start(bf16[384,5120]{1,0:T(8,128)(2,1)S(1)} %fusion.2) | copy-start | bytes 11796484
  38.5 3.4 %copy-start.8 = (f32[128]{0:T(128)S(1)}, f32[128]{0:T(128)}, u32[]{:S(2)}) copy-start(f32[128]{0:T(128)} %param.21) | copy-start | bytes 1540
  41.9 1.2 %copy-start.10 = (f32[64]{0:T(128)S(1)}, f32[64]{0:T(128)}, u32[]{:S(2)}) copy-start(f32[64]{0:T(128)} %multiply_exponential_fusion) | copy-start | bytes 772
  45.1 4.0 %copy-start.3 = (bf16[384,64]{0,1:T(8,128)(2,1)S(1)}, bf16[384,64]{0,1:T(8,128)(2,1)}, u32[]{:S(2)}) copy-start(bf16[384,64]{0,1:T(8,128)(2,1)} %copy.35) | copy-start | bytes 147460
  45.1 4.0 %copy-start.9 = (s32[384]{0:T(512)S(1)}, s32[384]{0:T(512)}, u32[]{:S(2)}) copy-start(s32[384]{0:T(512)} %eq.245) | copy-start | bytes 4612
  48.9 2.6 %copy-start.5 = (s32[256]{0:T(256)S(1)}, s32[256]{0:T(256)}, u32[]{:S(2)}) copy-start(s32[256]{0:T(256)} %select_reduce_fusion) | copy-start | bytes 3076
  49.8 9.4 %collective-permute-start.10 = (bf16[48,896]{1,0:T(8,128)(2,1)S(1)}, bf16[48,896]{1,0:T(8,128)(2,1)S(1)}, u32[]{:S(2)}, u32[]{:S(2)}) collective-permute-start(bf16[48,896]{1,0:T(8,128)(2,1)S(1)} %get-tuple-element.44), channel_id=1, source_target_pairs={{0,4},{4,8},{8,12},{12,16},{16,20},{20,24},{24,28},{28,0},{1,5},{5... | collective-permute-start | bytes 258056 | tf_op jit(solution)/shard_map/ppermute | solution.py:243
  51.6 7.7 %collective-permute-start.11 = (bf16[48,896]{1,0:T(8,128)(2,1)S(1)}, bf16[48,896]{1,0:T(8,128)(2,1)S(1)}, u32[]{:S(2)}, u32[]{:S(2)}) collective-permute-start(bf16[48,896]{1,0:T(8,128)(2,1)S(1)} %get-tuple-element.43), channel_id=1, source_target_pairs={{0,8},{4,12},{8,16},{12,20},{16,24},{20,28},{24,0},{28,4},{1,9},{5... | collective-permute-start | bytes 258056 | tf_op jit(solution)/shard_map/ppermute | solution.py:243
  51.9 12.1 %collective-permute-start.12 = (bf16[48,896]{1,0:T(8,128)(2,1)S(1)}, bf16[48,896]{1,0:T(8,128)(2,1)S(1)}, u32[]{:S(2)}, u32[]{:S(2)}) collective-permute-start(bf16[48,896]{1,0:T(8,128)(2,1)S(1)} %get-tuple-element.42), channel_id=1, source_target_pairs={{0,12},{4,16},{8,20},{12,24},{16,28},{20,0},{24,4},{28,8},{1,13},{... | collective-permute-start | bytes 258056 | tf_op jit(solution)/shard_map/ppermute | solution.py:243
  54.4 10.2 %collective-permute-start.13 = (bf16[48,896]{1,0:T(8,128)(2,1)S(1)}, bf16[48,896]{1,0:T(8,128)(2,1)S(1)}, u32[]{:S(2)}, u32[]{:S(2)}) collective-permute-start(bf16[48,896]{1,0:T(8,128)(2,1)S(1)} %get-tuple-element.41), channel_id=1, source_target_pairs={{0,16},{4,20},{8,24},{12,28},{16,0},{20,4},{24,8},{28,12},{1,17},{... | collective-permute-start | bytes 258056 | tf_op jit(solution)/shard_map/ppermute | solution.py:243
  55.9 8.7 %collective-permute-start.14 = (bf16[48,896]{1,0:T(8,128)(2,1)S(1)}, bf16[48,896]{1,0:T(8,128)(2,1)S(1)}, u32[]{:S(2)}, u32[]{:S(2)}) collective-permute-start(bf16[48,896]{1,0:T(8,128)(2,1)S(1)} %get-tuple-element.40), channel_id=1, source_target_pairs={{0,20},{4,24},{8,28},{12,0},{16,4},{20,8},{24,12},{28,16},{1,21},{... | collective-permute-start | bytes 258056 | tf_op jit(solution)/shard_map/ppermute | solution.py:243
  59.2 7.3 %collective-permute-start.15 = (bf16[48,896]{1,0:T(8,128)(2,1)S(1)}, bf16[48,896]{1,0:T(8,128)(2,1)S(1)}, u32[]{:S(2)}, u32[]{:S(2)}) collective-permute-start(bf16[48,896]{1,0:T(8,128)(2,1)S(1)} %get-tuple-element.39), channel_id=1, source_target_pairs={{0,24},{4,28},{8,0},{12,4},{16,8},{20,12},{24,16},{28,20},{1,25},{... | collective-permute-start | bytes 258056 | tf_op jit(solution)/shard_map/ppermute | solution.py:243
  59.3 7.2 %collective-permute-start.16 = (bf16[48,896]{1,0:T(8,128)(2,1)S(1)}, bf16[48,896]{1,0:T(8,128)(2,1)S(1)}, u32[]{:S(2)}, u32[]{:S(2)}) collective-permute-start(bf16[48,896]{1,0:T(8,128)(2,1)S(1)} %get-tuple-element.38), channel_id=1, source_target_pairs={{0,28},{4,0},{8,4},{12,8},{16,12},{20,16},{24,20},{28,24},{1,29},{... | collective-permute-start | bytes 258056 | tf_op jit(solution)/shard_map/ppermute | solution.py:243
  68.6 5.4 %slice-start = ((s8[6553600]{0:T(1024)(128)(4,1)}), s8[4194304]{0:T(1024)(128)(4,1)S(1)}, s32[]{:S(2)}) async-start(s8[6553600]{0:T(1024)(128)(4,1)} %bitcast.301), calls=%async_computation | async-start | bytes 8388608
  68.6 5.4 %slice-start.1 = ((s8[6553600]{0:T(1024)(128)(4,1)}), s8[2359296]{0:T(1024)(128)(4,1)S(1)}, s32[]{:S(2)}) async-start(s8[6553600]{0:T(1024)(128)(4,1)} %bitcast.301), calls=%async_computation.1 | async-start | bytes 4718592
  73.0 7.8 %collective-permute-start.23 = (f32[2,64,1280]{2,1,0:T(8,128)S(1)}, f32[2,64,1280]{2,1,0:T(8,128)S(1)}, u32[]{:S(2)}, u32[]{:S(2)}) collective-permute-start(f32[2,64,1280]{2,1,0:T(8,128)S(1)} %pad_maximum_fusion.4), channel_id=1, source_target_pairs={{0,1},{1,0},{2,3},{3,2},{4,5},{5,4},{6,7},{7,6},{8,9},{9,8},{10,11... | collective-permute-start | bytes 1966088 | tf_op jit(solution)/shard_map/ppermute | solution.py:261
  74.0 2.0 %copy-start.7 = (pred[64,128]{1,0:T(8,128)(4,1)S(1)}, pred[64,128]{1,0:T(8,128)(4,1)}, u32[]{:S(2)}) copy-start(pred[64,128]{1,0:T(8,128)(4,1)} %compare_and_fusion.1) | copy-start | bytes 24580
  75.4 6.1 %collective-permute-start.21 = (f32[2,64,1280]{2,1,0:T(8,128)S(1)}, f32[2,64,1280]{2,1,0:T(8,128)S(1)}, u32[]{:S(2)}, u32[]{:S(2)}) collective-permute-start(f32[2,64,1280]{2,1,0:T(8,128)S(1)} %pad_maximum_fusion.3), channel_id=1, source_target_pairs={{0,1},{1,0},{2,3},{3,2},{4,5},{5,4},{6,7},{7,6},{8,9},{9,8},{10,11... | collective-permute-start | bytes 1966088 | tf_op jit(solution)/shard_map/ppermute | solution.py:261
  76.8 1.5 %copy-start.6 = (pred[64,64]{0,1:T(8,128)(4,1)S(1)}, pred[64,64]{0,1:T(8,128)(4,1)}, u32[]{:S(2)}) copy-start(pred[64,64]{0,1:T(8,128)(4,1)} %compare_and_fusion.2) | copy-start | bytes 12292
  78.2 5.0 %collective-permute-start.19 = (f32[2,64,1280]{2,1,0:T(8,128)S(1)}, f32[2,64,1280]{2,1,0:T(8,128)S(1)}, u32[]{:S(2)}, u32[]{:S(2)}) collective-permute-start(f32[2,64,1280]{2,1,0:T(8,128)S(1)} %pad_maximum_fusion.2), channel_id=1, source_target_pairs={{0,1},{1,0},{2,3},{3,2},{4,5},{5,4},{6,7},{7,6},{8,9},{9,8},{10,11... | collective-permute-start | bytes 1966088 | tf_op jit(solution)/shard_map/ppermute | solution.py:261
  80.3 3.6 %collective-permute-start.17 = (f32[2,64,1280]{2,1,0:T(8,128)S(1)}, f32[2,64,1280]{2,1,0:T(8,128)S(1)}, u32[]{:S(2)}, u32[]{:S(2)}) collective-permute-start(f32[2,64,1280]{2,1,0:T(8,128)S(1)} %pad_maximum_fusion.1), channel_id=1, source_target_pairs={{0,1},{1,0},{2,3},{3,2},{4,5},{5,4},{6,7},{7,6},{8,9},{9,8},{10,11... | collective-permute-start | bytes 1966088 | tf_op jit(solution)/shard_map/ppermute | solution.py:261
  80.9 10.6 %collective-permute-start.24 = (f32[1,64,1280]{2,1,0:T(8,128)S(1)}, f32[1,64,1280]{2,1,0:T(8,128)S(1)}, u32[]{:S(2)}, u32[]{:S(2)}) collective-permute-start(f32[1,64,1280]{2,1,0:T(8,128)S(1)} %get-tuple-element.21), channel_id=1, source_target_pairs={{0,2},{1,3},{2,0},{3,1},{4,6},{5,7},{6,4},{7,5},{8,10},{9,11},{10,... | collective-permute-start | bytes 983048 | tf_op jit(solution)/shard_map/ppermute | solution.py:261
  81.6 16.9 %collective-permute-start.22 = (f32[1,64,1280]{2,1,0:T(8,128)S(1)}, f32[1,64,1280]{2,1,0:T(8,128)S(1)}, u32[]{:S(2)}, u32[]{:S(2)}) collective-permute-start(f32[1,64,1280]{2,1,0:T(8,128)S(1)} %get-tuple-element.18), channel_id=1, source_target_pairs={{0,2},{1,3},{2,0},{3,1},{4,6},{5,7},{6,4},{7,5},{8,10},{9,11},{10,... | collective-permute-start | bytes 983048 | tf_op jit(solution)/shard_map/ppermute | solution.py:261
  83.3 22.3 %collective-permute-start.20 = (f32[1,64,1280]{2,1,0:T(8,128)S(1)}, f32[1,64,1280]{2,1,0:T(8,128)S(1)}, u32[]{:S(2)}, u32[]{:S(2)}) collective-permute-start(f32[1,64,1280]{2,1,0:T(8,128)S(1)} %get-tuple-element.15), channel_id=1, source_target_pairs={{0,2},{1,3},{2,0},{3,1},{4,6},{5,7},{6,4},{7,5},{8,10},{9,11},{10,... | collective-permute-start | bytes 983048 | tf_op jit(solution)/shard_map/ppermute | solution.py:261
  84.1 27.6 %collective-permute-start.18 = (f32[1,64,1280]{2,1,0:T(8,128)S(1)}, f32[1,64,1280]{2,1,0:T(8,128)S(1)}, u32[]{:S(2)}, u32[]{:S(2)}) collective-permute-start(f32[1,64,1280]{2,1,0:T(8,128)S(1)} %get-tuple-element.12), channel_id=1, source_target_pairs={{0,2},{1,3},{2,0},{3,1},{4,6},{5,7},{6,4},{7,5},{8,10},{9,11},{10,... | collective-permute-start | bytes 983048 | tf_op jit(solution)/shard_map/ppermute | solution.py:261

commit v14 on v10

--- a/solution.py
+++ b/solution.py
@@ -147,10 +147,15 @@
     else:
         shifted_dest = my_dest
     places = to_work_order(send_places(shifted_dest, ctx_count, group_cap, pack_len))
-    send_hot = (
-        places[None, :] == jnp.arange(ctx_count * group_cap, dtype=jnp.int32)[:, None]
-    ).astype(jnp.bfloat16)
-    outgoing = jnp.dot(send_hot, qkv, preferred_element_type=jnp.float32).astype(jnp.bfloat16)
+    send_hit = places[None, :] == jnp.arange(ctx_count * group_cap, dtype=jnp.int32)[:, None]
+    work_rows = jnp.arange(group_rows, dtype=jnp.int32)
+    source_rows = jnp.where(
+        jnp.any(send_hit, axis=1),
+        jnp.sum(jnp.where(send_hit, work_rows[None, :], 0), axis=1),
+        group_rows,
+    )
+    padded_qkv = jnp.concatenate([qkv, jnp.zeros((1, qkv.shape[1]), qkv.dtype)], axis=0)
+    outgoing = jnp.take(padded_qkv, source_rows, axis=0)
     arrived = exchange(outgoing, "ctx", ctx_count)
 
     mine = (pool_dest >= 0) & (pool_dest // pack_len == ctx_index)

time: 112 us -> 120 us (1.071)
  local copies, waits for them, and re-layouts: 6.52 us -> 10.2 us
  other arithmetic: 18.4 us -> 21.7 us
    dot_general x1, matrix products: 3.28 us -> 7.41 us  [project(): jnp.dot(normalized_input, w_query, preferred_element_type=jnp.float32)]
    dot_general x1, matrix products: 3.77 us -> 1.24 us  [project(): jnp.dot(normalized_input, value_projection_weight, preferred_element_type...]
    gather x0 -> x1, local copies, waits for them, and re-layouts: none -> 2.28 us  [local(): outgoing = jnp.take(padded_qkv, source_rows, axis=0)]
    unnamed x44, local copies, waits for them, and re-layouts: 0.9 us -> 2.75 us
    concatenate x2 -> x0, local copies, waits for them, and re-layouts: 1.42 us -> none  [apply_rotary(): jnp.concatenate([first_half * cosine - second_half * sine_table, second_h...]
where the time goes in v14:
time: 120 us; the launch traced here: 119 us
  waiting for transfers between devices  33.7 us (28%)
  starting transfers between devices  32 us (27%)
  other arithmetic  21.7 us (18%)
  matrix products  20.5 us (17%)
  local copies, waits for them, and re-layouts  10.2 us (8%)
    ppermute x8, waiting for transfers between devices, halving_scatter(): got = lax.ppermute(send, axis_name, pairs)  25.9 us
    ppermute x7, starting transfers between devices, shift_gather(): lax.ppermute(part, axis_name, [(i, (i + shift) % count) for i in range(co...  12.5 us
    ppermute x7, starting transfers between devices, exchange(): arrived.append(lax.ppermute(chunks[shift], axis_name, pairs))  10.9 us
    dot_general x4, matrix products, local(): jnp.dot(mixed_heads, w_out, preferred_element_type=jnp.float32)  8.09 us
    dot_general x1, matrix products, project(): jnp.dot(normalized_input, w_query, preferred_element_type=jnp.float32)  7.41 us
    ppermute x7, waiting for transfers between devices, exchange(): arrived.append(lax.ppermute(chunks[shift], axis_name, pairs))  5.67 us
    ppermute x8, starting transfers between devices, halving_scatter(): got = lax.ppermute(send, axis_name, pairs)  5.57 us
    convert_element_type x1, other arithmetic, project(): normalized_input = (values_wide * lax.rsqrt(jnp.mean(values_wide * values...  4.47 us
  transfers between devices with their start and end apart: 25, of which 9 were waited for; matrix products, arithmetic and copies ran while one was open for 17% of the time, Pallas kernels for 0%

profile of v14, /device:TPU:0, one launch (start us, length us, event | category | flops | bytes accessed | tf_op | source)
XLA Modules:
  0.0 118.8 jit_solution(14868330540610400815)
XLA Ops:
  0.0 3.0 %collective-permute-start = (bf16[96,5120]{1,0:T(8,128)(2,1)}, bf16[96,5120]{1,0:T(8,128)(2,1)S(1)}, u32[]{:S(2)}, u32[]{:S(2)}) collective-permute-start(bf16[96,5120]{1,0:T(8,128)(2,1)} %param.14), channel_id=1, source_target_pairs={{0,2},{1,3},{2,0},{3,1},{4,6},{5,7},{6,4},{7,5},{8,10},{9,11},{10,... | collective-permute-start | bytes 2949128 | tf_op jit(solution)/shard_map/ppermute | solution.py:291
  3.0 1.5 %collective-permute-start.3 = (s32[1,8]{1,0:T(1,128)}, s32[1,8]{1,0:T(1,128)S(1)}, u32[]{:S(2)}, u32[]{:S(2)}) collective-permute-start(s32[1,8]{1,0:T(1,128)} %param.16), channel_id=1, source_target_pairs={{0,4},{4,8},{8,12},{12,16},{16,20},{20,24},{24,28},{28,0},{1,5},{5... | collective-permute-start | bytes 104 | tf_op jit(solution)/shard_map/ppermute | solution.py:228
  4.5 1.6 %collective-permute-start.4 = (s32[1,8]{1,0:T(1,128)}, s32[1,8]{1,0:T(1,128)S(1)}, u32[]{:S(2)}, u32[]{:S(2)}) collective-permute-start(s32[1,8]{1,0:T(1,128)} %param.16), channel_id=1, source_target_pairs={{0,8},{4,12},{8,16},{12,20},{16,24},{20,28},{24,0},{28,4},{1,9},{5... | collective-permute-start | bytes 104 | tf_op jit(solution)/shard_map/ppermute | solution.py:228
  6.1 2.5 %collective-permute-start.5 = (s32[1,8]{1,0:T(1,128)}, s32[1,8]{1,0:T(1,128)S(1)}, u32[]{:S(2)}, u32[]{:S(2)}) collective-permute-start(s32[1,8]{1,0:T(1,128)} %param.16), channel_id=1, source_target_pairs={{0,12},{4,16},{8,20},{12,24},{16,28},{20,0},{24,4},{28,8},{1,13},{... | collective-permute-start | bytes 104 | tf_op jit(solution)/shard_map/ppermute | solution.py:228
  8.6 0.6 multiply_exponential_fusion
  9.2 0.7 constant_dynamic-update-slice_fusion.7
  9.9 0.7 reshape.903
  10.8 0.9 reduce-window.30
  12.1 0.7 compare_and_fusion.4
  12.8 0.6 gather_fusion.3
  13.3 0.6 gather_fusion.2
  14.4 0.8 reduce-window.32
  15.6 0.5 compare_and_fusion.6
  16.2 0.6 pad_clamp_fusion
  16.8 0.7 subtract_select_fusion
  17.6 0.9 reduce-window.21
  18.9 0.7 fusion.75
  19.9 1.3 %collective-permute-start.6 = (s32[1,8]{1,0:T(1,128)}, s32[1,8]{1,0:T(1,128)S(1)}, u32[]{:S(2)}, u32[]{:S(2)}) collective-permute-start(s32[1,8]{1,0:T(1,128)} %param.16), channel_id=1, source_target_pairs={{0,16},{4,20},{8,24},{12,28},{16,0},{20,4},{24,8},{28,12},{1,17},{... | collective-permute-start | bytes 104 | tf_op jit(solution)/shard_map/ppermute | solution.py:228
  21.2 2.6 %collective-permute-start.7 = (s32[1,8]{1,0:T(1,128)}, s32[1,8]{1,0:T(1,128)S(1)}, u32[]{:S(2)}, u32[]{:S(2)}) collective-permute-start(s32[1,8]{1,0:T(1,128)} %param.16), channel_id=1, source_target_pairs={{0,20},{4,24},{8,28},{12,0},{16,4},{20,8},{24,12},{28,16},{1,21},{... | collective-permute-start | bytes 104 | tf_op jit(solution)/shard_map/ppermute | solution.py:228
  23.9 1.3 %collective-permute-start.8 = (s32[1,8]{1,0:T(1,128)}, s32[1,8]{1,0:T(1,128)S(1)}, u32[]{:S(2)}, u32[]{:S(2)}) collective-permute-start(s32[1,8]{1,0:T(1,128)} %param.16), channel_id=1, source_target_pairs={{0,24},{4,28},{8,0},{12,4},{16,8},{20,12},{24,16},{28,20},{1,25},{... | collective-permute-start | bytes 104 | tf_op jit(solution)/shard_map/ppermute | solution.py:228
  25.2 1.6 %collective-permute-start.9 = (s32[1,8]{1,0:T(1,128)}, s32[1,8]{1,0:T(1,128)S(1)}, u32[]{:S(2)}, u32[]{:S(2)}) collective-permute-start(s32[1,8]{1,0:T(1,128)} %param.16), channel_id=1, source_target_pairs={{0,28},{4,0},{8,4},{12,8},{16,12},{20,16},{24,20},{28,24},{1,29},{... | collective-permute-start | bytes 104 | tf_op jit(solution)/shard_map/ppermute | solution.py:228
  26.9 0.7 collective-permute-done.8
  27.6 1.3 %collective-permute-done.9 = s32[1,8]{1,0:T(1,128)S(1)} collective-permute-done((s32[1,8]{1,0:T(1,128)}, s32[1,8]{1,0:T(1,128)S(1)}, u32[]{:S(2)}, u32[]{:S(2)}) %collective-permute-start.9) | collective-permute-done | bytes 64 | tf_op jit(solution)/shard_map/ppermute | solution.py:228
  28.9 0.6 gather_fusion
  29.8 1.1 multiply_cosine_fusion.1
  30.9 2.3 %fusion = f32[384]{0:T(512)S(1)} fusion(bf16[96,5120]{1,0:T(8,128)(2,1)} %collective-permute-done.2, bf16[96,5120]{1,0:T(8,128)(2,1)} %collective-permute-done.1, bf16[96,5120]{1,0:T(8,128)(2,1)S(1)} %collective-permute-done, bf16[96,5120]{1,0:T(8,128)(2,1)} %param.14), kind=kLoop, calls=%fused_computation.6 | loop fusion | flops 19660416 | bytes 3933696 | tf_op jit(solution)/shard_map/reduce_sum | solution.py:108
  33.2 4.5 %fusion.2 = bf16[384,5120]{1,0:T(8,128)(2,1)S(1)} fusion(f32[5120]{0:T(1024)S(1)} %copy-done.5, f32[384]{0:T(512)S(1)} %add_rsqrt_fusion, bf16[96,5120]{1,0:T(8,128)(2,1)} %collective-permute-done.2, bf16[96,5120]{1,0:T(8,128)(2,1)} %collective-permute-done.1, bf16[96,5120]{1,0:T(8,128)(2,1)S(1)} %collective-permute-done, bf16[96,5120]{1,0:T(8,128)(2,1)S(1)} %copy-done.3), kind=kLoop, calls=%fused_computation.8 | loop fusion | flops 21626880 | bytes 7886336 | tf_op jit(solution)/shard_map/convert_element_type | solution.py:110
  37.7 1.9 %copy-done.1 = bf16[384,5120]{1,0:T(8,128)(2,1)} copy-done((bf16[384,5120]{1,0:T(8,128)(2,1)}, bf16[384,5120]{1,0:T(8,128)(2,1)S(1)}, u32[]{:S(2)}) %copy-start.1) | copy-done | bytes 3932184
  39.6 1.2 %fusion.13 = bf16[384,128]{0,1:T(8,128)(2,1)S(1)} fusion(bf16[384,5120]{1,0:T(8,128)(2,1)S(1)} %fusion.2, bf16[5120,128]{1,0:T(8,128)(2,1)S(1)} %copy-done, f32[128]{0:T(128)S(1)} %copy-done.11), kind=kOutput, calls=%fused_computation.31 | convolution fusion | flops 503414784 | bytes 5341696 | tf_op jit(solution)/shard_map/dot_general | solution.py:126
  40.8 0.8 copy.37
  41.6 7.4 %convolution_add_fusion = f32[384,640]{1,0:T(8,128)S(1)} fusion(bf16[384,5120]{1,0:T(8,128)(2,1)} %copy-done.1, bf16[5120,640]{1,0:T(8,128)(2,1)} %param.18, f32[640]{0:T(1024)S(1)} %copy-done.12), kind=kOutput, calls=%fused_computation.17 | convolution fusion | flops 2516828160 | bytes 11471360 | tf_op jit(solution)/shard_map/dot_general | solution.py:112
  49.1 1.2 %convolution_add_fusion.2 = f32[384,128]{1,0:T(8,128)S(1)} fusion(bf16[384,5120]{1,0:T(8,128)(2,1)S(1)} %copy-done.2, bf16[5120,128]{1,0:T(8,128)(2,1)S(1)} %copy-done.4, f32[128]{0:T(128)S(1)} %copy-done.8), kind=kOutput, calls=%fused_computation.24 | convolution fusion | flops 503365632 | bytes 5440000 | tf_op jit(solution)/shard_map/dot_general | solution.py:115
  50.3 1.5 %fusion.52 = (bf16[384,64]{1,0:T(8,128)(2,1)}, bf16[384,64]{1,0:T(8,128)(2,1)}) fusion(f32[384,1,128]{2,0,1:T(8,128)S(1)} %bitcast.294, f32[64]{0:T(128)S(1)} %copy-done.10, f32[384]{0:T(512)S(1)} %subtract_convert_fusion.1), kind=kLoop, calls=%fused_computation.124 | loop fusion | flops 221184 | bytes 296704 | tf_op jit(solution)/shard_map/concatenate | solution.py:48
  51.8 0.3 copy.35
  52.6 1.1 fusion.22
  53.8 2.3 %gather_fusion.1 = bf16[384,896]{1,0:T(8,128)(2,1)S(1)} fusion(bf16[385,896]{1,0:T(8,128)(2,1)S(1)} %fusion.22, s32[1024]{0:T(1024)S(1)} %copy-done.7), kind=kCustom, calls=%fused_computation.3 | custom fusion | bytes 1377792 | tf_op jit(solution)/shard_map/jit(_take)/gather | solution.py:158
  56.3 1.8 %collective-permute-start.10 = (bf16[48,896]{1,0:T(8,128)(2,1)S(1)}, bf16[48,896]{1,0:T(8,128)(2,1)S(1)}, u32[]{:S(2)}, u32[]{:S(2)}) collective-permute-start(bf16[48,896]{1,0:T(8,128)(2,1)S(1)} %get-tuple-element.46), channel_id=1, source_target_pairs={{0,4},{4,8},{8,12},{12,16},{16,20},{20,24},{24,28},{28,0},{1,5},{5... | collective-permute-start | bytes 258056 | tf_op jit(solution)/shard_map/ppermute | solution.py:244
  58.1 0.4 select_reduce_fusion
  58.8 2.6 %collective-permute-start.12 = (bf16[48,896]{1,0:T(8,128)(2,1)S(1)}, bf16[48,896]{1,0:T(8,128)(2,1)S(1)}, u32[]{:S(2)}, u32[]{:S(2)}) collective-permute-start(bf16[48,896]{1,0:T(8,128)(2,1)S(1)} %get-tuple-element.44), channel_id=1, source_target_pairs={{0,12},{4,16},{8,20},{12,24},{16,28},{20,0},{24,4},{28,8},{1,13},{... | collective-permute-start | bytes 258056 | tf_op jit(solution)/shard_map/ppermute | solution.py:244
  61.3 1.5 %collective-permute-start.13 = (bf16[48,896]{1,0:T(8,128)(2,1)S(1)}, bf16[48,896]{1,0:T(8,128)(2,1)S(1)}, u32[]{:S(2)}, u32[]{:S(2)}) collective-permute-start(bf16[48,896]{1,0:T(8,128)(2,1)S(1)} %get-tuple-element.43), channel_id=1, source_target_pairs={{0,16},{4,20},{8,24},{12,28},{16,0},{20,4},{24,8},{28,12},{1,17},{... | collective-permute-start | bytes 258056 | tf_op jit(solution)/shard_map/ppermute | solution.py:244
  62.8 3.3 %collective-permute-start.14 = (bf16[48,896]{1,0:T(8,128)(2,1)S(1)}, bf16[48,896]{1,0:T(8,128)(2,1)S(1)}, u32[]{:S(2)}, u32[]{:S(2)}) collective-permute-start(bf16[48,896]{1,0:T(8,128)(2,1)S(1)} %get-tuple-element.42), channel_id=1, source_target_pairs={{0,20},{4,24},{8,28},{12,0},{16,4},{20,8},{24,12},{28,16},{1,21},{... | collective-permute-start | bytes 258056 | tf_op jit(solution)/shard_map/ppermute | solution.py:244
  66.2 1.4 %collective-permute-start.16 = (bf16[48,896]{1,0:T(8,128)(2,1)S(1)}, bf16[48,896]{1,0:T(8,128)(2,1)S(1)}, u32[]{:S(2)}, u32[]{:S(2)}) collective-permute-start(bf16[48,896]{1,0:T(8,128)(2,1)S(1)} %get-tuple-element.40), channel_id=1, source_target_pairs={{0,28},{4,0},{8,4},{12,8},{16,12},{20,16},{24,20},{28,24},{1,29},{... | collective-permute-start | bytes 258056 | tf_op jit(solution)/shard_map/ppermute | solution.py:244
  67.7 2.9 %collective-permute-done.12 = bf16[48,896]{1,0:T(8,128)(2,1)S(1)} collective-permute-done((bf16[48,896]{1,0:T(8,128)(2,1)S(1)}, bf16[48,896]{1,0:T(8,128)(2,1)S(1)}, u32[]{:S(2)}, u32[]{:S(2)}) %collective-permute-start.12) | collective-permute-done | bytes 86048 | tf_op jit(solution)/shard_map/ppermute | solution.py:244
  70.5 1.0 collective-permute-done.13
  71.5 1.8 %collective-permute-done.15 = bf16[48,896]{1,0:T(8,128)(2,1)S(1)} collective-permute-done((bf16[48,896]{1,0:T(8,128)(2,1)S(1)}, bf16[48,896]{1,0:T(8,128)(2,1)S(1)}, u32[]{:S(2)}, u32[]{:S(2)}) %collective-permute-start.15) | collective-permute-done | bytes 86048 | tf_op jit(solution)/shard_map/ppermute | solution.py:244
  73.4 0.5 convolution_convert_fusion
  74.4 0.3 fusion.17
  74.8 4.3 %fusion.53 = f32[64,5120]{1,0:T(8,128)S(1)} fusion(bf16[640,5120]{1,0:T(8,128)(2,1)} %param.24, bf16[8,8,5,128]{3,2,1,0:T(8,128)(2,1)S(1)} %bitcast.295), kind=kOutput, calls=%fused_computation.126 | convolution fusion | flops 419430400 | bytes 7946240 | tf_op jit(solution)/shard_map/dot_general | solution.py:218
  79.3 0.3 fusion.131
  79.8 0.3 fusion.16
  80.2 1.3 %fusion.56 = f32[64,5120]{1,0:T(8,128)S(1)} fusion(bf16[640,5120]{1,0:T(8,128)(2,1)S(1)} %bitcast.291, bf16[8,8,5,128]{3,2,1,0:T(8,128)(2,1)S(1)} %bitcast.296), kind=kOutput, calls=%fused_computation.129 | convolution fusion | flops 419430400 | bytes 7946240 | tf_op jit(solution)/shard_map/dot_general | solution.py:218
  81.6 0.6 collective-permute-start.21
  83.0 1.3 %fusion.59 = f32[64,5120]{1,0:T(8,128)S(1)} fusion(bf16[640,5120]{1,0:T(8,128)(2,1)S(1)} %bitcast.291, bf16[8,8,5,128]{3,2,1,0:T(8,128)(2,1)S(1)} %bitcast.297), kind=kOutput, calls=%fused_computation.132 | convolution fusion | flops 419430400 | bytes 7946240 | tf_op jit(solution)/shard_map/dot_general | solution.py:218
  85.0 1.3 %fusion.62 = f32[64,5120]{1,0:T(8,128)S(1)} fusion(bf16[640,5120]{1,0:T(8,128)(2,1)S(1)} %bitcast.291, bf16[8,8,5,128]{3,2,1,0:T(8,128)(2,1)S(1)} %bitcast.298), kind=kOutput, calls=%fused_computation.135 | convolution fusion | flops 419430400 | bytes 7946240 | tf_op jit(solution)/shard_map/dot_general | solution.py:218
  86.4 0.5 collective-permute-start.17
  87.1 0.6 collective-permute-start.24
  87.8 1.5 %collective-permute-start.22 = (f32[1,64,1280]{2,1,0:T(8,128)S(1)}, f32[1,64,1280]{2,1,0:T(8,128)S(1)}, u32[]{:S(2)}, u32[]{:S(2)}) collective-permute-start(f32[1,64,1280]{2,1,0:T(8,128)S(1)} %get-tuple-element.18), channel_id=1, source_target_pairs={{0,2},{1,3},{2,0},{3,1},{4,6},{5,7},{6,4},{7,5},{8,10},{9,11},{10,... | collective-permute-start | bytes 983048 | tf_op jit(solution)/shard_map/ppermute | solution.py:262
  89.5 0.6 collective-permute-start.20
  90.3 1.5 %collective-permute-start.18 = (f32[1,64,1280]{2,1,0:T(8,128)S(1)}, f32[1,64,1280]{2,1,0:T(8,128)S(1)}, u32[]{:S(2)}, u32[]{:S(2)}) collective-permute-start(f32[1,64,1280]{2,1,0:T(8,128)S(1)} %get-tuple-element.12), channel_id=1, source_target_pairs={{0,2},{1,3},{2,0},{3,1},{4,6},{5,7},{6,4},{7,5},{8,10},{9,11},{10,... | collective-permute-start | bytes 983048 | tf_op jit(solution)/shard_map/ppermute | solution.py:262
  91.8 6.0 %collective-permute-done.24 = f32[1,64,1280]{2,1,0:T(8,128)S(1)} collective-permute-done((f32[1,64,1280]{2,1,0:T(8,128)S(1)}, f32[1,64,1280]{2,1,0:T(8,128)S(1)}, u32[]{:S(2)}, u32[]{:S(2)}) %collective-permute-start.24) | collective-permute-done | bytes 327712 | tf_op jit(solution)/shard_map/ppermute | solution.py:262
  97.8 7.0 %collective-permute-done.22 = f32[1,64,1280]{2,1,0:T(8,128)S(1)} collective-permute-done((f32[1,64,1280]{2,1,0:T(8,128)S(1)}, f32[1,64,1280]{2,1,0:T(8,128)S(1)}, u32[]{:S(2)}, u32[]{:S(2)}) %collective-permute-start.22) | collective-permute-done | bytes 327712 | tf_op jit(solution)/shard_map/ppermute | solution.py:262
  104.8 7.0 %collective-permute-done.20 = f32[1,64,1280]{2,1,0:T(8,128)S(1)} collective-permute-done((f32[1,64,1280]{2,1,0:T(8,128)S(1)}, f32[1,64,1280]{2,1,0:T(8,128)S(1)}, u32[]{:S(2)}, u32[]{:S(2)}) %collective-permute-start.20) | collective-permute-done | bytes 327712 | tf_op jit(solution)/shard_map/ppermute | solution.py:262
  111.8 6.0 %collective-permute-done.18 = f32[1,64,1280]{2,1,0:T(8,128)S(1)} collective-permute-done((f32[1,64,1280]{2,1,0:T(8,128)S(1)}, f32[1,64,1280]{2,1,0:T(8,128)S(1)}, u32[]{:S(2)}, u32[]{:S(2)}) %collective-permute-start.18) | collective-permute-done | bytes 327712 | tf_op jit(solution)/shard_map/ppermute | solution.py:262
  117.9 0.9 pad_maximum_fusion.5
  (156 shorter events, 7.5 us)
Async XLA Ops:
  0.0 39.6 %copy-start = (bf16[5120,128]{1,0:T(8,128)(2,1)S(1)}, bf16[5120,128]{1,0:T(8,128)(2,1)}, u32[]{:S(2)}) copy-start(bf16[5120,128]{1,0:T(8,128)(2,1)} %param.22) | copy-start | bytes 3932164
  0.0 33.2 %copy-start.3 = (bf16[96,5120]{1,0:T(8,128)(2,1)S(1)}, bf16[96,5120]{1,0:T(8,128)(2,1)}, u32[]{:S(2)}) copy-start(bf16[96,5120]{1,0:T(8,128)(2,1)} %param.14) | copy-start | bytes 2949124
  0.0 33.2 %copy-start.5 = (f32[5120]{0:T(1024)S(1)}, f32[5120]{0:T(1024)}, u32[]{:S(2)}) copy-start(f32[5120]{0:T(1024)} %param.17) | copy-start | bytes 61444
  0.0 27.5 %collective-permute-start = (bf16[96,5120]{1,0:T(8,128)(2,1)}, bf16[96,5120]{1,0:T(8,128)(2,1)S(1)}, u32[]{:S(2)}, u32[]{:S(2)}) collective-permute-start(bf16[96,5120]{1,0:T(8,128)(2,1)} %param.14), channel_id=1, source_target_pairs={{0,2},{1,3},{2,0},{3,1},{4,6},{5,7},{6,4},{7,5},{8,10},{9,11},{10,... | collective-permute-start | bytes 2949128 | tf_op jit(solution)/shard_map/ppermute | solution.py:291
  3.0 27.9 %collective-permute-start.1 = (bf16[96,5120]{1,0:T(8,128)(2,1)}, bf16[96,5120]{1,0:T(8,128)(2,1)}, u32[]{:S(2)}, u32[]{:S(2)}) collective-permute-start(bf16[96,5120]{1,0:T(8,128)(2,1)} %param.14), channel_id=1, source_target_pairs={{0,1},{1,0},{2,3},{3,2},{4,5},{5,4},{6,7},{7,6},{8,9},{9,8},{10,11... | collective-permute-start | bytes 2949128 | tf_op jit(solution)/shard_map/ppermute | solution.py:291
  3.0 16.9 %collective-permute-start.3 = (s32[1,8]{1,0:T(1,128)}, s32[1,8]{1,0:T(1,128)S(1)}, u32[]{:S(2)}, u32[]{:S(2)}) collective-permute-start(s32[1,8]{1,0:T(1,128)} %param.16), channel_id=1, source_target_pairs={{0,4},{4,8},{8,12},{12,16},{16,20},{20,24},{24,28},{28,0},{1,5},{5... | collective-permute-start | bytes 104 | tf_op jit(solution)/shard_map/ppermute | solution.py:228
  4.5 16.7 %collective-permute-start.4 = (s32[1,8]{1,0:T(1,128)}, s32[1,8]{1,0:T(1,128)S(1)}, u32[]{:S(2)}, u32[]{:S(2)}) collective-permute-start(s32[1,8]{1,0:T(1,128)} %param.16), channel_id=1, source_target_pairs={{0,8},{4,12},{8,16},{12,20},{16,24},{20,28},{24,0},{28,4},{1,9},{5... | collective-permute-start | bytes 104 | tf_op jit(solution)/shard_map/ppermute | solution.py:228
  6.1 17.8 %collective-permute-start.5 = (s32[1,8]{1,0:T(1,128)}, s32[1,8]{1,0:T(1,128)S(1)}, u32[]{:S(2)}, u32[]{:S(2)}) collective-permute-start(s32[1,8]{1,0:T(1,128)} %param.16), channel_id=1, source_target_pairs={{0,12},{4,16},{8,20},{12,24},{16,28},{20,0},{24,4},{28,8},{1,13},{... | collective-permute-start | bytes 104 | tf_op jit(solution)/shard_map/ppermute | solution.py:228
  19.9 5.3 %collective-permute-start.6 = (s32[1,8]{1,0:T(1,128)}, s32[1,8]{1,0:T(1,128)S(1)}, u32[]{:S(2)}, u32[]{:S(2)}) collective-permute-start(s32[1,8]{1,0:T(1,128)} %param.16), channel_id=1, source_target_pairs={{0,16},{4,20},{8,24},{12,28},{16,0},{20,4},{24,8},{28,12},{1,17},{... | collective-permute-start | bytes 104 | tf_op jit(solution)/shard_map/ppermute | solution.py:228
  21.2 5.6 %collective-permute-start.7 = (s32[1,8]{1,0:T(1,128)}, s32[1,8]{1,0:T(1,128)S(1)}, u32[]{:S(2)}, u32[]{:S(2)}) collective-permute-start(s32[1,8]{1,0:T(1,128)} %param.16), channel_id=1, source_target_pairs={{0,20},{4,24},{8,28},{12,0},{16,4},{20,8},{24,12},{28,16},{1,21},{... | collective-permute-start | bytes 104 | tf_op jit(solution)/shard_map/ppermute | solution.py:228
  23.9 3.7 %collective-permute-start.8 = (s32[1,8]{1,0:T(1,128)}, s32[1,8]{1,0:T(1,128)S(1)}, u32[]{:S(2)}, u32[]{:S(2)}) collective-permute-start(s32[1,8]{1,0:T(1,128)} %param.16), channel_id=1, source_target_pairs={{0,24},{4,28},{8,0},{12,4},{16,8},{20,12},{24,16},{28,20},{1,25},{... | collective-permute-start | bytes 104 | tf_op jit(solution)/shard_map/ppermute | solution.py:228
  25.2 3.7 %collective-permute-start.9 = (s32[1,8]{1,0:T(1,128)}, s32[1,8]{1,0:T(1,128)S(1)}, u32[]{:S(2)}, u32[]{:S(2)}) collective-permute-start(s32[1,8]{1,0:T(1,128)} %param.16), channel_id=1, source_target_pairs={{0,28},{4,0},{8,4},{12,8},{16,12},{20,16},{24,20},{28,24},{1,29},{... | collective-permute-start | bytes 104 | tf_op jit(solution)/shard_map/ppermute | solution.py:228
  27.6 3.4 %collective-permute-start.2 = (bf16[96,5120]{1,0:T(8,128)(2,1)S(1)}, bf16[96,5120]{1,0:T(8,128)(2,1)}, u32[]{:S(2)}, u32[]{:S(2)}) collective-permute-start(bf16[96,5120]{1,0:T(8,128)(2,1)S(1)} %collective-permute-done), channel_id=1, source_target_pairs={{0,1},{1,0},{2,3},{3,2},{4,5},{5,4},{6,7},{7,6},{8,9},{9,8},{10,11... | collective-permute-start | bytes 2949128 | tf_op jit(solution)/shard_map/ppermute | solution.py:291
  33.2 6.4 %copy-start.11 = (f32[128]{0:T(128)S(1)}, f32[128]{0:T(128)}, u32[]{:S(2)}) copy-start(f32[128]{0:T(128)} %param.23) | copy-start | bytes 1540
  37.7 1.9 %copy-start.1 = (bf16[384,5120]{1,0:T(8,128)(2,1)}, bf16[384,5120]{1,0:T(8,128)(2,1)S(1)}, u32[]{:S(2)}) copy-start(bf16[384,5120]{1,0:T(8,128)(2,1)S(1)} %fusion.2) | copy-start | bytes 11796484
  39.6 2.0 %copy-start.12 = (f32[640]{0:T(1024)S(1)}, f32[640]{0:T(1024)}, u32[]{:S(2)}) copy-start(f32[640]{0:T(1024)} %param.19) | copy-start | bytes 7684
  41.6 7.4 %copy-start.2 = (bf16[384,5120]{1,0:T(8,128)(2,1)S(1)}, bf16[384,5120]{1,0:T(8,128)(2,1)}, u32[]{:S(2)}) copy-start(bf16[384,5120]{1,0:T(8,128)(2,1)} %copy-done.1) | copy-start | bytes 11796484
  41.6 7.4 %copy-start.4 = (bf16[5120,128]{1,0:T(8,128)(2,1)S(1)}, bf16[5120,128]{1,0:T(8,128)(2,1)}, u32[]{:S(2)}) copy-start(bf16[5120,128]{1,0:T(8,128)(2,1)} %param.20) | copy-start | bytes 3932164
  41.6 7.4 %copy-start.8 = (f32[128]{0:T(128)S(1)}, f32[128]{0:T(128)}, u32[]{:S(2)}) copy-start(f32[128]{0:T(128)} %param.21) | copy-start | bytes 1540
  49.0 1.3 %copy-start.10 = (f32[64]{0:T(128)S(1)}, f32[64]{0:T(128)}, u32[]{:S(2)}) copy-start(f32[64]{0:T(128)} %multiply_exponential_fusion) | copy-start | bytes 772
  50.3 3.5 %copy-start.7 = (s32[1024]{0:T(1024)S(1)}, s32[1024]{0:T(1024)}, u32[]{:S(2)}) copy-start(s32[1024]{0:T(1024)} %pad_clamp_fusion) | copy-start | bytes 12292
  52.6 3.4 %copy-start.9 = (pred[384]{0:T(512)(128)(4,1)S(1)}, pred[384]{0:T(512)(128)(4,1)}, u32[]{:S(2)}) copy-start(pred[384]{0:T(512)(128)(4,1)} %get-tuple-element.26) | copy-start | bytes 1156
  56.0 17.9 %copy-start.6 = (pred[64,256]{1,0:T(8,128)(4,1)S(1)}, pred[64,256]{1,0:T(8,128)(4,1)}, u32[]{:S(2)}) copy-start(pred[64,256]{1,0:T(8,128)(4,1)} %fusion.75) | copy-start | bytes 49156
  56.3 9.8 %collective-permute-start.10 = (bf16[48,896]{1,0:T(8,128)(2,1)S(1)}, bf16[48,896]{1,0:T(8,128)(2,1)S(1)}, u32[]{:S(2)}, u32[]{:S(2)}) collective-permute-start(bf16[48,896]{1,0:T(8,128)(2,1)S(1)} %get-tuple-element.46), channel_id=1, source_target_pairs={{0,4},{4,8},{8,12},{12,16},{16,20},{20,24},{24,28},{28,0},{1,5},{5... | collective-permute-start | bytes 258056 | tf_op jit(solution)/shard_map/ppermute | solution.py:244
  58.5 7.7 %collective-permute-start.11 = (bf16[48,896]{1,0:T(8,128)(2,1)S(1)}, bf16[48,896]{1,0:T(8,128)(2,1)S(1)}, u32[]{:S(2)}, u32[]{:S(2)}) collective-permute-start(bf16[48,896]{1,0:T(8,128)(2,1)S(1)} %get-tuple-element.45), channel_id=1, source_target_pairs={{0,8},{4,12},{8,16},{12,20},{16,24},{20,28},{24,0},{28,4},{1,9},{5... | collective-permute-start | bytes 258056 | tf_op jit(solution)/shard_map/ppermute | solution.py:244
  58.8 11.7 %collective-permute-start.12 = (bf16[48,896]{1,0:T(8,128)(2,1)S(1)}, bf16[48,896]{1,0:T(8,128)(2,1)S(1)}, u32[]{:S(2)}, u32[]{:S(2)}) collective-permute-start(bf16[48,896]{1,0:T(8,128)(2,1)S(1)} %get-tuple-element.44), channel_id=1, source_target_pairs={{0,12},{4,16},{8,20},{12,24},{16,28},{20,0},{24,4},{28,8},{1,13},{... | collective-permute-start | bytes 258056 | tf_op jit(solution)/shard_map/ppermute | solution.py:244
  61.3 10.2 %collective-permute-start.13 = (bf16[48,896]{1,0:T(8,128)(2,1)S(1)}, bf16[48,896]{1,0:T(8,128)(2,1)S(1)}, u32[]{:S(2)}, u32[]{:S(2)}) collective-permute-start(bf16[48,896]{1,0:T(8,128)(2,1)S(1)} %get-tuple-element.43), channel_id=1, source_target_pairs={{0,16},{4,20},{8,24},{12,28},{16,0},{20,4},{24,8},{28,12},{1,17},{... | collective-permute-start | bytes 258056 | tf_op jit(solution)/shard_map/ppermute | solution.py:244
  62.8 8.7 %collective-permute-start.14 = (bf16[48,896]{1,0:T(8,128)(2,1)S(1)}, bf16[48,896]{1,0:T(8,128)(2,1)S(1)}, u32[]{:S(2)}, u32[]{:S(2)}) collective-permute-start(bf16[48,896]{1,0:T(8,128)(2,1)S(1)} %get-tuple-element.42), channel_id=1, source_target_pairs={{0,20},{4,24},{8,28},{12,0},{16,4},{20,8},{24,12},{28,16},{1,21},{... | collective-permute-start | bytes 258056 | tf_op jit(solution)/shard_map/ppermute | solution.py:244
  66.1 7.3 %collective-permute-start.15 = (bf16[48,896]{1,0:T(8,128)(2,1)S(1)}, bf16[48,896]{1,0:T(8,128)(2,1)S(1)}, u32[]{:S(2)}, u32[]{:S(2)}) collective-permute-start(bf16[48,896]{1,0:T(8,128)(2,1)S(1)} %get-tuple-element.41), channel_id=1, source_target_pairs={{0,24},{4,28},{8,0},{12,4},{16,8},{20,12},{24,16},{28,20},{1,25},{... | collective-permute-start | bytes 258056 | tf_op jit(solution)/shard_map/ppermute | solution.py:244
  66.2 7.2 %collective-permute-start.16 = (bf16[48,896]{1,0:T(8,128)(2,1)S(1)}, bf16[48,896]{1,0:T(8,128)(2,1)S(1)}, u32[]{:S(2)}, u32[]{:S(2)}) collective-permute-start(bf16[48,896]{1,0:T(8,128)(2,1)S(1)} %get-tuple-element.40), channel_id=1, source_target_pairs={{0,28},{4,0},{8,4},{12,8},{16,12},{20,16},{24,20},{28,24},{1,29},{... | collective-permute-start | bytes 258056 | tf_op jit(solution)/shard_map/ppermute | solution.py:244
  74.8 5.4 %slice-start = ((s8[6553600]{0:T(1024)(128)(4,1)}), s8[4194304]{0:T(1024)(128)(4,1)S(1)}, s32[]{:S(2)}) async-start(s8[6553600]{0:T(1024)(128)(4,1)} %bitcast.290), calls=%async_computation | async-start | bytes 8388608
  74.8 5.4 %slice-start.1 = ((s8[6553600]{0:T(1024)(128)(4,1)}), s8[2359296]{0:T(1024)(128)(4,1)S(1)}, s32[]{:S(2)}) async-start(s8[6553600]{0:T(1024)(128)(4,1)} %bitcast.290), calls=%async_computation.1 | async-start | bytes 4718592
  79.2 7.8 %collective-permute-start.23 = (f32[2,64,1280]{2,1,0:T(8,128)S(1)}, f32[2,64,1280]{2,1,0:T(8,128)S(1)}, u32[]{:S(2)}, u32[]{:S(2)}) collective-permute-start(f32[2,64,1280]{2,1,0:T(8,128)S(1)} %pad_maximum_fusion.4), channel_id=1, source_target_pairs={{0,1},{1,0},{2,3},{3,2},{4,5},{5,4},{6,7},{7,6},{8,9},{9,8},{10,11... | collective-permute-start | bytes 1966088 | tf_op jit(solution)/shard_map/ppermute | solution.py:262
  81.6 6.1 %collective-permute-start.21 = (f32[2,64,1280]{2,1,0:T(8,128)S(1)}, f32[2,64,1280]{2,1,0:T(8,128)S(1)}, u32[]{:S(2)}, u32[]{:S(2)}) collective-permute-start(f32[2,64,1280]{2,1,0:T(8,128)S(1)} %pad_maximum_fusion.3), channel_id=1, source_target_pairs={{0,1},{1,0},{2,3},{3,2},{4,5},{5,4},{6,7},{7,6},{8,9},{9,8},{10,11... | collective-permute-start | bytes 1966088 | tf_op jit(solution)/shard_map/ppermute | solution.py:262
  84.4 5.0 %collective-permute-start.19 = (f32[2,64,1280]{2,1,0:T(8,128)S(1)}, f32[2,64,1280]{2,1,0:T(8,128)S(1)}, u32[]{:S(2)}, u32[]{:S(2)}) collective-permute-start(f32[2,64,1280]{2,1,0:T(8,128)S(1)} %pad_maximum_fusion.2), channel_id=1, source_target_pairs={{0,1},{1,0},{2,3},{3,2},{4,5},{5,4},{6,7},{7,6},{8,9},{9,8},{10,11... | collective-permute-start | bytes 1966088 | tf_op jit(solution)/shard_map/ppermute | solution.py:262
  86.4 3.7 %collective-permute-start.17 = (f32[2,64,1280]{2,1,0:T(8,128)S(1)}, f32[2,64,1280]{2,1,0:T(8,128)S(1)}, u32[]{:S(2)}, u32[]{:S(2)}) collective-permute-start(f32[2,64,1280]{2,1,0:T(8,128)S(1)} %pad_maximum_fusion.1), channel_id=1, source_target_pairs={{0,1},{1,0},{2,3},{3,2},{4,5},{5,4},{6,7},{7,6},{8,9},{9,8},{10,11... | collective-permute-start | bytes 1966088 | tf_op jit(solution)/shard_map/ppermute | solution.py:262
  87.1 10.6 %collective-permute-start.24 = (f32[1,64,1280]{2,1,0:T(8,128)S(1)}, f32[1,64,1280]{2,1,0:T(8,128)S(1)}, u32[]{:S(2)}, u32[]{:S(2)}) collective-permute-start(f32[1,64,1280]{2,1,0:T(8,128)S(1)} %get-tuple-element.21), channel_id=1, source_target_pairs={{0,2},{1,3},{2,0},{3,1},{4,6},{5,7},{6,4},{7,5},{8,10},{9,11},{10,... | collective-permute-start | bytes 983048 | tf_op jit(solution)/shard_map/ppermute | solution.py:262
  87.8 16.9 %collective-permute-start.22 = (f32[1,64,1280]{2,1,0:T(8,128)S(1)}, f32[1,64,1280]{2,1,0:T(8,128)S(1)}, u32[]{:S(2)}, u32[]{:S(2)}) collective-permute-start(f32[1,64,1280]{2,1,0:T(8,128)S(1)} %get-tuple-element.18), channel_id=1, source_target_pairs={{0,2},{1,3},{2,0},{3,1},{4,6},{5,7},{6,4},{7,5},{8,10},{9,11},{10,... | collective-permute-start | bytes 983048 | tf_op jit(solution)/shard_map/ppermute | solution.py:262
  89.5 22.3 %collective-permute-start.20 = (f32[1,64,1280]{2,1,0:T(8,128)S(1)}, f32[1,64,1280]{2,1,0:T(8,128)S(1)}, u32[]{:S(2)}, u32[]{:S(2)}) collective-permute-start(f32[1,64,1280]{2,1,0:T(8,128)S(1)} %get-tuple-element.15), channel_id=1, source_target_pairs={{0,2},{1,3},{2,0},{3,1},{4,6},{5,7},{6,4},{7,5},{8,10},{9,11},{10,... | collective-permute-start | bytes 983048 | tf_op jit(solution)/shard_map/ppermute | solution.py:262
  90.3 27.6 %collective-permute-start.18 = (f32[1,64,1280]{2,1,0:T(8,128)S(1)}, f32[1,64,1280]{2,1,0:T(8,128)S(1)}, u32[]{:S(2)}, u32[]{:S(2)}) collective-permute-start(f32[1,64,1280]{2,1,0:T(8,128)S(1)} %get-tuple-element.12), channel_id=1, source_target_pairs={{0,2},{1,3},{2,0},{3,1},{4,6},{5,7},{6,4},{7,5},{8,10},{9,11},{10,... | collective-permute-start | bytes 983048 | tf_op jit(solution)/shard_map/ppermute | solution.py:262

commit v15 on v10

--- a/solution.py
+++ b/solution.py
@@ -111,21 +111,21 @@
         query_matrix = (
             jnp.dot(normalized_input, w_query, preferred_element_type=jnp.float32) + q_bias
         )
-        key_rows = (
-            jnp.dot(normalized_input, key_projection_weight, preferred_element_type=jnp.float32)
-            + key_bias_vector
-        )
-        query_matrix, key_rows = lax.optimization_barrier((query_matrix, key_rows))
+        key_value = jnp.dot(
+            normalized_input,
+            jnp.concatenate([key_projection_weight, value_projection_weight], axis=1),
+            preferred_element_type=jnp.float32,
+        ) + jnp.concatenate([key_bias_vector, value_bias_vector])
+        kv_cols = key_projection_weight.shape[1]
+        query_matrix, key_value = lax.optimization_barrier((query_matrix, key_value))
+        key_rows = key_value[:, :kv_cols]
         query_matrix = apply_rotary(
             query_matrix.reshape(count, local_heads, head_dim), starts, head_dim
         ).astype(jnp.bfloat16)
         key_rows = apply_rotary(
             key_rows.reshape(count, local_kv, head_dim), starts, head_dim
         ).astype(jnp.bfloat16)
-        value_rows = (
-            jnp.dot(normalized_input, value_projection_weight, preferred_element_type=jnp.float32)
-            + value_bias_vector
-        ).astype(jnp.bfloat16)
+        value_rows = key_value[:, kv_cols:].astype(jnp.bfloat16)
         return jnp.concatenate(
             [
                 query_matrix.reshape(count, local_heads * head_dim),

time: 112 us -> 109 us (0.973)
  other arithmetic: 18.4 us -> 12.5 us
  starting transfers between devices: 32.2 us -> 34.2 us
  matrix products: 19.5 us -> 21.3 us
  waiting for transfers between devices: 33.6 us -> 31.9 us
    convert_element_type x1 -> x0, other arithmetic: 4.47 us -> none  [project(): normalized_input = (values_wide * lax.rsqrt(jnp.mean(values_wide * values...]
    dot_general x1, matrix products: 3.28 us -> 7.56 us  [project(): jnp.dot(normalized_input, w_query, preferred_element_type=jnp.float32)]
    dot_general x2 -> x1, matrix products: 4.98 us -> 2.49 us  [project(): jnp.dot(normalized_input, jnp.concatenate([key_projection_weight, value_p...]
    ppermute x7, waiting for transfers between devices: 5.65 us -> 3.61 us  [exchange(): arrived.append(lax.ppermute(chunks[shift], axis_name, pairs))]
    concatenate x2, local copies, waits for them, and re-layouts: 1.42 us -> 0.2 us  [apply_rotary(): jnp.concatenate([first_half * cosine - second_half * sine_table, second_h...]
    optimization_barrier x1, local copies, waits for them, and re-layouts: 0.33 us -> 1.54 us  [project(): lax.optimization_barrier((query_matrix, key_value))]
where the time goes in v15:
time: 109 us; the launch traced here: 107 us
  starting transfers between devices  34.2 us (31%)
  waiting for transfers between devices  31.9 us (29%)
  matrix products  21.3 us (20%)
  other arithmetic  12.5 us (11%)
  local copies, waits for them, and re-layouts  6.64 us (6%)
    ppermute x8, waiting for transfers between devices, halving_scatter(): got = lax.ppermute(send, axis_name, pairs)  26.2 us
    ppermute x7, starting transfers between devices, shift_gather(): lax.ppermute(part, axis_name, [(i, (i + shift) % count) for i in range(co...  12.5 us
    ppermute x7, starting transfers between devices, exchange(): arrived.append(lax.ppermute(chunks[shift], axis_name, pairs))  12.1 us
    dot_general x4, matrix products, local(): jnp.dot(mixed_heads, w_out, preferred_element_type=jnp.float32)  8.08 us
    dot_general x1, matrix products, project(): jnp.dot(normalized_input, w_query, preferred_element_type=jnp.float32)  7.56 us
    ppermute x8, starting transfers between devices, halving_scatter(): got = lax.ppermute(send, axis_name, pairs)  6.54 us
    ppermute x7, waiting for transfers between devices, exchange(): arrived.append(lax.ppermute(chunks[shift], axis_name, pairs))  3.61 us
    ppermute x3, starting transfers between devices, xor_gather(): pieces = pieces + [lax.ppermute(p, axis_name, pairs) for p in pieces]  3.01 us
  transfers between devices with their start and end apart: 25, of which 9 were waited for; matrix products, arithmetic and copies ran while one was open for 17% of the time, Pallas kernels for 0%

profile of v15, /device:TPU:0, one launch (start us, length us, event | category | flops | bytes accessed | tf_op | source)
XLA Modules:
  0.0 107.1 jit_solution(9807346908216237544)
XLA Ops:
  0.0 3.0 %collective-permute-start = (bf16[96,5120]{1,0:T(8,128)(2,1)}, bf16[96,5120]{1,0:T(8,128)(2,1)S(1)}, u32[]{:S(2)}, u32[]{:S(2)}) collective-permute-start(bf16[96,5120]{1,0:T(8,128)(2,1)} %param.14), channel_id=1, source_target_pairs={{0,2},{1,3},{2,0},{3,1},{4,6},{5,7},{6,4},{7,5},{8,10},{9,11},{10,... | collective-permute-start | bytes 2949128 | tf_op jit(solution)/shard_map/ppermute | solution.py:286
  3.0 1.5 %collective-permute-start.3 = (s32[1,8]{1,0:T(1,128)}, s32[1,8]{1,0:T(1,128)S(1)}, u32[]{:S(2)}, u32[]{:S(2)}) collective-permute-start(s32[1,8]{1,0:T(1,128)} %param.16), channel_id=1, source_target_pairs={{0,4},{4,8},{8,12},{12,16},{16,20},{20,24},{24,28},{28,0},{1,5},{5... | collective-permute-start | bytes 104 | tf_op jit(solution)/shard_map/ppermute | solution.py:223
  4.5 1.6 %collective-permute-start.4 = (s32[1,8]{1,0:T(1,128)}, s32[1,8]{1,0:T(1,128)S(1)}, u32[]{:S(2)}, u32[]{:S(2)}) collective-permute-start(s32[1,8]{1,0:T(1,128)} %param.16), channel_id=1, source_target_pairs={{0,8},{4,12},{8,16},{12,20},{16,24},{20,28},{24,0},{28,4},{1,9},{5... | collective-permute-start | bytes 104 | tf_op jit(solution)/shard_map/ppermute | solution.py:223
  6.1 2.5 %collective-permute-start.5 = (s32[1,8]{1,0:T(1,128)}, s32[1,8]{1,0:T(1,128)S(1)}, u32[]{:S(2)}, u32[]{:S(2)}) collective-permute-start(s32[1,8]{1,0:T(1,128)} %param.16), channel_id=1, source_target_pairs={{0,12},{4,16},{8,20},{12,24},{16,28},{20,0},{24,4},{28,8},{1,13},{... | collective-permute-start | bytes 104 | tf_op jit(solution)/shard_map/ppermute | solution.py:223
  8.7 0.7 constant_dynamic-update-slice_fusion.7
  9.4 0.7 reshape.874
  10.3 0.8 reduce-window.32
  11.4 0.9 reduce-window.30
  12.2 0.2 slice_reduce_fusion
  12.7 0.7 compare_and_fusion.4
  13.4 0.6 gather_fusion.2
  13.9 0.6 gather_fusion.1
  14.8 0.7 subtract_select_fusion
  15.6 0.9 reduce-window.21
  16.5 0.2 slice_reduce_fusion.1
  16.9 0.7 pad_maximum_fusion.7
  18.0 1.3 %collective-permute-start.6 = (s32[1,8]{1,0:T(1,128)}, s32[1,8]{1,0:T(1,128)S(1)}, u32[]{:S(2)}, u32[]{:S(2)}) collective-permute-start(s32[1,8]{1,0:T(1,128)} %param.16), channel_id=1, source_target_pairs={{0,16},{4,20},{8,24},{12,28},{16,0},{20,4},{24,8},{28,12},{1,17},{... | collective-permute-start | bytes 104 | tf_op jit(solution)/shard_map/ppermute | solution.py:223
  19.3 2.6 %collective-permute-start.7 = (s32[1,8]{1,0:T(1,128)}, s32[1,8]{1,0:T(1,128)S(1)}, u32[]{:S(2)}, u32[]{:S(2)}) collective-permute-start(s32[1,8]{1,0:T(1,128)} %param.16), channel_id=1, source_target_pairs={{0,20},{4,24},{8,28},{12,0},{16,4},{20,8},{24,12},{28,16},{1,21},{... | collective-permute-start | bytes 104 | tf_op jit(solution)/shard_map/ppermute | solution.py:223
  22.0 1.3 %collective-permute-start.8 = (s32[1,8]{1,0:T(1,128)}, s32[1,8]{1,0:T(1,128)S(1)}, u32[]{:S(2)}, u32[]{:S(2)}) collective-permute-start(s32[1,8]{1,0:T(1,128)} %param.16), channel_id=1, source_target_pairs={{0,24},{4,28},{8,0},{12,4},{16,8},{20,12},{24,16},{28,20},{1,25},{... | collective-permute-start | bytes 104 | tf_op jit(solution)/shard_map/ppermute | solution.py:223
  23.3 1.6 %collective-permute-start.9 = (s32[1,8]{1,0:T(1,128)}, s32[1,8]{1,0:T(1,128)S(1)}, u32[]{:S(2)}, u32[]{:S(2)}) collective-permute-start(s32[1,8]{1,0:T(1,128)} %param.16), channel_id=1, source_target_pairs={{0,28},{4,0},{8,4},{12,8},{16,12},{20,16},{24,20},{28,24},{1,29},{... | collective-permute-start | bytes 104 | tf_op jit(solution)/shard_map/ppermute | solution.py:223
  25.0 0.7 collective-permute-done.8
  25.7 1.3 %collective-permute-done.9 = s32[1,8]{1,0:T(1,128)S(1)} collective-permute-done((s32[1,8]{1,0:T(1,128)}, s32[1,8]{1,0:T(1,128)S(1)}, u32[]{:S(2)}, u32[]{:S(2)}) %collective-permute-start.9) | collective-permute-done | bytes 64 | tf_op jit(solution)/shard_map/ppermute | solution.py:223
  27.0 0.6 gather_fusion
  27.9 0.4 multiply_cosine_fusion.1
  28.4 2.1 %fusion = f32[384]{0:T(512)S(1)} fusion(bf16[96,5120]{1,0:T(8,128)(2,1)} %collective-permute-done.2, bf16[96,5120]{1,0:T(8,128)(2,1)S(1)} %collective-permute-done.1, bf16[96,5120]{1,0:T(8,128)(2,1)S(1)} %collective-permute-done, bf16[96,5120]{1,0:T(8,128)(2,1)} %param.14), kind=kLoop, calls=%fused_computation.5 | loop fusion | flops 19660416 | bytes 3933696 | tf_op jit(solution)/shard_map/reduce_sum | solution.py:108
  30.6 7.6 %convolution_add_fusion = f32[384,640]{1,0:T(8,128)} fusion(bf16[5120,640]{1,0:T(8,128)(2,1)} %param.18, f32[5120]{0:T(1024)S(1)} %copy-done.3, f32[384]{0:T(512)S(1)} %add_rsqrt_fusion, f32[640]{0:T(1024)S(1)} %copy-done.4, bf16[96,5120]{1,0:T(8,128)(2,1)} %collective-permute-done.2, bf16[96,5120]{1,0:T(8,128)(2,1)S(1)} %collective-permute-done.1, ...), kind=kOutput, calls=%fused_computation.16 | convolution fusion | flops 2538455040 | bytes 11493376 | tf_op jit(solution)/shard_map/dot_general | solution.py:112
  38.1 2.5 %fusion.7 = f32[384,256]{1,0:T(8,128)S(1)} fusion(bf16[5120,128]{1,0:T(8,128)(2,1)S(1)} %copy-done.1, bf16[5120,128]{1,0:T(8,128)(2,1)S(1)} %copy-done.2, f32[5120]{0:T(1024)S(1)} %copy-done.3, f32[384]{0:T(512)S(1)} %add_rsqrt_fusion, f32[256]{0:T(256)S(1)} %pad_maximum_fusion.7, bf16[96,5120]{1,0:T(8,128)(2,1)} %collective-permute-done.2, ...), kind=kOutput, calls=%fused_computation.18 | convolution fusion | flops 1033601024 | bytes 6969856 | tf_op jit(solution)/shard_map/dot_general | solution.py:114
  40.8 0.8 fusion.60
  41.8 1.5 %copy.35 = f32[384,640]{0,1:T(8,128)S(1)} copy(f32[384,640]{1,0:T(8,128)} %convolution_add_fusion) | data formatting | bytes 1966080 | tf_op jit(solution)/shard_map/optimization_barrier | solution.py:120
  43.6 0.6 convolution_convert_fusion
  44.2 1.8 %collective-permute-start.10 = (bf16[48,896]{1,0:T(8,128)(2,1)S(1)}, bf16[48,896]{1,0:T(8,128)(2,1)S(1)}, u32[]{:S(2)}, u32[]{:S(2)}) collective-permute-start(bf16[48,896]{1,0:T(8,128)(2,1)S(1)} %get-tuple-element.44), channel_id=1, source_target_pairs={{0,4},{4,8},{8,12},{12,16},{16,20},{20,24},{24,28},{28,0},{1,5},{5... | collective-permute-start | bytes 258056 | tf_op jit(solution)/shard_map/ppermute | solution.py:239
  46.0 0.4 select_reduce_fusion
  46.4 1.0 collective-permute-start.11
  47.4 2.5 %collective-permute-start.12 = (bf16[48,896]{1,0:T(8,128)(2,1)S(1)}, bf16[48,896]{1,0:T(8,128)(2,1)S(1)}, u32[]{:S(2)}, u32[]{:S(2)}) collective-permute-start(bf16[48,896]{1,0:T(8,128)(2,1)S(1)} %get-tuple-element.42), channel_id=1, source_target_pairs={{0,12},{4,16},{8,20},{12,24},{16,28},{20,0},{24,4},{28,8},{1,13},{... | collective-permute-start | bytes 258056 | tf_op jit(solution)/shard_map/ppermute | solution.py:239
  49.9 1.2 %collective-permute-start.13 = (bf16[48,896]{1,0:T(8,128)(2,1)S(1)}, bf16[48,896]{1,0:T(8,128)(2,1)S(1)}, u32[]{:S(2)}, u32[]{:S(2)}) collective-permute-start(bf16[48,896]{1,0:T(8,128)(2,1)S(1)} %get-tuple-element.41), channel_id=1, source_target_pairs={{0,16},{4,20},{8,24},{12,28},{16,0},{20,4},{24,8},{28,12},{1,17},{... | collective-permute-start | bytes 258056 | tf_op jit(solution)/shard_map/ppermute | solution.py:239
  51.2 2.9 %collective-permute-start.14 = (bf16[48,896]{1,0:T(8,128)(2,1)S(1)}, bf16[48,896]{1,0:T(8,128)(2,1)S(1)}, u32[]{:S(2)}, u32[]{:S(2)}) collective-permute-start(bf16[48,896]{1,0:T(8,128)(2,1)S(1)} %get-tuple-element.40), channel_id=1, source_target_pairs={{0,20},{4,24},{8,28},{12,0},{16,4},{20,8},{24,12},{28,16},{1,21},{... | collective-permute-start | bytes 258056 | tf_op jit(solution)/shard_map/ppermute | solution.py:239
  54.0 1.1 %collective-permute-start.15 = (bf16[48,896]{1,0:T(8,128)(2,1)S(1)}, bf16[48,896]{1,0:T(8,128)(2,1)S(1)}, u32[]{:S(2)}, u32[]{:S(2)}) collective-permute-start(bf16[48,896]{1,0:T(8,128)(2,1)S(1)} %get-tuple-element.39), channel_id=1, source_target_pairs={{0,24},{4,28},{8,0},{12,4},{16,8},{20,12},{24,16},{28,20},{1,25},{... | collective-permute-start | bytes 258056 | tf_op jit(solution)/shard_map/ppermute | solution.py:239
  55.2 1.6 %collective-permute-start.16 = (bf16[48,896]{1,0:T(8,128)(2,1)S(1)}, bf16[48,896]{1,0:T(8,128)(2,1)S(1)}, u32[]{:S(2)}, u32[]{:S(2)}) collective-permute-start(bf16[48,896]{1,0:T(8,128)(2,1)S(1)} %get-tuple-element.38), channel_id=1, source_target_pairs={{0,28},{4,0},{8,4},{12,8},{16,12},{20,16},{24,20},{28,24},{1,29},{... | collective-permute-start | bytes 258056 | tf_op jit(solution)/shard_map/ppermute | solution.py:239
  56.8 2.2 %collective-permute-done.12 = bf16[48,896]{1,0:T(8,128)(2,1)S(1)} collective-permute-done((bf16[48,896]{1,0:T(8,128)(2,1)S(1)}, bf16[48,896]{1,0:T(8,128)(2,1)S(1)}, u32[]{:S(2)}, u32[]{:S(2)}) %collective-permute-start.12) | collective-permute-done | bytes 86048 | tf_op jit(solution)/shard_map/ppermute | solution.py:239
  59.1 1.2 %collective-permute-done.13 = bf16[48,896]{1,0:T(8,128)(2,1)S(1)} collective-permute-done((bf16[48,896]{1,0:T(8,128)(2,1)S(1)}, bf16[48,896]{1,0:T(8,128)(2,1)S(1)}, u32[]{:S(2)}, u32[]{:S(2)}) %collective-permute-start.13) | collective-permute-done | bytes 86048 | tf_op jit(solution)/shard_map/ppermute | solution.py:239
  60.6 0.5 convolution_convert_fusion.1
  61.1 0.3 fusion.139
  61.4 0.2 fusion.45
  61.6 0.3 fusion.21
  61.9 4.3 %fusion.61 = f32[64,5120]{1,0:T(8,128)S(1)} fusion(bf16[640,5120]{1,0:T(8,128)(2,1)} %param.24, bf16[8,8,5,128]{3,2,1,0:T(8,128)(2,1)S(1)} %bitcast.289), kind=kOutput, calls=%fused_computation.127 | convolution fusion | flops 419430400 | bytes 7946240 | tf_op jit(solution)/shard_map/dot_general | solution.py:213
  66.4 0.3 fusion.140
  66.7 0.2 fusion.44
  66.9 0.3 fusion.20
  67.3 1.3 %fusion.64 = f32[64,5120]{1,0:T(8,128)S(1)} fusion(bf16[640,5120]{1,0:T(8,128)(2,1)S(1)} %bitcast.287, bf16[8,8,5,128]{3,2,1,0:T(8,128)(2,1)S(1)} %bitcast.290), kind=kOutput, calls=%fused_computation.130 | convolution fusion | flops 419430400 | bytes 7946240 | tf_op jit(solution)/shard_map/dot_general | solution.py:213
  68.7 0.6 collective-permute-start.21
  69.3 0.3 fusion.141
  69.8 0.3 fusion.23
  70.1 1.3 %fusion.67 = f32[64,5120]{1,0:T(8,128)S(1)} fusion(bf16[640,5120]{1,0:T(8,128)(2,1)S(1)} %bitcast.287, bf16[8,8,5,128]{3,2,1,0:T(8,128)(2,1)S(1)} %bitcast.291), kind=kOutput, calls=%fused_computation.133 | convolution fusion | flops 419430400 | bytes 7946240 | tf_op jit(solution)/shard_map/dot_general | solution.py:213
  71.6 0.2 fusion.142
  71.8 0.2 fusion.22
  72.2 1.3 %fusion.70 = f32[64,5120]{1,0:T(8,128)S(1)} fusion(bf16[640,5120]{1,0:T(8,128)(2,1)S(1)} %bitcast.287, bf16[8,8,5,128]{3,2,1,0:T(8,128)(2,1)S(1)} %bitcast.292), kind=kOutput, calls=%fused_computation.136 | convolution fusion | flops 419430400 | bytes 7946240 | tf_op jit(solution)/shard_map/dot_general | solution.py:213
  73.6 0.6 collective-permute-start.17
  74.2 3.0 %collective-permute-start.24 = (f32[1,64,1280]{2,1,0:T(8,128)S(1)}, f32[1,64,1280]{2,1,0:T(8,128)S(1)}, u32[]{:S(2)}, u32[]{:S(2)}) collective-permute-start(f32[1,64,1280]{2,1,0:T(8,128)S(1)} %get-tuple-element.21), channel_id=1, source_target_pairs={{0,2},{1,3},{2,0},{3,1},{4,6},{5,7},{6,4},{7,5},{8,10},{9,11},{10,... | collective-permute-start | bytes 983048 | tf_op jit(solution)/shard_map/ppermute | solution.py:257
  77.5 2.1 %collective-permute-start.20 = (f32[1,64,1280]{2,1,0:T(8,128)S(1)}, f32[1,64,1280]{2,1,0:T(8,128)S(1)}, u32[]{:S(2)}, u32[]{:S(2)}) collective-permute-start(f32[1,64,1280]{2,1,0:T(8,128)S(1)} %get-tuple-element.15), channel_id=1, source_target_pairs={{0,2},{1,3},{2,0},{3,1},{4,6},{5,7},{6,4},{7,5},{8,10},{9,11},{10,... | collective-permute-start | bytes 983048 | tf_op jit(solution)/shard_map/ppermute | solution.py:257
  79.9 5.9 %collective-permute-done.24 = f32[1,64,1280]{2,1,0:T(8,128)S(1)} collective-permute-done((f32[1,64,1280]{2,1,0:T(8,128)S(1)}, f32[1,64,1280]{2,1,0:T(8,128)S(1)}, u32[]{:S(2)}, u32[]{:S(2)}) %collective-permute-start.24) | collective-permute-done | bytes 327712 | tf_op jit(solution)/shard_map/ppermute | solution.py:257
  85.8 7.0 %collective-permute-done.22 = f32[1,64,1280]{2,1,0:T(8,128)S(1)} collective-permute-done((f32[1,64,1280]{2,1,0:T(8,128)S(1)}, f32[1,64,1280]{2,1,0:T(8,128)S(1)}, u32[]{:S(2)}, u32[]{:S(2)}) %collective-permute-start.22) | collective-permute-done | bytes 327712 | tf_op jit(solution)/shard_map/ppermute | solution.py:257
  92.8 7.0 %collective-permute-done.20 = f32[1,64,1280]{2,1,0:T(8,128)S(1)} collective-permute-done((f32[1,64,1280]{2,1,0:T(8,128)S(1)}, f32[1,64,1280]{2,1,0:T(8,128)S(1)}, u32[]{:S(2)}, u32[]{:S(2)}) %collective-permute-start.20) | collective-permute-done | bytes 327712 | tf_op jit(solution)/shard_map/ppermute | solution.py:257
  99.8 6.4 %collective-permute-done.18 = f32[1,64,1280]{2,1,0:T(8,128)S(1)} collective-permute-done((f32[1,64,1280]{2,1,0:T(8,128)S(1)}, f32[1,64,1280]{2,1,0:T(8,128)S(1)}, u32[]{:S(2)}, u32[]{:S(2)}) %collective-permute-start.18) | collective-permute-done | bytes 327712 | tf_op jit(solution)/shard_map/ppermute | solution.py:257
  106.3 0.9 pad_maximum_fusion.5
  (135 shorter events, 4.9 us)
Async XLA Ops:
  0.0 30.5 %copy-start = (bf16[96,5120]{1,0:T(8,128)(2,1)S(1)}, bf16[96,5120]{1,0:T(8,128)(2,1)}, u32[]{:S(2)}) copy-start(bf16[96,5120]{1,0:T(8,128)(2,1)} %param.14) | copy-start | bytes 2949124
  0.0 30.5 %copy-start.3 = (f32[5120]{0:T(1024)S(1)}, f32[5120]{0:T(1024)}, u32[]{:S(2)}) copy-start(f32[5120]{0:T(1024)} %param.17) | copy-start | bytes 61444
  0.0 30.5 %copy-start.4 = (f32[640]{0:T(1024)S(1)}, f32[640]{0:T(1024)}, u32[]{:S(2)}) copy-start(f32[640]{0:T(1024)} %param.19) | copy-start | bytes 7684
  0.0 25.6 %collective-permute-start = (bf16[96,5120]{1,0:T(8,128)(2,1)}, bf16[96,5120]{1,0:T(8,128)(2,1)S(1)}, u32[]{:S(2)}, u32[]{:S(2)}) collective-permute-start(bf16[96,5120]{1,0:T(8,128)(2,1)} %param.14), channel_id=1, source_target_pairs={{0,2},{1,3},{2,0},{3,1},{4,6},{5,7},{6,4},{7,5},{8,10},{9,11},{10,... | collective-permute-start | bytes 2949128 | tf_op jit(solution)/shard_map/ppermute | solution.py:286
  3.0 25.3 %collective-permute-start.1 = (bf16[96,5120]{1,0:T(8,128)(2,1)}, bf16[96,5120]{1,0:T(8,128)(2,1)S(1)}, u32[]{:S(2)}, u32[]{:S(2)}) collective-permute-start(bf16[96,5120]{1,0:T(8,128)(2,1)} %param.14), channel_id=1, source_target_pairs={{0,1},{1,0},{2,3},{3,2},{4,5},{5,4},{6,7},{7,6},{8,9},{9,8},{10,11... | collective-permute-start | bytes 2949128 | tf_op jit(solution)/shard_map/ppermute | solution.py:286
  3.0 15.0 %collective-permute-start.3 = (s32[1,8]{1,0:T(1,128)}, s32[1,8]{1,0:T(1,128)S(1)}, u32[]{:S(2)}, u32[]{:S(2)}) collective-permute-start(s32[1,8]{1,0:T(1,128)} %param.16), channel_id=1, source_target_pairs={{0,4},{4,8},{8,12},{12,16},{16,20},{20,24},{24,28},{28,0},{1,5},{5... | collective-permute-start | bytes 104 | tf_op jit(solution)/shard_map/ppermute | solution.py:223
  4.5 14.8 %collective-permute-start.4 = (s32[1,8]{1,0:T(1,128)}, s32[1,8]{1,0:T(1,128)S(1)}, u32[]{:S(2)}, u32[]{:S(2)}) collective-permute-start(s32[1,8]{1,0:T(1,128)} %param.16), channel_id=1, source_target_pairs={{0,8},{4,12},{8,16},{12,20},{16,24},{20,28},{24,0},{28,4},{1,9},{5... | collective-permute-start | bytes 104 | tf_op jit(solution)/shard_map/ppermute | solution.py:223
  6.1 15.8 %collective-permute-start.5 = (s32[1,8]{1,0:T(1,128)}, s32[1,8]{1,0:T(1,128)S(1)}, u32[]{:S(2)}, u32[]{:S(2)}) collective-permute-start(s32[1,8]{1,0:T(1,128)} %param.16), channel_id=1, source_target_pairs={{0,12},{4,16},{8,20},{12,24},{16,28},{20,0},{24,4},{28,8},{1,13},{... | collective-permute-start | bytes 104 | tf_op jit(solution)/shard_map/ppermute | solution.py:223
  18.0 5.3 %collective-permute-start.6 = (s32[1,8]{1,0:T(1,128)}, s32[1,8]{1,0:T(1,128)S(1)}, u32[]{:S(2)}, u32[]{:S(2)}) collective-permute-start(s32[1,8]{1,0:T(1,128)} %param.16), channel_id=1, source_target_pairs={{0,16},{4,20},{8,24},{12,28},{16,0},{20,4},{24,8},{28,12},{1,17},{... | collective-permute-start | bytes 104 | tf_op jit(solution)/shard_map/ppermute | solution.py:223
  19.3 5.6 %collective-permute-start.7 = (s32[1,8]{1,0:T(1,128)}, s32[1,8]{1,0:T(1,128)S(1)}, u32[]{:S(2)}, u32[]{:S(2)}) collective-permute-start(s32[1,8]{1,0:T(1,128)} %param.16), channel_id=1, source_target_pairs={{0,20},{4,24},{8,28},{12,0},{16,4},{20,8},{24,12},{28,16},{1,21},{... | collective-permute-start | bytes 104 | tf_op jit(solution)/shard_map/ppermute | solution.py:223
  22.0 3.7 %collective-permute-start.8 = (s32[1,8]{1,0:T(1,128)}, s32[1,8]{1,0:T(1,128)S(1)}, u32[]{:S(2)}, u32[]{:S(2)}) collective-permute-start(s32[1,8]{1,0:T(1,128)} %param.16), channel_id=1, source_target_pairs={{0,24},{4,28},{8,0},{12,4},{16,8},{20,12},{24,16},{28,20},{1,25},{... | collective-permute-start | bytes 104 | tf_op jit(solution)/shard_map/ppermute | solution.py:223
  23.3 3.7 %collective-permute-start.9 = (s32[1,8]{1,0:T(1,128)}, s32[1,8]{1,0:T(1,128)S(1)}, u32[]{:S(2)}, u32[]{:S(2)}) collective-permute-start(s32[1,8]{1,0:T(1,128)} %param.16), channel_id=1, source_target_pairs={{0,28},{4,0},{8,4},{12,8},{16,12},{20,16},{24,20},{28,24},{1,29},{... | collective-permute-start | bytes 104 | tf_op jit(solution)/shard_map/ppermute | solution.py:223
  25.6 2.7 %collective-permute-start.2 = (bf16[96,5120]{1,0:T(8,128)(2,1)S(1)}, bf16[96,5120]{1,0:T(8,128)(2,1)}, u32[]{:S(2)}, u32[]{:S(2)}) collective-permute-start(bf16[96,5120]{1,0:T(8,128)(2,1)S(1)} %collective-permute-done), channel_id=1, source_target_pairs={{0,1},{1,0},{2,3},{3,2},{4,5},{5,4},{6,7},{7,6},{8,9},{9,8},{10,11... | collective-permute-start | bytes 2949128 | tf_op jit(solution)/shard_map/ppermute | solution.py:286
  30.5 7.6 %copy-start.1 = (bf16[5120,128]{1,0:T(8,128)(2,1)S(1)}, bf16[5120,128]{1,0:T(8,128)(2,1)}, u32[]{:S(2)}) copy-start(bf16[5120,128]{1,0:T(8,128)(2,1)} %param.22) | copy-start | bytes 3932164
  30.5 7.6 %copy-start.2 = (bf16[5120,128]{1,0:T(8,128)(2,1)S(1)}, bf16[5120,128]{1,0:T(8,128)(2,1)}, u32[]{:S(2)}) copy-start(bf16[5120,128]{1,0:T(8,128)(2,1)} %param.20) | copy-start | bytes 3932164
  44.2 9.8 %collective-permute-start.10 = (bf16[48,896]{1,0:T(8,128)(2,1)S(1)}, bf16[48,896]{1,0:T(8,128)(2,1)S(1)}, u32[]{:S(2)}, u32[]{:S(2)}) collective-permute-start(bf16[48,896]{1,0:T(8,128)(2,1)S(1)} %get-tuple-element.44), channel_id=1, source_target_pairs={{0,4},{4,8},{8,12},{12,16},{16,20},{20,24},{24,28},{28,0},{1,5},{5... | collective-permute-start | bytes 258056 | tf_op jit(solution)/shard_map/ppermute | solution.py:239
  46.4 8.8 %collective-permute-start.11 = (bf16[48,896]{1,0:T(8,128)(2,1)S(1)}, bf16[48,896]{1,0:T(8,128)(2,1)S(1)}, u32[]{:S(2)}, u32[]{:S(2)}) collective-permute-start(bf16[48,896]{1,0:T(8,128)(2,1)S(1)} %get-tuple-element.43), channel_id=1, source_target_pairs={{0,8},{4,12},{8,16},{12,20},{16,24},{20,28},{24,0},{28,4},{1,9},{5... | collective-permute-start | bytes 258056 | tf_op jit(solution)/shard_map/ppermute | solution.py:239
  47.4 11.7 %collective-permute-start.12 = (bf16[48,896]{1,0:T(8,128)(2,1)S(1)}, bf16[48,896]{1,0:T(8,128)(2,1)S(1)}, u32[]{:S(2)}, u32[]{:S(2)}) collective-permute-start(bf16[48,896]{1,0:T(8,128)(2,1)S(1)} %get-tuple-element.42), channel_id=1, source_target_pairs={{0,12},{4,16},{8,20},{12,24},{16,28},{20,0},{24,4},{28,8},{1,13},{... | collective-permute-start | bytes 258056 | tf_op jit(solution)/shard_map/ppermute | solution.py:239
  49.9 10.4 %collective-permute-start.13 = (bf16[48,896]{1,0:T(8,128)(2,1)S(1)}, bf16[48,896]{1,0:T(8,128)(2,1)S(1)}, u32[]{:S(2)}, u32[]{:S(2)}) collective-permute-start(bf16[48,896]{1,0:T(8,128)(2,1)S(1)} %get-tuple-element.41), channel_id=1, source_target_pairs={{0,16},{4,20},{8,24},{12,28},{16,0},{20,4},{24,8},{28,12},{1,17},{... | collective-permute-start | bytes 258056 | tf_op jit(solution)/shard_map/ppermute | solution.py:239
  51.2 9.2 %collective-permute-start.14 = (bf16[48,896]{1,0:T(8,128)(2,1)S(1)}, bf16[48,896]{1,0:T(8,128)(2,1)S(1)}, u32[]{:S(2)}, u32[]{:S(2)}) collective-permute-start(bf16[48,896]{1,0:T(8,128)(2,1)S(1)} %get-tuple-element.40), channel_id=1, source_target_pairs={{0,20},{4,24},{8,28},{12,0},{16,4},{20,8},{24,12},{28,16},{1,21},{... | collective-permute-start | bytes 258056 | tf_op jit(solution)/shard_map/ppermute | solution.py:239
  54.0 6.4 %collective-permute-start.15 = (bf16[48,896]{1,0:T(8,128)(2,1)S(1)}, bf16[48,896]{1,0:T(8,128)(2,1)S(1)}, u32[]{:S(2)}, u32[]{:S(2)}) collective-permute-start(bf16[48,896]{1,0:T(8,128)(2,1)S(1)} %get-tuple-element.39), channel_id=1, source_target_pairs={{0,24},{4,28},{8,0},{12,4},{16,8},{20,12},{24,16},{28,20},{1,25},{... | collective-permute-start | bytes 258056 | tf_op jit(solution)/shard_map/ppermute | solution.py:239
  55.2 5.3 %collective-permute-start.16 = (bf16[48,896]{1,0:T(8,128)(2,1)S(1)}, bf16[48,896]{1,0:T(8,128)(2,1)S(1)}, u32[]{:S(2)}, u32[]{:S(2)}) collective-permute-start(bf16[48,896]{1,0:T(8,128)(2,1)S(1)} %get-tuple-element.38), channel_id=1, source_target_pairs={{0,28},{4,0},{8,4},{12,8},{16,12},{20,16},{24,20},{28,24},{1,29},{... | collective-permute-start | bytes 258056 | tf_op jit(solution)/shard_map/ppermute | solution.py:239
  61.9 5.4 %slice-start = ((s8[6553600]{0:T(1024)(128)(4,1)}), s8[4194304]{0:T(1024)(128)(4,1)S(1)}, s32[]{:S(2)}) async-start(s8[6553600]{0:T(1024)(128)(4,1)} %bitcast.286), calls=%async_computation | async-start | bytes 8388608
  61.9 5.4 %slice-start.1 = ((s8[6553600]{0:T(1024)(128)(4,1)}), s8[2359296]{0:T(1024)(128)(4,1)S(1)}, s32[]{:S(2)}) async-start(s8[6553600]{0:T(1024)(128)(4,1)} %bitcast.286), calls=%async_computation.1 | async-start | bytes 4718592
  66.3 7.8 %collective-permute-start.23 = (f32[2,64,1280]{2,1,0:T(8,128)S(1)}, f32[2,64,1280]{2,1,0:T(8,128)S(1)}, u32[]{:S(2)}, u32[]{:S(2)}) collective-permute-start(f32[2,64,1280]{2,1,0:T(8,128)S(1)} %pad_maximum_fusion.4), channel_id=1, source_target_pairs={{0,1},{1,0},{2,3},{3,2},{4,5},{5,4},{6,7},{7,6},{8,9},{9,8},{10,11... | collective-permute-start | bytes 1966088 | tf_op jit(solution)/shard_map/ppermute | solution.py:257
  68.7 8.5 %collective-permute-start.21 = (f32[2,64,1280]{2,1,0:T(8,128)S(1)}, f32[2,64,1280]{2,1,0:T(8,128)S(1)}, u32[]{:S(2)}, u32[]{:S(2)}) collective-permute-start(f32[2,64,1280]{2,1,0:T(8,128)S(1)} %pad_maximum_fusion.3), channel_id=1, source_target_pairs={{0,1},{1,0},{2,3},{3,2},{4,5},{5,4},{6,7},{7,6},{8,9},{9,8},{10,11... | collective-permute-start | bytes 1966088 | tf_op jit(solution)/shard_map/ppermute | solution.py:257
  71.5 5.9 %collective-permute-start.19 = (f32[2,64,1280]{2,1,0:T(8,128)S(1)}, f32[2,64,1280]{2,1,0:T(8,128)S(1)}, u32[]{:S(2)}, u32[]{:S(2)}) collective-permute-start(f32[2,64,1280]{2,1,0:T(8,128)S(1)} %pad_maximum_fusion.2), channel_id=1, source_target_pairs={{0,1},{1,0},{2,3},{3,2},{4,5},{5,4},{6,7},{7,6},{8,9},{9,8},{10,11... | collective-permute-start | bytes 1966088 | tf_op jit(solution)/shard_map/ppermute | solution.py:257
  73.6 6.1 %collective-permute-start.17 = (f32[2,64,1280]{2,1,0:T(8,128)S(1)}, f32[2,64,1280]{2,1,0:T(8,128)S(1)}, u32[]{:S(2)}, u32[]{:S(2)}) collective-permute-start(f32[2,64,1280]{2,1,0:T(8,128)S(1)} %pad_maximum_fusion.1), channel_id=1, source_target_pairs={{0,1},{1,0},{2,3},{3,2},{4,5},{5,4},{6,7},{7,6},{8,9},{9,8},{10,11... | collective-permute-start | bytes 1966088 | tf_op jit(solution)/shard_map/ppermute | solution.py:257
  74.2 11.5 %collective-permute-start.24 = (f32[1,64,1280]{2,1,0:T(8,128)S(1)}, f32[1,64,1280]{2,1,0:T(8,128)S(1)}, u32[]{:S(2)}, u32[]{:S(2)}) collective-permute-start(f32[1,64,1280]{2,1,0:T(8,128)S(1)} %get-tuple-element.21), channel_id=1, source_target_pairs={{0,2},{1,3},{2,0},{3,1},{4,6},{5,7},{6,4},{7,5},{8,10},{9,11},{10,... | collective-permute-start | bytes 983048 | tf_op jit(solution)/shard_map/ppermute | solution.py:257
  77.3 15.4 %collective-permute-start.22 = (f32[1,64,1280]{2,1,0:T(8,128)S(1)}, f32[1,64,1280]{2,1,0:T(8,128)S(1)}, u32[]{:S(2)}, u32[]{:S(2)}) collective-permute-start(f32[1,64,1280]{2,1,0:T(8,128)S(1)} %get-tuple-element.18), channel_id=1, source_target_pairs={{0,2},{1,3},{2,0},{3,1},{4,6},{5,7},{6,4},{7,5},{8,10},{9,11},{10,... | collective-permute-start | bytes 983048 | tf_op jit(solution)/shard_map/ppermute | solution.py:257
  77.5 22.2 %collective-permute-start.20 = (f32[1,64,1280]{2,1,0:T(8,128)S(1)}, f32[1,64,1280]{2,1,0:T(8,128)S(1)}, u32[]{:S(2)}, u32[]{:S(2)}) collective-permute-start(f32[1,64,1280]{2,1,0:T(8,128)S(1)} %get-tuple-element.15), channel_id=1, source_target_pairs={{0,2},{1,3},{2,0},{3,1},{4,6},{5,7},{6,4},{7,5},{8,10},{9,11},{10,... | collective-permute-start | bytes 983048 | tf_op jit(solution)/shard_map/ppermute | solution.py:257
  79.8 26.4 %collective-permute-start.18 = (f32[1,64,1280]{2,1,0:T(8,128)S(1)}, f32[1,64,1280]{2,1,0:T(8,128)S(1)}, u32[]{:S(2)}, u32[]{:S(2)}) collective-permute-start(f32[1,64,1280]{2,1,0:T(8,128)S(1)} %get-tuple-element.12), channel_id=1, source_target_pairs={{0,2},{1,3},{2,0},{3,1},{4,6},{5,7},{6,4},{7,5},{8,10},{9,11},{10,... | collective-permute-start | bytes 983048 | tf_op jit(solution)/shard_map/ppermute | solution.py:257

commit v16 on v15

--- a/solution.py
+++ b/solution.py
@@ -181,7 +181,7 @@
     segment = jnp.sum((own_ends[None, :] <= slot_ids[:, None]).astype(jnp.int32), axis=1)
 
     score_scale = 1.0 / math.sqrt(head_dim)
-    chunk_count = 4 if pack_len % 32 == 0 else 1
+    chunk_count = 8 if pack_len % 64 == 0 else 1
     chunk_len = pack_len // chunk_count
     results = []
     for chunk in range(chunk_count):

time: 109 us -> 116 us (1.064)
  matrix products: 21.3 us -> 26.6 us
  starting transfers between devices: 34.2 us -> 37.4 us
  waiting for transfers between devices: 31.9 us -> 30 us
    dot_general x4 -> x8, matrix products: 8.08 us -> 12.9 us  [local(): jnp.dot(mixed_heads, w_out, preferred_element_type=jnp.float32)]
    ppermute x8 -> x16, starting transfers between devices: 6.54 us -> 10.5 us  [halving_scatter(): got = lax.ppermute(send, axis_name, pairs)]
    ppermute x8 -> x16, waiting for transfers between devices: 26.2 us -> 22.2 us  [halving_scatter(): got = lax.ppermute(send, axis_name, pairs)]
    ppermute x7, waiting for transfers between devices: 3.61 us -> 5.67 us  [exchange(): arrived.append(lax.ppermute(chunks[shift], axis_name, pairs))]
    dot_general x1, matrix products: 2.49 us -> 1.28 us  [project(): jnp.dot(normalized_input, jnp.concatenate([key_projection_weight, value_p...]
  transfers between devices with their start and end apart: 25 -> 33, of which waited for: 9 -> 13; matrix products, arithmetic and copies ran while one was open for 17% -> 23% of each run, Pallas kernels for 0% -> 0%
where the time goes in v16:
time: 116 us; the launch traced here: 115 us
  starting transfers between devices  37.4 us (32%)
  waiting for transfers between devices  30 us (26%)
  matrix products  26.6 us (23%)
  other arithmetic  13.1 us (11%)
  local copies, waits for them, and re-layouts  6.9 us (6%)
    ppermute x16, waiting for transfers between devices, halving_scatter(): got = lax.ppermute(send, axis_name, pairs)  22.2 us
    dot_general x8, matrix products, local(): jnp.dot(mixed_heads, w_out, preferred_element_type=jnp.float32)  12.9 us
    ppermute x7, starting transfers between devices, shift_gather(): lax.ppermute(part, axis_name, [(i, (i + shift) % count) for i in range(co...  12.5 us
    ppermute x7, starting transfers between devices, exchange(): arrived.append(lax.ppermute(chunks[shift], axis_name, pairs))  11.4 us
    ppermute x16, starting transfers between devices, halving_scatter(): got = lax.ppermute(send, axis_name, pairs)  10.5 us
    dot_general x1, matrix products, project(): jnp.dot(normalized_input, w_query, preferred_element_type=jnp.float32)  7.59 us
    ppermute x7, waiting for transfers between devices, exchange(): arrived.append(lax.ppermute(chunks[shift], axis_name, pairs))  5.67 us
    ppermute x3, starting transfers between devices, xor_gather(): pieces = pieces + [lax.ppermute(p, axis_name, pairs) for p in pieces]  2.94 us
  transfers between devices with their start and end apart: 33, of which 13 were waited for; matrix products, arithmetic and copies ran while one was open for 23% of the time, Pallas kernels for 0%

profile of v16, /device:TPU:0, one launch (start us, length us, event | category | flops | bytes accessed | tf_op | source)
XLA Modules:
  0.0 114.8 jit_solution(13178962366935157634)
XLA Ops:
  0.0 2.9 %collective-permute-start = (bf16[96,5120]{1,0:T(8,128)(2,1)}, bf16[96,5120]{1,0:T(8,128)(2,1)S(1)}, u32[]{:S(2)}, u32[]{:S(2)}) collective-permute-start(bf16[96,5120]{1,0:T(8,128)(2,1)} %param.14), channel_id=1, source_target_pairs={{0,2},{1,3},{2,0},{3,1},{4,6},{5,7},{6,4},{7,5},{8,10},{9,11},{10,... | collective-permute-start | bytes 2949128 | tf_op jit(solution)/shard_map/ppermute | solution.py:286
  2.9 1.5 %collective-permute-start.3 = (s32[1,8]{1,0:T(1,128)}, s32[1,8]{1,0:T(1,128)S(1)}, u32[]{:S(2)}, u32[]{:S(2)}) collective-permute-start(s32[1,8]{1,0:T(1,128)} %param.16), channel_id=1, source_target_pairs={{0,4},{4,8},{8,12},{12,16},{16,20},{20,24},{24,28},{28,0},{1,5},{5... | collective-permute-start | bytes 104 | tf_op jit(solution)/shard_map/ppermute | solution.py:223
  4.5 1.6 %collective-permute-start.4 = (s32[1,8]{1,0:T(1,128)}, s32[1,8]{1,0:T(1,128)S(1)}, u32[]{:S(2)}, u32[]{:S(2)}) collective-permute-start(s32[1,8]{1,0:T(1,128)} %param.16), channel_id=1, source_target_pairs={{0,8},{4,12},{8,16},{12,20},{16,24},{20,28},{24,0},{28,4},{1,9},{5... | collective-permute-start | bytes 104 | tf_op jit(solution)/shard_map/ppermute | solution.py:223
  6.0 2.5 %collective-permute-start.5 = (s32[1,8]{1,0:T(1,128)}, s32[1,8]{1,0:T(1,128)S(1)}, u32[]{:S(2)}, u32[]{:S(2)}) collective-permute-start(s32[1,8]{1,0:T(1,128)} %param.16), channel_id=1, source_target_pairs={{0,12},{4,16},{8,20},{12,24},{16,28},{20,0},{24,4},{28,8},{1,13},{... | collective-permute-start | bytes 104 | tf_op jit(solution)/shard_map/ppermute | solution.py:223
  8.6 0.7 constant_dynamic-update-slice_fusion.7
  9.3 0.7 reshape.1230
  10.2 0.8 reduce-window.32
  11.4 0.9 reduce-window.30
  12.7 0.7 compare_and_fusion.8
  13.5 0.6 gather_fusion.2
  14.0 0.6 gather_fusion.1
  14.9 0.7 subtract_select_fusion
  15.7 0.9 reduce-window.21
  17.2 0.7 pad_maximum_fusion.10
  18.5 1.3 %collective-permute-start.6 = (s32[1,8]{1,0:T(1,128)}, s32[1,8]{1,0:T(1,128)S(1)}, u32[]{:S(2)}, u32[]{:S(2)}) collective-permute-start(s32[1,8]{1,0:T(1,128)} %param.16), channel_id=1, source_target_pairs={{0,16},{4,20},{8,24},{12,28},{16,0},{20,4},{24,8},{28,12},{1,17},{... | collective-permute-start | bytes 104 | tf_op jit(solution)/shard_map/ppermute | solution.py:223
  19.9 2.6 %collective-permute-start.7 = (s32[1,8]{1,0:T(1,128)}, s32[1,8]{1,0:T(1,128)S(1)}, u32[]{:S(2)}, u32[]{:S(2)}) collective-permute-start(s32[1,8]{1,0:T(1,128)} %param.16), channel_id=1, source_target_pairs={{0,20},{4,24},{8,28},{12,0},{16,4},{20,8},{24,12},{28,16},{1,21},{... | collective-permute-start | bytes 104 | tf_op jit(solution)/shard_map/ppermute | solution.py:223
  22.5 1.3 %collective-permute-start.8 = (s32[1,8]{1,0:T(1,128)}, s32[1,8]{1,0:T(1,128)S(1)}, u32[]{:S(2)}, u32[]{:S(2)}) collective-permute-start(s32[1,8]{1,0:T(1,128)} %param.16), channel_id=1, source_target_pairs={{0,24},{4,28},{8,0},{12,4},{16,8},{20,12},{24,16},{28,20},{1,25},{... | collective-permute-start | bytes 104 | tf_op jit(solution)/shard_map/ppermute | solution.py:223
  23.9 1.6 %collective-permute-start.9 = (s32[1,8]{1,0:T(1,128)}, s32[1,8]{1,0:T(1,128)S(1)}, u32[]{:S(2)}, u32[]{:S(2)}) collective-permute-start(s32[1,8]{1,0:T(1,128)} %param.16), channel_id=1, source_target_pairs={{0,28},{4,0},{8,4},{12,8},{16,12},{20,16},{24,20},{28,24},{1,29},{... | collective-permute-start | bytes 104 | tf_op jit(solution)/shard_map/ppermute | solution.py:223
  25.5 0.7 collective-permute-done.8
  26.2 1.3 %collective-permute-done.9 = s32[1,8]{1,0:T(1,128)S(1)} collective-permute-done((s32[1,8]{1,0:T(1,128)}, s32[1,8]{1,0:T(1,128)S(1)}, u32[]{:S(2)}, u32[]{:S(2)}) %collective-permute-start.9) | collective-permute-done | bytes 64 | tf_op jit(solution)/shard_map/ppermute | solution.py:223
  27.6 0.6 gather_fusion
  28.9 2.0 %fusion = f32[384]{0:T(512)S(1)} fusion(bf16[96,5120]{1,0:T(8,128)(2,1)S(1)} %collective-permute-done.2, bf16[96,5120]{1,0:T(8,128)(2,1)S(1)} %collective-permute-done.1, bf16[96,5120]{1,0:T(8,128)(2,1)S(1)} %collective-permute-done, bf16[96,5120]{1,0:T(8,128)(2,1)} %param.14), kind=kLoop, calls=%fused_computation.5 | loop fusion | flops 19660416 | bytes 3933696 | tf_op jit(solution)/shard_map/reduce_sum | solution.py:108
  31.0 7.6 %convolution_add_fusion = f32[384,640]{1,0:T(8,128)} fusion(bf16[5120,640]{1,0:T(8,128)(2,1)} %param.18, f32[5120]{0:T(1024)} %param.17, f32[384]{0:T(512)S(1)} %add_rsqrt_fusion, f32[640]{0:T(1024)} %param.19, bf16[96,5120]{1,0:T(8,128)(2,1)S(1)} %collective-permute-done.2, bf16[96,5120]{1,0:T(8,128)(2,1)S(1)} %collective-permute-done.1, ...), kind=kOutput, calls=%fused_computation.16 | convolution fusion | flops 2538455040 | bytes 11493376 | tf_op jit(solution)/shard_map/dot_general | solution.py:112
  38.6 1.3 %fusion.7 = f32[384,256]{1,0:T(8,128)S(1)} fusion(bf16[5120,128]{1,0:T(8,128)(2,1)S(1)} %copy-done.2, bf16[5120,128]{1,0:T(8,128)(2,1)S(1)} %copy-done.3, f32[5120]{0:T(1024)S(1)} %copy-done.4, f32[384]{0:T(512)S(1)} %add_rsqrt_fusion, f32[256]{0:T(256)S(1)} %pad_maximum_fusion.10, bf16[96,5120]{1,0:T(8,128)(2,1)S(1)} %collective-permute-done.2, ...), kind=kOutput, calls=%fused_computation.18 | convolution fusion | flops 1033601024 | bytes 6969856 | tf_op jit(solution)/shard_map/dot_general | solution.py:114
  40.0 0.8 fusion.82
  41.1 1.5 %copy.47 = f32[384,640]{0,1:T(8,128)S(1)} copy(f32[384,640]{1,0:T(8,128)} %convolution_add_fusion) | data formatting | bytes 1966080 | tf_op jit(solution)/shard_map/optimization_barrier | solution.py:120
  42.8 0.6 convolution_convert_fusion
  43.5 1.8 %collective-permute-start.10 = (bf16[48,896]{1,0:T(8,128)(2,1)S(1)}, bf16[48,896]{1,0:T(8,128)(2,1)S(1)}, u32[]{:S(2)}, u32[]{:S(2)}) collective-permute-start(bf16[48,896]{1,0:T(8,128)(2,1)S(1)} %get-tuple-element.48), channel_id=1, source_target_pairs={{0,4},{4,8},{8,12},{12,16},{16,20},{20,24},{24,28},{28,0},{1,5},{5... | collective-permute-start | bytes 258056 | tf_op jit(solution)/shard_map/ppermute | solution.py:239
  46.0 3.1 %collective-permute-start.12 = (bf16[48,896]{1,0:T(8,128)(2,1)S(1)}, bf16[48,896]{1,0:T(8,128)(2,1)S(1)}, u32[]{:S(2)}, u32[]{:S(2)}) collective-permute-start(bf16[48,896]{1,0:T(8,128)(2,1)S(1)} %get-tuple-element.46), channel_id=1, source_target_pairs={{0,12},{4,16},{8,20},{12,24},{16,28},{20,0},{24,4},{28,8},{1,13},{... | collective-permute-start | bytes 258056 | tf_op jit(solution)/shard_map/ppermute | solution.py:239
  49.0 1.0 collective-permute-start.13
  50.0 3.3 %collective-permute-start.14 = (bf16[48,896]{1,0:T(8,128)(2,1)S(1)}, bf16[48,896]{1,0:T(8,128)(2,1)S(1)}, u32[]{:S(2)}, u32[]{:S(2)}) collective-permute-start(bf16[48,896]{1,0:T(8,128)(2,1)S(1)} %get-tuple-element.44), channel_id=1, source_target_pairs={{0,20},{4,24},{8,28},{12,0},{16,4},{20,8},{24,12},{28,16},{1,21},{... | collective-permute-start | bytes 258056 | tf_op jit(solution)/shard_map/ppermute | solution.py:239
  53.7 1.6 %collective-permute-start.16 = (bf16[48,896]{1,0:T(8,128)(2,1)S(1)}, bf16[48,896]{1,0:T(8,128)(2,1)S(1)}, u32[]{:S(2)}, u32[]{:S(2)}) collective-permute-start(bf16[48,896]{1,0:T(8,128)(2,1)S(1)} %get-tuple-element.42), channel_id=1, source_target_pairs={{0,28},{4,0},{8,4},{12,8},{16,12},{20,16},{24,20},{28,24},{1,29},{... | collective-permute-start | bytes 258056 | tf_op jit(solution)/shard_map/ppermute | solution.py:239
  55.3 2.9 %collective-permute-done.12 = bf16[48,896]{1,0:T(8,128)(2,1)S(1)} collective-permute-done((bf16[48,896]{1,0:T(8,128)(2,1)S(1)}, bf16[48,896]{1,0:T(8,128)(2,1)S(1)}, u32[]{:S(2)}, u32[]{:S(2)}) %collective-permute-start.12) | collective-permute-done | bytes 86048 | tf_op jit(solution)/shard_map/ppermute | solution.py:239
  58.2 1.1 collective-permute-done.13
  59.3 1.7 %collective-permute-done.15 = bf16[48,896]{1,0:T(8,128)(2,1)S(1)} collective-permute-done((bf16[48,896]{1,0:T(8,128)(2,1)S(1)}, bf16[48,896]{1,0:T(8,128)(2,1)S(1)}, u32[]{:S(2)}, u32[]{:S(2)}) %collective-permute-start.15) | collective-permute-done | bytes 86048 | tf_op jit(solution)/shard_map/ppermute | solution.py:239
  62.1 4.2 %fusion.120 = f32[32,5120]{1,0:T(8,128)S(1)} fusion(bf16[640,5120]{1,0:T(8,128)(2,1)} %param.24, bf16[4,8,5,128]{3,2,1,0:T(8,128)(2,1)S(1)} %bitcast.531), kind=kOutput, calls=%fused_computation.250 | convolution fusion | flops 209715200 | bytes 7249920 | tf_op jit(solution)/shard_map/dot_general | solution.py:213
  67.2 1.2 %fusion.117 = f32[32,5120]{1,0:T(8,128)S(1)} fusion(bf16[640,5120]{1,0:T(8,128)(2,1)S(1)} %bitcast.527, bf16[4,8,5,128]{3,2,1,0:T(8,128)(2,1)S(1)} %bitcast.532), kind=kOutput, calls=%fused_computation.247 | convolution fusion | flops 209715200 | bytes 7249920 | tf_op jit(solution)/shard_map/dot_general | solution.py:213
  68.5 0.6 collective-permute-start.19
  69.8 1.2 %fusion.114 = f32[32,5120]{1,0:T(8,128)S(1)} fusion(bf16[640,5120]{1,0:T(8,128)(2,1)S(1)} %bitcast.527, bf16[4,8,5,128]{3,2,1,0:T(8,128)(2,1)S(1)} %bitcast.533), kind=kOutput, calls=%fused_computation.244 | convolution fusion | flops 209715200 | bytes 7249920 | tf_op jit(solution)/shard_map/dot_general | solution.py:213
  71.8 1.2 %fusion.111 = f32[32,5120]{1,0:T(8,128)S(1)} fusion(bf16[640,5120]{1,0:T(8,128)(2,1)S(1)} %bitcast.527, bf16[4,8,5,128]{3,2,1,0:T(8,128)(2,1)S(1)} %bitcast.534), kind=kOutput, calls=%fused_computation.241 | convolution fusion | flops 209715200 | bytes 7249920 | tf_op jit(solution)/shard_map/dot_general | solution.py:213
  73.2 0.6 collective-permute-start.23
  74.4 1.2 %fusion.108 = f32[32,5120]{1,0:T(8,128)S(1)} fusion(bf16[640,5120]{1,0:T(8,128)(2,1)S(1)} %bitcast.527, bf16[4,8,5,128]{3,2,1,0:T(8,128)(2,1)S(1)} %bitcast.535), kind=kOutput, calls=%fused_computation.238 | convolution fusion | flops 209715200 | bytes 7249920 | tf_op jit(solution)/shard_map/dot_general | solution.py:213
  76.6 1.2 %fusion.105 = f32[32,5120]{1,0:T(8,128)S(1)} fusion(bf16[640,5120]{1,0:T(8,128)(2,1)S(1)} %bitcast.527, bf16[4,8,5,128]{3,2,1,0:T(8,128)(2,1)S(1)} %bitcast.536), kind=kOutput, calls=%fused_computation.235 | convolution fusion | flops 209715200 | bytes 7249920 | tf_op jit(solution)/shard_map/dot_general | solution.py:213
  78.6 1.2 %fusion.102 = f32[32,5120]{1,0:T(8,128)S(1)} fusion(bf16[640,5120]{1,0:T(8,128)(2,1)S(1)} %bitcast.527, bf16[4,8,5,128]{3,2,1,0:T(8,128)(2,1)S(1)} %bitcast.537), kind=kOutput, calls=%fused_computation.232 | convolution fusion | flops 209715200 | bytes 7249920 | tf_op jit(solution)/shard_map/dot_general | solution.py:213
  80.6 1.2 %fusion.99 = f32[32,5120]{1,0:T(8,128)S(1)} fusion(bf16[640,5120]{1,0:T(8,128)(2,1)S(1)} %bitcast.527, bf16[4,8,5,128]{3,2,1,0:T(8,128)(2,1)S(1)} %bitcast.538), kind=kOutput, calls=%fused_computation.229 | convolution fusion | flops 209715200 | bytes 7249920 | tf_op jit(solution)/shard_map/dot_general | solution.py:213
  82.0 0.6 collective-permute-start.27
  82.7 0.6 collective-permute-start.31
  83.4 1.0 collective-permute-start.18
  84.4 1.2 %collective-permute-start.20 = (f32[1,32,1280]{2,1,0:T(8,128)S(1)}, f32[1,32,1280]{2,1,0:T(8,128)S(1)}, u32[]{:S(2)}, u32[]{:S(2)}) collective-permute-start(f32[1,32,1280]{2,1,0:T(8,128)S(1)} %get-tuple-element.30), channel_id=1, source_target_pairs={{0,2},{1,3},{2,0},{3,1},{4,6},{5,7},{6,4},{7,5},{8,10},{9,11},{10,... | collective-permute-start | bytes 491528 | tf_op jit(solution)/shard_map/ppermute | solution.py:257
  85.7 1.0 collective-permute-start.22
  86.7 1.2 %collective-permute-start.24 = (f32[1,32,1280]{2,1,0:T(8,128)S(1)}, f32[1,32,1280]{2,1,0:T(8,128)S(1)}, u32[]{:S(2)}, u32[]{:S(2)}) collective-permute-start(f32[1,32,1280]{2,1,0:T(8,128)S(1)} %get-tuple-element.24), channel_id=1, source_target_pairs={{0,2},{1,3},{2,0},{3,1},{4,6},{5,7},{6,4},{7,5},{8,10},{9,11},{10,... | collective-permute-start | bytes 491528 | tf_op jit(solution)/shard_map/ppermute | solution.py:257
  88.0 1.0 collective-permute-start.26
  89.0 1.5 %collective-permute-done.18 = f32[1,32,1280]{2,1,0:T(8,128)S(1)} collective-permute-done((f32[1,32,1280]{2,1,0:T(8,128)S(1)}, f32[1,32,1280]{2,1,0:T(8,128)S(1)}, u32[]{:S(2)}, u32[]{:S(2)}) %collective-permute-start.18) | collective-permute-done | bytes 163872 | tf_op jit(solution)/shard_map/ppermute | solution.py:257
  90.5 0.9 collective-permute-start.28
  91.4 2.6 %collective-permute-done.20 = f32[1,32,1280]{2,1,0:T(8,128)S(1)} collective-permute-done((f32[1,32,1280]{2,1,0:T(8,128)S(1)}, f32[1,32,1280]{2,1,0:T(8,128)S(1)}, u32[]{:S(2)}, u32[]{:S(2)}) %collective-permute-start.20) | collective-permute-done | bytes 163872 | tf_op jit(solution)/shard_map/ppermute | solution.py:257
  94.0 0.9 collective-permute-start.30
  94.9 2.6 %collective-permute-done.22 = f32[1,32,1280]{2,1,0:T(8,128)S(1)} collective-permute-done((f32[1,32,1280]{2,1,0:T(8,128)S(1)}, f32[1,32,1280]{2,1,0:T(8,128)S(1)}, u32[]{:S(2)}, u32[]{:S(2)}) %collective-permute-start.22) | collective-permute-done | bytes 163872 | tf_op jit(solution)/shard_map/ppermute | solution.py:257
  97.5 0.9 collective-permute-start.32
  98.4 2.6 %collective-permute-done.24 = f32[1,32,1280]{2,1,0:T(8,128)S(1)} collective-permute-done((f32[1,32,1280]{2,1,0:T(8,128)S(1)}, f32[1,32,1280]{2,1,0:T(8,128)S(1)}, u32[]{:S(2)}, u32[]{:S(2)}) %collective-permute-start.24) | collective-permute-done | bytes 163872 | tf_op jit(solution)/shard_map/ppermute | solution.py:257
  101.1 3.5 %collective-permute-done.26 = f32[1,32,1280]{2,1,0:T(8,128)S(1)} collective-permute-done((f32[1,32,1280]{2,1,0:T(8,128)S(1)}, f32[1,32,1280]{2,1,0:T(8,128)S(1)}, u32[]{:S(2)}, u32[]{:S(2)}) %collective-permute-start.26) | collective-permute-done | bytes 163872 | tf_op jit(solution)/shard_map/ppermute | solution.py:257
  104.6 3.5 %collective-permute-done.28 = f32[1,32,1280]{2,1,0:T(8,128)S(1)} collective-permute-done((f32[1,32,1280]{2,1,0:T(8,128)S(1)}, f32[1,32,1280]{2,1,0:T(8,128)S(1)}, u32[]{:S(2)}, u32[]{:S(2)}) %collective-permute-start.28) | collective-permute-done | bytes 163872 | tf_op jit(solution)/shard_map/ppermute | solution.py:257
  108.1 3.5 %collective-permute-done.30 = f32[1,32,1280]{2,1,0:T(8,128)S(1)} collective-permute-done((f32[1,32,1280]{2,1,0:T(8,128)S(1)}, f32[1,32,1280]{2,1,0:T(8,128)S(1)}, u32[]{:S(2)}, u32[]{:S(2)}) %collective-permute-start.30) | collective-permute-done | bytes 163872 | tf_op jit(solution)/shard_map/ppermute | solution.py:257
  111.6 2.5 %collective-permute-done.32 = f32[1,32,1280]{2,1,0:T(8,128)S(1)} collective-permute-done((f32[1,32,1280]{2,1,0:T(8,128)S(1)}, f32[1,32,1280]{2,1,0:T(8,128)S(1)}, u32[]{:S(2)}, u32[]{:S(2)}) %collective-permute-start.32) | collective-permute-done | bytes 163872 | tf_op jit(solution)/shard_map/ppermute | solution.py:257
  114.1 0.7 fusion.90
  (202 shorter events, 12.6 us)
Async XLA Ops:
  0.0 26.2 %collective-permute-start = (bf16[96,5120]{1,0:T(8,128)(2,1)}, bf16[96,5120]{1,0:T(8,128)(2,1)S(1)}, u32[]{:S(2)}, u32[]{:S(2)}) collective-permute-start(bf16[96,5120]{1,0:T(8,128)(2,1)} %param.14), channel_id=1, source_target_pairs={{0,2},{1,3},{2,0},{3,1},{4,6},{5,7},{6,4},{7,5},{8,10},{9,11},{10,... | collective-permute-start | bytes 2949128 | tf_op jit(solution)/shard_map/ppermute | solution.py:286
  2.9 26.0 %collective-permute-start.1 = (bf16[96,5120]{1,0:T(8,128)(2,1)}, bf16[96,5120]{1,0:T(8,128)(2,1)S(1)}, u32[]{:S(2)}, u32[]{:S(2)}) collective-permute-start(bf16[96,5120]{1,0:T(8,128)(2,1)} %param.14), channel_id=1, source_target_pairs={{0,1},{1,0},{2,3},{3,2},{4,5},{5,4},{6,7},{7,6},{8,9},{9,8},{10,11... | collective-permute-start | bytes 2949128 | tf_op jit(solution)/shard_map/ppermute | solution.py:286
  2.9 15.6 %collective-permute-start.3 = (s32[1,8]{1,0:T(1,128)}, s32[1,8]{1,0:T(1,128)S(1)}, u32[]{:S(2)}, u32[]{:S(2)}) collective-permute-start(s32[1,8]{1,0:T(1,128)} %param.16), channel_id=1, source_target_pairs={{0,4},{4,8},{8,12},{12,16},{16,20},{20,24},{24,28},{28,0},{1,5},{5... | collective-permute-start | bytes 104 | tf_op jit(solution)/shard_map/ppermute | solution.py:223
  4.5 15.4 %collective-permute-start.4 = (s32[1,8]{1,0:T(1,128)}, s32[1,8]{1,0:T(1,128)S(1)}, u32[]{:S(2)}, u32[]{:S(2)}) collective-permute-start(s32[1,8]{1,0:T(1,128)} %param.16), channel_id=1, source_target_pairs={{0,8},{4,12},{8,16},{12,20},{16,24},{20,28},{24,0},{28,4},{1,9},{5... | collective-permute-start | bytes 104 | tf_op jit(solution)/shard_map/ppermute | solution.py:223
  6.0 16.5 %collective-permute-start.5 = (s32[1,8]{1,0:T(1,128)}, s32[1,8]{1,0:T(1,128)S(1)}, u32[]{:S(2)}, u32[]{:S(2)}) collective-permute-start(s32[1,8]{1,0:T(1,128)} %param.16), channel_id=1, source_target_pairs={{0,12},{4,16},{8,20},{12,24},{16,28},{20,0},{24,4},{28,8},{1,13},{... | collective-permute-start | bytes 104 | tf_op jit(solution)/shard_map/ppermute | solution.py:223
  18.5 5.3 %collective-permute-start.6 = (s32[1,8]{1,0:T(1,128)}, s32[1,8]{1,0:T(1,128)S(1)}, u32[]{:S(2)}, u32[]{:S(2)}) collective-permute-start(s32[1,8]{1,0:T(1,128)} %param.16), channel_id=1, source_target_pairs={{0,16},{4,20},{8,24},{12,28},{16,0},{20,4},{24,8},{28,12},{1,17},{... | collective-permute-start | bytes 104 | tf_op jit(solution)/shard_map/ppermute | solution.py:223
  19.9 5.6 %collective-permute-start.7 = (s32[1,8]{1,0:T(1,128)}, s32[1,8]{1,0:T(1,128)S(1)}, u32[]{:S(2)}, u32[]{:S(2)}) collective-permute-start(s32[1,8]{1,0:T(1,128)} %param.16), channel_id=1, source_target_pairs={{0,20},{4,24},{8,28},{12,0},{16,4},{20,8},{24,12},{28,16},{1,21},{... | collective-permute-start | bytes 104 | tf_op jit(solution)/shard_map/ppermute | solution.py:223
  22.5 3.7 %collective-permute-start.8 = (s32[1,8]{1,0:T(1,128)}, s32[1,8]{1,0:T(1,128)S(1)}, u32[]{:S(2)}, u32[]{:S(2)}) collective-permute-start(s32[1,8]{1,0:T(1,128)} %param.16), channel_id=1, source_target_pairs={{0,24},{4,28},{8,0},{12,4},{16,8},{20,12},{24,16},{28,20},{1,25},{... | collective-permute-start | bytes 104 | tf_op jit(solution)/shard_map/ppermute | solution.py:223
  23.9 3.7 %collective-permute-start.9 = (s32[1,8]{1,0:T(1,128)}, s32[1,8]{1,0:T(1,128)S(1)}, u32[]{:S(2)}, u32[]{:S(2)}) collective-permute-start(s32[1,8]{1,0:T(1,128)} %param.16), channel_id=1, source_target_pairs={{0,28},{4,0},{8,4},{12,8},{16,12},{20,16},{24,20},{28,24},{1,29},{... | collective-permute-start | bytes 104 | tf_op jit(solution)/shard_map/ppermute | solution.py:223
  26.2 2.7 %collective-permute-start.2 = (bf16[96,5120]{1,0:T(8,128)(2,1)S(1)}, bf16[96,5120]{1,0:T(8,128)(2,1)S(1)}, u32[]{:S(2)}, u32[]{:S(2)}) collective-permute-start(bf16[96,5120]{1,0:T(8,128)(2,1)S(1)} %collective-permute-done), channel_id=1, source_target_pairs={{0,1},{1,0},{2,3},{3,2},{4,5},{5,4},{6,7},{7,6},{8,9},{9,8},{10,11... | collective-permute-start | bytes 2949128 | tf_op jit(solution)/shard_map/ppermute | solution.py:286
  30.9 7.6 %copy-start = (bf16[96,5120]{1,0:T(8,128)(2,1)S(1)}, bf16[96,5120]{1,0:T(8,128)(2,1)}, u32[]{:S(2)}) copy-start(bf16[96,5120]{1,0:T(8,128)(2,1)} %param.14) | copy-start | bytes 2949124
  30.9 7.6 %copy-start.2 = (bf16[5120,128]{1,0:T(8,128)(2,1)S(1)}, bf16[5120,128]{1,0:T(8,128)(2,1)}, u32[]{:S(2)}) copy-start(bf16[5120,128]{1,0:T(8,128)(2,1)} %param.22) | copy-start | bytes 3932164
  30.9 7.6 %copy-start.3 = (bf16[5120,128]{1,0:T(8,128)(2,1)S(1)}, bf16[5120,128]{1,0:T(8,128)(2,1)}, u32[]{:S(2)}) copy-start(bf16[5120,128]{1,0:T(8,128)(2,1)} %param.20) | copy-start | bytes 3932164
  30.9 7.6 %copy-start.4 = (f32[5120]{0:T(1024)S(1)}, f32[5120]{0:T(1024)}, u32[]{:S(2)}) copy-start(f32[5120]{0:T(1024)} %param.17) | copy-start | bytes 61444
  43.5 9.8 %collective-permute-start.10 = (bf16[48,896]{1,0:T(8,128)(2,1)S(1)}, bf16[48,896]{1,0:T(8,128)(2,1)S(1)}, u32[]{:S(2)}, u32[]{:S(2)}) collective-permute-start(bf16[48,896]{1,0:T(8,128)(2,1)S(1)} %get-tuple-element.48), channel_id=1, source_target_pairs={{0,4},{4,8},{8,12},{12,16},{16,20},{20,24},{24,28},{28,0},{1,5},{5... | collective-permute-start | bytes 258056 | tf_op jit(solution)/shard_map/ppermute | solution.py:239
  45.7 8.0 %collective-permute-start.11 = (bf16[48,896]{1,0:T(8,128)(2,1)S(1)}, bf16[48,896]{1,0:T(8,128)(2,1)S(1)}, u32[]{:S(2)}, u32[]{:S(2)}) collective-permute-start(bf16[48,896]{1,0:T(8,128)(2,1)S(1)} %get-tuple-element.47), channel_id=1, source_target_pairs={{0,8},{4,12},{8,16},{12,20},{16,24},{20,28},{24,0},{28,4},{1,9},{5... | collective-permute-start | bytes 258056 | tf_op jit(solution)/shard_map/ppermute | solution.py:239
  46.0 12.2 %collective-permute-start.12 = (bf16[48,896]{1,0:T(8,128)(2,1)S(1)}, bf16[48,896]{1,0:T(8,128)(2,1)S(1)}, u32[]{:S(2)}, u32[]{:S(2)}) collective-permute-start(bf16[48,896]{1,0:T(8,128)(2,1)S(1)} %get-tuple-element.46), channel_id=1, source_target_pairs={{0,12},{4,16},{8,20},{12,24},{16,28},{20,0},{24,4},{28,8},{1,13},{... | collective-permute-start | bytes 258056 | tf_op jit(solution)/shard_map/ppermute | solution.py:239
  49.0 10.3 %collective-permute-start.13 = (bf16[48,896]{1,0:T(8,128)(2,1)S(1)}, bf16[48,896]{1,0:T(8,128)(2,1)S(1)}, u32[]{:S(2)}, u32[]{:S(2)}) collective-permute-start(bf16[48,896]{1,0:T(8,128)(2,1)S(1)} %get-tuple-element.45), channel_id=1, source_target_pairs={{0,16},{4,20},{8,24},{12,28},{16,0},{20,4},{24,8},{28,12},{1,17},{... | collective-permute-start | bytes 258056 | tf_op jit(solution)/shard_map/ppermute | solution.py:239
  50.0 9.3 %collective-permute-start.14 = (bf16[48,896]{1,0:T(8,128)(2,1)S(1)}, bf16[48,896]{1,0:T(8,128)(2,1)S(1)}, u32[]{:S(2)}, u32[]{:S(2)}) collective-permute-start(bf16[48,896]{1,0:T(8,128)(2,1)S(1)} %get-tuple-element.44), channel_id=1, source_target_pairs={{0,20},{4,24},{8,28},{12,0},{16,4},{20,8},{24,12},{28,16},{1,21},{... | collective-permute-start | bytes 258056 | tf_op jit(solution)/shard_map/ppermute | solution.py:239
  53.3 7.8 %collective-permute-start.15 = (bf16[48,896]{1,0:T(8,128)(2,1)S(1)}, bf16[48,896]{1,0:T(8,128)(2,1)S(1)}, u32[]{:S(2)}, u32[]{:S(2)}) collective-permute-start(bf16[48,896]{1,0:T(8,128)(2,1)S(1)} %get-tuple-element.43), channel_id=1, source_target_pairs={{0,24},{4,28},{8,0},{12,4},{16,8},{20,12},{24,16},{28,20},{1,25},{... | collective-permute-start | bytes 258056 | tf_op jit(solution)/shard_map/ppermute | solution.py:239
  53.7 13.5 %slice-start = ((s8[6553600]{0:T(1024)(128)(4,1)}), s8[4194304]{0:T(1024)(128)(4,1)S(1)}, s32[]{:S(2)}) async-start(s8[6553600]{0:T(1024)(128)(4,1)} %bitcast.526), calls=%async_computation | async-start | bytes 8388608
  53.7 7.4 %collective-permute-start.16 = (bf16[48,896]{1,0:T(8,128)(2,1)S(1)}, bf16[48,896]{1,0:T(8,128)(2,1)S(1)}, u32[]{:S(2)}, u32[]{:S(2)}) collective-permute-start(bf16[48,896]{1,0:T(8,128)(2,1)S(1)} %get-tuple-element.42), channel_id=1, source_target_pairs={{0,28},{4,0},{8,4},{12,8},{16,12},{20,16},{24,20},{28,24},{1,29},{... | collective-permute-start | bytes 258056 | tf_op jit(solution)/shard_map/ppermute | solution.py:239
  62.1 5.1 %slice-start.1 = ((s8[6553600]{0:T(1024)(128)(4,1)}), s8[2359296]{0:T(1024)(128)(4,1)S(1)}, s32[]{:S(2)}) async-start(s8[6553600]{0:T(1024)(128)(4,1)} %bitcast.526), calls=%async_computation.1 | async-start | bytes 4718592
  66.4 15.6 %collective-permute-start.17 = (f32[2,32,1280]{2,1,0:T(8,128)S(1)}, f32[2,32,1280]{2,1,0:T(8,128)S(1)}, u32[]{:S(2)}, u32[]{:S(2)}) collective-permute-start(f32[2,32,1280]{2,1,0:T(8,128)S(1)} %pad_maximum_fusion.2), channel_id=1, source_target_pairs={{0,1},{1,0},{2,3},{3,2},{4,5},{5,4},{6,7},{7,6},{8,9},{9,8},{10,11... | collective-permute-start | bytes 983048 | tf_op jit(solution)/shard_map/ppermute | solution.py:257
  68.5 14.1 %collective-permute-start.19 = (f32[2,32,1280]{2,1,0:T(8,128)S(1)}, f32[2,32,1280]{2,1,0:T(8,128)S(1)}, u32[]{:S(2)}, u32[]{:S(2)}) collective-permute-start(f32[2,32,1280]{2,1,0:T(8,128)S(1)} %pad_maximum_fusion.3), channel_id=1, source_target_pairs={{0,1},{1,0},{2,3},{3,2},{4,5},{5,4},{6,7},{7,6},{8,9},{9,8},{10,11... | collective-permute-start | bytes 983048 | tf_op jit(solution)/shard_map/ppermute | solution.py:257
  71.1 11.7 %collective-permute-start.21 = (f32[2,32,1280]{2,1,0:T(8,128)S(1)}, f32[2,32,1280]{2,1,0:T(8,128)S(1)}, u32[]{:S(2)}, u32[]{:S(2)}) collective-permute-start(f32[2,32,1280]{2,1,0:T(8,128)S(1)} %pad_maximum_fusion.4), channel_id=1, source_target_pairs={{0,1},{1,0},{2,3},{3,2},{4,5},{5,4},{6,7},{7,6},{8,9},{9,8},{10,11... | collective-permute-start | bytes 983048 | tf_op jit(solution)/shard_map/ppermute | solution.py:257
  73.2 10.2 %collective-permute-start.23 = (f32[2,32,1280]{2,1,0:T(8,128)S(1)}, f32[2,32,1280]{2,1,0:T(8,128)S(1)}, u32[]{:S(2)}, u32[]{:S(2)}) collective-permute-start(f32[2,32,1280]{2,1,0:T(8,128)S(1)} %pad_maximum_fusion.5), channel_id=1, source_target_pairs={{0,1},{1,0},{2,3},{3,2},{4,5},{5,4},{6,7},{7,6},{8,9},{9,8},{10,11... | collective-permute-start | bytes 983048 | tf_op jit(solution)/shard_map/ppermute | solution.py:257
  75.7 8.6 %collective-permute-start.25 = (f32[2,32,1280]{2,1,0:T(8,128)S(1)}, f32[2,32,1280]{2,1,0:T(8,128)S(1)}, u32[]{:S(2)}, u32[]{:S(2)}) collective-permute-start(f32[2,32,1280]{2,1,0:T(8,128)S(1)} %pad_maximum_fusion.6), channel_id=1, source_target_pairs={{0,1},{1,0},{2,3},{3,2},{4,5},{5,4},{6,7},{7,6},{8,9},{9,8},{10,11... | collective-permute-start | bytes 983048 | tf_op jit(solution)/shard_map/ppermute | solution.py:257
  82.0 3.7 %collective-permute-start.27 = (f32[2,32,1280]{2,1,0:T(8,128)S(1)}, f32[2,32,1280]{2,1,0:T(8,128)S(1)}, u32[]{:S(2)}, u32[]{:S(2)}) collective-permute-start(f32[2,32,1280]{2,1,0:T(8,128)S(1)} %pad_maximum_fusion.7), channel_id=1, source_target_pairs={{0,1},{1,0},{2,3},{3,2},{4,5},{5,4},{6,7},{7,6},{8,9},{9,8},{10,11... | collective-permute-start | bytes 983048 | tf_op jit(solution)/shard_map/ppermute | solution.py:257
  82.6 4.1 %collective-permute-start.29 = (f32[2,32,1280]{2,1,0:T(8,128)S(1)}, f32[2,32,1280]{2,1,0:T(8,128)S(1)}, u32[]{:S(2)}, u32[]{:S(2)}) collective-permute-start(f32[2,32,1280]{2,1,0:T(8,128)S(1)} %pad_maximum_fusion.8), channel_id=1, source_target_pairs={{0,1},{1,0},{2,3},{3,2},{4,5},{5,4},{6,7},{7,6},{8,9},{9,8},{10,11... | collective-permute-start | bytes 983048 | tf_op jit(solution)/shard_map/ppermute | solution.py:257
  82.7 5.2 %collective-permute-start.31 = (f32[2,32,1280]{2,1,0:T(8,128)S(1)}, f32[2,32,1280]{2,1,0:T(8,128)S(1)}, u32[]{:S(2)}, u32[]{:S(2)}) collective-permute-start(f32[2,32,1280]{2,1,0:T(8,128)S(1)} %pad_maximum_fusion.9), channel_id=1, source_target_pairs={{0,1},{1,0},{2,3},{3,2},{4,5},{5,4},{6,7},{7,6},{8,9},{9,8},{10,11... | collective-permute-start | bytes 983048 | tf_op jit(solution)/shard_map/ppermute | solution.py:257
  83.4 7.1 %collective-permute-start.18 = (f32[1,32,1280]{2,1,0:T(8,128)S(1)}, f32[1,32,1280]{2,1,0:T(8,128)S(1)}, u32[]{:S(2)}, u32[]{:S(2)}) collective-permute-start(f32[1,32,1280]{2,1,0:T(8,128)S(1)} %get-tuple-element.33), channel_id=1, source_target_pairs={{0,2},{1,3},{2,0},{3,1},{4,6},{5,7},{6,4},{7,5},{8,10},{9,11},{10,... | collective-permute-start | bytes 491528 | tf_op jit(solution)/shard_map/ppermute | solution.py:257
  84.4 9.6 %collective-permute-start.20 = (f32[1,32,1280]{2,1,0:T(8,128)S(1)}, f32[1,32,1280]{2,1,0:T(8,128)S(1)}, u32[]{:S(2)}, u32[]{:S(2)}) collective-permute-start(f32[1,32,1280]{2,1,0:T(8,128)S(1)} %get-tuple-element.30), channel_id=1, source_target_pairs={{0,2},{1,3},{2,0},{3,1},{4,6},{5,7},{6,4},{7,5},{8,10},{9,11},{10,... | collective-permute-start | bytes 491528 | tf_op jit(solution)/shard_map/ppermute | solution.py:257
  85.7 11.9 %collective-permute-start.22 = (f32[1,32,1280]{2,1,0:T(8,128)S(1)}, f32[1,32,1280]{2,1,0:T(8,128)S(1)}, u32[]{:S(2)}, u32[]{:S(2)}) collective-permute-start(f32[1,32,1280]{2,1,0:T(8,128)S(1)} %get-tuple-element.27), channel_id=1, source_target_pairs={{0,2},{1,3},{2,0},{3,1},{4,6},{5,7},{6,4},{7,5},{8,10},{9,11},{10,... | collective-permute-start | bytes 491528 | tf_op jit(solution)/shard_map/ppermute | solution.py:257
  86.7 14.3 %collective-permute-start.24 = (f32[1,32,1280]{2,1,0:T(8,128)S(1)}, f32[1,32,1280]{2,1,0:T(8,128)S(1)}, u32[]{:S(2)}, u32[]{:S(2)}) collective-permute-start(f32[1,32,1280]{2,1,0:T(8,128)S(1)} %get-tuple-element.24), channel_id=1, source_target_pairs={{0,2},{1,3},{2,0},{3,1},{4,6},{5,7},{6,4},{7,5},{8,10},{9,11},{10,... | collective-permute-start | bytes 491528 | tf_op jit(solution)/shard_map/ppermute | solution.py:257
  88.0 16.6 %collective-permute-start.26 = (f32[1,32,1280]{2,1,0:T(8,128)S(1)}, f32[1,32,1280]{2,1,0:T(8,128)S(1)}, u32[]{:S(2)}, u32[]{:S(2)}) collective-permute-start(f32[1,32,1280]{2,1,0:T(8,128)S(1)} %get-tuple-element.21), channel_id=1, source_target_pairs={{0,2},{1,3},{2,0},{3,1},{4,6},{5,7},{6,4},{7,5},{8,10},{9,11},{10,... | collective-permute-start | bytes 491528 | tf_op jit(solution)/shard_map/ppermute | solution.py:257
  90.5 17.6 %collective-permute-start.28 = (f32[1,32,1280]{2,1,0:T(8,128)S(1)}, f32[1,32,1280]{2,1,0:T(8,128)S(1)}, u32[]{:S(2)}, u32[]{:S(2)}) collective-permute-start(f32[1,32,1280]{2,1,0:T(8,128)S(1)} %get-tuple-element.18), channel_id=1, source_target_pairs={{0,2},{1,3},{2,0},{3,1},{4,6},{5,7},{6,4},{7,5},{8,10},{9,11},{10,... | collective-permute-start | bytes 491528 | tf_op jit(solution)/shard_map/ppermute | solution.py:257
  94.0 17.6 %collective-permute-start.30 = (f32[1,32,1280]{2,1,0:T(8,128)S(1)}, f32[1,32,1280]{2,1,0:T(8,128)S(1)}, u32[]{:S(2)}, u32[]{:S(2)}) collective-permute-start(f32[1,32,1280]{2,1,0:T(8,128)S(1)} %get-tuple-element.15), channel_id=1, source_target_pairs={{0,2},{1,3},{2,0},{3,1},{4,6},{5,7},{6,4},{7,5},{8,10},{9,11},{10,... | collective-permute-start | bytes 491528 | tf_op jit(solution)/shard_map/ppermute | solution.py:257
  97.5 16.6 %collective-permute-start.32 = (f32[1,32,1280]{2,1,0:T(8,128)S(1)}, f32[1,32,1280]{2,1,0:T(8,128)S(1)}, u32[]{:S(2)}, u32[]{:S(2)}) collective-permute-start(f32[1,32,1280]{2,1,0:T(8,128)S(1)} %get-tuple-element.12), channel_id=1, source_target_pairs={{0,2},{1,3},{2,0},{3,1},{4,6},{5,7},{6,4},{7,5},{8,10},{9,11},{10,... | collective-permute-start | bytes 491528 | tf_op jit(solution)/shard_map/ppermute | solution.py:257
  111.6 2.5 %copy-start.1 = (bf16[256,1280]{1,0:T(8,128)(2,1)}, bf16[256,1280]{1,0:T(8,128)(2,1)S(1)}, u32[]{:S(2)}) copy-start(bf16[256,1280]{1,0:T(8,128)(2,1)S(1)} %fusion.89) | copy-start | bytes 1966084

commit v17 on v16

--- a/solution.py
+++ b/solution.py
@@ -181,7 +181,7 @@
     segment = jnp.sum((own_ends[None, :] <= slot_ids[:, None]).astype(jnp.int32), axis=1)
 
     score_scale = 1.0 / math.sqrt(head_dim)
-    chunk_count = 8 if pack_len % 64 == 0 else 1
+    chunk_count = 2 if pack_len % 16 == 0 else 1
     chunk_len = pack_len // chunk_count
     results = []
     for chunk in range(chunk_count):

time: 116 us -> 135 us (1.16)
  the two profiles are of different devices: /device:TPU:0 before, /device:TPU:16 now
where the time goes in v17:
time: 135 us; the launch traced here: 134 us
  waiting for transfers between devices  69 us (51%)
  starting transfers between devices  23 us (17%)
  other arithmetic  17.6 us (13%)
  matrix products  17.5 us (13%)
  local copies, waits for them, and re-layouts  6.5 us (5%)
    ppermute x4, waiting for transfers between devices, halving_scatter(): got = lax.ppermute(send, axis_name, pairs)  27.4 us
    ppermute x3, waiting for transfers between devices, xor_gather(): pieces = pieces + [lax.ppermute(p, axis_name, pairs) for p in pieces]  20.4 us
    ppermute x7, waiting for transfers between devices, exchange(): arrived.append(lax.ppermute(chunks[shift], axis_name, pairs))  17.5 us
    ppermute x7, starting transfers between devices, shift_gather(): lax.ppermute(part, axis_name, [(i, (i + shift) % count) for i in range(co...  9.9 us
    ppermute x7, starting transfers between devices, exchange(): arrived.append(lax.ppermute(chunks[shift], axis_name, pairs))  8.93 us
    dot_general x1, matrix products, project(): jnp.dot(normalized_input, w_query, preferred_element_type=jnp.float32)  7.57 us
    another operation x6, other arithmetic, halving_scatter(): jnp.stack([jnp.where(bit == 0, hi, lo) for (_, lo), hi in zip(lows, highs)])  6.58 us
    dot_general x2, matrix products, local(): jnp.dot(mixed_heads, w_out, preferred_element_type=jnp.float32)  5.48 us
  transfers between devices with their start and end apart: 21, of which 8 were waited for; matrix products, arithmetic and copies ran while one was open for 13% of the time, Pallas kernels for 0%

profile of v17, /device:TPU:16, one launch (start us, length us, event | category | flops | bytes accessed | tf_op | source)
XLA Modules:
  0.0 134.2 jit_solution(16527125030753995030)
XLA Ops:
  0.0 0.5 collective-permute-start.8
  0.5 4.4 %collective-permute-start.7 = (s32[1,8]{1,0:T(1,128)}, s32[1,8]{1,0:T(1,128)S(1)}, u32[]{:S(2)}, u32[]{:S(2)}) collective-permute-start(s32[1,8]{1,0:T(1,128)} %param.16), channel_id=1, source_target_pairs={{0,20},{4,24},{8,28},{12,0},{16,4},{20,8},{24,12},{28,16},{1,21},{... | collective-permute-start | bytes 104 | tf_op jit(solution)/shard_map/ppermute | solution.py:223
  5.0 2.0 %collective-permute-start.5 = (s32[1,8]{1,0:T(1,128)}, s32[1,8]{1,0:T(1,128)S(1)}, u32[]{:S(2)}, u32[]{:S(2)}) collective-permute-start(s32[1,8]{1,0:T(1,128)} %param.16), channel_id=1, source_target_pairs={{0,12},{4,16},{8,20},{12,24},{16,28},{20,0},{24,4},{28,8},{1,13},{... | collective-permute-start | bytes 104 | tf_op jit(solution)/shard_map/ppermute | solution.py:223
  6.9 2.4 %collective-permute-start.3 = (s32[1,8]{1,0:T(1,128)}, s32[1,8]{1,0:T(1,128)S(1)}, u32[]{:S(2)}, u32[]{:S(2)}) collective-permute-start(s32[1,8]{1,0:T(1,128)} %param.16), channel_id=1, source_target_pairs={{0,4},{4,8},{8,12},{12,16},{16,20},{20,24},{24,28},{28,0},{1,5},{5... | collective-permute-start | bytes 104 | tf_op jit(solution)/shard_map/ppermute | solution.py:223
  9.4 0.7 constant_dynamic-update-slice_fusion.7
  10.1 0.7 reshape.696
  11.0 0.8 reduce-window.32
  11.9 0.7 compare_and_fusion.2
  12.7 0.9 reduce-window.30
  13.5 0.2 slice_reduce_fusion
  14.0 0.6 gather_fusion.2
  14.6 0.6 gather_fusion.1
  15.4 0.7 subtract_select_fusion
  16.2 0.9 reduce-window.21
  17.0 0.2 slice_reduce_fusion.1
  17.4 0.7 pad_maximum_fusion.5
  18.4 3.6 %collective-permute-done.4 = s32[1,8]{1,0:T(1,128)S(1)} collective-permute-done((s32[1,8]{1,0:T(1,128)}, s32[1,8]{1,0:T(1,128)S(1)}, u32[]{:S(2)}, u32[]{:S(2)}) %collective-permute-start.4) | collective-permute-done | bytes 64 | tf_op jit(solution)/shard_map/ppermute | solution.py:223
  22.0 1.5 %collective-permute-start = (bf16[96,5120]{1,0:T(8,128)(2,1)}, bf16[96,5120]{1,0:T(8,128)(2,1)S(1)}, u32[]{:S(2)}, u32[]{:S(2)}) collective-permute-start(bf16[96,5120]{1,0:T(8,128)(2,1)} %param.14), channel_id=1, source_target_pairs={{0,2},{1,3},{2,0},{3,1},{4,6},{5,7},{6,4},{7,5},{8,10},{9,11},{10,... | collective-permute-start | bytes 2949128 | tf_op jit(solution)/shard_map/ppermute | solution.py:286
  23.5 0.5 collective-permute-start.9
  24.1 19.1 %collective-permute-done = bf16[96,5120]{1,0:T(8,128)(2,1)S(1)} collective-permute-done((bf16[96,5120]{1,0:T(8,128)(2,1)}, bf16[96,5120]{1,0:T(8,128)(2,1)S(1)}, u32[]{:S(2)}, u32[]{:S(2)}) %collective-permute-start) | collective-permute-done | bytes 983072 | tf_op jit(solution)/shard_map/ppermute | solution.py:286
  43.2 0.6 gather_fusion
  43.8 0.2 reduce_window_sum.54
  44.1 0.4 multiply_cosine_fusion.1
  44.6 1.3 collective-permute-done.2
  45.9 2.1 %fusion = f32[384]{0:T(512)S(1)} fusion(bf16[96,5120]{1,0:T(8,128)(2,1)} %collective-permute-done.2, bf16[96,5120]{1,0:T(8,128)(2,1)S(1)} %collective-permute-done.1, bf16[96,5120]{1,0:T(8,128)(2,1)S(1)} %collective-permute-done, bf16[96,5120]{1,0:T(8,128)(2,1)} %param.14), kind=kLoop, calls=%fused_computation.5 | loop fusion | flops 19660416 | bytes 3933696 | tf_op jit(solution)/shard_map/reduce_sum | solution.py:108
  48.1 7.6 %convolution_add_fusion = f32[384,640]{1,0:T(8,128)} fusion(bf16[5120,640]{1,0:T(8,128)(2,1)} %param.18, f32[5120]{0:T(1024)S(1)} %copy-done.4, f32[384]{0:T(512)S(1)} %add_rsqrt_fusion, f32[640]{0:T(1024)S(1)} %copy-done.5, bf16[96,5120]{1,0:T(8,128)(2,1)} %collective-permute-done.2, bf16[96,5120]{1,0:T(8,128)(2,1)S(1)} %collective-permute-done.1, ...), kind=kOutput, calls=%fused_computation.18 | convolution fusion | flops 2538455040 | bytes 11493376 | tf_op jit(solution)/shard_map/dot_general | solution.py:112
  55.6 2.5 %fusion.8 = f32[384,256]{1,0:T(8,128)S(1)} fusion(bf16[5120,128]{1,0:T(8,128)(2,1)S(1)} %copy-done.2, bf16[5120,128]{1,0:T(8,128)(2,1)S(1)} %copy-done.3, f32[5120]{0:T(1024)S(1)} %copy-done.4, f32[384]{0:T(512)S(1)} %add_rsqrt_fusion, f32[256]{0:T(256)S(1)} %pad_maximum_fusion.5, bf16[96,5120]{1,0:T(8,128)(2,1)} %collective-permute-done.2, ...), kind=kOutput, calls=%fused_computation.22 | convolution fusion | flops 1033601024 | bytes 6969856 | tf_op jit(solution)/shard_map/dot_general | solution.py:114
  58.2 1.5 %copy.35 = f32[384,640]{0,1:T(8,128)S(1)} copy(f32[384,640]{1,0:T(8,128)} %convolution_add_fusion) | data formatting | bytes 1966080 | tf_op jit(solution)/shard_map/optimization_barrier | solution.py:120
  59.7 0.8 fusion.45
  60.7 0.1 copy.38
  60.8 0.1 copy.37
  60.9 0.1 subtract_convert_fusion
  61.1 0.6 convolution_convert_fusion
  61.8 0.4 collective-permute-start.10
  62.1 0.4 select_reduce_fusion
  62.5 2.7 %collective-permute-start.16 = (bf16[48,896]{1,0:T(8,128)(2,1)S(1)}, bf16[48,896]{1,0:T(8,128)(2,1)S(1)}, u32[]{:S(2)}, u32[]{:S(2)}) collective-permute-start(bf16[48,896]{1,0:T(8,128)(2,1)S(1)} %get-tuple-element.28), channel_id=1, source_target_pairs={{0,28},{4,0},{8,4},{12,8},{16,12},{20,16},{24,20},{28,24},{1,29},{... | collective-permute-start | bytes 258056 | tf_op jit(solution)/shard_map/ppermute | solution.py:239
  65.3 3.9 %collective-permute-start.14 = (bf16[48,896]{1,0:T(8,128)(2,1)S(1)}, bf16[48,896]{1,0:T(8,128)(2,1)S(1)}, u32[]{:S(2)}, u32[]{:S(2)}) collective-permute-start(bf16[48,896]{1,0:T(8,128)(2,1)S(1)} %get-tuple-element.30), channel_id=1, source_target_pairs={{0,20},{4,24},{8,28},{12,0},{16,4},{20,8},{24,12},{28,16},{1,21},{... | collective-permute-start | bytes 258056 | tf_op jit(solution)/shard_map/ppermute | solution.py:239
  69.2 2.0 %collective-permute-start.11 = (bf16[48,896]{1,0:T(8,128)(2,1)S(1)}, bf16[48,896]{1,0:T(8,128)(2,1)S(1)}, u32[]{:S(2)}, u32[]{:S(2)}) collective-permute-start(bf16[48,896]{1,0:T(8,128)(2,1)S(1)} %get-tuple-element.33), channel_id=1, source_target_pairs={{0,8},{4,12},{8,16},{12,20},{16,24},{20,28},{24,0},{28,4},{1,9},{5... | collective-permute-start | bytes 258056 | tf_op jit(solution)/shard_map/ppermute | solution.py:239
  71.1 11.3 %collective-permute-done.11 = bf16[48,896]{1,0:T(8,128)(2,1)S(1)} collective-permute-done((bf16[48,896]{1,0:T(8,128)(2,1)S(1)}, bf16[48,896]{1,0:T(8,128)(2,1)S(1)}, u32[]{:S(2)}, u32[]{:S(2)}) %collective-permute-start.11) | collective-permute-done | bytes 86048 | tf_op jit(solution)/shard_map/ppermute | solution.py:239
  82.4 6.3 %collective-permute-done.12 = bf16[48,896]{1,0:T(8,128)(2,1)S(1)} collective-permute-done((bf16[48,896]{1,0:T(8,128)(2,1)S(1)}, bf16[48,896]{1,0:T(8,128)(2,1)S(1)}, u32[]{:S(2)}, u32[]{:S(2)}) %collective-permute-start.12) | collective-permute-done | bytes 86048 | tf_op jit(solution)/shard_map/ppermute | solution.py:239
  88.8 0.5 convolution_convert_fusion.1
  89.3 0.2 copy.39
  89.5 0.2 fusion.99
  89.8 0.2 convolution_convert_fusion.3
  90.0 0.2 copy.43
  90.2 0.2 fusion.98
  90.4 0.1 fusion.29
  90.6 0.3 convolution_convert_fusion.2
  90.9 4.2 %fusion.101 = f32[128,5120]{1,0:T(8,128)S(1)} fusion(bf16[128,640]{0,1:T(8,128)(2,1)S(1)} %bitcast.163, bf16[640,5120]{1,0:T(8,128)(2,1)} %param.24), kind=kOutput, calls=%fused_computation.254 | convolution fusion | flops 838860800 | bytes 9338880 | tf_op jit(solution)/shard_map/dot_general | solution.py:213
  95.1 0.1 select_bitcast_fusion.2
  95.3 1.3 pad_maximum_fusion.2
  96.6 1.2 fusion.100
  97.9 0.1 select_bitcast_fusion.5
  98.0 1.2 pad_maximum_fusion.1
  99.2 0.5 collective-permute-start.17
  99.7 0.3 collective-permute-done.19
  100.0 2.3 %select_bitcast_fusion = (f32[1,128,1280]{2,1,0:T(8,128)S(1)}, f32[128,1280]{1,0:T(8,128)S(1)}, f32[128,1280]{1,0:T(8,128)S(1)}) fusion(pred[]{:T(512)S(6)} %eq.144, f32[2,128,1280]{2,1,0:T(8,128)} %collective-permute-done.19, f32[128,5120]{1,0:T(8,128)} %copy-done, pred[]{:T(512)S(6)} %eq.145), kind=kLoop, calls=%fused_computation.49 | loop fusion | flops 819200 | bytes 5898242 | tf_op jit(solution)/shard_map/stack | solution.py:255
  102.3 1.6 %collective-permute-start.20 = (f32[1,128,1280]{2,1,0:T(8,128)S(1)}, f32[1,128,1280]{2,1,0:T(8,128)S(1)}, u32[]{:S(2)}, u32[]{:S(2)}) collective-permute-start(f32[1,128,1280]{2,1,0:T(8,128)S(1)} %get-tuple-element.15), channel_id=1, source_target_pairs={{0,2},{1,3},{2,0},{3,1},{4,6},{5,7},{6,4},{7,5},{8,10},{9,11},{10,... | collective-permute-start | bytes 1966088 | tf_op jit(solution)/shard_map/ppermute | solution.py:257
  103.8 1.5 %select_bitcast_fusion.3 = (f32[1,128,1280]{2,1,0:T(8,128)S(1)}, f32[128,1280]{1,0:T(8,128)S(1)}, f32[128,1280]{1,0:T(8,128)S(1)}) fusion(pred[]{:T(512)S(6)} %eq.144, f32[2,128,1280]{2,1,0:T(8,128)} %collective-permute-done.17, f32[128,5120]{1,0:T(8,128)S(1)} %fusion.100, pred[]{:T(512)S(6)} %eq.145), kind=kLoop, calls=%fused_computation.54 | loop fusion | flops 819200 | bytes 5898242 | tf_op jit(solution)/shard_map/stack | solution.py:255
  105.3 0.6 collective-permute-start.18
  105.9 14.0 %collective-permute-done.20 = f32[1,128,1280]{2,1,0:T(8,128)S(1)} collective-permute-done((f32[1,128,1280]{2,1,0:T(8,128)S(1)}, f32[1,128,1280]{2,1,0:T(8,128)S(1)}, u32[]{:S(2)}, u32[]{:S(2)}) %collective-permute-start.20) | collective-permute-done | bytes 655392 | tf_op jit(solution)/shard_map/ppermute | solution.py:257
  120.0 13.1 %collective-permute-done.18 = f32[1,128,1280]{2,1,0:T(8,128)S(1)} collective-permute-done((f32[1,128,1280]{2,1,0:T(8,128)S(1)}, f32[1,128,1280]{2,1,0:T(8,128)S(1)}, u32[]{:S(2)}, u32[]{:S(2)}) %collective-permute-start.18) | collective-permute-done | bytes 655392 | tf_op jit(solution)/shard_map/ppermute | solution.py:257
  133.1 0.1 fusion.28
  133.3 0.9 pad_maximum_fusion.3
  (103 shorter events, 2.3 us)
Async XLA Ops:
  0.0 48.0 %copy-start.1 = (bf16[96,5120]{1,0:T(8,128)(2,1)S(1)}, bf16[96,5120]{1,0:T(8,128)(2,1)}, u32[]{:S(2)}) copy-start(bf16[96,5120]{1,0:T(8,128)(2,1)} %param.14) | copy-start | bytes 2949124
  0.0 48.0 %copy-start.4 = (f32[5120]{0:T(1024)S(1)}, f32[5120]{0:T(1024)}, u32[]{:S(2)}) copy-start(f32[5120]{0:T(1024)} %param.17) | copy-start | bytes 61444
  0.0 48.0 %copy-start.5 = (f32[640]{0:T(1024)S(1)}, f32[640]{0:T(1024)}, u32[]{:S(2)}) copy-start(f32[640]{0:T(1024)} %param.19) | copy-start | bytes 7684
  0.0 24.1 %collective-permute-start.8 = (s32[1,8]{1,0:T(1,128)}, s32[1,8]{1,0:T(1,128)S(1)}, u32[]{:S(2)}, u32[]{:S(2)}) collective-permute-start(s32[1,8]{1,0:T(1,128)} %param.16), channel_id=1, source_target_pairs={{0,24},{4,28},{8,0},{12,4},{16,8},{20,12},{24,16},{28,20},{1,25},{... | collective-permute-start | bytes 104 | tf_op jit(solution)/shard_map/ppermute | solution.py:223
  0.5 23.6 %collective-permute-start.7 = (s32[1,8]{1,0:T(1,128)}, s32[1,8]{1,0:T(1,128)S(1)}, u32[]{:S(2)}, u32[]{:S(2)}) collective-permute-start(s32[1,8]{1,0:T(1,128)} %param.16), channel_id=1, source_target_pairs={{0,20},{4,24},{8,28},{12,0},{16,4},{20,8},{24,12},{28,16},{1,21},{... | collective-permute-start | bytes 104 | tf_op jit(solution)/shard_map/ppermute | solution.py:223
  5.0 19.1 %collective-permute-start.6 = (s32[1,8]{1,0:T(1,128)}, s32[1,8]{1,0:T(1,128)S(1)}, u32[]{:S(2)}, u32[]{:S(2)}) collective-permute-start(s32[1,8]{1,0:T(1,128)} %param.16), channel_id=1, source_target_pairs={{0,16},{4,20},{8,24},{12,28},{16,0},{20,4},{24,8},{28,12},{1,17},{... | collective-permute-start | bytes 104 | tf_op jit(solution)/shard_map/ppermute | solution.py:223
  5.0 18.6 %collective-permute-start.5 = (s32[1,8]{1,0:T(1,128)}, s32[1,8]{1,0:T(1,128)S(1)}, u32[]{:S(2)}, u32[]{:S(2)}) collective-permute-start(s32[1,8]{1,0:T(1,128)} %param.16), channel_id=1, source_target_pairs={{0,12},{4,16},{8,20},{12,24},{16,28},{20,0},{24,4},{28,8},{1,13},{... | collective-permute-start | bytes 104 | tf_op jit(solution)/shard_map/ppermute | solution.py:223
  6.9 11.4 %collective-permute-start.3 = (s32[1,8]{1,0:T(1,128)}, s32[1,8]{1,0:T(1,128)S(1)}, u32[]{:S(2)}, u32[]{:S(2)}) collective-permute-start(s32[1,8]{1,0:T(1,128)} %param.16), channel_id=1, source_target_pairs={{0,4},{4,8},{8,12},{12,16},{16,20},{20,24},{24,28},{28,0},{1,5},{5... | collective-permute-start | bytes 104 | tf_op jit(solution)/shard_map/ppermute | solution.py:223
  18.3 3.7 %collective-permute-start.4 = (s32[1,8]{1,0:T(1,128)}, s32[1,8]{1,0:T(1,128)S(1)}, u32[]{:S(2)}, u32[]{:S(2)}) collective-permute-start(s32[1,8]{1,0:T(1,128)} %param.16), channel_id=1, source_target_pairs={{0,8},{4,12},{8,16},{12,20},{16,24},{20,28},{24,0},{28,4},{1,9},{5... | collective-permute-start | bytes 104 | tf_op jit(solution)/shard_map/ppermute | solution.py:223
  22.0 21.2 %collective-permute-start = (bf16[96,5120]{1,0:T(8,128)(2,1)}, bf16[96,5120]{1,0:T(8,128)(2,1)S(1)}, u32[]{:S(2)}, u32[]{:S(2)}) collective-permute-start(bf16[96,5120]{1,0:T(8,128)(2,1)} %param.14), channel_id=1, source_target_pairs={{0,2},{1,3},{2,0},{3,1},{4,6},{5,7},{6,4},{7,5},{8,10},{9,11},{10,... | collective-permute-start | bytes 2949128 | tf_op jit(solution)/shard_map/ppermute | solution.py:286
  23.5 19.7 %collective-permute-start.9 = (s32[1,8]{1,0:T(1,128)}, s32[1,8]{1,0:T(1,128)S(1)}, u32[]{:S(2)}, u32[]{:S(2)}) collective-permute-start(s32[1,8]{1,0:T(1,128)} %param.16), channel_id=1, source_target_pairs={{0,28},{4,0},{8,4},{12,8},{16,12},{20,16},{24,20},{28,24},{1,29},{... | collective-permute-start | bytes 104 | tf_op jit(solution)/shard_map/ppermute | solution.py:223
  24.1 20.5 %collective-permute-start.1 = (bf16[96,5120]{1,0:T(8,128)(2,1)}, bf16[96,5120]{1,0:T(8,128)(2,1)S(1)}, u32[]{:S(2)}, u32[]{:S(2)}) collective-permute-start(bf16[96,5120]{1,0:T(8,128)(2,1)} %param.14), channel_id=1, source_target_pairs={{0,1},{1,0},{2,3},{3,2},{4,5},{5,4},{6,7},{7,6},{8,9},{9,8},{10,11... | collective-permute-start | bytes 2949128 | tf_op jit(solution)/shard_map/ppermute | solution.py:286
  43.2 2.7 %collective-permute-start.2 = (bf16[96,5120]{1,0:T(8,128)(2,1)S(1)}, bf16[96,5120]{1,0:T(8,128)(2,1)}, u32[]{:S(2)}, u32[]{:S(2)}) collective-permute-start(bf16[96,5120]{1,0:T(8,128)(2,1)S(1)} %collective-permute-done), channel_id=1, source_target_pairs={{0,1},{1,0},{2,3},{3,2},{4,5},{5,4},{6,7},{7,6},{8,9},{9,8},{10,11... | collective-permute-start | bytes 2949128 | tf_op jit(solution)/shard_map/ppermute | solution.py:286
  48.0 7.6 %copy-start.2 = (bf16[5120,128]{1,0:T(8,128)(2,1)S(1)}, bf16[5120,128]{1,0:T(8,128)(2,1)}, u32[]{:S(2)}) copy-start(bf16[5120,128]{1,0:T(8,128)(2,1)} %param.22) | copy-start | bytes 3932164
  48.1 7.6 %copy-start.3 = (bf16[5120,128]{1,0:T(8,128)(2,1)S(1)}, bf16[5120,128]{1,0:T(8,128)(2,1)}, u32[]{:S(2)}) copy-start(bf16[5120,128]{1,0:T(8,128)(2,1)} %param.20) | copy-start | bytes 3932164
  61.8 7.4 %collective-permute-start.10 = (bf16[48,896]{1,0:T(8,128)(2,1)S(1)}, bf16[48,896]{1,0:T(8,128)(2,1)S(1)}, u32[]{:S(2)}, u32[]{:S(2)}) collective-permute-start(bf16[48,896]{1,0:T(8,128)(2,1)S(1)} %get-tuple-element.34), channel_id=1, source_target_pairs={{0,4},{4,8},{8,12},{12,16},{16,20},{20,24},{24,28},{28,0},{1,5},{5... | collective-permute-start | bytes 258056 | tf_op jit(solution)/shard_map/ppermute | solution.py:239
  62.5 26.2 %collective-permute-start.16 = (bf16[48,896]{1,0:T(8,128)(2,1)S(1)}, bf16[48,896]{1,0:T(8,128)(2,1)S(1)}, u32[]{:S(2)}, u32[]{:S(2)}) collective-permute-start(bf16[48,896]{1,0:T(8,128)(2,1)S(1)} %get-tuple-element.28), channel_id=1, source_target_pairs={{0,28},{4,0},{8,4},{12,8},{16,12},{20,16},{24,20},{28,24},{1,29},{... | collective-permute-start | bytes 258056 | tf_op jit(solution)/shard_map/ppermute | solution.py:239
  65.2 23.6 %collective-permute-start.15 = (bf16[48,896]{1,0:T(8,128)(2,1)S(1)}, bf16[48,896]{1,0:T(8,128)(2,1)S(1)}, u32[]{:S(2)}, u32[]{:S(2)}) collective-permute-start(bf16[48,896]{1,0:T(8,128)(2,1)S(1)} %get-tuple-element.29), channel_id=1, source_target_pairs={{0,24},{4,28},{8,0},{12,4},{16,8},{20,12},{24,16},{28,20},{1,25},{... | collective-permute-start | bytes 258056 | tf_op jit(solution)/shard_map/ppermute | solution.py:239
  65.3 23.5 %collective-permute-start.14 = (bf16[48,896]{1,0:T(8,128)(2,1)S(1)}, bf16[48,896]{1,0:T(8,128)(2,1)S(1)}, u32[]{:S(2)}, u32[]{:S(2)}) collective-permute-start(bf16[48,896]{1,0:T(8,128)(2,1)S(1)} %get-tuple-element.30), channel_id=1, source_target_pairs={{0,20},{4,24},{8,28},{12,0},{16,4},{20,8},{24,12},{28,16},{1,21},{... | collective-permute-start | bytes 258056 | tf_op jit(solution)/shard_map/ppermute | solution.py:239
  69.2 19.6 %collective-permute-start.13 = (bf16[48,896]{1,0:T(8,128)(2,1)S(1)}, bf16[48,896]{1,0:T(8,128)(2,1)S(1)}, u32[]{:S(2)}, u32[]{:S(2)}) collective-permute-start(bf16[48,896]{1,0:T(8,128)(2,1)S(1)} %get-tuple-element.31), channel_id=1, source_target_pairs={{0,16},{4,20},{8,24},{12,28},{16,0},{20,4},{24,8},{28,12},{1,17},{... | collective-permute-start | bytes 258056 | tf_op jit(solution)/shard_map/ppermute | solution.py:239
  69.2 13.2 %collective-permute-start.11 = (bf16[48,896]{1,0:T(8,128)(2,1)S(1)}, bf16[48,896]{1,0:T(8,128)(2,1)S(1)}, u32[]{:S(2)}, u32[]{:S(2)}) collective-permute-start(bf16[48,896]{1,0:T(8,128)(2,1)S(1)} %get-tuple-element.33), channel_id=1, source_target_pairs={{0,8},{4,12},{8,16},{12,20},{16,24},{20,28},{24,0},{28,4},{1,9},{5... | collective-permute-start | bytes 258056 | tf_op jit(solution)/shard_map/ppermute | solution.py:239
  82.4 6.3 %collective-permute-start.12 = (bf16[48,896]{1,0:T(8,128)(2,1)S(1)}, bf16[48,896]{1,0:T(8,128)(2,1)S(1)}, u32[]{:S(2)}, u32[]{:S(2)}) collective-permute-start(bf16[48,896]{1,0:T(8,128)(2,1)S(1)} %get-tuple-element.32), channel_id=1, source_target_pairs={{0,12},{4,16},{8,20},{12,24},{16,28},{20,0},{24,4},{28,8},{1,13},{... | collective-permute-start | bytes 258056 | tf_op jit(solution)/shard_map/ppermute | solution.py:239
  90.8 5.8 %slice-start = ((s8[6553600]{0:T(1024)(128)(4,1)}), s8[4194304]{0:T(1024)(128)(4,1)S(1)}, s32[]{:S(2)}) async-start(s8[6553600]{0:T(1024)(128)(4,1)} %bitcast.156), calls=%async_computation | async-start | bytes 8388608
  90.8 5.7 %slice-start.1 = ((s8[6553600]{0:T(1024)(128)(4,1)}), s8[2359296]{0:T(1024)(128)(4,1)S(1)}, s32[]{:S(2)}) async-start(s8[6553600]{0:T(1024)(128)(4,1)} %bitcast.156), calls=%async_computation.1 | async-start | bytes 4718592
  95.1 2.7 %copy-start = (f32[128,5120]{1,0:T(8,128)}, f32[128,5120]{1,0:T(8,128)S(1)}, u32[]{:S(2)}) copy-start(f32[128,5120]{1,0:T(8,128)S(1)} %fusion.101) | copy-start | bytes 7864324
  96.6 3.4 %collective-permute-start.19 = (f32[2,128,1280]{2,1,0:T(8,128)}, f32[2,128,1280]{2,1,0:T(8,128)}, u32[]{:S(2)}, u32[]{:S(2)}) collective-permute-start(f32[2,128,1280]{2,1,0:T(8,128)} %pad_maximum_fusion.2), channel_id=1, source_target_pairs={{0,1},{1,0},{2,3},{3,2},{4,5},{5,4},{6,7},{7,6},{8,9},{9,8},{10,11... | collective-permute-start | bytes 3932168 | tf_op jit(solution)/shard_map/ppermute | solution.py:257
  99.2 4.7 %collective-permute-start.17 = (f32[2,128,1280]{2,1,0:T(8,128)}, f32[2,128,1280]{2,1,0:T(8,128)}, u32[]{:S(2)}, u32[]{:S(2)}) collective-permute-start(f32[2,128,1280]{2,1,0:T(8,128)} %pad_maximum_fusion.1), channel_id=1, source_target_pairs={{0,1},{1,0},{2,3},{3,2},{4,5},{5,4},{6,7},{7,6},{8,9},{9,8},{10,11... | collective-permute-start | bytes 3932168 | tf_op jit(solution)/shard_map/ppermute | solution.py:257
  102.3 17.6 %collective-permute-start.20 = (f32[1,128,1280]{2,1,0:T(8,128)S(1)}, f32[1,128,1280]{2,1,0:T(8,128)S(1)}, u32[]{:S(2)}, u32[]{:S(2)}) collective-permute-start(f32[1,128,1280]{2,1,0:T(8,128)S(1)} %get-tuple-element.15), channel_id=1, source_target_pairs={{0,2},{1,3},{2,0},{3,1},{4,6},{5,7},{6,4},{7,5},{8,10},{9,11},{10,... | collective-permute-start | bytes 1966088 | tf_op jit(solution)/shard_map/ppermute | solution.py:257
  105.3 27.8 %collective-permute-start.18 = (f32[1,128,1280]{2,1,0:T(8,128)S(1)}, f32[1,128,1280]{2,1,0:T(8,128)S(1)}, u32[]{:S(2)}, u32[]{:S(2)}) collective-permute-start(f32[1,128,1280]{2,1,0:T(8,128)S(1)} %get-tuple-element.12), channel_id=1, source_target_pairs={{0,2},{1,3},{2,0},{3,1},{4,6},{5,7},{6,4},{7,5},{8,10},{9,11},{10,... | collective-permute-start | bytes 1966088 | tf_op jit(solution)/shard_map/ppermute | solution.py:257

commit v18 on v15

--- a/solution.py
+++ b/solution.py
@@ -283,7 +283,11 @@
     pieces, masks = [part], [0]
     for stage in reversed(range(bits)):
         pairs = [(i, i ^ (1 << stage)) for i in range(count)]
-        pieces = pieces + [lax.ppermute(p, axis_name, pairs) for p in pieces]
+        sent = pieces
+        if stage == bits - 1 and part.shape[0] % 16 == 0:
+            half = part.shape[0] // 2
+            sent = [part[:half], part[half:]]
+        pieces = pieces + [lax.ppermute(p, axis_name, pairs) for p in sent]
         masks = masks + [m ^ (1 << stage) for m in masks]
     return pieces, me ^ jnp.asarray(masks, dtype=jnp.int32)
 

time: 109 us -> 127 us (1.17)
  waiting for transfers between devices: 31.9 us -> 53.4 us
  local copies, waits for them, and re-layouts: 6.64 us -> 12 us
  starting transfers between devices: 34.2 us -> 30.3 us
  matrix products: 21.3 us -> 18.2 us
  other arithmetic: 12.5 us -> 10.8 us
    ppermute x3 -> x5, waiting for transfers between devices: 0.01 us -> 19.9 us  [xor_gather(): pieces = pieces + [lax.ppermute(p, axis_name, pairs) for p in sent]]
    unnamed x28 -> x43, local copies, waits for them, and re-layouts: 0.88 us -> 6.09 us
    ppermute x7, waiting for transfers between devices: 3.61 us -> 7.54 us  [exchange(): arrived.append(lax.ppermute(chunks[shift], axis_name, pairs))]
    ppermute x7, starting transfers between devices: 12.1 us -> 8.83 us  [exchange(): arrived.append(lax.ppermute(chunks[shift], axis_name, pairs))]
    ppermute x7, waiting for transfers between devices: 2.04 us -> 0.08 us  [shift_gather(): lax.ppermute(part, axis_name, [(i, (i + shift) % count) for i in range(co...]
    dot_general x1, matrix products: 7.56 us -> 5.71 us  [project(): jnp.dot(normalized_input, w_query, preferred_element_type=jnp.float32)]
    ppermute x7, starting transfers between devices: 12.5 us -> 13.8 us  [shift_gather(): lax.ppermute(part, axis_name, [(i, (i + shift) % count) for i in range(co...]
    ppermute x3 -> x5, starting transfers between devices: 3.01 us -> 2.03 us  [xor_gather(): pieces = pieces + [lax.ppermute(p, axis_name, pairs) for p in sent]]
  transfers between devices with their start and end apart: 25 -> 27, of which waited for: 9 -> 10; matrix products, arithmetic and copies ran while one was open for 17% -> 17% of each run, Pallas kernels for 0% -> 0%
where the time goes in v18:
time: 127 us; the launch traced here: 125 us
  waiting for transfers between devices  53.4 us (42%)
  starting transfers between devices  30.3 us (24%)
  matrix products  18.2 us (14%)
  local copies, waits for them, and re-layouts  12 us (9%)
  other arithmetic  10.8 us (9%)
    ppermute x8, waiting for transfers between devices, halving_scatter(): got = lax.ppermute(send, axis_name, pairs)  25.9 us
    ppermute x5, waiting for transfers between devices, xor_gather(): pieces = pieces + [lax.ppermute(p, axis_name, pairs) for p in sent]  19.9 us
    ppermute x7, starting transfers between devices, shift_gather(): lax.ppermute(part, axis_name, [(i, (i + shift) % count) for i in range(co...  13.8 us
    ppermute x7, starting transfers between devices, exchange(): arrived.append(lax.ppermute(chunks[shift], axis_name, pairs))  8.83 us
    dot_general x4, matrix products, local(): jnp.dot(mixed_heads, w_out, preferred_element_type=jnp.float32)  8.09 us
    ppermute x7, waiting for transfers between devices, exchange(): arrived.append(lax.ppermute(chunks[shift], axis_name, pairs))  7.54 us
    unnamed x43, local copies, waits for them, and re-layouts  6.09 us
    dot_general x1, matrix products, project(): jnp.dot(normalized_input, w_query, preferred_element_type=jnp.float32)  5.71 us
  transfers between devices with their start and end apart: 27, of which 10 were waited for; matrix products, arithmetic and copies ran while one was open for 17% of the time, Pallas kernels for 0%

profile of v18, /device:TPU:0, one launch (start us, length us, event | category | flops | bytes accessed | tf_op | source)
XLA Modules:
  0.0 125.5 jit_solution(2935628537792670869)
XLA Ops:
  0.0 3.0 %collective-permute-start.5 = (s32[1,8]{1,0:T(1,128)}, s32[1,8]{1,0:T(1,128)S(1)}, u32[]{:S(2)}, u32[]{:S(2)}) collective-permute-start(s32[1,8]{1,0:T(1,128)} %param.16), channel_id=1, source_target_pairs={{0,4},{4,8},{8,12},{12,16},{16,20},{20,24},{24,28},{28,0},{1,5},{5... | collective-permute-start | bytes 104 | tf_op jit(solution)/shard_map/ppermute | solution.py:223
  3.0 1.6 %collective-permute-start.6 = (s32[1,8]{1,0:T(1,128)}, s32[1,8]{1,0:T(1,128)S(1)}, u32[]{:S(2)}, u32[]{:S(2)}) collective-permute-start(s32[1,8]{1,0:T(1,128)} %param.16), channel_id=1, source_target_pairs={{0,8},{4,12},{8,16},{12,20},{16,24},{20,28},{24,0},{28,4},{1,9},{5... | collective-permute-start | bytes 104 | tf_op jit(solution)/shard_map/ppermute | solution.py:223
  4.6 2.5 %collective-permute-start.7 = (s32[1,8]{1,0:T(1,128)}, s32[1,8]{1,0:T(1,128)S(1)}, u32[]{:S(2)}, u32[]{:S(2)}) collective-permute-start(s32[1,8]{1,0:T(1,128)} %param.16), channel_id=1, source_target_pairs={{0,12},{4,16},{8,20},{12,24},{16,28},{20,0},{24,4},{28,8},{1,13},{... | collective-permute-start | bytes 104 | tf_op jit(solution)/shard_map/ppermute | solution.py:223
  7.2 1.2 collective-permute-start.8
  8.4 2.2 %constant_dynamic-update-slice_fusion.5 = bf16[384,5120]{1,0:T(8,128)(2,1)} fusion(bf16[96,5120]{1,0:T(8,128)(2,1)} %param.14), kind=kLoop, calls=%fused_computation.164 | loop fusion | bytes 1966080
  10.6 1.2 fusion.137
  12.6 0.9 reduce-window.30
  13.5 0.2 slice_reduce_fusion
  14.0 0.6 gather_fusion.2
  14.5 0.6 gather_fusion.1
  15.5 0.9 reduce-window.21
  17.2 2.7 %collective-permute-start.9 = (s32[1,8]{1,0:T(1,128)S(1)}, s32[1,8]{1,0:T(1,128)S(1)}, u32[]{:S(2)}, u32[]{:S(2)}) collective-permute-start(s32[1,8]{1,0:T(1,128)S(1)} %copy-done.9), channel_id=1, source_target_pairs={{0,20},{4,24},{8,28},{12,0},{16,4},{20,8},{24,12},{28,16},{1,21},{... | collective-permute-start | bytes 104 | tf_op jit(solution)/shard_map/ppermute | solution.py:223
  19.9 1.3 %collective-permute-start.10 = (s32[1,8]{1,0:T(1,128)S(1)}, s32[1,8]{1,0:T(1,128)S(1)}, u32[]{:S(2)}, u32[]{:S(2)}) collective-permute-start(s32[1,8]{1,0:T(1,128)S(1)} %copy-done.9), channel_id=1, source_target_pairs={{0,24},{4,28},{8,0},{12,4},{16,8},{20,12},{24,16},{28,20},{1,25},{... | collective-permute-start | bytes 104 | tf_op jit(solution)/shard_map/ppermute | solution.py:223
  21.3 1.4 %collective-permute-start.11 = (s32[1,8]{1,0:T(1,128)S(1)}, s32[1,8]{1,0:T(1,128)S(1)}, u32[]{:S(2)}, u32[]{:S(2)}) collective-permute-start(s32[1,8]{1,0:T(1,128)S(1)} %copy-done.9), channel_id=1, source_target_pairs={{0,28},{4,0},{8,4},{12,8},{16,12},{20,16},{24,20},{28,24},{1,29},{... | collective-permute-start | bytes 104 | tf_op jit(solution)/shard_map/ppermute | solution.py:223
  22.7 1.5 %collective-permute-start = (bf16[48,5120]{1,0:T(8,128)(2,1)S(1)}, bf16[48,5120]{1,0:T(8,128)(2,1)S(1)}, u32[]{:S(2)}, u32[]{:S(2)}) collective-permute-start(bf16[48,5120]{1,0:T(8,128)(2,1)S(1)} %get-tuple-element.39), channel_id=1, source_target_pairs={{0,2},{1,3},{2,0},{3,1},{4,6},{5,7},{6,4},{7,5},{8,10},{9,11},{10,... | collective-permute-start | bytes 1474568 | tf_op jit(solution)/shard_map/ppermute | solution.py:290
  24.2 0.5 collective-permute-start.1
  24.8 0.6 gather_fusion
  25.8 0.4 multiply_cosine_fusion.1
  26.2 10.7 %collective-permute-done = bf16[48,5120]{1,0:T(8,128)(2,1)S(1)} collective-permute-done((bf16[48,5120]{1,0:T(8,128)(2,1)S(1)}, bf16[48,5120]{1,0:T(8,128)(2,1)S(1)}, u32[]{:S(2)}, u32[]{:S(2)}) %collective-permute-start) | collective-permute-done | bytes 491552 | tf_op jit(solution)/shard_map/ppermute | solution.py:290
  36.9 9.2 %collective-permute-done.1 = bf16[48,5120]{1,0:T(8,128)(2,1)S(1)} collective-permute-done((bf16[48,5120]{1,0:T(8,128)(2,1)S(1)}, bf16[48,5120]{1,0:T(8,128)(2,1)S(1)}, u32[]{:S(2)}, u32[]{:S(2)}) %collective-permute-start.1) | collective-permute-done | bytes 491552 | tf_op jit(solution)/shard_map/ppermute | solution.py:290
  46.0 0.8 constant_dynamic-update-slice_fusion.4
  46.9 0.8 constant_dynamic-update-slice_fusion.3
  47.7 1.0 constant_dynamic-update-slice_fusion.2
  48.7 0.8 constant_dynamic-update-slice_fusion.1
  49.6 0.8 constant_dynamic-update-slice_fusion
  50.4 3.1 %fusion = f32[384]{0:T(512)S(1)} fusion(bf16[384,5120]{1,0:T(8,128)(2,1)} %constant_dynamic-update-slice_fusion), kind=kLoop, calls=%fused_computation.5 | loop fusion | flops 5897856 | bytes 3933696 | tf_op jit(solution)/shard_map/reduce_sum | solution.py:108
  53.7 5.7 %convolution_add_fusion = f32[384,640]{1,0:T(8,128)S(1)} fusion(bf16[5120,640]{1,0:T(8,128)(2,1)} %param.18, bf16[384,5120]{1,0:T(8,128)(2,1)S(1)} %copy-done, f32[5120]{0:T(1024)S(1)} %copy-done.7, f32[384]{0:T(512)S(1)} %add_rsqrt_fusion, f32[640]{0:T(1024)S(1)} %copy-done.8), kind=kOutput, calls=%fused_computation.15 | convolution fusion | flops 2524692480 | bytes 11493376 | tf_op jit(solution)/shard_map/dot_general | solution.py:112
  59.4 1.3 %fusion.7 = f32[384,256]{1,0:T(8,128)S(1)} fusion(bf16[5120,128]{1,0:T(8,128)(2,1)S(1)} %copy-done.5, bf16[5120,128]{1,0:T(8,128)(2,1)S(1)} %copy-done.6, bf16[384,5120]{1,0:T(8,128)(2,1)S(1)} %copy-done, f32[5120]{0:T(1024)S(1)} %copy-done.7, f32[384]{0:T(512)S(1)} %add_rsqrt_fusion, f32[256]{0:T(256)S(1)} %pad_maximum_fusion.6), kind=kOutput, calls=%fused_computation.17 | convolution fusion | flops 1019838464 | bytes 6969856 | tf_op jit(solution)/shard_map/dot_general | solution.py:114
  60.9 0.8 fusion.60
  61.9 0.3 copy.35
  62.5 0.6 convolution_convert_fusion
  63.1 0.7 collective-permute-start.12
  63.8 0.4 select_reduce_fusion
  64.2 0.7 collective-permute-start.13
  65.0 1.2 collective-permute-start.14
  66.1 3.5 %collective-permute-start.15 = (bf16[48,896]{1,0:T(8,128)(2,1)S(1)}, bf16[48,896]{1,0:T(8,128)(2,1)S(1)}, u32[]{:S(2)}, u32[]{:S(2)}) collective-permute-start(bf16[48,896]{1,0:T(8,128)(2,1)S(1)} %get-tuple-element.43), channel_id=1, source_target_pairs={{0,16},{4,20},{8,24},{12,28},{16,0},{20,4},{24,8},{28,12},{1,17},{... | collective-permute-start | bytes 258056 | tf_op jit(solution)/shard_map/ppermute | solution.py:239
  69.6 1.7 %collective-permute-done.12 = bf16[48,896]{1,0:T(8,128)(2,1)S(1)} collective-permute-done((bf16[48,896]{1,0:T(8,128)(2,1)S(1)}, bf16[48,896]{1,0:T(8,128)(2,1)S(1)}, u32[]{:S(2)}, u32[]{:S(2)}) %collective-permute-start.12) | collective-permute-done | bytes 86048 | tf_op jit(solution)/shard_map/ppermute | solution.py:239
  71.3 0.7 collective-permute-start.17
  72.0 2.0 %collective-permute-start.18 = (bf16[48,896]{1,0:T(8,128)(2,1)S(1)}, bf16[48,896]{1,0:T(8,128)(2,1)S(1)}, u32[]{:S(2)}, u32[]{:S(2)}) collective-permute-start(bf16[48,896]{1,0:T(8,128)(2,1)S(1)} %get-tuple-element.40), channel_id=1, source_target_pairs={{0,28},{4,0},{8,4},{12,8},{16,12},{20,16},{24,20},{28,24},{1,29},{... | collective-permute-start | bytes 258056 | tf_op jit(solution)/shard_map/ppermute | solution.py:239
  74.1 4.3 %collective-permute-done.14 = bf16[48,896]{1,0:T(8,128)(2,1)S(1)} collective-permute-done((bf16[48,896]{1,0:T(8,128)(2,1)S(1)}, bf16[48,896]{1,0:T(8,128)(2,1)S(1)}, u32[]{:S(2)}, u32[]{:S(2)}) %collective-permute-start.14) | collective-permute-done | bytes 86048 | tf_op jit(solution)/shard_map/ppermute | solution.py:239
  78.4 1.6 %collective-permute-done.17 = bf16[48,896]{1,0:T(8,128)(2,1)S(1)} collective-permute-done((bf16[48,896]{1,0:T(8,128)(2,1)S(1)}, bf16[48,896]{1,0:T(8,128)(2,1)S(1)}, u32[]{:S(2)}, u32[]{:S(2)}) %collective-permute-start.17) | collective-permute-done | bytes 86048 | tf_op jit(solution)/shard_map/ppermute | solution.py:239
  80.1 0.5 convolution_convert_fusion.1
  80.6 0.3 fusion.140
  81.1 0.3 fusion.21
  81.4 4.3 %fusion.61 = f32[64,5120]{1,0:T(8,128)S(1)} fusion(bf16[640,5120]{1,0:T(8,128)(2,1)} %param.24, bf16[8,8,5,128]{3,2,1,0:T(8,128)(2,1)S(1)} %bitcast.289), kind=kOutput, calls=%fused_computation.126 | convolution fusion | flops 419430400 | bytes 7946240 | tf_op jit(solution)/shard_map/dot_general | solution.py:213
  85.9 0.3 fusion.141
  86.4 0.3 fusion.20
  86.8 1.3 %fusion.64 = f32[64,5120]{1,0:T(8,128)S(1)} fusion(bf16[640,5120]{1,0:T(8,128)(2,1)S(1)} %bitcast.287, bf16[8,8,5,128]{3,2,1,0:T(8,128)(2,1)S(1)} %bitcast.290), kind=kOutput, calls=%fused_computation.129 | convolution fusion | flops 419430400 | bytes 7946240 | tf_op jit(solution)/shard_map/dot_general | solution.py:213
  88.2 0.6 collective-permute-start.23
  88.8 0.3 fusion.142
  89.3 0.3 fusion.23
  89.6 1.3 %fusion.67 = f32[64,5120]{1,0:T(8,128)S(1)} fusion(bf16[640,5120]{1,0:T(8,128)(2,1)S(1)} %bitcast.287, bf16[8,8,5,128]{3,2,1,0:T(8,128)(2,1)S(1)} %bitcast.291), kind=kOutput, calls=%fused_computation.132 | convolution fusion | flops 419430400 | bytes 7946240 | tf_op jit(solution)/shard_map/dot_general | solution.py:213
  91.4 0.2 fusion.22
  91.7 1.3 %fusion.70 = f32[64,5120]{1,0:T(8,128)S(1)} fusion(bf16[640,5120]{1,0:T(8,128)(2,1)S(1)} %bitcast.287, bf16[8,8,5,128]{3,2,1,0:T(8,128)(2,1)S(1)} %bitcast.292), kind=kOutput, calls=%fused_computation.135 | convolution fusion | flops 419430400 | bytes 7946240 | tf_op jit(solution)/shard_map/dot_general | solution.py:213
  93.1 0.6 collective-permute-start.19
  93.7 1.6 %collective-permute-start.26 = (f32[1,64,1280]{2,1,0:T(8,128)S(1)}, f32[1,64,1280]{2,1,0:T(8,128)S(1)}, u32[]{:S(2)}, u32[]{:S(2)}) collective-permute-start(f32[1,64,1280]{2,1,0:T(8,128)S(1)} %get-tuple-element.21), channel_id=1, source_target_pairs={{0,2},{1,3},{2,0},{3,1},{4,6},{5,7},{6,4},{7,5},{8,10},{9,11},{10,... | collective-permute-start | bytes 983048 | tf_op jit(solution)/shard_map/ppermute | solution.py:257
  95.4 0.6 collective-permute-start.24
  96.1 1.6 %collective-permute-start.22 = (f32[1,64,1280]{2,1,0:T(8,128)S(1)}, f32[1,64,1280]{2,1,0:T(8,128)S(1)}, u32[]{:S(2)}, u32[]{:S(2)}) collective-permute-start(f32[1,64,1280]{2,1,0:T(8,128)S(1)} %get-tuple-element.15), channel_id=1, source_target_pairs={{0,2},{1,3},{2,0},{3,1},{4,6},{5,7},{6,4},{7,5},{8,10},{9,11},{10,... | collective-permute-start | bytes 983048 | tf_op jit(solution)/shard_map/ppermute | solution.py:257
  97.8 0.6 collective-permute-start.20
  98.4 6.0 %collective-permute-done.26 = f32[1,64,1280]{2,1,0:T(8,128)S(1)} collective-permute-done((f32[1,64,1280]{2,1,0:T(8,128)S(1)}, f32[1,64,1280]{2,1,0:T(8,128)S(1)}, u32[]{:S(2)}, u32[]{:S(2)}) %collective-permute-start.26) | collective-permute-done | bytes 327712 | tf_op jit(solution)/shard_map/ppermute | solution.py:257
  104.4 7.0 %collective-permute-done.24 = f32[1,64,1280]{2,1,0:T(8,128)S(1)} collective-permute-done((f32[1,64,1280]{2,1,0:T(8,128)S(1)}, f32[1,64,1280]{2,1,0:T(8,128)S(1)}, u32[]{:S(2)}, u32[]{:S(2)}) %collective-permute-start.24) | collective-permute-done | bytes 327712 | tf_op jit(solution)/shard_map/ppermute | solution.py:257
  111.4 7.0 %collective-permute-done.22 = f32[1,64,1280]{2,1,0:T(8,128)S(1)} collective-permute-done((f32[1,64,1280]{2,1,0:T(8,128)S(1)}, f32[1,64,1280]{2,1,0:T(8,128)S(1)}, u32[]{:S(2)}, u32[]{:S(2)}) %collective-permute-start.22) | collective-permute-done | bytes 327712 | tf_op jit(solution)/shard_map/ppermute | solution.py:257
  118.5 6.0 %collective-permute-done.20 = f32[1,64,1280]{2,1,0:T(8,128)S(1)} collective-permute-done((f32[1,64,1280]{2,1,0:T(8,128)S(1)}, f32[1,64,1280]{2,1,0:T(8,128)S(1)}, u32[]{:S(2)}, u32[]{:S(2)}) %collective-permute-start.20) | collective-permute-done | bytes 327712 | tf_op jit(solution)/shard_map/ppermute | solution.py:257
  124.6 0.9 pad_maximum_fusion.4
  (156 shorter events, 5.9 us)
Async XLA Ops:
  0.0 13.9 %copy-start.4 = (s32[4]{0:T(128)S(1)}, s32[4]{0:T(128)}, u32[]{:S(2)}) copy-start(s32[4]{0:T(128)} %constant.167.clone) | copy-start | bytes 52
  0.0 11.9 %copy-start.9 = (s32[1,8]{1,0:T(1,128)S(1)}, s32[1,8]{1,0:T(1,128)}, u32[]{:S(2)}) copy-start(s32[1,8]{1,0:T(1,128)} %param.16) | copy-start | bytes 100
  0.0 11.9 %copy-start.1 = (s32[3072]{0:T(1024)S(1)}, s32[3072]{0:T(1024)}, u32[]{:S(2)}) copy-start(s32[3072]{0:T(1024)} %param.15) | copy-start | bytes 36868
  0.0 16.8 %copy-start.2 = (f32[128]{0:T(128)S(1)}, f32[128]{0:T(128)}, u32[]{:S(2)}) copy-start(f32[128]{0:T(128)} %param.23) | copy-start | bytes 1540
  0.0 16.8 %copy-start.3 = (f32[128]{0:T(128)S(1)}, f32[128]{0:T(128)}, u32[]{:S(2)}) copy-start(f32[128]{0:T(128)} %param.21) | copy-start | bytes 1540
  0.0 17.2 %collective-permute-start.5 = (s32[1,8]{1,0:T(1,128)}, s32[1,8]{1,0:T(1,128)S(1)}, u32[]{:S(2)}, u32[]{:S(2)}) collective-permute-start(s32[1,8]{1,0:T(1,128)} %param.16), channel_id=1, source_target_pairs={{0,4},{4,8},{8,12},{12,16},{16,20},{20,24},{24,28},{28,0},{1,5},{5... | collective-permute-start | bytes 104 | tf_op jit(solution)/shard_map/ppermute | solution.py:223
  3.0 16.9 %collective-permute-start.6 = (s32[1,8]{1,0:T(1,128)}, s32[1,8]{1,0:T(1,128)S(1)}, u32[]{:S(2)}, u32[]{:S(2)}) collective-permute-start(s32[1,8]{1,0:T(1,128)} %param.16), channel_id=1, source_target_pairs={{0,8},{4,12},{8,16},{12,20},{16,24},{20,28},{24,0},{28,4},{1,9},{5... | collective-permute-start | bytes 104 | tf_op jit(solution)/shard_map/ppermute | solution.py:223
  4.6 16.7 %collective-permute-start.7 = (s32[1,8]{1,0:T(1,128)}, s32[1,8]{1,0:T(1,128)S(1)}, u32[]{:S(2)}, u32[]{:S(2)}) collective-permute-start(s32[1,8]{1,0:T(1,128)} %param.16), channel_id=1, source_target_pairs={{0,12},{4,16},{8,20},{12,24},{16,28},{20,0},{24,4},{28,8},{1,13},{... | collective-permute-start | bytes 104 | tf_op jit(solution)/shard_map/ppermute | solution.py:223
  7.2 15.6 %collective-permute-start.8 = (s32[1,8]{1,0:T(1,128)}, s32[1,8]{1,0:T(1,128)S(1)}, u32[]{:S(2)}, u32[]{:S(2)}) collective-permute-start(s32[1,8]{1,0:T(1,128)} %param.16), channel_id=1, source_target_pairs={{0,16},{4,20},{8,24},{12,28},{16,0},{20,4},{24,8},{28,12},{1,17},{... | collective-permute-start | bytes 104 | tf_op jit(solution)/shard_map/ppermute | solution.py:223
  8.4 39.3 %collective-permute-start.2 = (bf16[96,5120]{1,0:T(8,128)(2,1)}, bf16[96,5120]{1,0:T(8,128)(2,1)S(1)}, u32[]{:S(2)}, u32[]{:S(2)}) collective-permute-start(bf16[96,5120]{1,0:T(8,128)(2,1)} %param.14), channel_id=1, source_target_pairs={{0,1},{1,0},{2,3},{3,2},{4,5},{5,4},{6,7},{7,6},{8,9},{9,8},{10,11... | collective-permute-start | bytes 2949128 | tf_op jit(solution)/shard_map/ppermute | solution.py:290
  17.2 7.0 %collective-permute-start.9 = (s32[1,8]{1,0:T(1,128)S(1)}, s32[1,8]{1,0:T(1,128)S(1)}, u32[]{:S(2)}, u32[]{:S(2)}) collective-permute-start(s32[1,8]{1,0:T(1,128)S(1)} %copy-done.9), channel_id=1, source_target_pairs={{0,20},{4,24},{8,28},{12,0},{16,4},{20,8},{24,12},{28,16},{1,21},{... | collective-permute-start | bytes 104 | tf_op jit(solution)/shard_map/ppermute | solution.py:223
  19.9 4.8 %collective-permute-start.10 = (s32[1,8]{1,0:T(1,128)S(1)}, s32[1,8]{1,0:T(1,128)S(1)}, u32[]{:S(2)}, u32[]{:S(2)}) collective-permute-start(s32[1,8]{1,0:T(1,128)S(1)} %copy-done.9), channel_id=1, source_target_pairs={{0,24},{4,28},{8,0},{12,4},{16,8},{20,12},{24,16},{28,20},{1,25},{... | collective-permute-start | bytes 104 | tf_op jit(solution)/shard_map/ppermute | solution.py:223
  21.3 3.5 %collective-permute-start.11 = (s32[1,8]{1,0:T(1,128)S(1)}, s32[1,8]{1,0:T(1,128)S(1)}, u32[]{:S(2)}, u32[]{:S(2)}) collective-permute-start(s32[1,8]{1,0:T(1,128)S(1)} %copy-done.9), channel_id=1, source_target_pairs={{0,28},{4,0},{8,4},{12,8},{16,12},{20,16},{24,20},{28,24},{1,29},{... | collective-permute-start | bytes 104 | tf_op jit(solution)/shard_map/ppermute | solution.py:223
  22.7 14.1 %collective-permute-start = (bf16[48,5120]{1,0:T(8,128)(2,1)S(1)}, bf16[48,5120]{1,0:T(8,128)(2,1)S(1)}, u32[]{:S(2)}, u32[]{:S(2)}) collective-permute-start(bf16[48,5120]{1,0:T(8,128)(2,1)S(1)} %get-tuple-element.39), channel_id=1, source_target_pairs={{0,2},{1,3},{2,0},{3,1},{4,6},{5,7},{6,4},{7,5},{8,10},{9,11},{10,... | collective-permute-start | bytes 1474568 | tf_op jit(solution)/shard_map/ppermute | solution.py:290
  24.2 21.8 %collective-permute-start.1 = (bf16[48,5120]{1,0:T(8,128)(2,1)S(1)}, bf16[48,5120]{1,0:T(8,128)(2,1)S(1)}, u32[]{:S(2)}, u32[]{:S(2)}) collective-permute-start(bf16[48,5120]{1,0:T(8,128)(2,1)S(1)} %get-tuple-element.38), channel_id=1, source_target_pairs={{0,2},{1,3},{2,0},{3,1},{4,6},{5,7},{6,4},{7,5},{8,10},{9,11},{10,... | collective-permute-start | bytes 1474568 | tf_op jit(solution)/shard_map/ppermute | solution.py:290
  36.8 11.9 %collective-permute-start.3 = (bf16[48,5120]{1,0:T(8,128)(2,1)S(1)}, bf16[48,5120]{1,0:T(8,128)(2,1)S(1)}, u32[]{:S(2)}, u32[]{:S(2)}) collective-permute-start(bf16[48,5120]{1,0:T(8,128)(2,1)S(1)} %collective-permute-done), channel_id=1, source_target_pairs={{0,1},{1,0},{2,3},{3,2},{4,5},{5,4},{6,7},{7,6},{8,9},{9,8},{10,11... | collective-permute-start | bytes 1474568 | tf_op jit(solution)/shard_map/ppermute | solution.py:290
  46.0 3.5 %collective-permute-start.4 = (bf16[48,5120]{1,0:T(8,128)(2,1)S(1)}, bf16[48,5120]{1,0:T(8,128)(2,1)S(1)}, u32[]{:S(2)}, u32[]{:S(2)}) collective-permute-start(bf16[48,5120]{1,0:T(8,128)(2,1)S(1)} %collective-permute-done.1), channel_id=1, source_target_pairs={{0,1},{1,0},{2,3},{3,2},{4,5},{5,4},{6,7},{7,6},{8,9},{9,8},{10,11... | collective-permute-start | bytes 1474568 | tf_op jit(solution)/shard_map/ppermute | solution.py:290
  47.7 5.8 %copy-start.7 = (f32[5120]{0:T(1024)S(1)}, f32[5120]{0:T(1024)}, u32[]{:S(2)}) copy-start(f32[5120]{0:T(1024)} %param.17) | copy-start | bytes 61444
  47.7 5.8 %copy-start.8 = (f32[640]{0:T(1024)S(1)}, f32[640]{0:T(1024)}, u32[]{:S(2)}) copy-start(f32[640]{0:T(1024)} %param.19) | copy-start | bytes 7684
  50.4 3.3 %copy-start = (bf16[384,5120]{1,0:T(8,128)(2,1)S(1)}, bf16[384,5120]{1,0:T(8,128)(2,1)}, u32[]{:S(2)}) copy-start(bf16[384,5120]{1,0:T(8,128)(2,1)} %constant_dynamic-update-slice_fusion) | copy-start | bytes 11796484
  53.7 5.7 %copy-start.5 = (bf16[5120,128]{1,0:T(8,128)(2,1)S(1)}, bf16[5120,128]{1,0:T(8,128)(2,1)}, u32[]{:S(2)}) copy-start(bf16[5120,128]{1,0:T(8,128)(2,1)} %param.22) | copy-start | bytes 3932164
  53.7 5.7 %copy-start.6 = (bf16[5120,128]{1,0:T(8,128)(2,1)S(1)}, bf16[5120,128]{1,0:T(8,128)(2,1)}, u32[]{:S(2)}) copy-start(bf16[5120,128]{1,0:T(8,128)(2,1)} %param.20) | copy-start | bytes 3932164
  63.1 8.2 %collective-permute-start.12 = (bf16[48,896]{1,0:T(8,128)(2,1)S(1)}, bf16[48,896]{1,0:T(8,128)(2,1)S(1)}, u32[]{:S(2)}, u32[]{:S(2)}) collective-permute-start(bf16[48,896]{1,0:T(8,128)(2,1)S(1)} %get-tuple-element.46), channel_id=1, source_target_pairs={{0,4},{4,8},{8,12},{12,16},{16,20},{20,24},{24,28},{28,0},{1,5},{5... | collective-permute-start | bytes 258056 | tf_op jit(solution)/shard_map/ppermute | solution.py:239
  64.2 7.8 %collective-permute-start.13 = (bf16[48,896]{1,0:T(8,128)(2,1)S(1)}, bf16[48,896]{1,0:T(8,128)(2,1)S(1)}, u32[]{:S(2)}, u32[]{:S(2)}) collective-permute-start(bf16[48,896]{1,0:T(8,128)(2,1)S(1)} %get-tuple-element.45), channel_id=1, source_target_pairs={{0,8},{4,12},{8,16},{12,20},{16,24},{20,28},{24,0},{28,4},{1,9},{5... | collective-permute-start | bytes 258056 | tf_op jit(solution)/shard_map/ppermute | solution.py:239
  65.0 13.4 %collective-permute-start.14 = (bf16[48,896]{1,0:T(8,128)(2,1)S(1)}, bf16[48,896]{1,0:T(8,128)(2,1)S(1)}, u32[]{:S(2)}, u32[]{:S(2)}) collective-permute-start(bf16[48,896]{1,0:T(8,128)(2,1)S(1)} %get-tuple-element.44), channel_id=1, source_target_pairs={{0,12},{4,16},{8,20},{12,24},{16,28},{20,0},{24,4},{28,8},{1,13},{... | collective-permute-start | bytes 258056 | tf_op jit(solution)/shard_map/ppermute | solution.py:239
  66.1 12.3 %collective-permute-start.15 = (bf16[48,896]{1,0:T(8,128)(2,1)S(1)}, bf16[48,896]{1,0:T(8,128)(2,1)S(1)}, u32[]{:S(2)}, u32[]{:S(2)}) collective-permute-start(bf16[48,896]{1,0:T(8,128)(2,1)S(1)} %get-tuple-element.43), channel_id=1, source_target_pairs={{0,16},{4,20},{8,24},{12,28},{16,0},{20,4},{24,8},{28,12},{1,17},{... | collective-permute-start | bytes 258056 | tf_op jit(solution)/shard_map/ppermute | solution.py:239
  69.6 8.8 %collective-permute-start.16 = (bf16[48,896]{1,0:T(8,128)(2,1)S(1)}, bf16[48,896]{1,0:T(8,128)(2,1)S(1)}, u32[]{:S(2)}, u32[]{:S(2)}) collective-permute-start(bf16[48,896]{1,0:T(8,128)(2,1)S(1)} %get-tuple-element.42), channel_id=1, source_target_pairs={{0,20},{4,24},{8,28},{12,0},{16,4},{20,8},{24,12},{28,16},{1,21},{... | collective-permute-start | bytes 258056 | tf_op jit(solution)/shard_map/ppermute | solution.py:239
  71.3 8.7 %collective-permute-start.17 = (bf16[48,896]{1,0:T(8,128)(2,1)S(1)}, bf16[48,896]{1,0:T(8,128)(2,1)S(1)}, u32[]{:S(2)}, u32[]{:S(2)}) collective-permute-start(bf16[48,896]{1,0:T(8,128)(2,1)S(1)} %get-tuple-element.41), channel_id=1, source_target_pairs={{0,24},{4,28},{8,0},{12,4},{16,8},{20,12},{24,16},{28,20},{1,25},{... | collective-permute-start | bytes 258056 | tf_op jit(solution)/shard_map/ppermute | solution.py:239
  72.0 8.0 %collective-permute-start.18 = (bf16[48,896]{1,0:T(8,128)(2,1)S(1)}, bf16[48,896]{1,0:T(8,128)(2,1)S(1)}, u32[]{:S(2)}, u32[]{:S(2)}) collective-permute-start(bf16[48,896]{1,0:T(8,128)(2,1)S(1)} %get-tuple-element.40), channel_id=1, source_target_pairs={{0,28},{4,0},{8,4},{12,8},{16,12},{20,16},{24,20},{28,24},{1,29},{... | collective-permute-start | bytes 258056 | tf_op jit(solution)/shard_map/ppermute | solution.py:239
  81.4 5.4 %slice-start = ((s8[6553600]{0:T(1024)(128)(4,1)}), s8[4194304]{0:T(1024)(128)(4,1)S(1)}, s32[]{:S(2)}) async-start(s8[6553600]{0:T(1024)(128)(4,1)} %bitcast.286), calls=%async_computation | async-start | bytes 8388608
  81.4 5.4 %slice-start.1 = ((s8[6553600]{0:T(1024)(128)(4,1)}), s8[2359296]{0:T(1024)(128)(4,1)S(1)}, s32[]{:S(2)}) async-start(s8[6553600]{0:T(1024)(128)(4,1)} %bitcast.286), calls=%async_computation.1 | async-start | bytes 4718592
  85.8 7.8 %collective-permute-start.25 = (f32[2,64,1280]{2,1,0:T(8,128)S(1)}, f32[2,64,1280]{2,1,0:T(8,128)S(1)}, u32[]{:S(2)}, u32[]{:S(2)}) collective-permute-start(f32[2,64,1280]{2,1,0:T(8,128)S(1)} %pad_maximum_fusion.3), channel_id=1, source_target_pairs={{0,1},{1,0},{2,3},{3,2},{4,5},{5,4},{6,7},{7,6},{8,9},{9,8},{10,11... | collective-permute-start | bytes 1966088 | tf_op jit(solution)/shard_map/ppermute | solution.py:257
  88.2 7.1 %collective-permute-start.23 = (f32[2,64,1280]{2,1,0:T(8,128)S(1)}, f32[2,64,1280]{2,1,0:T(8,128)S(1)}, u32[]{:S(2)}, u32[]{:S(2)}) collective-permute-start(f32[2,64,1280]{2,1,0:T(8,128)S(1)} %pad_maximum_fusion.2), channel_id=1, source_target_pairs={{0,1},{1,0},{2,3},{3,2},{4,5},{5,4},{6,7},{7,6},{8,9},{9,8},{10,11... | collective-permute-start | bytes 1966088 | tf_op jit(solution)/shard_map/ppermute | solution.py:257
  91.0 5.0 %collective-permute-start.21 = (f32[2,64,1280]{2,1,0:T(8,128)S(1)}, f32[2,64,1280]{2,1,0:T(8,128)S(1)}, u32[]{:S(2)}, u32[]{:S(2)}) collective-permute-start(f32[2,64,1280]{2,1,0:T(8,128)S(1)} %pad_maximum_fusion.1), channel_id=1, source_target_pairs={{0,1},{1,0},{2,3},{3,2},{4,5},{5,4},{6,7},{7,6},{8,9},{9,8},{10,11... | collective-permute-start | bytes 1966088 | tf_op jit(solution)/shard_map/ppermute | solution.py:257
  93.1 4.6 %collective-permute-start.19 = (f32[2,64,1280]{2,1,0:T(8,128)S(1)}, f32[2,64,1280]{2,1,0:T(8,128)S(1)}, u32[]{:S(2)}, u32[]{:S(2)}) collective-permute-start(f32[2,64,1280]{2,1,0:T(8,128)S(1)} %pad_maximum_fusion), channel_id=1, source_target_pairs={{0,1},{1,0},{2,3},{3,2},{4,5},{5,4},{6,7},{7,6},{8,9},{9,8},{10,11... | collective-permute-start | bytes 1966088 | tf_op jit(solution)/shard_map/ppermute | solution.py:257
  93.7 10.6 %collective-permute-start.26 = (f32[1,64,1280]{2,1,0:T(8,128)S(1)}, f32[1,64,1280]{2,1,0:T(8,128)S(1)}, u32[]{:S(2)}, u32[]{:S(2)}) collective-permute-start(f32[1,64,1280]{2,1,0:T(8,128)S(1)} %get-tuple-element.21), channel_id=1, source_target_pairs={{0,2},{1,3},{2,0},{3,1},{4,6},{5,7},{6,4},{7,5},{8,10},{9,11},{10,... | collective-permute-start | bytes 983048 | tf_op jit(solution)/shard_map/ppermute | solution.py:257
  95.4 16.0 %collective-permute-start.24 = (f32[1,64,1280]{2,1,0:T(8,128)S(1)}, f32[1,64,1280]{2,1,0:T(8,128)S(1)}, u32[]{:S(2)}, u32[]{:S(2)}) collective-permute-start(f32[1,64,1280]{2,1,0:T(8,128)S(1)} %get-tuple-element.18), channel_id=1, source_target_pairs={{0,2},{1,3},{2,0},{3,1},{4,6},{5,7},{6,4},{7,5},{8,10},{9,11},{10,... | collective-permute-start | bytes 983048 | tf_op jit(solution)/shard_map/ppermute | solution.py:257
  96.1 22.3 %collective-permute-start.22 = (f32[1,64,1280]{2,1,0:T(8,128)S(1)}, f32[1,64,1280]{2,1,0:T(8,128)S(1)}, u32[]{:S(2)}, u32[]{:S(2)}) collective-permute-start(f32[1,64,1280]{2,1,0:T(8,128)S(1)} %get-tuple-element.15), channel_id=1, source_target_pairs={{0,2},{1,3},{2,0},{3,1},{4,6},{5,7},{6,4},{7,5},{8,10},{9,11},{10,... | collective-permute-start | bytes 983048 | tf_op jit(solution)/shard_map/ppermute | solution.py:257
  97.8 26.7 %collective-permute-start.20 = (f32[1,64,1280]{2,1,0:T(8,128)S(1)}, f32[1,64,1280]{2,1,0:T(8,128)S(1)}, u32[]{:S(2)}, u32[]{:S(2)}) collective-permute-start(f32[1,64,1280]{2,1,0:T(8,128)S(1)} %get-tuple-element.12), channel_id=1, source_target_pairs={{0,2},{1,3},{2,0},{3,1},{4,6},{5,7},{6,4},{7,5},{8,10},{9,11},{10,... | collective-permute-start | bytes 983048 | tf_op jit(solution)/shard_map/ppermute | solution.py:257

commit v19 on v15

--- a/solution.py
+++ b/solution.py
@@ -29,10 +29,7 @@
 
 
 def select_rows(index, values):
-    picked = jnp.dot(
-        one_hot_rows(index, values.shape[0]), values, preferred_element_type=jnp.float32
-    )
-    return picked.astype(values.dtype)
+    return jnp.dot(one_hot_rows(index, values.shape[0]), values, preferred_element_type=values.dtype)
 
 
 def apply_rotary(values, sequence_starts, head_dim):
@@ -150,7 +147,7 @@
     send_hot = (
         places[None, :] == jnp.arange(ctx_count * group_cap, dtype=jnp.int32)[:, None]
     ).astype(jnp.bfloat16)
-    outgoing = jnp.dot(send_hot, qkv, preferred_element_type=jnp.float32).astype(jnp.bfloat16)
+    outgoing = jnp.dot(send_hot, qkv, preferred_element_type=jnp.bfloat16)
     arrived = exchange(outgoing, "ctx", ctx_count)
 
     mine = (pool_dest >= 0) & (pool_dest // pack_len == ctx_index)

time: 109 us -> 109 us (level)
  no operation moved by 1% of the time
where the time goes in v19:
time: 109 us; the launch traced here: 107 us
  starting transfers between devices  34.2 us (31%)
  waiting for transfers between devices  31.9 us (29%)
  matrix products  21.3 us (20%)
  other arithmetic  12.5 us (11%)
  local copies, waits for them, and re-layouts  6.64 us (6%)
    ppermute x8, waiting for transfers between devices, halving_scatter(): got = lax.ppermute(send, axis_name, pairs)  26.2 us
    ppermute x7, starting transfers between devices, shift_gather(): lax.ppermute(part, axis_name, [(i, (i + shift) % count) for i in range(co...  12.5 us
    ppermute x7, starting transfers between devices, exchange(): arrived.append(lax.ppermute(chunks[shift], axis_name, pairs))  12.1 us
    dot_general x4, matrix products, local(): jnp.dot(mixed_heads, w_out, preferred_element_type=jnp.float32)  8.08 us
    dot_general x1, matrix products, project(): jnp.dot(normalized_input, w_query, preferred_element_type=jnp.float32)  7.56 us
    ppermute x8, starting transfers between devices, halving_scatter(): got = lax.ppermute(send, axis_name, pairs)  6.54 us
    ppermute x7, waiting for transfers between devices, exchange(): arrived.append(lax.ppermute(chunks[shift], axis_name, pairs))  3.61 us
    ppermute x3, starting transfers between devices, xor_gather(): pieces = pieces + [lax.ppermute(p, axis_name, pairs) for p in pieces]  3.01 us
  transfers between devices with their start and end apart: 25, of which 9 were waited for; matrix products, arithmetic and copies ran while one was open for 17% of the time, Pallas kernels for 0%

profile of v19, /device:TPU:0, one launch (start us, length us, event | category | flops | bytes accessed | tf_op | source)
XLA Modules:
  0.0 107.1 jit_solution(9807346908216237544)
XLA Ops:
  0.0 3.0 %collective-permute-start = (bf16[96,5120]{1,0:T(8,128)(2,1)}, bf16[96,5120]{1,0:T(8,128)(2,1)S(1)}, u32[]{:S(2)}, u32[]{:S(2)}) collective-permute-start(bf16[96,5120]{1,0:T(8,128)(2,1)} %param.14), channel_id=1, source_target_pairs={{0,2},{1,3},{2,0},{3,1},{4,6},{5,7},{6,4},{7,5},{8,10},{9,11},{10,... | collective-permute-start | bytes 2949128 | tf_op jit(solution)/shard_map/ppermute | solution.py:283
  3.0 1.5 %collective-permute-start.3 = (s32[1,8]{1,0:T(1,128)}, s32[1,8]{1,0:T(1,128)S(1)}, u32[]{:S(2)}, u32[]{:S(2)}) collective-permute-start(s32[1,8]{1,0:T(1,128)} %param.16), channel_id=1, source_target_pairs={{0,4},{4,8},{8,12},{12,16},{16,20},{20,24},{24,28},{28,0},{1,5},{5... | collective-permute-start | bytes 104 | tf_op jit(solution)/shard_map/ppermute | solution.py:220
  4.5 1.6 %collective-permute-start.4 = (s32[1,8]{1,0:T(1,128)}, s32[1,8]{1,0:T(1,128)S(1)}, u32[]{:S(2)}, u32[]{:S(2)}) collective-permute-start(s32[1,8]{1,0:T(1,128)} %param.16), channel_id=1, source_target_pairs={{0,8},{4,12},{8,16},{12,20},{16,24},{20,28},{24,0},{28,4},{1,9},{5... | collective-permute-start | bytes 104 | tf_op jit(solution)/shard_map/ppermute | solution.py:220
  6.1 2.5 %collective-permute-start.5 = (s32[1,8]{1,0:T(1,128)}, s32[1,8]{1,0:T(1,128)S(1)}, u32[]{:S(2)}, u32[]{:S(2)}) collective-permute-start(s32[1,8]{1,0:T(1,128)} %param.16), channel_id=1, source_target_pairs={{0,12},{4,16},{8,20},{12,24},{16,28},{20,0},{24,4},{28,8},{1,13},{... | collective-permute-start | bytes 104 | tf_op jit(solution)/shard_map/ppermute | solution.py:220
  8.7 0.7 constant_dynamic-update-slice_fusion.7
  9.4 0.7 reshape.874
  10.3 0.8 reduce-window.32
  11.4 0.9 reduce-window.30
  12.2 0.2 slice_reduce_fusion
  12.7 0.7 compare_and_fusion.4
  13.4 0.6 gather_fusion.2
  13.9 0.6 gather_fusion.1
  14.8 0.7 subtract_select_fusion
  15.6 0.9 reduce-window.21
  16.5 0.2 slice_reduce_fusion.1
  16.9 0.7 pad_maximum_fusion.7
  18.0 1.3 %collective-permute-start.6 = (s32[1,8]{1,0:T(1,128)}, s32[1,8]{1,0:T(1,128)S(1)}, u32[]{:S(2)}, u32[]{:S(2)}) collective-permute-start(s32[1,8]{1,0:T(1,128)} %param.16), channel_id=1, source_target_pairs={{0,16},{4,20},{8,24},{12,28},{16,0},{20,4},{24,8},{28,12},{1,17},{... | collective-permute-start | bytes 104 | tf_op jit(solution)/shard_map/ppermute | solution.py:220
  19.3 2.6 %collective-permute-start.7 = (s32[1,8]{1,0:T(1,128)}, s32[1,8]{1,0:T(1,128)S(1)}, u32[]{:S(2)}, u32[]{:S(2)}) collective-permute-start(s32[1,8]{1,0:T(1,128)} %param.16), channel_id=1, source_target_pairs={{0,20},{4,24},{8,28},{12,0},{16,4},{20,8},{24,12},{28,16},{1,21},{... | collective-permute-start | bytes 104 | tf_op jit(solution)/shard_map/ppermute | solution.py:220
  22.0 1.3 %collective-permute-start.8 = (s32[1,8]{1,0:T(1,128)}, s32[1,8]{1,0:T(1,128)S(1)}, u32[]{:S(2)}, u32[]{:S(2)}) collective-permute-start(s32[1,8]{1,0:T(1,128)} %param.16), channel_id=1, source_target_pairs={{0,24},{4,28},{8,0},{12,4},{16,8},{20,12},{24,16},{28,20},{1,25},{... | collective-permute-start | bytes 104 | tf_op jit(solution)/shard_map/ppermute | solution.py:220
  23.3 1.6 %collective-permute-start.9 = (s32[1,8]{1,0:T(1,128)}, s32[1,8]{1,0:T(1,128)S(1)}, u32[]{:S(2)}, u32[]{:S(2)}) collective-permute-start(s32[1,8]{1,0:T(1,128)} %param.16), channel_id=1, source_target_pairs={{0,28},{4,0},{8,4},{12,8},{16,12},{20,16},{24,20},{28,24},{1,29},{... | collective-permute-start | bytes 104 | tf_op jit(solution)/shard_map/ppermute | solution.py:220
  25.0 0.7 collective-permute-done.8
  25.7 1.3 %collective-permute-done.9 = s32[1,8]{1,0:T(1,128)S(1)} collective-permute-done((s32[1,8]{1,0:T(1,128)}, s32[1,8]{1,0:T(1,128)S(1)}, u32[]{:S(2)}, u32[]{:S(2)}) %collective-permute-start.9) | collective-permute-done | bytes 64 | tf_op jit(solution)/shard_map/ppermute | solution.py:220
  27.0 0.6 gather_fusion
  27.9 0.4 multiply_cosine_fusion.1
  28.4 2.1 %fusion = f32[384]{0:T(512)S(1)} fusion(bf16[96,5120]{1,0:T(8,128)(2,1)} %collective-permute-done.2, bf16[96,5120]{1,0:T(8,128)(2,1)S(1)} %collective-permute-done.1, bf16[96,5120]{1,0:T(8,128)(2,1)S(1)} %collective-permute-done, bf16[96,5120]{1,0:T(8,128)(2,1)} %param.14), kind=kLoop, calls=%fused_computation.5 | loop fusion | flops 19660416 | bytes 3933696 | tf_op jit(solution)/shard_map/reduce_sum | solution.py:105
  30.6 7.6 %convolution_add_fusion = f32[384,640]{1,0:T(8,128)} fusion(bf16[5120,640]{1,0:T(8,128)(2,1)} %param.18, f32[5120]{0:T(1024)S(1)} %copy-done.3, f32[384]{0:T(512)S(1)} %add_rsqrt_fusion, f32[640]{0:T(1024)S(1)} %copy-done.4, bf16[96,5120]{1,0:T(8,128)(2,1)} %collective-permute-done.2, bf16[96,5120]{1,0:T(8,128)(2,1)S(1)} %collective-permute-done.1, ...), kind=kOutput, calls=%fused_computation.15 | convolution fusion | flops 2538455040 | bytes 11493376 | tf_op jit(solution)/shard_map/dot_general | solution.py:109
  38.1 2.5 %fusion.7 = f32[384,256]{1,0:T(8,128)S(1)} fusion(bf16[5120,128]{1,0:T(8,128)(2,1)S(1)} %copy-done.1, bf16[5120,128]{1,0:T(8,128)(2,1)S(1)} %copy-done.2, f32[5120]{0:T(1024)S(1)} %copy-done.3, f32[384]{0:T(512)S(1)} %add_rsqrt_fusion, f32[256]{0:T(256)S(1)} %pad_maximum_fusion.7, bf16[96,5120]{1,0:T(8,128)(2,1)} %collective-permute-done.2, ...), kind=kOutput, calls=%fused_computation.16 | convolution fusion | flops 1033601024 | bytes 6969856 | tf_op jit(solution)/shard_map/dot_general | solution.py:111
  40.8 0.8 fusion.62
  41.8 1.5 %copy.35 = f32[384,640]{0,1:T(8,128)S(1)} copy(f32[384,640]{1,0:T(8,128)} %convolution_add_fusion) | data formatting | bytes 1966080 | tf_op jit(solution)/shard_map/optimization_barrier | solution.py:117
  43.6 0.6 fusion.24
  44.2 1.8 %collective-permute-start.10 = (bf16[48,896]{1,0:T(8,128)(2,1)S(1)}, bf16[48,896]{1,0:T(8,128)(2,1)S(1)}, u32[]{:S(2)}, u32[]{:S(2)}) collective-permute-start(bf16[48,896]{1,0:T(8,128)(2,1)S(1)} %get-tuple-element.44), channel_id=1, source_target_pairs={{0,4},{4,8},{8,12},{12,16},{16,20},{20,24},{24,28},{28,0},{1,5},{5... | collective-permute-start | bytes 258056 | tf_op jit(solution)/shard_map/ppermute | solution.py:236
  46.0 0.4 select_reduce_fusion
  46.4 1.0 collective-permute-start.11
  47.4 2.5 %collective-permute-start.12 = (bf16[48,896]{1,0:T(8,128)(2,1)S(1)}, bf16[48,896]{1,0:T(8,128)(2,1)S(1)}, u32[]{:S(2)}, u32[]{:S(2)}) collective-permute-start(bf16[48,896]{1,0:T(8,128)(2,1)S(1)} %get-tuple-element.42), channel_id=1, source_target_pairs={{0,12},{4,16},{8,20},{12,24},{16,28},{20,0},{24,4},{28,8},{1,13},{... | collective-permute-start | bytes 258056 | tf_op jit(solution)/shard_map/ppermute | solution.py:236
  49.9 1.2 %collective-permute-start.13 = (bf16[48,896]{1,0:T(8,128)(2,1)S(1)}, bf16[48,896]{1,0:T(8,128)(2,1)S(1)}, u32[]{:S(2)}, u32[]{:S(2)}) collective-permute-start(bf16[48,896]{1,0:T(8,128)(2,1)S(1)} %get-tuple-element.41), channel_id=1, source_target_pairs={{0,16},{4,20},{8,24},{12,28},{16,0},{20,4},{24,8},{28,12},{1,17},{... | collective-permute-start | bytes 258056 | tf_op jit(solution)/shard_map/ppermute | solution.py:236
  51.2 2.9 %collective-permute-start.14 = (bf16[48,896]{1,0:T(8,128)(2,1)S(1)}, bf16[48,896]{1,0:T(8,128)(2,1)S(1)}, u32[]{:S(2)}, u32[]{:S(2)}) collective-permute-start(bf16[48,896]{1,0:T(8,128)(2,1)S(1)} %get-tuple-element.40), channel_id=1, source_target_pairs={{0,20},{4,24},{8,28},{12,0},{16,4},{20,8},{24,12},{28,16},{1,21},{... | collective-permute-start | bytes 258056 | tf_op jit(solution)/shard_map/ppermute | solution.py:236
  54.0 1.1 %collective-permute-start.15 = (bf16[48,896]{1,0:T(8,128)(2,1)S(1)}, bf16[48,896]{1,0:T(8,128)(2,1)S(1)}, u32[]{:S(2)}, u32[]{:S(2)}) collective-permute-start(bf16[48,896]{1,0:T(8,128)(2,1)S(1)} %get-tuple-element.39), channel_id=1, source_target_pairs={{0,24},{4,28},{8,0},{12,4},{16,8},{20,12},{24,16},{28,20},{1,25},{... | collective-permute-start | bytes 258056 | tf_op jit(solution)/shard_map/ppermute | solution.py:236
  55.2 1.6 %collective-permute-start.16 = (bf16[48,896]{1,0:T(8,128)(2,1)S(1)}, bf16[48,896]{1,0:T(8,128)(2,1)S(1)}, u32[]{:S(2)}, u32[]{:S(2)}) collective-permute-start(bf16[48,896]{1,0:T(8,128)(2,1)S(1)} %get-tuple-element.38), channel_id=1, source_target_pairs={{0,28},{4,0},{8,4},{12,8},{16,12},{20,16},{24,20},{28,24},{1,29},{... | collective-permute-start | bytes 258056 | tf_op jit(solution)/shard_map/ppermute | solution.py:236
  56.8 2.2 %collective-permute-done.12 = bf16[48,896]{1,0:T(8,128)(2,1)S(1)} collective-permute-done((bf16[48,896]{1,0:T(8,128)(2,1)S(1)}, bf16[48,896]{1,0:T(8,128)(2,1)S(1)}, u32[]{:S(2)}, u32[]{:S(2)}) %collective-permute-start.12) | collective-permute-done | bytes 86048 | tf_op jit(solution)/shard_map/ppermute | solution.py:236
  59.1 1.2 %collective-permute-done.13 = bf16[48,896]{1,0:T(8,128)(2,1)S(1)} collective-permute-done((bf16[48,896]{1,0:T(8,128)(2,1)S(1)}, bf16[48,896]{1,0:T(8,128)(2,1)S(1)}, u32[]{:S(2)}, u32[]{:S(2)}) %collective-permute-start.13) | collective-permute-done | bytes 86048 | tf_op jit(solution)/shard_map/ppermute | solution.py:236
  60.6 0.5 fusion.32
  61.1 0.3 fusion.141
  61.4 0.2 fusion.47
  61.6 0.3 fusion.21
  61.9 4.3 %fusion.63 = f32[64,5120]{1,0:T(8,128)S(1)} fusion(bf16[640,5120]{1,0:T(8,128)(2,1)} %param.24, bf16[8,8,5,128]{3,2,1,0:T(8,128)(2,1)S(1)} %bitcast.289), kind=kOutput, calls=%fused_computation.127 | convolution fusion | flops 419430400 | bytes 7946240 | tf_op jit(solution)/shard_map/dot_general | solution.py:210
  66.4 0.3 fusion.142
  66.7 0.2 fusion.46
  66.9 0.3 fusion.20
  67.3 1.3 %fusion.66 = f32[64,5120]{1,0:T(8,128)S(1)} fusion(bf16[640,5120]{1,0:T(8,128)(2,1)S(1)} %bitcast.287, bf16[8,8,5,128]{3,2,1,0:T(8,128)(2,1)S(1)} %bitcast.290), kind=kOutput, calls=%fused_computation.130 | convolution fusion | flops 419430400 | bytes 7946240 | tf_op jit(solution)/shard_map/dot_general | solution.py:210
  68.7 0.6 collective-permute-start.21
  69.3 0.3 fusion.143
  69.8 0.3 fusion.23
  70.1 1.3 %fusion.69 = f32[64,5120]{1,0:T(8,128)S(1)} fusion(bf16[640,5120]{1,0:T(8,128)(2,1)S(1)} %bitcast.287, bf16[8,8,5,128]{3,2,1,0:T(8,128)(2,1)S(1)} %bitcast.291), kind=kOutput, calls=%fused_computation.133 | convolution fusion | flops 419430400 | bytes 7946240 | tf_op jit(solution)/shard_map/dot_general | solution.py:210
  71.6 0.2 fusion.144
  71.8 0.2 fusion.22
  72.2 1.3 %fusion.72 = f32[64,5120]{1,0:T(8,128)S(1)} fusion(bf16[640,5120]{1,0:T(8,128)(2,1)S(1)} %bitcast.287, bf16[8,8,5,128]{3,2,1,0:T(8,128)(2,1)S(1)} %bitcast.292), kind=kOutput, calls=%fused_computation.136 | convolution fusion | flops 419430400 | bytes 7946240 | tf_op jit(solution)/shard_map/dot_general | solution.py:210
  73.6 0.6 collective-permute-start.17
  74.2 3.0 %collective-permute-start.24 = (f32[1,64,1280]{2,1,0:T(8,128)S(1)}, f32[1,64,1280]{2,1,0:T(8,128)S(1)}, u32[]{:S(2)}, u32[]{:S(2)}) collective-permute-start(f32[1,64,1280]{2,1,0:T(8,128)S(1)} %get-tuple-element.21), channel_id=1, source_target_pairs={{0,2},{1,3},{2,0},{3,1},{4,6},{5,7},{6,4},{7,5},{8,10},{9,11},{10,... | collective-permute-start | bytes 983048 | tf_op jit(solution)/shard_map/ppermute | solution.py:254
  77.5 2.1 %collective-permute-start.20 = (f32[1,64,1280]{2,1,0:T(8,128)S(1)}, f32[1,64,1280]{2,1,0:T(8,128)S(1)}, u32[]{:S(2)}, u32[]{:S(2)}) collective-permute-start(f32[1,64,1280]{2,1,0:T(8,128)S(1)} %get-tuple-element.15), channel_id=1, source_target_pairs={{0,2},{1,3},{2,0},{3,1},{4,6},{5,7},{6,4},{7,5},{8,10},{9,11},{10,... | collective-permute-start | bytes 983048 | tf_op jit(solution)/shard_map/ppermute | solution.py:254
  79.9 5.9 %collective-permute-done.24 = f32[1,64,1280]{2,1,0:T(8,128)S(1)} collective-permute-done((f32[1,64,1280]{2,1,0:T(8,128)S(1)}, f32[1,64,1280]{2,1,0:T(8,128)S(1)}, u32[]{:S(2)}, u32[]{:S(2)}) %collective-permute-start.24) | collective-permute-done | bytes 327712 | tf_op jit(solution)/shard_map/ppermute | solution.py:254
  85.8 7.0 %collective-permute-done.22 = f32[1,64,1280]{2,1,0:T(8,128)S(1)} collective-permute-done((f32[1,64,1280]{2,1,0:T(8,128)S(1)}, f32[1,64,1280]{2,1,0:T(8,128)S(1)}, u32[]{:S(2)}, u32[]{:S(2)}) %collective-permute-start.22) | collective-permute-done | bytes 327712 | tf_op jit(solution)/shard_map/ppermute | solution.py:254
  92.8 7.0 %collective-permute-done.20 = f32[1,64,1280]{2,1,0:T(8,128)S(1)} collective-permute-done((f32[1,64,1280]{2,1,0:T(8,128)S(1)}, f32[1,64,1280]{2,1,0:T(8,128)S(1)}, u32[]{:S(2)}, u32[]{:S(2)}) %collective-permute-start.20) | collective-permute-done | bytes 327712 | tf_op jit(solution)/shard_map/ppermute | solution.py:254
  99.8 6.4 %collective-permute-done.18 = f32[1,64,1280]{2,1,0:T(8,128)S(1)} collective-permute-done((f32[1,64,1280]{2,1,0:T(8,128)S(1)}, f32[1,64,1280]{2,1,0:T(8,128)S(1)}, u32[]{:S(2)}, u32[]{:S(2)}) %collective-permute-start.18) | collective-permute-done | bytes 327712 | tf_op jit(solution)/shard_map/ppermute | solution.py:254
  106.3 0.9 pad_maximum_fusion.5
  (135 shorter events, 4.9 us)
Async XLA Ops:
  0.0 30.5 %copy-start = (bf16[96,5120]{1,0:T(8,128)(2,1)S(1)}, bf16[96,5120]{1,0:T(8,128)(2,1)}, u32[]{:S(2)}) copy-start(bf16[96,5120]{1,0:T(8,128)(2,1)} %param.14) | copy-start | bytes 2949124
  0.0 30.5 %copy-start.3 = (f32[5120]{0:T(1024)S(1)}, f32[5120]{0:T(1024)}, u32[]{:S(2)}) copy-start(f32[5120]{0:T(1024)} %param.17) | copy-start | bytes 61444
  0.0 30.5 %copy-start.4 = (f32[640]{0:T(1024)S(1)}, f32[640]{0:T(1024)}, u32[]{:S(2)}) copy-start(f32[640]{0:T(1024)} %param.19) | copy-start | bytes 7684
  0.0 25.6 %collective-permute-start = (bf16[96,5120]{1,0:T(8,128)(2,1)}, bf16[96,5120]{1,0:T(8,128)(2,1)S(1)}, u32[]{:S(2)}, u32[]{:S(2)}) collective-permute-start(bf16[96,5120]{1,0:T(8,128)(2,1)} %param.14), channel_id=1, source_target_pairs={{0,2},{1,3},{2,0},{3,1},{4,6},{5,7},{6,4},{7,5},{8,10},{9,11},{10,... | collective-permute-start | bytes 2949128 | tf_op jit(solution)/shard_map/ppermute | solution.py:283
  3.0 25.3 %collective-permute-start.1 = (bf16[96,5120]{1,0:T(8,128)(2,1)}, bf16[96,5120]{1,0:T(8,128)(2,1)S(1)}, u32[]{:S(2)}, u32[]{:S(2)}) collective-permute-start(bf16[96,5120]{1,0:T(8,128)(2,1)} %param.14), channel_id=1, source_target_pairs={{0,1},{1,0},{2,3},{3,2},{4,5},{5,4},{6,7},{7,6},{8,9},{9,8},{10,11... | collective-permute-start | bytes 2949128 | tf_op jit(solution)/shard_map/ppermute | solution.py:283
  3.0 15.0 %collective-permute-start.3 = (s32[1,8]{1,0:T(1,128)}, s32[1,8]{1,0:T(1,128)S(1)}, u32[]{:S(2)}, u32[]{:S(2)}) collective-permute-start(s32[1,8]{1,0:T(1,128)} %param.16), channel_id=1, source_target_pairs={{0,4},{4,8},{8,12},{12,16},{16,20},{20,24},{24,28},{28,0},{1,5},{5... | collective-permute-start | bytes 104 | tf_op jit(solution)/shard_map/ppermute | solution.py:220
  4.5 14.8 %collective-permute-start.4 = (s32[1,8]{1,0:T(1,128)}, s32[1,8]{1,0:T(1,128)S(1)}, u32[]{:S(2)}, u32[]{:S(2)}) collective-permute-start(s32[1,8]{1,0:T(1,128)} %param.16), channel_id=1, source_target_pairs={{0,8},{4,12},{8,16},{12,20},{16,24},{20,28},{24,0},{28,4},{1,9},{5... | collective-permute-start | bytes 104 | tf_op jit(solution)/shard_map/ppermute | solution.py:220
  6.1 15.8 %collective-permute-start.5 = (s32[1,8]{1,0:T(1,128)}, s32[1,8]{1,0:T(1,128)S(1)}, u32[]{:S(2)}, u32[]{:S(2)}) collective-permute-start(s32[1,8]{1,0:T(1,128)} %param.16), channel_id=1, source_target_pairs={{0,12},{4,16},{8,20},{12,24},{16,28},{20,0},{24,4},{28,8},{1,13},{... | collective-permute-start | bytes 104 | tf_op jit(solution)/shard_map/ppermute | solution.py:220
  18.0 5.3 %collective-permute-start.6 = (s32[1,8]{1,0:T(1,128)}, s32[1,8]{1,0:T(1,128)S(1)}, u32[]{:S(2)}, u32[]{:S(2)}) collective-permute-start(s32[1,8]{1,0:T(1,128)} %param.16), channel_id=1, source_target_pairs={{0,16},{4,20},{8,24},{12,28},{16,0},{20,4},{24,8},{28,12},{1,17},{... | collective-permute-start | bytes 104 | tf_op jit(solution)/shard_map/ppermute | solution.py:220
  19.3 5.6 %collective-permute-start.7 = (s32[1,8]{1,0:T(1,128)}, s32[1,8]{1,0:T(1,128)S(1)}, u32[]{:S(2)}, u32[]{:S(2)}) collective-permute-start(s32[1,8]{1,0:T(1,128)} %param.16), channel_id=1, source_target_pairs={{0,20},{4,24},{8,28},{12,0},{16,4},{20,8},{24,12},{28,16},{1,21},{... | collective-permute-start | bytes 104 | tf_op jit(solution)/shard_map/ppermute | solution.py:220
  22.0 3.7 %collective-permute-start.8 = (s32[1,8]{1,0:T(1,128)}, s32[1,8]{1,0:T(1,128)S(1)}, u32[]{:S(2)}, u32[]{:S(2)}) collective-permute-start(s32[1,8]{1,0:T(1,128)} %param.16), channel_id=1, source_target_pairs={{0,24},{4,28},{8,0},{12,4},{16,8},{20,12},{24,16},{28,20},{1,25},{... | collective-permute-start | bytes 104 | tf_op jit(solution)/shard_map/ppermute | solution.py:220
  23.3 3.7 %collective-permute-start.9 = (s32[1,8]{1,0:T(1,128)}, s32[1,8]{1,0:T(1,128)S(1)}, u32[]{:S(2)}, u32[]{:S(2)}) collective-permute-start(s32[1,8]{1,0:T(1,128)} %param.16), channel_id=1, source_target_pairs={{0,28},{4,0},{8,4},{12,8},{16,12},{20,16},{24,20},{28,24},{1,29},{... | collective-permute-start | bytes 104 | tf_op jit(solution)/shard_map/ppermute | solution.py:220
  25.6 2.7 %collective-permute-start.2 = (bf16[96,5120]{1,0:T(8,128)(2,1)S(1)}, bf16[96,5120]{1,0:T(8,128)(2,1)}, u32[]{:S(2)}, u32[]{:S(2)}) collective-permute-start(bf16[96,5120]{1,0:T(8,128)(2,1)S(1)} %collective-permute-done), channel_id=1, source_target_pairs={{0,1},{1,0},{2,3},{3,2},{4,5},{5,4},{6,7},{7,6},{8,9},{9,8},{10,11... | collective-permute-start | bytes 2949128 | tf_op jit(solution)/shard_map/ppermute | solution.py:283
  30.5 7.6 %copy-start.1 = (bf16[5120,128]{1,0:T(8,128)(2,1)S(1)}, bf16[5120,128]{1,0:T(8,128)(2,1)}, u32[]{:S(2)}) copy-start(bf16[5120,128]{1,0:T(8,128)(2,1)} %param.22) | copy-start | bytes 3932164
  30.5 7.6 %copy-start.2 = (bf16[5120,128]{1,0:T(8,128)(2,1)S(1)}, bf16[5120,128]{1,0:T(8,128)(2,1)}, u32[]{:S(2)}) copy-start(bf16[5120,128]{1,0:T(8,128)(2,1)} %param.20) | copy-start | bytes 3932164
  44.2 9.8 %collective-permute-start.10 = (bf16[48,896]{1,0:T(8,128)(2,1)S(1)}, bf16[48,896]{1,0:T(8,128)(2,1)S(1)}, u32[]{:S(2)}, u32[]{:S(2)}) collective-permute-start(bf16[48,896]{1,0:T(8,128)(2,1)S(1)} %get-tuple-element.44), channel_id=1, source_target_pairs={{0,4},{4,8},{8,12},{12,16},{16,20},{20,24},{24,28},{28,0},{1,5},{5... | collective-permute-start | bytes 258056 | tf_op jit(solution)/shard_map/ppermute | solution.py:236
  46.4 8.8 %collective-permute-start.11 = (bf16[48,896]{1,0:T(8,128)(2,1)S(1)}, bf16[48,896]{1,0:T(8,128)(2,1)S(1)}, u32[]{:S(2)}, u32[]{:S(2)}) collective-permute-start(bf16[48,896]{1,0:T(8,128)(2,1)S(1)} %get-tuple-element.43), channel_id=1, source_target_pairs={{0,8},{4,12},{8,16},{12,20},{16,24},{20,28},{24,0},{28,4},{1,9},{5... | collective-permute-start | bytes 258056 | tf_op jit(solution)/shard_map/ppermute | solution.py:236
  47.4 11.7 %collective-permute-start.12 = (bf16[48,896]{1,0:T(8,128)(2,1)S(1)}, bf16[48,896]{1,0:T(8,128)(2,1)S(1)}, u32[]{:S(2)}, u32[]{:S(2)}) collective-permute-start(bf16[48,896]{1,0:T(8,128)(2,1)S(1)} %get-tuple-element.42), channel_id=1, source_target_pairs={{0,12},{4,16},{8,20},{12,24},{16,28},{20,0},{24,4},{28,8},{1,13},{... | collective-permute-start | bytes 258056 | tf_op jit(solution)/shard_map/ppermute | solution.py:236
  49.9 10.4 %collective-permute-start.13 = (bf16[48,896]{1,0:T(8,128)(2,1)S(1)}, bf16[48,896]{1,0:T(8,128)(2,1)S(1)}, u32[]{:S(2)}, u32[]{:S(2)}) collective-permute-start(bf16[48,896]{1,0:T(8,128)(2,1)S(1)} %get-tuple-element.41), channel_id=1, source_target_pairs={{0,16},{4,20},{8,24},{12,28},{16,0},{20,4},{24,8},{28,12},{1,17},{... | collective-permute-start | bytes 258056 | tf_op jit(solution)/shard_map/ppermute | solution.py:236
  51.2 9.2 %collective-permute-start.14 = (bf16[48,896]{1,0:T(8,128)(2,1)S(1)}, bf16[48,896]{1,0:T(8,128)(2,1)S(1)}, u32[]{:S(2)}, u32[]{:S(2)}) collective-permute-start(bf16[48,896]{1,0:T(8,128)(2,1)S(1)} %get-tuple-element.40), channel_id=1, source_target_pairs={{0,20},{4,24},{8,28},{12,0},{16,4},{20,8},{24,12},{28,16},{1,21},{... | collective-permute-start | bytes 258056 | tf_op jit(solution)/shard_map/ppermute | solution.py:236
  54.0 6.4 %collective-permute-start.15 = (bf16[48,896]{1,0:T(8,128)(2,1)S(1)}, bf16[48,896]{1,0:T(8,128)(2,1)S(1)}, u32[]{:S(2)}, u32[]{:S(2)}) collective-permute-start(bf16[48,896]{1,0:T(8,128)(2,1)S(1)} %get-tuple-element.39), channel_id=1, source_target_pairs={{0,24},{4,28},{8,0},{12,4},{16,8},{20,12},{24,16},{28,20},{1,25},{... | collective-permute-start | bytes 258056 | tf_op jit(solution)/shard_map/ppermute | solution.py:236
  55.2 5.3 %collective-permute-start.16 = (bf16[48,896]{1,0:T(8,128)(2,1)S(1)}, bf16[48,896]{1,0:T(8,128)(2,1)S(1)}, u32[]{:S(2)}, u32[]{:S(2)}) collective-permute-start(bf16[48,896]{1,0:T(8,128)(2,1)S(1)} %get-tuple-element.38), channel_id=1, source_target_pairs={{0,28},{4,0},{8,4},{12,8},{16,12},{20,16},{24,20},{28,24},{1,29},{... | collective-permute-start | bytes 258056 | tf_op jit(solution)/shard_map/ppermute | solution.py:236
  61.9 5.4 %slice-start = ((s8[6553600]{0:T(1024)(128)(4,1)}), s8[4194304]{0:T(1024)(128)(4,1)S(1)}, s32[]{:S(2)}) async-start(s8[6553600]{0:T(1024)(128)(4,1)} %bitcast.286), calls=%async_computation | async-start | bytes 8388608
  61.9 5.4 %slice-start.1 = ((s8[6553600]{0:T(1024)(128)(4,1)}), s8[2359296]{0:T(1024)(128)(4,1)S(1)}, s32[]{:S(2)}) async-start(s8[6553600]{0:T(1024)(128)(4,1)} %bitcast.286), calls=%async_computation.1 | async-start | bytes 4718592
  66.3 7.8 %collective-permute-start.23 = (f32[2,64,1280]{2,1,0:T(8,128)S(1)}, f32[2,64,1280]{2,1,0:T(8,128)S(1)}, u32[]{:S(2)}, u32[]{:S(2)}) collective-permute-start(f32[2,64,1280]{2,1,0:T(8,128)S(1)} %pad_maximum_fusion.4), channel_id=1, source_target_pairs={{0,1},{1,0},{2,3},{3,2},{4,5},{5,4},{6,7},{7,6},{8,9},{9,8},{10,11... | collective-permute-start | bytes 1966088 | tf_op jit(solution)/shard_map/ppermute | solution.py:254
  68.7 8.5 %collective-permute-start.21 = (f32[2,64,1280]{2,1,0:T(8,128)S(1)}, f32[2,64,1280]{2,1,0:T(8,128)S(1)}, u32[]{:S(2)}, u32[]{:S(2)}) collective-permute-start(f32[2,64,1280]{2,1,0:T(8,128)S(1)} %pad_maximum_fusion.3), channel_id=1, source_target_pairs={{0,1},{1,0},{2,3},{3,2},{4,5},{5,4},{6,7},{7,6},{8,9},{9,8},{10,11... | collective-permute-start | bytes 1966088 | tf_op jit(solution)/shard_map/ppermute | solution.py:254
  71.5 5.9 %collective-permute-start.19 = (f32[2,64,1280]{2,1,0:T(8,128)S(1)}, f32[2,64,1280]{2,1,0:T(8,128)S(1)}, u32[]{:S(2)}, u32[]{:S(2)}) collective-permute-start(f32[2,64,1280]{2,1,0:T(8,128)S(1)} %pad_maximum_fusion.2), channel_id=1, source_target_pairs={{0,1},{1,0},{2,3},{3,2},{4,5},{5,4},{6,7},{7,6},{8,9},{9,8},{10,11... | collective-permute-start | bytes 1966088 | tf_op jit(solution)/shard_map/ppermute | solution.py:254
  73.6 6.1 %collective-permute-start.17 = (f32[2,64,1280]{2,1,0:T(8,128)S(1)}, f32[2,64,1280]{2,1,0:T(8,128)S(1)}, u32[]{:S(2)}, u32[]{:S(2)}) collective-permute-start(f32[2,64,1280]{2,1,0:T(8,128)S(1)} %pad_maximum_fusion.1), channel_id=1, source_target_pairs={{0,1},{1,0},{2,3},{3,2},{4,5},{5,4},{6,7},{7,6},{8,9},{9,8},{10,11... | collective-permute-start | bytes 1966088 | tf_op jit(solution)/shard_map/ppermute | solution.py:254
  74.2 11.5 %collective-permute-start.24 = (f32[1,64,1280]{2,1,0:T(8,128)S(1)}, f32[1,64,1280]{2,1,0:T(8,128)S(1)}, u32[]{:S(2)}, u32[]{:S(2)}) collective-permute-start(f32[1,64,1280]{2,1,0:T(8,128)S(1)} %get-tuple-element.21), channel_id=1, source_target_pairs={{0,2},{1,3},{2,0},{3,1},{4,6},{5,7},{6,4},{7,5},{8,10},{9,11},{10,... | collective-permute-start | bytes 983048 | tf_op jit(solution)/shard_map/ppermute | solution.py:254
  77.3 15.4 %collective-permute-start.22 = (f32[1,64,1280]{2,1,0:T(8,128)S(1)}, f32[1,64,1280]{2,1,0:T(8,128)S(1)}, u32[]{:S(2)}, u32[]{:S(2)}) collective-permute-start(f32[1,64,1280]{2,1,0:T(8,128)S(1)} %get-tuple-element.18), channel_id=1, source_target_pairs={{0,2},{1,3},{2,0},{3,1},{4,6},{5,7},{6,4},{7,5},{8,10},{9,11},{10,... | collective-permute-start | bytes 983048 | tf_op jit(solution)/shard_map/ppermute | solution.py:254
  77.5 22.2 %collective-permute-start.20 = (f32[1,64,1280]{2,1,0:T(8,128)S(1)}, f32[1,64,1280]{2,1,0:T(8,128)S(1)}, u32[]{:S(2)}, u32[]{:S(2)}) collective-permute-start(f32[1,64,1280]{2,1,0:T(8,128)S(1)} %get-tuple-element.15), channel_id=1, source_target_pairs={{0,2},{1,3},{2,0},{3,1},{4,6},{5,7},{6,4},{7,5},{8,10},{9,11},{10,... | collective-permute-start | bytes 983048 | tf_op jit(solution)/shard_map/ppermute | solution.py:254
  79.8 26.4 %collective-permute-start.18 = (f32[1,64,1280]{2,1,0:T(8,128)S(1)}, f32[1,64,1280]{2,1,0:T(8,128)S(1)}, u32[]{:S(2)}, u32[]{:S(2)}) collective-permute-start(f32[1,64,1280]{2,1,0:T(8,128)S(1)} %get-tuple-element.12), channel_id=1, source_target_pairs={{0,2},{1,3},{2,0},{3,1},{4,6},{5,7},{6,4},{7,5},{8,10},{9,11},{10,... | collective-permute-start | bytes 983048 | tf_op jit(solution)/shard_map/ppermute | solution.py:254

commit v20 on v15

--- a/solution.py
+++ b/solution.py
@@ -126,14 +126,11 @@
             key_rows.reshape(count, local_kv, head_dim), starts, head_dim
         ).astype(jnp.bfloat16)
         value_rows = key_value[:, kv_cols:].astype(jnp.bfloat16)
-        return jnp.concatenate(
-            [
-                query_matrix.reshape(count, local_heads * head_dim),
-                key_rows.reshape(count, local_kv * head_dim),
-                value_rows,
-            ],
-            axis=1,
-        )
+        return [
+            query_matrix.reshape(count, local_heads * head_dim),
+            key_rows.reshape(count, local_kv * head_dim),
+            value_rows,
+        ]
 
     qkv = project(jnp.concatenate(pieces, axis=0), sequence_starts)
 
@@ -150,7 +147,13 @@
     send_hot = (
         places[None, :] == jnp.arange(ctx_count * group_cap, dtype=jnp.int32)[:, None]
     ).astype(jnp.bfloat16)
-    outgoing = jnp.dot(send_hot, qkv, preferred_element_type=jnp.float32).astype(jnp.bfloat16)
+    outgoing = jnp.concatenate(
+        [
+            jnp.dot(send_hot, part, preferred_element_type=jnp.float32).astype(jnp.bfloat16)
+            for part in qkv
+        ],
+        axis=1,
+    )
     arrived = exchange(outgoing, "ctx", ctx_count)
 
     mine = (pool_dest >= 0) & (pool_dest // pack_len == ctx_index)

time: 109 us -> 109 us (level)
  no operation moved by 1% of the time
where the time goes in v20:
time: 109 us; the launch traced here: 107 us
  starting transfers between devices  34.3 us (31%)
  waiting for transfers between devices  31.8 us (29%)
  matrix products  21.7 us (20%)
  other arithmetic  12.6 us (12%)
  local copies, waits for them, and re-layouts  6.28 us (6%)
    ppermute x8, waiting for transfers between devices, halving_scatter(): got = lax.ppermute(send, axis_name, pairs)  26.2 us
    ppermute x7, starting transfers between devices, shift_gather(): lax.ppermute(part, axis_name, [(i, (i + shift) % count) for i in range(co...  12.5 us
    ppermute x7, starting transfers between devices, exchange(): arrived.append(lax.ppermute(chunks[shift], axis_name, pairs))  12.2 us
    dot_general x4, matrix products, local(): jnp.dot(mixed_heads, w_out, preferred_element_type=jnp.float32)  8.08 us
    dot_general x1, matrix products, project(): jnp.dot(normalized_input, w_query, preferred_element_type=jnp.float32)  7.56 us
    ppermute x8, starting transfers between devices, halving_scatter(): got = lax.ppermute(send, axis_name, pairs)  6.55 us
    ppermute x7, waiting for transfers between devices, exchange(): arrived.append(lax.ppermute(chunks[shift], axis_name, pairs))  3.6 us
    ppermute x3, starting transfers between devices, xor_gather(): pieces = pieces + [lax.ppermute(p, axis_name, pairs) for p in pieces]  3.01 us
  transfers between devices with their start and end apart: 25, of which 9 were waited for; matrix products, arithmetic and copies ran while one was open for 17% of the time, Pallas kernels for 0%

profile of v20, /device:TPU:0, one launch (start us, length us, event | category | flops | bytes accessed | tf_op | source)
XLA Modules:
  0.0 107.2 jit_solution(13190930555412616876)
XLA Ops:
  0.0 3.0 %collective-permute-start = (bf16[96,5120]{1,0:T(8,128)(2,1)}, bf16[96,5120]{1,0:T(8,128)(2,1)S(1)}, u32[]{:S(2)}, u32[]{:S(2)}) collective-permute-start(bf16[96,5120]{1,0:T(8,128)(2,1)} %param.14), channel_id=1, source_target_pairs={{0,2},{1,3},{2,0},{3,1},{4,6},{5,7},{6,4},{7,5},{8,10},{9,11},{10,... | collective-permute-start | bytes 2949128 | tf_op jit(solution)/shard_map/ppermute | solution.py:289
  3.0 1.5 %collective-permute-start.3 = (s32[1,8]{1,0:T(1,128)}, s32[1,8]{1,0:T(1,128)S(1)}, u32[]{:S(2)}, u32[]{:S(2)}) collective-permute-start(s32[1,8]{1,0:T(1,128)} %param.16), channel_id=1, source_target_pairs={{0,4},{4,8},{8,12},{12,16},{16,20},{20,24},{24,28},{28,0},{1,5},{5... | collective-permute-start | bytes 104 | tf_op jit(solution)/shard_map/ppermute | solution.py:226
  4.5 1.6 %collective-permute-start.4 = (s32[1,8]{1,0:T(1,128)}, s32[1,8]{1,0:T(1,128)S(1)}, u32[]{:S(2)}, u32[]{:S(2)}) collective-permute-start(s32[1,8]{1,0:T(1,128)} %param.16), channel_id=1, source_target_pairs={{0,8},{4,12},{8,16},{12,20},{16,24},{20,28},{24,0},{28,4},{1,9},{5... | collective-permute-start | bytes 104 | tf_op jit(solution)/shard_map/ppermute | solution.py:226
  6.1 2.5 %collective-permute-start.5 = (s32[1,8]{1,0:T(1,128)}, s32[1,8]{1,0:T(1,128)S(1)}, u32[]{:S(2)}, u32[]{:S(2)}) collective-permute-start(s32[1,8]{1,0:T(1,128)} %param.16), channel_id=1, source_target_pairs={{0,12},{4,16},{8,20},{12,24},{16,28},{20,0},{24,4},{28,8},{1,13},{... | collective-permute-start | bytes 104 | tf_op jit(solution)/shard_map/ppermute | solution.py:226
  8.6 0.7 reshape.874
  9.5 0.7 constant_dynamic-update-slice_fusion.7
  10.2 0.8 reduce-window.32
  11.3 0.7 compare_and_fusion.4
  12.0 0.9 reduce-window.30
  12.9 0.2 slice_reduce_fusion
  13.3 0.6 gather_fusion.2
  13.9 0.6 gather_fusion.1
  14.8 0.7 subtract_select_fusion
  15.6 0.9 reduce-window.21
  16.5 0.2 slice_reduce_fusion.1
  16.9 0.7 pad_maximum_fusion.8
  18.0 1.3 %collective-permute-start.6 = (s32[1,8]{1,0:T(1,128)}, s32[1,8]{1,0:T(1,128)S(1)}, u32[]{:S(2)}, u32[]{:S(2)}) collective-permute-start(s32[1,8]{1,0:T(1,128)} %param.16), channel_id=1, source_target_pairs={{0,16},{4,20},{8,24},{12,28},{16,0},{20,4},{24,8},{28,12},{1,17},{... | collective-permute-start | bytes 104 | tf_op jit(solution)/shard_map/ppermute | solution.py:226
  19.3 2.6 %collective-permute-start.7 = (s32[1,8]{1,0:T(1,128)}, s32[1,8]{1,0:T(1,128)S(1)}, u32[]{:S(2)}, u32[]{:S(2)}) collective-permute-start(s32[1,8]{1,0:T(1,128)} %param.16), channel_id=1, source_target_pairs={{0,20},{4,24},{8,28},{12,0},{16,4},{20,8},{24,12},{28,16},{1,21},{... | collective-permute-start | bytes 104 | tf_op jit(solution)/shard_map/ppermute | solution.py:226
  21.9 1.3 %collective-permute-start.8 = (s32[1,8]{1,0:T(1,128)}, s32[1,8]{1,0:T(1,128)S(1)}, u32[]{:S(2)}, u32[]{:S(2)}) collective-permute-start(s32[1,8]{1,0:T(1,128)} %param.16), channel_id=1, source_target_pairs={{0,24},{4,28},{8,0},{12,4},{16,8},{20,12},{24,16},{28,20},{1,25},{... | collective-permute-start | bytes 104 | tf_op jit(solution)/shard_map/ppermute | solution.py:226
  23.3 1.6 %collective-permute-start.9 = (s32[1,8]{1,0:T(1,128)}, s32[1,8]{1,0:T(1,128)S(1)}, u32[]{:S(2)}, u32[]{:S(2)}) collective-permute-start(s32[1,8]{1,0:T(1,128)} %param.16), channel_id=1, source_target_pairs={{0,28},{4,0},{8,4},{12,8},{16,12},{20,16},{24,20},{28,24},{1,29},{... | collective-permute-start | bytes 104 | tf_op jit(solution)/shard_map/ppermute | solution.py:226
  24.9 0.7 collective-permute-done.8
  25.6 1.3 %collective-permute-done.9 = s32[1,8]{1,0:T(1,128)S(1)} collective-permute-done((s32[1,8]{1,0:T(1,128)}, s32[1,8]{1,0:T(1,128)S(1)}, u32[]{:S(2)}, u32[]{:S(2)}) %collective-permute-start.9) | collective-permute-done | bytes 64 | tf_op jit(solution)/shard_map/ppermute | solution.py:226
  27.0 0.6 gather_fusion
  27.9 0.4 multiply_cosine_fusion.1
  28.4 2.1 %fusion = f32[384]{0:T(512)S(1)} fusion(bf16[96,5120]{1,0:T(8,128)(2,1)} %collective-permute-done.2, bf16[96,5120]{1,0:T(8,128)(2,1)S(1)} %collective-permute-done.1, bf16[96,5120]{1,0:T(8,128)(2,1)S(1)} %collective-permute-done, bf16[96,5120]{1,0:T(8,128)(2,1)} %param.14), kind=kLoop, calls=%fused_computation.5 | loop fusion | flops 19660416 | bytes 3933696 | tf_op jit(solution)/shard_map/reduce_sum | solution.py:108
  30.5 7.6 %convolution_add_fusion = f32[384,640]{1,0:T(8,128)} fusion(bf16[5120,640]{1,0:T(8,128)(2,1)} %param.18, f32[5120]{0:T(1024)S(1)} %copy-done.3, f32[384]{0:T(512)S(1)} %add_rsqrt_fusion, f32[640]{0:T(1024)S(1)} %copy-done.4, bf16[96,5120]{1,0:T(8,128)(2,1)} %collective-permute-done.2, bf16[96,5120]{1,0:T(8,128)(2,1)S(1)} %collective-permute-done.1, ...), kind=kOutput, calls=%fused_computation.15 | convolution fusion | flops 2538455040 | bytes 11493376 | tf_op jit(solution)/shard_map/dot_general | solution.py:112
  38.1 2.4 %fusion.7 = f32[384,256]{1,0:T(8,128)S(1)} fusion(bf16[5120,128]{1,0:T(8,128)(2,1)S(1)} %copy-done.1, bf16[5120,128]{1,0:T(8,128)(2,1)S(1)} %copy-done.2, f32[5120]{0:T(1024)S(1)} %copy-done.3, f32[384]{0:T(512)S(1)} %add_rsqrt_fusion, f32[256]{0:T(256)S(1)} %pad_maximum_fusion.8, bf16[96,5120]{1,0:T(8,128)(2,1)} %collective-permute-done.2, ...), kind=kOutput, calls=%fused_computation.18 | convolution fusion | flops 1033601024 | bytes 6969856 | tf_op jit(solution)/shard_map/dot_general | solution.py:114
  40.6 0.3 convolution_convert_fusion.2
  40.8 0.8 fusion.58
  41.7 1.5 %copy.36 = f32[384,640]{0,1:T(8,128)S(1)} copy(f32[384,640]{1,0:T(8,128)} %convolution_add_fusion) | data formatting | bytes 1966080 | tf_op jit(solution)/shard_map/optimization_barrier | solution.py:120
  43.4 0.4 convolution_convert_fusion
  43.9 0.3 convolution_convert_fusion.3
  44.3 1.8 %collective-permute-start.10 = (bf16[48,896]{1,0:T(8,128)(2,1)S(1)}, bf16[48,896]{1,0:T(8,128)(2,1)S(1)}, u32[]{:S(2)}, u32[]{:S(2)}) collective-permute-start(bf16[48,896]{1,0:T(8,128)(2,1)S(1)} %get-tuple-element.44), channel_id=1, source_target_pairs={{0,4},{4,8},{8,12},{12,16},{16,20},{20,24},{24,28},{28,0},{1,5},{5... | collective-permute-start | bytes 258056 | tf_op jit(solution)/shard_map/ppermute | solution.py:242
  46.1 0.4 select_reduce_fusion
  46.6 1.0 collective-permute-start.11
  47.5 2.5 %collective-permute-start.12 = (bf16[48,896]{1,0:T(8,128)(2,1)S(1)}, bf16[48,896]{1,0:T(8,128)(2,1)S(1)}, u32[]{:S(2)}, u32[]{:S(2)}) collective-permute-start(bf16[48,896]{1,0:T(8,128)(2,1)S(1)} %get-tuple-element.42), channel_id=1, source_target_pairs={{0,12},{4,16},{8,20},{12,24},{16,28},{20,0},{24,4},{28,8},{1,13},{... | collective-permute-start | bytes 258056 | tf_op jit(solution)/shard_map/ppermute | solution.py:242
  50.1 1.2 %collective-permute-start.13 = (bf16[48,896]{1,0:T(8,128)(2,1)S(1)}, bf16[48,896]{1,0:T(8,128)(2,1)S(1)}, u32[]{:S(2)}, u32[]{:S(2)}) collective-permute-start(bf16[48,896]{1,0:T(8,128)(2,1)S(1)} %get-tuple-element.41), channel_id=1, source_target_pairs={{0,16},{4,20},{8,24},{12,28},{16,0},{20,4},{24,8},{28,12},{1,17},{... | collective-permute-start | bytes 258056 | tf_op jit(solution)/shard_map/ppermute | solution.py:242
  51.3 2.8 %collective-permute-start.14 = (bf16[48,896]{1,0:T(8,128)(2,1)S(1)}, bf16[48,896]{1,0:T(8,128)(2,1)S(1)}, u32[]{:S(2)}, u32[]{:S(2)}) collective-permute-start(bf16[48,896]{1,0:T(8,128)(2,1)S(1)} %get-tuple-element.40), channel_id=1, source_target_pairs={{0,20},{4,24},{8,28},{12,0},{16,4},{20,8},{24,12},{28,16},{1,21},{... | collective-permute-start | bytes 258056 | tf_op jit(solution)/shard_map/ppermute | solution.py:242
  54.1 1.1 %collective-permute-start.15 = (bf16[48,896]{1,0:T(8,128)(2,1)S(1)}, bf16[48,896]{1,0:T(8,128)(2,1)S(1)}, u32[]{:S(2)}, u32[]{:S(2)}) collective-permute-start(bf16[48,896]{1,0:T(8,128)(2,1)S(1)} %get-tuple-element.39), channel_id=1, source_target_pairs={{0,24},{4,28},{8,0},{12,4},{16,8},{20,12},{24,16},{28,20},{1,25},{... | collective-permute-start | bytes 258056 | tf_op jit(solution)/shard_map/ppermute | solution.py:242
  55.3 1.6 %collective-permute-start.16 = (bf16[48,896]{1,0:T(8,128)(2,1)S(1)}, bf16[48,896]{1,0:T(8,128)(2,1)S(1)}, u32[]{:S(2)}, u32[]{:S(2)}) collective-permute-start(bf16[48,896]{1,0:T(8,128)(2,1)S(1)} %get-tuple-element.38), channel_id=1, source_target_pairs={{0,28},{4,0},{8,4},{12,8},{16,12},{20,16},{24,20},{28,24},{1,29},{... | collective-permute-start | bytes 258056 | tf_op jit(solution)/shard_map/ppermute | solution.py:242
  57.0 2.2 %collective-permute-done.12 = bf16[48,896]{1,0:T(8,128)(2,1)S(1)} collective-permute-done((bf16[48,896]{1,0:T(8,128)(2,1)S(1)}, bf16[48,896]{1,0:T(8,128)(2,1)S(1)}, u32[]{:S(2)}, u32[]{:S(2)}) %collective-permute-start.12) | collective-permute-done | bytes 86048 | tf_op jit(solution)/shard_map/ppermute | solution.py:242
  59.2 1.2 %collective-permute-done.13 = bf16[48,896]{1,0:T(8,128)(2,1)S(1)} collective-permute-done((bf16[48,896]{1,0:T(8,128)(2,1)S(1)}, bf16[48,896]{1,0:T(8,128)(2,1)S(1)}, u32[]{:S(2)}, u32[]{:S(2)}) %collective-permute-start.13) | collective-permute-done | bytes 86048 | tf_op jit(solution)/shard_map/ppermute | solution.py:242
  60.7 0.5 convolution_convert_fusion.1
  61.2 0.3 fusion.137
  61.7 0.3 fusion.21
  62.0 4.3 %fusion.59 = f32[64,5120]{1,0:T(8,128)S(1)} fusion(bf16[640,5120]{1,0:T(8,128)(2,1)} %param.24, bf16[8,8,5,128]{3,2,1,0:T(8,128)(2,1)S(1)} %bitcast.291), kind=kOutput, calls=%fused_computation.128 | convolution fusion | flops 419430400 | bytes 7946240 | tf_op jit(solution)/shard_map/dot_general | solution.py:216
  66.5 0.3 fusion.138
  67.0 0.3 fusion.20
  67.4 1.3 %fusion.62 = f32[64,5120]{1,0:T(8,128)S(1)} fusion(bf16[640,5120]{1,0:T(8,128)(2,1)S(1)} %bitcast.288, bf16[8,8,5,128]{3,2,1,0:T(8,128)(2,1)S(1)} %bitcast.292), kind=kOutput, calls=%fused_computation.131 | convolution fusion | flops 419430400 | bytes 7946240 | tf_op jit(solution)/shard_map/dot_general | solution.py:216
  68.8 0.6 collective-permute-start.21
  69.4 0.3 fusion.139
  69.9 0.3 fusion.23
  70.2 1.3 %fusion.65 = f32[64,5120]{1,0:T(8,128)S(1)} fusion(bf16[640,5120]{1,0:T(8,128)(2,1)S(1)} %bitcast.288, bf16[8,8,5,128]{3,2,1,0:T(8,128)(2,1)S(1)} %bitcast.293), kind=kOutput, calls=%fused_computation.134 | convolution fusion | flops 419430400 | bytes 7946240 | tf_op jit(solution)/shard_map/dot_general | solution.py:216
  71.7 0.2 fusion.140
  71.9 0.2 fusion.22
  72.3 1.3 %fusion.68 = f32[64,5120]{1,0:T(8,128)S(1)} fusion(bf16[640,5120]{1,0:T(8,128)(2,1)S(1)} %bitcast.288, bf16[8,8,5,128]{3,2,1,0:T(8,128)(2,1)S(1)} %bitcast.294), kind=kOutput, calls=%fused_computation.137 | convolution fusion | flops 419430400 | bytes 7946240 | tf_op jit(solution)/shard_map/dot_general | solution.py:216
  73.7 0.6 collective-permute-start.17
  74.3 3.0 %collective-permute-start.24 = (f32[1,64,1280]{2,1,0:T(8,128)S(1)}, f32[1,64,1280]{2,1,0:T(8,128)S(1)}, u32[]{:S(2)}, u32[]{:S(2)}) collective-permute-start(f32[1,64,1280]{2,1,0:T(8,128)S(1)} %get-tuple-element.21), channel_id=1, source_target_pairs={{0,2},{1,3},{2,0},{3,1},{4,6},{5,7},{6,4},{7,5},{8,10},{9,11},{10,... | collective-permute-start | bytes 983048 | tf_op jit(solution)/shard_map/ppermute | solution.py:260
  77.7 2.1 %collective-permute-start.20 = (f32[1,64,1280]{2,1,0:T(8,128)S(1)}, f32[1,64,1280]{2,1,0:T(8,128)S(1)}, u32[]{:S(2)}, u32[]{:S(2)}) collective-permute-start(f32[1,64,1280]{2,1,0:T(8,128)S(1)} %get-tuple-element.15), channel_id=1, source_target_pairs={{0,2},{1,3},{2,0},{3,1},{4,6},{5,7},{6,4},{7,5},{8,10},{9,11},{10,... | collective-permute-start | bytes 983048 | tf_op jit(solution)/shard_map/ppermute | solution.py:260
  80.0 5.9 %collective-permute-done.24 = f32[1,64,1280]{2,1,0:T(8,128)S(1)} collective-permute-done((f32[1,64,1280]{2,1,0:T(8,128)S(1)}, f32[1,64,1280]{2,1,0:T(8,128)S(1)}, u32[]{:S(2)}, u32[]{:S(2)}) %collective-permute-start.24) | collective-permute-done | bytes 327712 | tf_op jit(solution)/shard_map/ppermute | solution.py:260
  85.9 7.0 %collective-permute-done.22 = f32[1,64,1280]{2,1,0:T(8,128)S(1)} collective-permute-done((f32[1,64,1280]{2,1,0:T(8,128)S(1)}, f32[1,64,1280]{2,1,0:T(8,128)S(1)}, u32[]{:S(2)}, u32[]{:S(2)}) %collective-permute-start.22) | collective-permute-done | bytes 327712 | tf_op jit(solution)/shard_map/ppermute | solution.py:260
  92.9 7.0 %collective-permute-done.20 = f32[1,64,1280]{2,1,0:T(8,128)S(1)} collective-permute-done((f32[1,64,1280]{2,1,0:T(8,128)S(1)}, f32[1,64,1280]{2,1,0:T(8,128)S(1)}, u32[]{:S(2)}, u32[]{:S(2)}) %collective-permute-start.20) | collective-permute-done | bytes 327712 | tf_op jit(solution)/shard_map/ppermute | solution.py:260
  100.0 6.4 %collective-permute-done.18 = f32[1,64,1280]{2,1,0:T(8,128)S(1)} collective-permute-done((f32[1,64,1280]{2,1,0:T(8,128)S(1)}, f32[1,64,1280]{2,1,0:T(8,128)S(1)}, u32[]{:S(2)}, u32[]{:S(2)}) %collective-permute-start.18) | collective-permute-done | bytes 327712 | tf_op jit(solution)/shard_map/ppermute | solution.py:260
  106.4 0.9 pad_maximum_fusion.6
  (134 shorter events, 5.0 us)
Async XLA Ops:
  0.0 30.5 %copy-start = (bf16[96,5120]{1,0:T(8,128)(2,1)S(1)}, bf16[96,5120]{1,0:T(8,128)(2,1)}, u32[]{:S(2)}) copy-start(bf16[96,5120]{1,0:T(8,128)(2,1)} %param.14) | copy-start | bytes 2949124
  0.0 30.5 %copy-start.3 = (f32[5120]{0:T(1024)S(1)}, f32[5120]{0:T(1024)}, u32[]{:S(2)}) copy-start(f32[5120]{0:T(1024)} %param.17) | copy-start | bytes 61444
  0.0 30.5 %copy-start.4 = (f32[640]{0:T(1024)S(1)}, f32[640]{0:T(1024)}, u32[]{:S(2)}) copy-start(f32[640]{0:T(1024)} %param.19) | copy-start | bytes 7684
  0.0 25.6 %collective-permute-start = (bf16[96,5120]{1,0:T(8,128)(2,1)}, bf16[96,5120]{1,0:T(8,128)(2,1)S(1)}, u32[]{:S(2)}, u32[]{:S(2)}) collective-permute-start(bf16[96,5120]{1,0:T(8,128)(2,1)} %param.14), channel_id=1, source_target_pairs={{0,2},{1,3},{2,0},{3,1},{4,6},{5,7},{6,4},{7,5},{8,10},{9,11},{10,... | collective-permute-start | bytes 2949128 | tf_op jit(solution)/shard_map/ppermute | solution.py:289
  3.0 25.3 %collective-permute-start.1 = (bf16[96,5120]{1,0:T(8,128)(2,1)}, bf16[96,5120]{1,0:T(8,128)(2,1)S(1)}, u32[]{:S(2)}, u32[]{:S(2)}) collective-permute-start(bf16[96,5120]{1,0:T(8,128)(2,1)} %param.14), channel_id=1, source_target_pairs={{0,1},{1,0},{2,3},{3,2},{4,5},{5,4},{6,7},{7,6},{8,9},{9,8},{10,11... | collective-permute-start | bytes 2949128 | tf_op jit(solution)/shard_map/ppermute | solution.py:289
  3.0 15.0 %collective-permute-start.3 = (s32[1,8]{1,0:T(1,128)}, s32[1,8]{1,0:T(1,128)S(1)}, u32[]{:S(2)}, u32[]{:S(2)}) collective-permute-start(s32[1,8]{1,0:T(1,128)} %param.16), channel_id=1, source_target_pairs={{0,4},{4,8},{8,12},{12,16},{16,20},{20,24},{24,28},{28,0},{1,5},{5... | collective-permute-start | bytes 104 | tf_op jit(solution)/shard_map/ppermute | solution.py:226
  4.5 14.8 %collective-permute-start.4 = (s32[1,8]{1,0:T(1,128)}, s32[1,8]{1,0:T(1,128)S(1)}, u32[]{:S(2)}, u32[]{:S(2)}) collective-permute-start(s32[1,8]{1,0:T(1,128)} %param.16), channel_id=1, source_target_pairs={{0,8},{4,12},{8,16},{12,20},{16,24},{20,28},{24,0},{28,4},{1,9},{5... | collective-permute-start | bytes 104 | tf_op jit(solution)/shard_map/ppermute | solution.py:226
  6.1 15.8 %collective-permute-start.5 = (s32[1,8]{1,0:T(1,128)}, s32[1,8]{1,0:T(1,128)S(1)}, u32[]{:S(2)}, u32[]{:S(2)}) collective-permute-start(s32[1,8]{1,0:T(1,128)} %param.16), channel_id=1, source_target_pairs={{0,12},{4,16},{8,20},{12,24},{16,28},{20,0},{24,4},{28,8},{1,13},{... | collective-permute-start | bytes 104 | tf_op jit(solution)/shard_map/ppermute | solution.py:226
  18.0 5.3 %collective-permute-start.6 = (s32[1,8]{1,0:T(1,128)}, s32[1,8]{1,0:T(1,128)S(1)}, u32[]{:S(2)}, u32[]{:S(2)}) collective-permute-start(s32[1,8]{1,0:T(1,128)} %param.16), channel_id=1, source_target_pairs={{0,16},{4,20},{8,24},{12,28},{16,0},{20,4},{24,8},{28,12},{1,17},{... | collective-permute-start | bytes 104 | tf_op jit(solution)/shard_map/ppermute | solution.py:226
  19.3 5.6 %collective-permute-start.7 = (s32[1,8]{1,0:T(1,128)}, s32[1,8]{1,0:T(1,128)S(1)}, u32[]{:S(2)}, u32[]{:S(2)}) collective-permute-start(s32[1,8]{1,0:T(1,128)} %param.16), channel_id=1, source_target_pairs={{0,20},{4,24},{8,28},{12,0},{16,4},{20,8},{24,12},{28,16},{1,21},{... | collective-permute-start | bytes 104 | tf_op jit(solution)/shard_map/ppermute | solution.py:226
  21.9 3.7 %collective-permute-start.8 = (s32[1,8]{1,0:T(1,128)}, s32[1,8]{1,0:T(1,128)S(1)}, u32[]{:S(2)}, u32[]{:S(2)}) collective-permute-start(s32[1,8]{1,0:T(1,128)} %param.16), channel_id=1, source_target_pairs={{0,24},{4,28},{8,0},{12,4},{16,8},{20,12},{24,16},{28,20},{1,25},{... | collective-permute-start | bytes 104 | tf_op jit(solution)/shard_map/ppermute | solution.py:226
  23.3 3.7 %collective-permute-start.9 = (s32[1,8]{1,0:T(1,128)}, s32[1,8]{1,0:T(1,128)S(1)}, u32[]{:S(2)}, u32[]{:S(2)}) collective-permute-start(s32[1,8]{1,0:T(1,128)} %param.16), channel_id=1, source_target_pairs={{0,28},{4,0},{8,4},{12,8},{16,12},{20,16},{24,20},{28,24},{1,29},{... | collective-permute-start | bytes 104 | tf_op jit(solution)/shard_map/ppermute | solution.py:226
  25.6 2.7 %collective-permute-start.2 = (bf16[96,5120]{1,0:T(8,128)(2,1)S(1)}, bf16[96,5120]{1,0:T(8,128)(2,1)}, u32[]{:S(2)}, u32[]{:S(2)}) collective-permute-start(bf16[96,5120]{1,0:T(8,128)(2,1)S(1)} %collective-permute-done), channel_id=1, source_target_pairs={{0,1},{1,0},{2,3},{3,2},{4,5},{5,4},{6,7},{7,6},{8,9},{9,8},{10,11... | collective-permute-start | bytes 2949128 | tf_op jit(solution)/shard_map/ppermute | solution.py:289
  30.5 7.6 %copy-start.1 = (bf16[5120,128]{1,0:T(8,128)(2,1)S(1)}, bf16[5120,128]{1,0:T(8,128)(2,1)}, u32[]{:S(2)}) copy-start(bf16[5120,128]{1,0:T(8,128)(2,1)} %param.22) | copy-start | bytes 3932164
  30.5 7.6 %copy-start.2 = (bf16[5120,128]{1,0:T(8,128)(2,1)S(1)}, bf16[5120,128]{1,0:T(8,128)(2,1)}, u32[]{:S(2)}) copy-start(bf16[5120,128]{1,0:T(8,128)(2,1)} %param.20) | copy-start | bytes 3932164
  44.3 9.8 %collective-permute-start.10 = (bf16[48,896]{1,0:T(8,128)(2,1)S(1)}, bf16[48,896]{1,0:T(8,128)(2,1)S(1)}, u32[]{:S(2)}, u32[]{:S(2)}) collective-permute-start(bf16[48,896]{1,0:T(8,128)(2,1)S(1)} %get-tuple-element.44), channel_id=1, source_target_pairs={{0,4},{4,8},{8,12},{12,16},{16,20},{20,24},{24,28},{28,0},{1,5},{5... | collective-permute-start | bytes 258056 | tf_op jit(solution)/shard_map/ppermute | solution.py:242
  46.6 8.8 %collective-permute-start.11 = (bf16[48,896]{1,0:T(8,128)(2,1)S(1)}, bf16[48,896]{1,0:T(8,128)(2,1)S(1)}, u32[]{:S(2)}, u32[]{:S(2)}) collective-permute-start(bf16[48,896]{1,0:T(8,128)(2,1)S(1)} %get-tuple-element.43), channel_id=1, source_target_pairs={{0,8},{4,12},{8,16},{12,20},{16,24},{20,28},{24,0},{28,4},{1,9},{5... | collective-permute-start | bytes 258056 | tf_op jit(solution)/shard_map/ppermute | solution.py:242
  47.5 11.7 %collective-permute-start.12 = (bf16[48,896]{1,0:T(8,128)(2,1)S(1)}, bf16[48,896]{1,0:T(8,128)(2,1)S(1)}, u32[]{:S(2)}, u32[]{:S(2)}) collective-permute-start(bf16[48,896]{1,0:T(8,128)(2,1)S(1)} %get-tuple-element.42), channel_id=1, source_target_pairs={{0,12},{4,16},{8,20},{12,24},{16,28},{20,0},{24,4},{28,8},{1,13},{... | collective-permute-start | bytes 258056 | tf_op jit(solution)/shard_map/ppermute | solution.py:242
  50.1 10.4 %collective-permute-start.13 = (bf16[48,896]{1,0:T(8,128)(2,1)S(1)}, bf16[48,896]{1,0:T(8,128)(2,1)S(1)}, u32[]{:S(2)}, u32[]{:S(2)}) collective-permute-start(bf16[48,896]{1,0:T(8,128)(2,1)S(1)} %get-tuple-element.41), channel_id=1, source_target_pairs={{0,16},{4,20},{8,24},{12,28},{16,0},{20,4},{24,8},{28,12},{1,17},{... | collective-permute-start | bytes 258056 | tf_op jit(solution)/shard_map/ppermute | solution.py:242
  51.3 9.2 %collective-permute-start.14 = (bf16[48,896]{1,0:T(8,128)(2,1)S(1)}, bf16[48,896]{1,0:T(8,128)(2,1)S(1)}, u32[]{:S(2)}, u32[]{:S(2)}) collective-permute-start(bf16[48,896]{1,0:T(8,128)(2,1)S(1)} %get-tuple-element.40), channel_id=1, source_target_pairs={{0,20},{4,24},{8,28},{12,0},{16,4},{20,8},{24,12},{28,16},{1,21},{... | collective-permute-start | bytes 258056 | tf_op jit(solution)/shard_map/ppermute | solution.py:242
  54.1 6.4 %collective-permute-start.15 = (bf16[48,896]{1,0:T(8,128)(2,1)S(1)}, bf16[48,896]{1,0:T(8,128)(2,1)S(1)}, u32[]{:S(2)}, u32[]{:S(2)}) collective-permute-start(bf16[48,896]{1,0:T(8,128)(2,1)S(1)} %get-tuple-element.39), channel_id=1, source_target_pairs={{0,24},{4,28},{8,0},{12,4},{16,8},{20,12},{24,16},{28,20},{1,25},{... | collective-permute-start | bytes 258056 | tf_op jit(solution)/shard_map/ppermute | solution.py:242
  55.3 5.3 %collective-permute-start.16 = (bf16[48,896]{1,0:T(8,128)(2,1)S(1)}, bf16[48,896]{1,0:T(8,128)(2,1)S(1)}, u32[]{:S(2)}, u32[]{:S(2)}) collective-permute-start(bf16[48,896]{1,0:T(8,128)(2,1)S(1)} %get-tuple-element.38), channel_id=1, source_target_pairs={{0,28},{4,0},{8,4},{12,8},{16,12},{20,16},{24,20},{28,24},{1,29},{... | collective-permute-start | bytes 258056 | tf_op jit(solution)/shard_map/ppermute | solution.py:242
  62.0 5.4 %slice-start = ((s8[6553600]{0:T(1024)(128)(4,1)}), s8[4194304]{0:T(1024)(128)(4,1)S(1)}, s32[]{:S(2)}) async-start(s8[6553600]{0:T(1024)(128)(4,1)} %bitcast.287), calls=%async_computation | async-start | bytes 8388608
  62.0 5.4 %slice-start.1 = ((s8[6553600]{0:T(1024)(128)(4,1)}), s8[2359296]{0:T(1024)(128)(4,1)S(1)}, s32[]{:S(2)}) async-start(s8[6553600]{0:T(1024)(128)(4,1)} %bitcast.287), calls=%async_computation.1 | async-start | bytes 4718592
  66.4 7.8 %collective-permute-start.23 = (f32[2,64,1280]{2,1,0:T(8,128)S(1)}, f32[2,64,1280]{2,1,0:T(8,128)S(1)}, u32[]{:S(2)}, u32[]{:S(2)}) collective-permute-start(f32[2,64,1280]{2,1,0:T(8,128)S(1)} %pad_maximum_fusion.5), channel_id=1, source_target_pairs={{0,1},{1,0},{2,3},{3,2},{4,5},{5,4},{6,7},{7,6},{8,9},{9,8},{10,11... | collective-permute-start | bytes 1966088 | tf_op jit(solution)/shard_map/ppermute | solution.py:260
  68.8 8.5 %collective-permute-start.21 = (f32[2,64,1280]{2,1,0:T(8,128)S(1)}, f32[2,64,1280]{2,1,0:T(8,128)S(1)}, u32[]{:S(2)}, u32[]{:S(2)}) collective-permute-start(f32[2,64,1280]{2,1,0:T(8,128)S(1)} %pad_maximum_fusion.4), channel_id=1, source_target_pairs={{0,1},{1,0},{2,3},{3,2},{4,5},{5,4},{6,7},{7,6},{8,9},{9,8},{10,11... | collective-permute-start | bytes 1966088 | tf_op jit(solution)/shard_map/ppermute | solution.py:260
  71.6 6.0 %collective-permute-start.19 = (f32[2,64,1280]{2,1,0:T(8,128)S(1)}, f32[2,64,1280]{2,1,0:T(8,128)S(1)}, u32[]{:S(2)}, u32[]{:S(2)}) collective-permute-start(f32[2,64,1280]{2,1,0:T(8,128)S(1)} %pad_maximum_fusion.3), channel_id=1, source_target_pairs={{0,1},{1,0},{2,3},{3,2},{4,5},{5,4},{6,7},{7,6},{8,9},{9,8},{10,11... | collective-permute-start | bytes 1966088 | tf_op jit(solution)/shard_map/ppermute | solution.py:260
  73.7 6.1 %collective-permute-start.17 = (f32[2,64,1280]{2,1,0:T(8,128)S(1)}, f32[2,64,1280]{2,1,0:T(8,128)S(1)}, u32[]{:S(2)}, u32[]{:S(2)}) collective-permute-start(f32[2,64,1280]{2,1,0:T(8,128)S(1)} %pad_maximum_fusion.2), channel_id=1, source_target_pairs={{0,1},{1,0},{2,3},{3,2},{4,5},{5,4},{6,7},{7,6},{8,9},{9,8},{10,11... | collective-permute-start | bytes 1966088 | tf_op jit(solution)/shard_map/ppermute | solution.py:260
  74.3 11.5 %collective-permute-start.24 = (f32[1,64,1280]{2,1,0:T(8,128)S(1)}, f32[1,64,1280]{2,1,0:T(8,128)S(1)}, u32[]{:S(2)}, u32[]{:S(2)}) collective-permute-start(f32[1,64,1280]{2,1,0:T(8,128)S(1)} %get-tuple-element.21), channel_id=1, source_target_pairs={{0,2},{1,3},{2,0},{3,1},{4,6},{5,7},{6,4},{7,5},{8,10},{9,11},{10,... | collective-permute-start | bytes 983048 | tf_op jit(solution)/shard_map/ppermute | solution.py:260
  77.5 15.4 %collective-permute-start.22 = (f32[1,64,1280]{2,1,0:T(8,128)S(1)}, f32[1,64,1280]{2,1,0:T(8,128)S(1)}, u32[]{:S(2)}, u32[]{:S(2)}) collective-permute-start(f32[1,64,1280]{2,1,0:T(8,128)S(1)} %get-tuple-element.18), channel_id=1, source_target_pairs={{0,2},{1,3},{2,0},{3,1},{4,6},{5,7},{6,4},{7,5},{8,10},{9,11},{10,... | collective-permute-start | bytes 983048 | tf_op jit(solution)/shard_map/ppermute | solution.py:260
  77.7 22.2 %collective-permute-start.20 = (f32[1,64,1280]{2,1,0:T(8,128)S(1)}, f32[1,64,1280]{2,1,0:T(8,128)S(1)}, u32[]{:S(2)}, u32[]{:S(2)}) collective-permute-start(f32[1,64,1280]{2,1,0:T(8,128)S(1)} %get-tuple-element.15), channel_id=1, source_target_pairs={{0,2},{1,3},{2,0},{3,1},{4,6},{5,7},{6,4},{7,5},{8,10},{9,11},{10,... | collective-permute-start | bytes 983048 | tf_op jit(solution)/shard_map/ppermute | solution.py:260
  79.9 26.4 %collective-permute-start.18 = (f32[1,64,1280]{2,1,0:T(8,128)S(1)}, f32[1,64,1280]{2,1,0:T(8,128)S(1)}, u32[]{:S(2)}, u32[]{:S(2)}) collective-permute-start(f32[1,64,1280]{2,1,0:T(8,128)S(1)} %get-tuple-element.12), channel_id=1, source_target_pairs={{0,2},{1,3},{2,0},{3,1},{4,6},{5,7},{6,4},{7,5},{8,10},{9,11},{10,... | collective-permute-start | bytes 983048 | tf_op jit(solution)/shard_map/ppermute | solution.py:260

commit v21 on v20

--- a/solution.py
+++ b/solution.py
@@ -169,15 +169,13 @@
     slot_ids = jnp.arange(pack_len, dtype=jnp.int32)
     names_slot = my_slot_of_row[None, :] == slot_ids[:, None]
     source_of_slot = jnp.sum(jnp.where(names_slot, arrived_index[None, :], 0), axis=1)
-    packed_qkv = select_rows(source_of_slot, arrived)
-
     q_width = local_heads * head_dim
     kv_width = local_kv * head_dim
-    query_matrix = packed_qkv[:, :q_width].reshape(pack_len, local_kv, query_group_count, head_dim)
-    projected_key_rows = packed_qkv[:, q_width : q_width + kv_width].reshape(
-        pack_len, local_kv, head_dim
-    )
-    projected_value_rows = packed_qkv[:, q_width + kv_width :].reshape(pack_len, local_kv, head_dim)
+    packed_q = select_rows(source_of_slot, arrived[:, :q_width])
+    packed_kv = select_rows(source_of_slot, arrived[:, q_width:])
+    query_matrix = packed_q.reshape(pack_len, local_kv, query_group_count, head_dim)
+    projected_key_rows = packed_kv[:, :kv_width].reshape(pack_len, local_kv, head_dim)
+    projected_value_rows = packed_kv[:, kv_width:].reshape(pack_len, local_kv, head_dim)
 
     own_lengths = seq_len[0]
     own_ends = jnp.cumsum(own_lengths).astype(jnp.int32)

time: 109 us -> 109 us (level)
  no operation moved by 1% of the time
where the time goes in v21:
time: 109 us; the launch traced here: 107 us
  starting transfers between devices  34.3 us (31%)
  waiting for transfers between devices  31.8 us (29%)
  matrix products  21.9 us (20%)
  other arithmetic  12.6 us (12%)
  local copies, waits for them, and re-layouts  6.28 us (6%)
    ppermute x8, waiting for transfers between devices, halving_scatter(): got = lax.ppermute(send, axis_name, pairs)  26.2 us
    ppermute x7, starting transfers between devices, shift_gather(): lax.ppermute(part, axis_name, [(i, (i + shift) % count) for i in range(co...  12.5 us
    ppermute x7, starting transfers between devices, exchange(): arrived.append(lax.ppermute(chunks[shift], axis_name, pairs))  12.2 us
    dot_general x4, matrix products, local(): jnp.dot(mixed_heads, w_out, preferred_element_type=jnp.float32)  8.08 us
    dot_general x1, matrix products, project(): jnp.dot(normalized_input, w_query, preferred_element_type=jnp.float32)  7.56 us
    ppermute x8, starting transfers between devices, halving_scatter(): got = lax.ppermute(send, axis_name, pairs)  6.55 us
    ppermute x7, waiting for transfers between devices, exchange(): arrived.append(lax.ppermute(chunks[shift], axis_name, pairs))  3.6 us
    ppermute x3, starting transfers between devices, xor_gather(): pieces = pieces + [lax.ppermute(p, axis_name, pairs) for p in pieces]  3.01 us
  transfers between devices with their start and end apart: 25, of which 9 were waited for; matrix products, arithmetic and copies ran while one was open for 17% of the time, Pallas kernels for 0%

profile of v21, /device:TPU:0, one launch (start us, length us, event | category | flops | bytes accessed | tf_op | source)
XLA Modules:
  0.0 107.5 jit_solution(745701926516569052)
XLA Ops:
  0.0 3.0 %collective-permute-start = (bf16[96,5120]{1,0:T(8,128)(2,1)}, bf16[96,5120]{1,0:T(8,128)(2,1)S(1)}, u32[]{:S(2)}, u32[]{:S(2)}) collective-permute-start(bf16[96,5120]{1,0:T(8,128)(2,1)} %param.14), channel_id=1, source_target_pairs={{0,2},{1,3},{2,0},{3,1},{4,6},{5,7},{6,4},{7,5},{8,10},{9,11},{10,... | collective-permute-start | bytes 2949128 | tf_op jit(solution)/shard_map/ppermute | solution.py:287
  3.0 1.5 %collective-permute-start.3 = (s32[1,8]{1,0:T(1,128)}, s32[1,8]{1,0:T(1,128)S(1)}, u32[]{:S(2)}, u32[]{:S(2)}) collective-permute-start(s32[1,8]{1,0:T(1,128)} %param.16), channel_id=1, source_target_pairs={{0,4},{4,8},{8,12},{12,16},{16,20},{20,24},{24,28},{28,0},{1,5},{5... | collective-permute-start | bytes 104 | tf_op jit(solution)/shard_map/ppermute | solution.py:224
  4.5 1.6 %collective-permute-start.4 = (s32[1,8]{1,0:T(1,128)}, s32[1,8]{1,0:T(1,128)S(1)}, u32[]{:S(2)}, u32[]{:S(2)}) collective-permute-start(s32[1,8]{1,0:T(1,128)} %param.16), channel_id=1, source_target_pairs={{0,8},{4,12},{8,16},{12,20},{16,24},{20,28},{24,0},{28,4},{1,9},{5... | collective-permute-start | bytes 104 | tf_op jit(solution)/shard_map/ppermute | solution.py:224
  6.1 2.5 %collective-permute-start.5 = (s32[1,8]{1,0:T(1,128)}, s32[1,8]{1,0:T(1,128)S(1)}, u32[]{:S(2)}, u32[]{:S(2)}) collective-permute-start(s32[1,8]{1,0:T(1,128)} %param.16), channel_id=1, source_target_pairs={{0,12},{4,16},{8,20},{12,24},{16,28},{20,0},{24,4},{28,8},{1,13},{... | collective-permute-start | bytes 104 | tf_op jit(solution)/shard_map/ppermute | solution.py:224
  8.6 0.7 reshape.874
  9.5 0.7 constant_dynamic-update-slice_fusion.7
  10.2 0.8 reduce-window.32
  11.3 0.7 compare_and_fusion.4
  12.0 0.9 reduce-window.30
  12.9 0.2 slice_reduce_fusion
  13.3 0.6 gather_fusion.2
  13.9 0.6 gather_fusion.1
  14.8 0.7 subtract_select_fusion
  15.6 0.9 reduce-window.21
  16.5 0.2 slice_reduce_fusion.1
  16.9 0.7 pad_maximum_fusion.8
  18.0 1.3 %collective-permute-start.6 = (s32[1,8]{1,0:T(1,128)}, s32[1,8]{1,0:T(1,128)S(1)}, u32[]{:S(2)}, u32[]{:S(2)}) collective-permute-start(s32[1,8]{1,0:T(1,128)} %param.16), channel_id=1, source_target_pairs={{0,16},{4,20},{8,24},{12,28},{16,0},{20,4},{24,8},{28,12},{1,17},{... | collective-permute-start | bytes 104 | tf_op jit(solution)/shard_map/ppermute | solution.py:224
  19.3 2.6 %collective-permute-start.7 = (s32[1,8]{1,0:T(1,128)}, s32[1,8]{1,0:T(1,128)S(1)}, u32[]{:S(2)}, u32[]{:S(2)}) collective-permute-start(s32[1,8]{1,0:T(1,128)} %param.16), channel_id=1, source_target_pairs={{0,20},{4,24},{8,28},{12,0},{16,4},{20,8},{24,12},{28,16},{1,21},{... | collective-permute-start | bytes 104 | tf_op jit(solution)/shard_map/ppermute | solution.py:224
  21.9 1.3 %collective-permute-start.8 = (s32[1,8]{1,0:T(1,128)}, s32[1,8]{1,0:T(1,128)S(1)}, u32[]{:S(2)}, u32[]{:S(2)}) collective-permute-start(s32[1,8]{1,0:T(1,128)} %param.16), channel_id=1, source_target_pairs={{0,24},{4,28},{8,0},{12,4},{16,8},{20,12},{24,16},{28,20},{1,25},{... | collective-permute-start | bytes 104 | tf_op jit(solution)/shard_map/ppermute | solution.py:224
  23.3 1.6 %collective-permute-start.9 = (s32[1,8]{1,0:T(1,128)}, s32[1,8]{1,0:T(1,128)S(1)}, u32[]{:S(2)}, u32[]{:S(2)}) collective-permute-start(s32[1,8]{1,0:T(1,128)} %param.16), channel_id=1, source_target_pairs={{0,28},{4,0},{8,4},{12,8},{16,12},{20,16},{24,20},{28,24},{1,29},{... | collective-permute-start | bytes 104 | tf_op jit(solution)/shard_map/ppermute | solution.py:224
  24.9 0.7 collective-permute-done.8
  25.6 1.3 %collective-permute-done.9 = s32[1,8]{1,0:T(1,128)S(1)} collective-permute-done((s32[1,8]{1,0:T(1,128)}, s32[1,8]{1,0:T(1,128)S(1)}, u32[]{:S(2)}, u32[]{:S(2)}) %collective-permute-start.9) | collective-permute-done | bytes 64 | tf_op jit(solution)/shard_map/ppermute | solution.py:224
  27.0 0.6 gather_fusion
  27.9 0.4 multiply_cosine_fusion.1
  28.4 2.1 %fusion = f32[384]{0:T(512)S(1)} fusion(bf16[96,5120]{1,0:T(8,128)(2,1)} %collective-permute-done.2, bf16[96,5120]{1,0:T(8,128)(2,1)S(1)} %collective-permute-done.1, bf16[96,5120]{1,0:T(8,128)(2,1)S(1)} %collective-permute-done, bf16[96,5120]{1,0:T(8,128)(2,1)} %param.14), kind=kLoop, calls=%fused_computation.5 | loop fusion | flops 19660416 | bytes 3933696 | tf_op jit(solution)/shard_map/reduce_sum | solution.py:108
  30.5 7.6 %convolution_add_fusion = f32[384,640]{1,0:T(8,128)} fusion(bf16[5120,640]{1,0:T(8,128)(2,1)} %param.18, f32[5120]{0:T(1024)S(1)} %copy-done.3, f32[384]{0:T(512)S(1)} %add_rsqrt_fusion, f32[640]{0:T(1024)S(1)} %copy-done.4, bf16[96,5120]{1,0:T(8,128)(2,1)} %collective-permute-done.2, bf16[96,5120]{1,0:T(8,128)(2,1)S(1)} %collective-permute-done.1, ...), kind=kOutput, calls=%fused_computation.15 | convolution fusion | flops 2538455040 | bytes 11493376 | tf_op jit(solution)/shard_map/dot_general | solution.py:112
  38.1 2.4 %fusion.7 = f32[384,256]{1,0:T(8,128)S(1)} fusion(bf16[5120,128]{1,0:T(8,128)(2,1)S(1)} %copy-done.1, bf16[5120,128]{1,0:T(8,128)(2,1)S(1)} %copy-done.2, f32[5120]{0:T(1024)S(1)} %copy-done.3, f32[384]{0:T(512)S(1)} %add_rsqrt_fusion, f32[256]{0:T(256)S(1)} %pad_maximum_fusion.8, bf16[96,5120]{1,0:T(8,128)(2,1)} %collective-permute-done.2, ...), kind=kOutput, calls=%fused_computation.18 | convolution fusion | flops 1033601024 | bytes 6969856 | tf_op jit(solution)/shard_map/dot_general | solution.py:114
  40.6 0.3 convolution_convert_fusion.3
  40.8 0.8 fusion.61
  41.7 1.5 %copy.36 = f32[384,640]{0,1:T(8,128)S(1)} copy(f32[384,640]{1,0:T(8,128)} %convolution_add_fusion) | data formatting | bytes 1966080 | tf_op jit(solution)/shard_map/optimization_barrier | solution.py:120
  43.4 0.4 convolution_convert_fusion
  43.9 0.3 convolution_convert_fusion.4
  44.3 1.8 %collective-permute-start.10 = (bf16[48,896]{1,0:T(8,128)(2,1)S(1)}, bf16[48,896]{1,0:T(8,128)(2,1)S(1)}, u32[]{:S(2)}, u32[]{:S(2)}) collective-permute-start(bf16[48,896]{1,0:T(8,128)(2,1)S(1)} %get-tuple-element.44), channel_id=1, source_target_pairs={{0,4},{4,8},{8,12},{12,16},{16,20},{20,24},{24,28},{28,0},{1,5},{5... | collective-permute-start | bytes 258056 | tf_op jit(solution)/shard_map/ppermute | solution.py:240
  46.1 0.4 select_reduce_fusion
  46.6 1.0 collective-permute-start.11
  47.5 2.5 %collective-permute-start.12 = (bf16[48,896]{1,0:T(8,128)(2,1)S(1)}, bf16[48,896]{1,0:T(8,128)(2,1)S(1)}, u32[]{:S(2)}, u32[]{:S(2)}) collective-permute-start(bf16[48,896]{1,0:T(8,128)(2,1)S(1)} %get-tuple-element.42), channel_id=1, source_target_pairs={{0,12},{4,16},{8,20},{12,24},{16,28},{20,0},{24,4},{28,8},{1,13},{... | collective-permute-start | bytes 258056 | tf_op jit(solution)/shard_map/ppermute | solution.py:240
  50.1 1.2 %collective-permute-start.13 = (bf16[48,896]{1,0:T(8,128)(2,1)S(1)}, bf16[48,896]{1,0:T(8,128)(2,1)S(1)}, u32[]{:S(2)}, u32[]{:S(2)}) collective-permute-start(bf16[48,896]{1,0:T(8,128)(2,1)S(1)} %get-tuple-element.41), channel_id=1, source_target_pairs={{0,16},{4,20},{8,24},{12,28},{16,0},{20,4},{24,8},{28,12},{1,17},{... | collective-permute-start | bytes 258056 | tf_op jit(solution)/shard_map/ppermute | solution.py:240
  51.3 2.8 %collective-permute-start.14 = (bf16[48,896]{1,0:T(8,128)(2,1)S(1)}, bf16[48,896]{1,0:T(8,128)(2,1)S(1)}, u32[]{:S(2)}, u32[]{:S(2)}) collective-permute-start(bf16[48,896]{1,0:T(8,128)(2,1)S(1)} %get-tuple-element.40), channel_id=1, source_target_pairs={{0,20},{4,24},{8,28},{12,0},{16,4},{20,8},{24,12},{28,16},{1,21},{... | collective-permute-start | bytes 258056 | tf_op jit(solution)/shard_map/ppermute | solution.py:240
  54.1 1.1 %collective-permute-start.15 = (bf16[48,896]{1,0:T(8,128)(2,1)S(1)}, bf16[48,896]{1,0:T(8,128)(2,1)S(1)}, u32[]{:S(2)}, u32[]{:S(2)}) collective-permute-start(bf16[48,896]{1,0:T(8,128)(2,1)S(1)} %get-tuple-element.39), channel_id=1, source_target_pairs={{0,24},{4,28},{8,0},{12,4},{16,8},{20,12},{24,16},{28,20},{1,25},{... | collective-permute-start | bytes 258056 | tf_op jit(solution)/shard_map/ppermute | solution.py:240
  55.3 1.6 %collective-permute-start.16 = (bf16[48,896]{1,0:T(8,128)(2,1)S(1)}, bf16[48,896]{1,0:T(8,128)(2,1)S(1)}, u32[]{:S(2)}, u32[]{:S(2)}) collective-permute-start(bf16[48,896]{1,0:T(8,128)(2,1)S(1)} %get-tuple-element.38), channel_id=1, source_target_pairs={{0,28},{4,0},{8,4},{12,8},{16,12},{20,16},{24,20},{28,24},{1,29},{... | collective-permute-start | bytes 258056 | tf_op jit(solution)/shard_map/ppermute | solution.py:240
  57.0 2.2 %collective-permute-done.12 = bf16[48,896]{1,0:T(8,128)(2,1)S(1)} collective-permute-done((bf16[48,896]{1,0:T(8,128)(2,1)S(1)}, bf16[48,896]{1,0:T(8,128)(2,1)S(1)}, u32[]{:S(2)}, u32[]{:S(2)}) %collective-permute-start.12) | collective-permute-done | bytes 86048 | tf_op jit(solution)/shard_map/ppermute | solution.py:240
  59.2 1.2 %collective-permute-done.13 = bf16[48,896]{1,0:T(8,128)(2,1)S(1)} collective-permute-done((bf16[48,896]{1,0:T(8,128)(2,1)S(1)}, bf16[48,896]{1,0:T(8,128)(2,1)S(1)}, u32[]{:S(2)}, u32[]{:S(2)}) %collective-permute-start.13) | collective-permute-done | bytes 86048 | tf_op jit(solution)/shard_map/ppermute | solution.py:240
  60.7 0.4 convolution_convert_fusion.1
  61.1 0.3 convolution_convert_fusion.2
  61.4 0.3 fusion.140
  61.9 0.3 fusion.21
  62.3 4.3 %fusion.62 = f32[64,5120]{1,0:T(8,128)S(1)} fusion(bf16[640,5120]{1,0:T(8,128)(2,1)} %param.24, bf16[8,8,5,128]{3,2,1,0:T(8,128)(2,1)S(1)} %bitcast.290), kind=kOutput, calls=%fused_computation.132 | convolution fusion | flops 419430400 | bytes 7946240 | tf_op jit(solution)/shard_map/dot_general | solution.py:214
  66.7 0.3 fusion.141
  67.3 0.3 fusion.20
  67.6 1.3 %fusion.65 = f32[64,5120]{1,0:T(8,128)S(1)} fusion(bf16[640,5120]{1,0:T(8,128)(2,1)S(1)} %bitcast.287, bf16[8,8,5,128]{3,2,1,0:T(8,128)(2,1)S(1)} %bitcast.291), kind=kOutput, calls=%fused_computation.135 | convolution fusion | flops 419430400 | bytes 7946240 | tf_op jit(solution)/shard_map/dot_general | solution.py:214
  69.0 0.6 collective-permute-start.21
  69.6 0.3 fusion.142
  70.1 0.3 fusion.23
  70.4 1.3 %fusion.68 = f32[64,5120]{1,0:T(8,128)S(1)} fusion(bf16[640,5120]{1,0:T(8,128)(2,1)S(1)} %bitcast.287, bf16[8,8,5,128]{3,2,1,0:T(8,128)(2,1)S(1)} %bitcast.292), kind=kOutput, calls=%fused_computation.138 | convolution fusion | flops 419430400 | bytes 7946240 | tf_op jit(solution)/shard_map/dot_general | solution.py:214
  72.2 0.2 fusion.22
  72.5 1.3 %fusion.71 = f32[64,5120]{1,0:T(8,128)S(1)} fusion(bf16[640,5120]{1,0:T(8,128)(2,1)S(1)} %bitcast.287, bf16[8,8,5,128]{3,2,1,0:T(8,128)(2,1)S(1)} %bitcast.293), kind=kOutput, calls=%fused_computation.141 | convolution fusion | flops 419430400 | bytes 7946240 | tf_op jit(solution)/shard_map/dot_general | solution.py:214
  73.9 0.6 collective-permute-start.17
  74.5 3.0 %collective-permute-start.24 = (f32[1,64,1280]{2,1,0:T(8,128)S(1)}, f32[1,64,1280]{2,1,0:T(8,128)S(1)}, u32[]{:S(2)}, u32[]{:S(2)}) collective-permute-start(f32[1,64,1280]{2,1,0:T(8,128)S(1)} %get-tuple-element.21), channel_id=1, source_target_pairs={{0,2},{1,3},{2,0},{3,1},{4,6},{5,7},{6,4},{7,5},{8,10},{9,11},{10,... | collective-permute-start | bytes 983048 | tf_op jit(solution)/shard_map/ppermute | solution.py:258
  77.9 2.1 %collective-permute-start.20 = (f32[1,64,1280]{2,1,0:T(8,128)S(1)}, f32[1,64,1280]{2,1,0:T(8,128)S(1)}, u32[]{:S(2)}, u32[]{:S(2)}) collective-permute-start(f32[1,64,1280]{2,1,0:T(8,128)S(1)} %get-tuple-element.15), channel_id=1, source_target_pairs={{0,2},{1,3},{2,0},{3,1},{4,6},{5,7},{6,4},{7,5},{8,10},{9,11},{10,... | collective-permute-start | bytes 983048 | tf_op jit(solution)/shard_map/ppermute | solution.py:258
  80.2 5.9 %collective-permute-done.24 = f32[1,64,1280]{2,1,0:T(8,128)S(1)} collective-permute-done((f32[1,64,1280]{2,1,0:T(8,128)S(1)}, f32[1,64,1280]{2,1,0:T(8,128)S(1)}, u32[]{:S(2)}, u32[]{:S(2)}) %collective-permute-start.24) | collective-permute-done | bytes 327712 | tf_op jit(solution)/shard_map/ppermute | solution.py:258
  86.1 7.0 %collective-permute-done.22 = f32[1,64,1280]{2,1,0:T(8,128)S(1)} collective-permute-done((f32[1,64,1280]{2,1,0:T(8,128)S(1)}, f32[1,64,1280]{2,1,0:T(8,128)S(1)}, u32[]{:S(2)}, u32[]{:S(2)}) %collective-permute-start.22) | collective-permute-done | bytes 327712 | tf_op jit(solution)/shard_map/ppermute | solution.py:258
  93.2 7.0 %collective-permute-done.20 = f32[1,64,1280]{2,1,0:T(8,128)S(1)} collective-permute-done((f32[1,64,1280]{2,1,0:T(8,128)S(1)}, f32[1,64,1280]{2,1,0:T(8,128)S(1)}, u32[]{:S(2)}, u32[]{:S(2)}) %collective-permute-start.20) | collective-permute-done | bytes 327712 | tf_op jit(solution)/shard_map/ppermute | solution.py:258
  100.2 6.4 %collective-permute-done.18 = f32[1,64,1280]{2,1,0:T(8,128)S(1)} collective-permute-done((f32[1,64,1280]{2,1,0:T(8,128)S(1)}, f32[1,64,1280]{2,1,0:T(8,128)S(1)}, u32[]{:S(2)}, u32[]{:S(2)}) %collective-permute-start.18) | collective-permute-done | bytes 327712 | tf_op jit(solution)/shard_map/ppermute | solution.py:258
  106.6 0.9 pad_maximum_fusion.6
  (135 shorter events, 5.2 us)
Async XLA Ops:
  0.0 30.5 %copy-start = (bf16[96,5120]{1,0:T(8,128)(2,1)S(1)}, bf16[96,5120]{1,0:T(8,128)(2,1)}, u32[]{:S(2)}) copy-start(bf16[96,5120]{1,0:T(8,128)(2,1)} %param.14) | copy-start | bytes 2949124
  0.0 30.5 %copy-start.3 = (f32[5120]{0:T(1024)S(1)}, f32[5120]{0:T(1024)}, u32[]{:S(2)}) copy-start(f32[5120]{0:T(1024)} %param.17) | copy-start | bytes 61444
  0.0 30.5 %copy-start.4 = (f32[640]{0:T(1024)S(1)}, f32[640]{0:T(1024)}, u32[]{:S(2)}) copy-start(f32[640]{0:T(1024)} %param.19) | copy-start | bytes 7684
  0.0 25.6 %collective-permute-start = (bf16[96,5120]{1,0:T(8,128)(2,1)}, bf16[96,5120]{1,0:T(8,128)(2,1)S(1)}, u32[]{:S(2)}, u32[]{:S(2)}) collective-permute-start(bf16[96,5120]{1,0:T(8,128)(2,1)} %param.14), channel_id=1, source_target_pairs={{0,2},{1,3},{2,0},{3,1},{4,6},{5,7},{6,4},{7,5},{8,10},{9,11},{10,... | collective-permute-start | bytes 2949128 | tf_op jit(solution)/shard_map/ppermute | solution.py:287
  3.0 25.3 %collective-permute-start.1 = (bf16[96,5120]{1,0:T(8,128)(2,1)}, bf16[96,5120]{1,0:T(8,128)(2,1)S(1)}, u32[]{:S(2)}, u32[]{:S(2)}) collective-permute-start(bf16[96,5120]{1,0:T(8,128)(2,1)} %param.14), channel_id=1, source_target_pairs={{0,1},{1,0},{2,3},{3,2},{4,5},{5,4},{6,7},{7,6},{8,9},{9,8},{10,11... | collective-permute-start | bytes 2949128 | tf_op jit(solution)/shard_map/ppermute | solution.py:287
  3.0 15.0 %collective-permute-start.3 = (s32[1,8]{1,0:T(1,128)}, s32[1,8]{1,0:T(1,128)S(1)}, u32[]{:S(2)}, u32[]{:S(2)}) collective-permute-start(s32[1,8]{1,0:T(1,128)} %param.16), channel_id=1, source_target_pairs={{0,4},{4,8},{8,12},{12,16},{16,20},{20,24},{24,28},{28,0},{1,5},{5... | collective-permute-start | bytes 104 | tf_op jit(solution)/shard_map/ppermute | solution.py:224
  4.5 14.8 %collective-permute-start.4 = (s32[1,8]{1,0:T(1,128)}, s32[1,8]{1,0:T(1,128)S(1)}, u32[]{:S(2)}, u32[]{:S(2)}) collective-permute-start(s32[1,8]{1,0:T(1,128)} %param.16), channel_id=1, source_target_pairs={{0,8},{4,12},{8,16},{12,20},{16,24},{20,28},{24,0},{28,4},{1,9},{5... | collective-permute-start | bytes 104 | tf_op jit(solution)/shard_map/ppermute | solution.py:224
  6.1 15.8 %collective-permute-start.5 = (s32[1,8]{1,0:T(1,128)}, s32[1,8]{1,0:T(1,128)S(1)}, u32[]{:S(2)}, u32[]{:S(2)}) collective-permute-start(s32[1,8]{1,0:T(1,128)} %param.16), channel_id=1, source_target_pairs={{0,12},{4,16},{8,20},{12,24},{16,28},{20,0},{24,4},{28,8},{1,13},{... | collective-permute-start | bytes 104 | tf_op jit(solution)/shard_map/ppermute | solution.py:224
  18.0 5.3 %collective-permute-start.6 = (s32[1,8]{1,0:T(1,128)}, s32[1,8]{1,0:T(1,128)S(1)}, u32[]{:S(2)}, u32[]{:S(2)}) collective-permute-start(s32[1,8]{1,0:T(1,128)} %param.16), channel_id=1, source_target_pairs={{0,16},{4,20},{8,24},{12,28},{16,0},{20,4},{24,8},{28,12},{1,17},{... | collective-permute-start | bytes 104 | tf_op jit(solution)/shard_map/ppermute | solution.py:224
  19.3 5.6 %collective-permute-start.7 = (s32[1,8]{1,0:T(1,128)}, s32[1,8]{1,0:T(1,128)S(1)}, u32[]{:S(2)}, u32[]{:S(2)}) collective-permute-start(s32[1,8]{1,0:T(1,128)} %param.16), channel_id=1, source_target_pairs={{0,20},{4,24},{8,28},{12,0},{16,4},{20,8},{24,12},{28,16},{1,21},{... | collective-permute-start | bytes 104 | tf_op jit(solution)/shard_map/ppermute | solution.py:224
  21.9 3.7 %collective-permute-start.8 = (s32[1,8]{1,0:T(1,128)}, s32[1,8]{1,0:T(1,128)S(1)}, u32[]{:S(2)}, u32[]{:S(2)}) collective-permute-start(s32[1,8]{1,0:T(1,128)} %param.16), channel_id=1, source_target_pairs={{0,24},{4,28},{8,0},{12,4},{16,8},{20,12},{24,16},{28,20},{1,25},{... | collective-permute-start | bytes 104 | tf_op jit(solution)/shard_map/ppermute | solution.py:224
  23.3 3.7 %collective-permute-start.9 = (s32[1,8]{1,0:T(1,128)}, s32[1,8]{1,0:T(1,128)S(1)}, u32[]{:S(2)}, u32[]{:S(2)}) collective-permute-start(s32[1,8]{1,0:T(1,128)} %param.16), channel_id=1, source_target_pairs={{0,28},{4,0},{8,4},{12,8},{16,12},{20,16},{24,20},{28,24},{1,29},{... | collective-permute-start | bytes 104 | tf_op jit(solution)/shard_map/ppermute | solution.py:224
  25.6 2.7 %collective-permute-start.2 = (bf16[96,5120]{1,0:T(8,128)(2,1)S(1)}, bf16[96,5120]{1,0:T(8,128)(2,1)}, u32[]{:S(2)}, u32[]{:S(2)}) collective-permute-start(bf16[96,5120]{1,0:T(8,128)(2,1)S(1)} %collective-permute-done), channel_id=1, source_target_pairs={{0,1},{1,0},{2,3},{3,2},{4,5},{5,4},{6,7},{7,6},{8,9},{9,8},{10,11... | collective-permute-start | bytes 2949128 | tf_op jit(solution)/shard_map/ppermute | solution.py:287
  30.5 7.6 %copy-start.1 = (bf16[5120,128]{1,0:T(8,128)(2,1)S(1)}, bf16[5120,128]{1,0:T(8,128)(2,1)}, u32[]{:S(2)}) copy-start(bf16[5120,128]{1,0:T(8,128)(2,1)} %param.22) | copy-start | bytes 3932164
  30.5 7.6 %copy-start.2 = (bf16[5120,128]{1,0:T(8,128)(2,1)S(1)}, bf16[5120,128]{1,0:T(8,128)(2,1)}, u32[]{:S(2)}) copy-start(bf16[5120,128]{1,0:T(8,128)(2,1)} %param.20) | copy-start | bytes 3932164
  44.3 9.8 %collective-permute-start.10 = (bf16[48,896]{1,0:T(8,128)(2,1)S(1)}, bf16[48,896]{1,0:T(8,128)(2,1)S(1)}, u32[]{:S(2)}, u32[]{:S(2)}) collective-permute-start(bf16[48,896]{1,0:T(8,128)(2,1)S(1)} %get-tuple-element.44), channel_id=1, source_target_pairs={{0,4},{4,8},{8,12},{12,16},{16,20},{20,24},{24,28},{28,0},{1,5},{5... | collective-permute-start | bytes 258056 | tf_op jit(solution)/shard_map/ppermute | solution.py:240
  46.6 8.8 %collective-permute-start.11 = (bf16[48,896]{1,0:T(8,128)(2,1)S(1)}, bf16[48,896]{1,0:T(8,128)(2,1)S(1)}, u32[]{:S(2)}, u32[]{:S(2)}) collective-permute-start(bf16[48,896]{1,0:T(8,128)(2,1)S(1)} %get-tuple-element.43), channel_id=1, source_target_pairs={{0,8},{4,12},{8,16},{12,20},{16,24},{20,28},{24,0},{28,4},{1,9},{5... | collective-permute-start | bytes 258056 | tf_op jit(solution)/shard_map/ppermute | solution.py:240
  47.5 11.7 %collective-permute-start.12 = (bf16[48,896]{1,0:T(8,128)(2,1)S(1)}, bf16[48,896]{1,0:T(8,128)(2,1)S(1)}, u32[]{:S(2)}, u32[]{:S(2)}) collective-permute-start(bf16[48,896]{1,0:T(8,128)(2,1)S(1)} %get-tuple-element.42), channel_id=1, source_target_pairs={{0,12},{4,16},{8,20},{12,24},{16,28},{20,0},{24,4},{28,8},{1,13},{... | collective-permute-start | bytes 258056 | tf_op jit(solution)/shard_map/ppermute | solution.py:240
  50.1 10.4 %collective-permute-start.13 = (bf16[48,896]{1,0:T(8,128)(2,1)S(1)}, bf16[48,896]{1,0:T(8,128)(2,1)S(1)}, u32[]{:S(2)}, u32[]{:S(2)}) collective-permute-start(bf16[48,896]{1,0:T(8,128)(2,1)S(1)} %get-tuple-element.41), channel_id=1, source_target_pairs={{0,16},{4,20},{8,24},{12,28},{16,0},{20,4},{24,8},{28,12},{1,17},{... | collective-permute-start | bytes 258056 | tf_op jit(solution)/shard_map/ppermute | solution.py:240
  51.3 9.2 %collective-permute-start.14 = (bf16[48,896]{1,0:T(8,128)(2,1)S(1)}, bf16[48,896]{1,0:T(8,128)(2,1)S(1)}, u32[]{:S(2)}, u32[]{:S(2)}) collective-permute-start(bf16[48,896]{1,0:T(8,128)(2,1)S(1)} %get-tuple-element.40), channel_id=1, source_target_pairs={{0,20},{4,24},{8,28},{12,0},{16,4},{20,8},{24,12},{28,16},{1,21},{... | collective-permute-start | bytes 258056 | tf_op jit(solution)/shard_map/ppermute | solution.py:240
  54.1 6.4 %collective-permute-start.15 = (bf16[48,896]{1,0:T(8,128)(2,1)S(1)}, bf16[48,896]{1,0:T(8,128)(2,1)S(1)}, u32[]{:S(2)}, u32[]{:S(2)}) collective-permute-start(bf16[48,896]{1,0:T(8,128)(2,1)S(1)} %get-tuple-element.39), channel_id=1, source_target_pairs={{0,24},{4,28},{8,0},{12,4},{16,8},{20,12},{24,16},{28,20},{1,25},{... | collective-permute-start | bytes 258056 | tf_op jit(solution)/shard_map/ppermute | solution.py:240
  55.3 5.3 %collective-permute-start.16 = (bf16[48,896]{1,0:T(8,128)(2,1)S(1)}, bf16[48,896]{1,0:T(8,128)(2,1)S(1)}, u32[]{:S(2)}, u32[]{:S(2)}) collective-permute-start(bf16[48,896]{1,0:T(8,128)(2,1)S(1)} %get-tuple-element.38), channel_id=1, source_target_pairs={{0,28},{4,0},{8,4},{12,8},{16,12},{20,16},{24,20},{28,24},{1,29},{... | collective-permute-start | bytes 258056 | tf_op jit(solution)/shard_map/ppermute | solution.py:240
  62.2 5.4 %slice-start = ((s8[6553600]{0:T(1024)(128)(4,1)}), s8[4194304]{0:T(1024)(128)(4,1)S(1)}, s32[]{:S(2)}) async-start(s8[6553600]{0:T(1024)(128)(4,1)} %bitcast.286), calls=%async_computation | async-start | bytes 8388608
  62.2 5.4 %slice-start.1 = ((s8[6553600]{0:T(1024)(128)(4,1)}), s8[2359296]{0:T(1024)(128)(4,1)S(1)}, s32[]{:S(2)}) async-start(s8[6553600]{0:T(1024)(128)(4,1)} %bitcast.286), calls=%async_computation.1 | async-start | bytes 4718592
  66.7 7.8 %collective-permute-start.23 = (f32[2,64,1280]{2,1,0:T(8,128)S(1)}, f32[2,64,1280]{2,1,0:T(8,128)S(1)}, u32[]{:S(2)}, u32[]{:S(2)}) collective-permute-start(f32[2,64,1280]{2,1,0:T(8,128)S(1)} %pad_maximum_fusion.5), channel_id=1, source_target_pairs={{0,1},{1,0},{2,3},{3,2},{4,5},{5,4},{6,7},{7,6},{8,9},{9,8},{10,11... | collective-permute-start | bytes 1966088 | tf_op jit(solution)/shard_map/ppermute | solution.py:258
  69.0 8.5 %collective-permute-start.21 = (f32[2,64,1280]{2,1,0:T(8,128)S(1)}, f32[2,64,1280]{2,1,0:T(8,128)S(1)}, u32[]{:S(2)}, u32[]{:S(2)}) collective-permute-start(f32[2,64,1280]{2,1,0:T(8,128)S(1)} %pad_maximum_fusion.4), channel_id=1, source_target_pairs={{0,1},{1,0},{2,3},{3,2},{4,5},{5,4},{6,7},{7,6},{8,9},{9,8},{10,11... | collective-permute-start | bytes 1966088 | tf_op jit(solution)/shard_map/ppermute | solution.py:258
  71.8 5.9 %collective-permute-start.19 = (f32[2,64,1280]{2,1,0:T(8,128)S(1)}, f32[2,64,1280]{2,1,0:T(8,128)S(1)}, u32[]{:S(2)}, u32[]{:S(2)}) collective-permute-start(f32[2,64,1280]{2,1,0:T(8,128)S(1)} %pad_maximum_fusion.3), channel_id=1, source_target_pairs={{0,1},{1,0},{2,3},{3,2},{4,5},{5,4},{6,7},{7,6},{8,9},{9,8},{10,11... | collective-permute-start | bytes 1966088 | tf_op jit(solution)/shard_map/ppermute | solution.py:258
  73.9 6.1 %collective-permute-start.17 = (f32[2,64,1280]{2,1,0:T(8,128)S(1)}, f32[2,64,1280]{2,1,0:T(8,128)S(1)}, u32[]{:S(2)}, u32[]{:S(2)}) collective-permute-start(f32[2,64,1280]{2,1,0:T(8,128)S(1)} %pad_maximum_fusion.2), channel_id=1, source_target_pairs={{0,1},{1,0},{2,3},{3,2},{4,5},{5,4},{6,7},{7,6},{8,9},{9,8},{10,11... | collective-permute-start | bytes 1966088 | tf_op jit(solution)/shard_map/ppermute | solution.py:258
  74.5 11.5 %collective-permute-start.24 = (f32[1,64,1280]{2,1,0:T(8,128)S(1)}, f32[1,64,1280]{2,1,0:T(8,128)S(1)}, u32[]{:S(2)}, u32[]{:S(2)}) collective-permute-start(f32[1,64,1280]{2,1,0:T(8,128)S(1)} %get-tuple-element.21), channel_id=1, source_target_pairs={{0,2},{1,3},{2,0},{3,1},{4,6},{5,7},{6,4},{7,5},{8,10},{9,11},{10,... | collective-permute-start | bytes 983048 | tf_op jit(solution)/shard_map/ppermute | solution.py:258
  77.7 15.4 %collective-permute-start.22 = (f32[1,64,1280]{2,1,0:T(8,128)S(1)}, f32[1,64,1280]{2,1,0:T(8,128)S(1)}, u32[]{:S(2)}, u32[]{:S(2)}) collective-permute-start(f32[1,64,1280]{2,1,0:T(8,128)S(1)} %get-tuple-element.18), channel_id=1, source_target_pairs={{0,2},{1,3},{2,0},{3,1},{4,6},{5,7},{6,4},{7,5},{8,10},{9,11},{10,... | collective-permute-start | bytes 983048 | tf_op jit(solution)/shard_map/ppermute | solution.py:258
  77.9 22.2 %collective-permute-start.20 = (f32[1,64,1280]{2,1,0:T(8,128)S(1)}, f32[1,64,1280]{2,1,0:T(8,128)S(1)}, u32[]{:S(2)}, u32[]{:S(2)}) collective-permute-start(f32[1,64,1280]{2,1,0:T(8,128)S(1)} %get-tuple-element.15), channel_id=1, source_target_pairs={{0,2},{1,3},{2,0},{3,1},{4,6},{5,7},{6,4},{7,5},{8,10},{9,11},{10,... | collective-permute-start | bytes 983048 | tf_op jit(solution)/shard_map/ppermute | solution.py:258
  80.1 26.4 %collective-permute-start.18 = (f32[1,64,1280]{2,1,0:T(8,128)S(1)}, f32[1,64,1280]{2,1,0:T(8,128)S(1)}, u32[]{:S(2)}, u32[]{:S(2)}) collective-permute-start(f32[1,64,1280]{2,1,0:T(8,128)S(1)} %get-tuple-element.12), channel_id=1, source_target_pairs={{0,2},{1,3},{2,0},{3,1},{4,6},{5,7},{6,4},{7,5},{8,10},{9,11},{10,... | collective-permute-start | bytes 983048 | tf_op jit(solution)/shard_map/ppermute | solution.py:258
